TPU v7x, 32 devices: a whole 2x2x4 slice. The times are simulated.
32 devices in a mesh: seq: 8 (over z, y), grp: 4 (over x, core).
Axes of the slice: x: 2, y: 2, z: 4, core: 2. Of those that a mesh axis runs over, the one named last changes fastest.
Arguments:
- query_rows: bfloat16 [4096, 8192], P(('seq', 'grp')), may hold values from -6 to 6
- key_matrix: bfloat16 [4096, 1024], P(('seq', 'grp')), may hold values from -6 to 6
- value_matrix: bfloat16 [4096, 1024], P(('seq', 'grp')), may hold values from -6 to 6
- vertical: int32 [64, 3], replicated, may hold values from 0 to 63, as said below
- slash_offsets: int32 [64, 3], replicated, may hold values from 0 to 8, as said below
Outputs:
- attended: bfloat16 [4096, 8192], P(('seq', 'grp'))
Inputs may be any that keep to these rules, and one draw needn't show every extreme that they name: Each head's vertical blocks are distinct and rise along the row. `slash_offsets`: column 0 is 0; each head's offsets are distinct and rise along the row.
All inputs are finite; a program needn't handle non-finite values.
Results may differ from a plain program's by a relative error of at most 0.0043.
Values may be sent and summed in bfloat16 or wider, within the bound.
No kernel may reach another device: no remote copies, remote signals or barrier semaphores. Data moves between devices by JAX's collectives and lax.ppermute only.
A program may use at most 64 MiB of HBM per device.

v0:
```python
import jax
import jax.numpy as jnp
from jax import lax
from jax.sharding import PartitionSpec as P

HEAD_DIMENSION = 128
MASK_BLOCK_SIZE = 64


def passed_along(shard, axis, by):
    length = lax.axis_size(axis)
    pairs = [(i, i + by) for i in range(length) if 0 <= i + by < length]
    return lax.ppermute(shard, axis, pairs)


def head_attention(
    query_block, slash_keys, slash_values, vert_keys, vert_values, offsets, vert_blocks, first_block
):
    block_count, block_size, head_size = query_block.shape
    vert_tiled = jnp.broadcast_to(vert_keys[None], (block_count,) + vert_keys.shape)
    vert_vtiled = jnp.broadcast_to(vert_values[None], (block_count,) + vert_values.shape)
    all_keys = jnp.concatenate([slash_keys, vert_tiled], 1).reshape(block_count, -1, head_size)
    all_values = jnp.concatenate([slash_values, vert_vtiled], 1).reshape(block_count, -1, head_size)
    scores = jnp.einsum(
        "qid,qkd->qik", query_block, all_keys, preferred_element_type=jnp.float32
    ) * head_size ** (-0.5)
    query_index = first_block + jnp.arange(block_count, dtype=jnp.int32)
    slash_block = query_index[:, None] - offsets[None, :]
    slash_good = slash_block >= 0
    vert_good = (vert_blocks[None, :] <= query_index[:, None]) & jnp.all(
        query_index[:, None, None] - vert_blocks[None, :, None] != offsets[None, None, :], axis=2
    )
    block_ids = jnp.concatenate(
        [slash_block, jnp.broadcast_to(vert_blocks[None, :], (block_count, vert_blocks.shape[0]))],
        1,
    )
    block_good = jnp.concatenate([slash_good, vert_good], 1)
    position = jnp.arange(block_size, dtype=jnp.int32)
    key_pos = (block_ids[:, :, None] * block_size + position[None, None, :]).reshape(
        block_count, -1
    )
    query_pos = query_index[:, None] * block_size + position[None, :]
    allowed = jnp.repeat(block_good, block_size, axis=1)[:, None, :] & (
        key_pos[:, None, :] <= query_pos[:, :, None]
    )
    masked = jnp.where(allowed, scores, -1e30)
    row_top = jnp.max(masked, axis=2, keepdims=True)
    weight = jnp.where(allowed, jnp.exp(masked - row_top), 0.0)
    row_total = jnp.sum(weight, axis=2, keepdims=True)
    rounded = weight.astype(jnp.bfloat16)
    result = (
        jnp.einsum("qik,qkd->qid", rounded, all_values, preferred_element_type=jnp.float32)
        / row_total
    )
    return result.astype(jnp.bfloat16)


def per_device(query_rows, key_matrix, value_matrix, vertical, slash_offsets):
    tok_rows = query_rows.shape[0]
    grp_count = lax.axis_size("grp")
    head_size = HEAD_DIMENSION
    block_size = MASK_BLOCK_SIZE
    local_heads = query_rows.shape[1] // (grp_count * head_size)
    local_kv = key_matrix.shape[1] // (grp_count * head_size)
    group_sharing_factor = local_heads // local_kv
    query_split = query_rows.reshape(tok_rows, grp_count, local_heads * head_size)
    key_split = key_matrix.reshape(tok_rows, grp_count, local_kv * head_size)
    value_split = value_matrix.reshape(tok_rows, grp_count, local_kv * head_size)
    query_group, key_group, value_group = (
        lax.all_to_all(query_split, "grp", split_axis=1, concat_axis=0, tiled=True),
        lax.all_to_all(key_split, "grp", split_axis=1, concat_axis=0, tiled=True),
        lax.all_to_all(value_split, "grp", split_axis=1, concat_axis=0, tiled=True),
    )
    group_rows = tok_rows * grp_count
    group_blocks = group_rows // block_size
    key_local = key_group.reshape(group_rows, local_kv, head_size)
    value_local = value_group.reshape(group_rows, local_kv, head_size)
    key_before, value_before = passed_along((key_local, value_local), "seq", 1)
    key_window = (
        jnp.concatenate([key_before, key_local], 0)
        .reshape(2 * group_blocks, block_size, local_kv, head_size)
        .transpose(2, 0, 1, 3)
    )
    value_window = (
        jnp.concatenate([value_before, value_local], 0)
        .reshape(2 * group_blocks, block_size, local_kv, head_size)
        .transpose(2, 0, 1, 3)
    )
    seq_index = lax.axis_index("seq")
    grp_index = lax.axis_index("grp")
    head_offsets = lax.dynamic_slice_in_dim(slash_offsets, grp_index * local_heads, local_heads, 0)
    head_verts = lax.dynamic_slice_in_dim(vertical, grp_index * local_heads, local_heads, 0)
    kv_index = jnp.arange(local_heads, dtype=jnp.int32) // group_sharing_factor
    owner_seq = head_verts // group_blocks
    local_block = head_verts % group_blocks
    key_own = key_window[:, group_blocks:]
    value_own = value_window[:, group_blocks:]
    picked_keys = key_own[kv_index[:, None], local_block]
    picked_values = value_own[kv_index[:, None], local_block]
    owned = (owner_seq == seq_index)[:, :, None, None]
    nothing = jnp.zeros((), jnp.float32)
    summed_keys, summed_values = lax.psum(
        (
            jnp.where(owned, picked_keys.astype(jnp.float32), nothing),
            jnp.where(owned, picked_values.astype(jnp.float32), nothing),
        ),
        "seq",
    )
    vert_keys = summed_keys.astype(jnp.bfloat16)
    vert_values = summed_values.astype(jnp.bfloat16)
    head_queries = (
        query_group.reshape(group_rows, local_heads, head_size)
        .transpose(1, 0, 2)
        .reshape(local_heads, group_blocks, block_size, head_size)
    )
    nearby = jnp.arange(group_blocks, dtype=jnp.int32)
    first_block = seq_index * group_blocks

    def per_head(items):
        queries_one, offsets, vert_blocks, vert_key, vert_value, kv_one = items
        window_index = group_blocks + nearby[:, None] - offsets[None, :]
        slash_keys = key_window[kv_one][window_index]
        slash_values = value_window[kv_one][window_index]
        return head_attention(
            queries_one,
            slash_keys,
            slash_values,
            vert_key,
            vert_value,
            offsets,
            vert_blocks,
            first_block,
        )

    results = lax.map(
        per_head, (head_queries, head_offsets, head_verts, vert_keys, vert_values, kv_index)
    )
    merged = (
        results.reshape(local_heads, group_rows, head_size)
        .transpose(1, 0, 2)
        .reshape(group_rows, 1, local_heads * head_size)
    )
    returned = lax.all_to_all(merged, "grp", split_axis=0, concat_axis=1, tiled=True)
    return returned.reshape(tok_rows, grp_count * local_heads * head_size)


def solution(mesh):
    return jax.shard_map(
        per_device,
        mesh=mesh,
        in_specs=(
            P(("seq", "grp"), None),
            P(("seq", "grp"), None),
            P(("seq", "grp"), None),
            P(),
            P(),
        ),
        out_specs=P(("seq", "grp"), None),
        check_vma=False,
    )
```

profile of v0, /device:TPU:0, one launch (start us, length us, event | category | flops | bytes accessed | tf_op | source)
XLA Modules:
  0.0 408.5 jit_solution(12489217705326246221)
XLA Ops:
  0.0 1.8 copy.79
  1.8 4.2 %all-to-all-start.2 = ((bf16[128,4,256]{2,0,1:T(8,128)(2,1)}), bf16[128,4,256]{2,0,1:T(8,128)(2,1)S(1)}, u32[]{:S(2)}, u32[]{:S(2)}) async-start(bf16[128,4,256]{2,0,1:T(8,128)(2,1)} %bitcast.88), calls=%async_computation.2 | async-start | bytes 524288 | tf_op jit(solution)/shard_map/all_to_all | solution.py:72
  6.3 1.7 copy.80
  8.0 4.1 all-to-all-done.2
  12.1 3.4 all-to-all-start.1
  15.6 4.1 collective-permute-start.1
  21.5 3.7 all-to-all-start
  25.3 4.1 collective-permute-start
  30.4 5.1 %collective-permute-done = bf16[512,2,128]{2,1,0:T(2,128)(2,1)S(1)} collective-permute-done((bf16[512,2,128]{2,1,0:T(2,128)(2,1)S(1)}, bf16[512,2,128]{2,1,0:T(2,128)(2,1)S(1)}, u32[]{:S(2)}, u32[]{:S(2)}) %collective-permute-start) | collective-permute-done | bytes 262176 | tf_op jit(solution)/shard_map/ppermute | solution.py:13
  37.3 1.8 gather_fusion.2
  39.1 1.8 gather_fusion.3
  40.9 3.3 convert_select_fusion
  44.3 128.2 %all-reduce.2 = (bf16[16,3,64,128]{3,2,1,0:T(8,128)(2,1)}, bf16[16,3,64,128]{3,2,1,0:T(8,128)(2,1)}) all-reduce(f32[16,3,64,128]{3,2,1,0:T(8,128)} %get-tuple-element.173, f32[16,3,64,128]{3,2,1,0:T(8,128)} %get-tuple-element.172), channel_id=1, replica_groups=mesh['seq'=8,'grp'=4] {'seq'}, use_global_device_ids=true, to_apply=%region_0.1 | all-reduce | flops 786432 | bytes 4718592 | tf_op jit(solution)/shard_map/psum | solution.py:102
  173.1 1.9 copy.61
  175.0 178.8 %while.11 = (s32[]{:T(128)}, bf16[16,8,64,128]{3,2,1,0:T(8,128)(2,1)}, s32[]{:T(128)}, s32[16,3]{1,0:T(8,128)S(1)}, s32[16,3]{1,0:T(8,128)S(1)}, /*index=5*/bf16...) while((s32[]{:T(128)}, ...), condition=%wide.region_6.7_spmd.clone, body=%wide.region_2.6_spmd.clone.sunk | while | flops 104339728 | bytes 11976439 | solution.py:135
  353.8 2.9 copy.62
  357.2 2.9 reduce
  360.1 2.9 copy.81
  363.0 2.8 reshape.314
  365.8 29.3 %all_to_all.60 = bf16[4,2,131072]{2,1,0:T(2,128)(2,1)S(1)} all-to-all(bf16[4,2,131072]{2,1,0:T(2,128)(2,1)} %reshape.314), channel_id=1, replica_groups=mesh['seq'=8,'grp'=4] {'grp'}, dimensions={0} | all-to-all | bytes 4194304 | tf_op jit(solution)/shard_map/all_to_all | solution.py:143
  395.1 3.3 reshape.315
  398.4 3.5 copy.66
  401.9 2.6 copy.64
  404.4 4.1 copy.65
  (578 shorter events, 153.9 us)
Async XLA Ops:
  0.0 6.0 %copy-start = (s32[64,3]{0,1:T(4,128)S(1)}, s32[64,3]{0,1:T(4,128)}, u32[]{:S(2)}) copy-start(s32[64,3]{0,1:T(4,128)} %param.10) | copy-start | bytes 2308
  0.0 19.6 %copy-start.2 = (bf16[128,8192]{1,0:T(8,128)(2,1)S(1)}, bf16[128,8192]{1,0:T(8,128)(2,1)}, u32[]{:S(2)}) copy-start(bf16[128,8192]{1,0:T(8,128)(2,1)} %param.7) | copy-start | bytes 6291460
  1.8 10.2 %all-to-all-start.2 = ((bf16[128,4,256]{2,0,1:T(8,128)(2,1)}), bf16[128,4,256]{2,0,1:T(8,128)(2,1)S(1)}, u32[]{:S(2)}, u32[]{:S(2)}) async-start(bf16[128,4,256]{2,0,1:T(8,128)(2,1)} %bitcast.88), calls=%async_computation.2 | async-start | bytes 524288 | tf_op jit(solution)/shard_map/all_to_all | solution.py:72
  12.1 9.4 %all-to-all-start.1 = ((bf16[128,4,256]{2,0,1:T(8,128)(2,1)}), bf16[128,4,256]{2,0,1:T(8,128)(2,1)S(1)}, u32[]{:S(2)}, u32[]{:S(2)}) async-start(bf16[128,4,256]{2,0,1:T(8,128)(2,1)} %bitcast.89), calls=%async_computation.1 | async-start | bytes 524288 | tf_op jit(solution)/shard_map/all_to_all | solution.py:71
  15.6 14.2 %collective-permute-start.1 = (bf16[512,2,128]{2,1,0:T(2,128)(2,1)S(1)}, bf16[512,2,128]{2,1,0:T(2,128)(2,1)S(1)}, u32[]{:S(2)}, u32[]{:S(2)}) collective-permute-start(bf16[512,2,128]{2,1,0:T(2,128)(2,1)S(1)} %reshape.263), channel_id=1, source_target_pairs={{0,4},{4,8},{8,12},{12,16},{16,20},{20,24},{24,28},{1,5},{5,9},{9,... | collective-permute-start | bytes 786440 | tf_op jit(solution)/shard_map/ppermute | solution.py:13
  21.5 7.9 %copy-start.3 = (s32[64,3]{0,1:T(4,128)S(1)}, s32[64,3]{0,1:T(4,128)}, u32[]{:S(2)}) copy-start(s32[64,3]{0,1:T(4,128)} %param.11) | copy-start | bytes 2308
  21.5 151.0 %all-to-all-start = ((bf16[128,4,2048]{2,0,1:T(8,128)(2,1)}), bf16[128,4,2048]{2,0,1:T(8,128)(2,1)S(1)}, u32[]{:S(2)}, u32[]{:S(2)}) async-start(bf16[128,4,2048]{2,0,1:T(8,128)(2,1)} %bitcast.87), calls=%async_computation | async-start | bytes 4194304 | tf_op jit(solution)/shard_map/all_to_all | solution.py:70
  25.3 10.2 %collective-permute-start = (bf16[512,2,128]{2,1,0:T(2,128)(2,1)S(1)}, bf16[512,2,128]{2,1,0:T(2,128)(2,1)S(1)}, u32[]{:S(2)}, u32[]{:S(2)}) collective-permute-start(bf16[512,2,128]{2,1,0:T(2,128)(2,1)S(1)} %reshape.260), channel_id=1, source_target_pairs={{0,4},{4,8},{8,12},{12,16},{16,20},{20,24},{24,28},{1,5},{5,9},{9,... | collective-permute-start | bytes 786440 | tf_op jit(solution)/shard_map/ppermute | solution.py:13
  36.5 0.8 copy-start.1
where the time goes:
time: 411 us; the launch traced here: 408 us
  blocking collectives  157 us (38%)
  local copies, waits for them, and re-layouts  109 us (27%)
  matrix products  48.8 us (12%)
  other arithmetic  33 us (8%)
  loops' own time  31.1 us (8%)
  starting transfers between devices  19.5 us (5%)
  waiting for transfers between devices  9.59 us (2%)
    psum x1, blocking collectives, per_device(): lax.psum((jnp.where(owned, picked_keys.astype(jnp.float32), nothing), jnp...  128 us
    another operation x1, loops' own time, per_device(): lax.map(per_head, (head_queries, head_offsets, head_verts, vert_keys, ver...  31.1 us
    all_to_all x1, blocking collectives, per_device(): lax.all_to_all(merged, 'grp', split_axis=0, concat_axis=1, tiled=True)  29.3 us
    dot_general x16, matrix products, head_attention(): jnp.einsum('qik,qkd->qid', rounded, all_values, preferred_element_type=jn...  26.6 us
    dot_general x16, matrix products, head_attention(): jnp.einsum('qid,qkd->qik', query_block, all_keys, preferred_element_type=...  22.1 us
    squeeze x16, local copies, waits for them, and re-layouts, per_head(): slash_values = value_window[kv_one][window_index]  16.3 us
    sub x16, other arithmetic, head_attention(): weight = jnp.where(allowed, jnp.exp(masked - row_top), 0.0)  16.2 us
    unnamed x16, local copies, waits for them, and re-layouts  16 us
  transfers between devices with their start and end apart: 5, of which 3 were waited for; matrix products, arithmetic and copies ran while one was open for 3% of the time, Pallas kernels for 0%

commit v1 on v0

v1 whole, which is shorter than its diff:
```python
import jax
import jax.numpy as jnp
from jax import lax
from jax.experimental import pallas as pl
from jax.experimental.pallas import tpu as pltpu
from jax.sharding import PartitionSpec as P

HEAD_DIMENSION = 128
MASK_BLOCK_SIZE = 64
SLASH_COUNT = 3
VERT_COUNT = 3


def passed_along(shard, axis, by):
    length = lax.axis_size(axis)
    pairs = [(i, i + by) for i in range(length) if 0 <= i + by < length]
    return lax.ppermute(shard, axis, pairs)


def attention_kernel(local_heads, group_blocks, sharing):
    block = MASK_BLOCK_SIZE
    key_count = (SLASH_COUNT + VERT_COUNT) * block
    scale = HEAD_DIMENSION ** (-0.5)

    def kernel(meta_ref, q_ref, k_ref, v_ref, vk_ref, vv_ref, o_ref):
        h = pl.program_id(0)
        first = meta_ref[2 * local_heads * SLASH_COUNT]
        offs = [meta_ref[h * SLASH_COUNT + j] for j in range(SLASH_COUNT)]
        verts = [meta_ref[local_heads * SLASH_COUNT + h * VERT_COUNT + j] for j in range(VERT_COUNT)]
        vert_keys = vk_ref[0]
        vert_values = vv_ref[0]
        col = lax.broadcasted_iota(jnp.int32, (block, key_count), 1)
        row = lax.broadcasted_iota(jnp.int32, (block, key_count), 0)
        col_block = col // block
        col_pos = col % block
        for b in range(group_blocks):
            qb = first + b
            q = q_ref[pl.ds(b * block, block), :]
            starts = [pl.multiple_of((group_blocks + b - offs[j]) * block, block) for j in range(SLASH_COUNT)]
            keys = jnp.concatenate([k_ref[pl.ds(s, block), :] for s in starts] + [vert_keys], 0)
            values = jnp.concatenate([v_ref[pl.ds(s, block), :] for s in starts] + [vert_values], 0)
            ids = [qb - offs[j] for j in range(SLASH_COUNT)] + verts
            goods = [qb - offs[j] >= 0 for j in range(SLASH_COUNT)]
            for v in verts:
                ok = v <= qb
                for o in offs:
                    ok = jnp.logical_and(ok, qb - v != o)
                goods.append(ok)
            block_id = jnp.full((block, key_count), ids[-1], jnp.int32)
            goods = [g.astype(jnp.int32) for g in goods]
            block_good = jnp.full((block, key_count), goods[-1], jnp.int32)
            for i in range(len(ids) - 2, -1, -1):
                here = col_block == i
                block_id = jnp.where(here, ids[i], block_id)
                block_good = jnp.where(here, goods[i], block_good)
            allowed = jnp.logical_and(block_good > 0, block_id * block + col_pos <= qb * block + row)
            scores = lax.dot_general(
                q, keys, (((1,), (1,)), ((), ())), preferred_element_type=jnp.float32
            ) * scale
            masked = jnp.where(allowed, scores, -1e30)
            top = jnp.max(masked, axis=1, keepdims=True)
            weight = jnp.where(allowed, jnp.exp(masked - top), 0.0)
            total = jnp.sum(weight, axis=1, keepdims=True)
            rounded = weight.astype(jnp.bfloat16)
            acc = jnp.dot(rounded, values, preferred_element_type=jnp.float32)
            o_ref[pl.ds(b * block, block), :] = (acc / total).astype(o_ref.dtype)

    return kernel


def attend(meta, queries, key_window, value_window, vert_keys, vert_values, local_heads, sharing):
    group_rows = queries.shape[0]
    group_blocks = group_rows // MASK_BLOCK_SIZE
    head_size = HEAD_DIMENSION
    window_rows = key_window.shape[0]
    vert_rows = vert_keys.shape[1]
    grid_spec = pltpu.PrefetchScalarGridSpec(
        num_scalar_prefetch=1,
        grid=(local_heads,),
        in_specs=[
            pl.BlockSpec((group_rows, head_size), lambda h, m: (0, h)),
            pl.BlockSpec((window_rows, head_size), lambda h, m: (0, h // sharing)),
            pl.BlockSpec((window_rows, head_size), lambda h, m: (0, h // sharing)),
            pl.BlockSpec((1, vert_rows, head_size), lambda h, m: (h, 0, 0)),
            pl.BlockSpec((1, vert_rows, head_size), lambda h, m: (h, 0, 0)),
        ],
        out_specs=pl.BlockSpec((group_rows, head_size), lambda h, m: (0, h)),
    )
    return pl.pallas_call(
        attention_kernel(local_heads, group_blocks, sharing),
        grid_spec=grid_spec,
        out_shape=jax.ShapeDtypeStruct(queries.shape, queries.dtype),
    )(meta, queries, key_window, value_window, vert_keys, vert_values)


def per_device(query_rows, key_matrix, value_matrix, vertical, slash_offsets):
    tok_rows = query_rows.shape[0]
    grp_count = lax.axis_size("grp")
    head_size = HEAD_DIMENSION
    block_size = MASK_BLOCK_SIZE
    local_heads = query_rows.shape[1] // (grp_count * head_size)
    local_kv = key_matrix.shape[1] // (grp_count * head_size)
    group_sharing_factor = local_heads // local_kv
    query_split = query_rows.reshape(tok_rows, grp_count, local_heads * head_size)
    key_split = key_matrix.reshape(tok_rows, grp_count, local_kv * head_size)
    value_split = value_matrix.reshape(tok_rows, grp_count, local_kv * head_size)
    query_group, key_group, value_group = (
        lax.all_to_all(query_split, "grp", split_axis=1, concat_axis=0, tiled=True),
        lax.all_to_all(key_split, "grp", split_axis=1, concat_axis=0, tiled=True),
        lax.all_to_all(value_split, "grp", split_axis=1, concat_axis=0, tiled=True),
    )
    group_rows = tok_rows * grp_count
    group_blocks = group_rows // block_size
    key_local = key_group.reshape(group_rows, local_kv * head_size)
    value_local = value_group.reshape(group_rows, local_kv * head_size)
    key_before, value_before = passed_along((key_local, value_local), "seq", 1)
    key_window = jnp.concatenate([key_before, key_local], 0)
    value_window = jnp.concatenate([value_before, value_local], 0)
    seq_index = lax.axis_index("seq")
    grp_index = lax.axis_index("grp")
    head_offsets = lax.dynamic_slice_in_dim(slash_offsets, grp_index * local_heads, local_heads, 0)
    head_verts = lax.dynamic_slice_in_dim(vertical, grp_index * local_heads, local_heads, 0)
    kv_index = jnp.arange(local_heads, dtype=jnp.int32) // group_sharing_factor
    owner_seq = head_verts // group_blocks
    local_block = head_verts % group_blocks
    key_blocks = key_local.reshape(group_blocks, block_size, local_kv, head_size)
    value_blocks = value_local.reshape(group_blocks, block_size, local_kv, head_size)
    picked_keys = key_blocks[local_block, :, kv_index[:, None], :]
    picked_values = value_blocks[local_block, :, kv_index[:, None], :]
    owned = (owner_seq == seq_index)[:, :, None, None]
    nothing = jnp.zeros((), picked_keys.dtype)
    summed_keys, summed_values = lax.psum(
        (jnp.where(owned, picked_keys, nothing), jnp.where(owned, picked_values, nothing)),
        "seq",
    )
    vert_keys = summed_keys.reshape(local_heads, -1, head_size)
    vert_values = summed_values.reshape(local_heads, -1, head_size)
    first_block = (seq_index * group_blocks).astype(jnp.int32)
    meta = jnp.concatenate(
        [
            head_offsets.reshape(-1).astype(jnp.int32),
            head_verts.reshape(-1).astype(jnp.int32),
            first_block[None],
        ]
    )
    queries = query_group.reshape(group_rows, local_heads * head_size)
    results = attend(
        meta, queries, key_window, value_window, vert_keys, vert_values, local_heads,
        group_sharing_factor,
    )
    merged = results.reshape(group_rows, 1, local_heads * head_size)
    returned = lax.all_to_all(merged, "grp", split_axis=0, concat_axis=1, tiled=True)
    return returned.reshape(tok_rows, grp_count * local_heads * head_size)


def solution(mesh):
    return jax.shard_map(
        per_device,
        mesh=mesh,
        in_specs=(
            P(("seq", "grp"), None),
            P(("seq", "grp"), None),
            P(("seq", "grp"), None),
            P(),
            P(),
        ),
        out_specs=P(("seq", "grp"), None),
        check_vma=False,
    )
```

time: 411 us -> 232 us (0.56)
  blocking collectives: 157 us -> 29.3 us
  waiting for transfers between devices: 9.59 us -> 97.3 us
  local copies, waits for them, and re-layouts: 109 us -> 25.9 us
  matrix products: 48.8 us -> 0 us
  Pallas kernels: 0 us -> 37.4 us
  loops' own time: 31.1 us -> 0 us
  other arithmetic: 33 us -> 8.8 us
  between operations: 0.15 us -> 13.5 us
    psum x1 -> x0, blocking collectives: 128 us -> none  [per_device(): lax.psum((jnp.where(owned, picked_keys.astype(jnp.float32), nothing), jnp...]
    psum x0 -> x1, waiting for transfers between devices: none -> 77.5 us  [per_device(): lax.psum((jnp.where(owned, picked_keys, nothing), jnp.where(owned, picked...]
    dot_general x32 -> x0, matrix products: 48.8 us -> none  [the longest x16 26.6 us: head_attention(): jnp.einsum('qik,qkd->qid', rounded, all_values, preferred_element_type=jn...]
    pallas_call x0 -> x1, Pallas kernels: none -> 37.4 us  [attend(): pl.pallas_call(attention_kernel(local_heads, group_blocks, sharing), grid...]
    another operation x1 -> x0, loops' own time: 31.1 us -> none  [per_device(): lax.map(per_head, (head_queries, head_offsets, head_verts, vert_keys, ver...]
    gather x34 -> x2, local copies, waits for them, and re-layouts: 23.6 us -> 2.65 us  [the longest x1 1.77 us: per_device(): picked_keys = key_blocks[local_block, :, kv_index[:, None], :]]
    sub x32 -> x0, other arithmetic: 17.4 us -> none  [the longest x16 16.2 us: head_attention(): weight = jnp.where(allowed, jnp.exp(masked - row_top), 0.0)]
    broadcast_in_dim x64 -> x0, local copies, waits for them, and re-layouts: 17 us -> none  [the longest x32 14.6 us: head_attention(): jnp.broadcast_to(vert_values[None], (block_count,) + vert_values.shape)]
  transfers between devices with their start and end apart: 5 -> 6, of which waited for: 3 -> 5; matrix products, arithmetic and copies ran while one was open for 3% -> 5% of each run, Pallas kernels for 0% -> 0%
where the time goes in v1:
time: 232 us; the launch traced here: 231 us
  waiting for transfers between devices  97.3 us (42%)
  Pallas kernels  37.4 us (16%)
  blocking collectives  29.3 us (13%)
  local copies, waits for them, and re-layouts  25.9 us (11%)
  starting transfers between devices  18.7 us (8%)
  between operations  13.5 us (6%)
  other arithmetic  8.8 us (4%)
    psum x1, waiting for transfers between devices, per_device(): lax.psum((jnp.where(owned, picked_keys, nothing), jnp.where(owned, picked...  77.5 us
    pallas_call x1, Pallas kernels, attend(): pl.pallas_call(attention_kernel(local_heads, group_blocks, sharing), grid...  37.4 us
    all_to_all x1, blocking collectives, per_device(): lax.all_to_all(merged, 'grp', split_axis=0, concat_axis=1, tiled=True)  29.3 us
    ppermute x2, waiting for transfers between devices, passed_along(): return lax.ppermute(shard, axis, pairs)  12.1 us
    unnamed x19, local copies, waits for them, and re-layouts  9.61 us
    ppermute x2, starting transfers between devices, passed_along(): return lax.ppermute(shard, axis, pairs)  7.48 us
    all_to_all x1, waiting for transfers between devices, per_device(): lax.all_to_all(key_split, 'grp', split_axis=1, concat_axis=0, tiled=True)  5.58 us
  transfers between devices with their start and end apart: 6, of which 5 were waited for; matrix products, arithmetic and copies ran while one was open for 5% of the time, Pallas kernels for 0%

profile of v1, /device:TPU:0, one launch (start us, length us, event | category | flops | bytes accessed | tf_op | source)
XLA Modules:
  0.0 230.9 jit_solution(6919702322194943056)
XLA Ops:
  6.5 1.7 copy.73
  8.2 4.2 %all-to-all-start.2 = ((bf16[128,4,256]{2,0,1:T(8,128)(2,1)}), bf16[128,4,256]{2,0,1:T(8,128)(2,1)S(1)}, u32[]{:S(2)}, u32[]{:S(2)}) async-start(bf16[128,4,256]{2,0,1:T(8,128)(2,1)} %bitcast.49), calls=%async_computation.2 | async-start | bytes 524288 | tf_op jit(solution)/shard_map/all_to_all | solution.py:110
  12.4 3.2 %copy.72 = bf16[16,4,8,2048]{3,2,0,1:T(8,128)(2,1)} copy(bf16[16,4,8,2048]{3,2,1,0:T(8,128)(2,1)} %bitcast.65) | data formatting | bytes 4194304 | tf_op jit(solution)/shard_map/reshape | solution.py:104
  16.4 2.0 all-to-all-done.2
  18.5 3.4 %all-to-all-start.1 = ((bf16[128,4,256]{2,0,1:T(8,128)(2,1)}), bf16[128,4,256]{2,0,1:T(8,128)(2,1)S(1)}, u32[]{:S(2)}, u32[]{:S(2)}) async-start(bf16[128,4,256]{2,0,1:T(8,128)(2,1)} %bitcast.50), calls=%async_computation.1 | async-start | bytes 524288 | tf_op jit(solution)/shard_map/all_to_all | solution.py:109
  22.3 5.6 %all-to-all-done.1 = bf16[128,4,256]{2,0,1:T(8,128)(2,1)S(1)} async-done(((bf16[128,4,256]{2,0,1:T(8,128)(2,1)}), bf16[128,4,256]{2,0,1:T(8,128)(2,1)S(1)}, u32[]{:S(2)}, u32[]{:S(2)}) %all-to-all-start.1) | async-done | bytes 262176 | tf_op jit(solution)/shard_map/all_to_all | solution.py:109
  27.9 3.6 %all-to-all-start = ((bf16[128,4,2048]{2,0,1:T(8,128)(2,1)}), bf16[128,4,2048]{2,0,1:T(8,128)(2,1)S(1)}, u32[]{:S(2)}, u32[]{:S(2)}) async-start(bf16[128,4,2048]{2,0,1:T(8,128)(2,1)} %bitcast.48), calls=%async_computation | async-start | bytes 4194304 | tf_op jit(solution)/shard_map/all_to_all | solution.py:108
  31.7 0.9 gather_fusion.1
  32.6 1.8 gather_fusion
  34.3 2.5 %broadcast_select_fusion = (bf16[16,3,64,128]{3,2,1,0:T(8,128)(2,1)}, bf16[16,3,64,128]{3,2,1,0:T(8,128)(2,1)}) fusion(bf16[16,3,64,128]{3,2,1,0:T(8,128)(2,1)S(1)} %bitcast.57, pred[16,3]{1,0:T(8,128)(4,1)S(1)} %copy.58, bf16[16,3,64,128]{3,2,1,0:T(8,128)(2,1)} %bitcast.58), kind=kLoop, calls=%fused_computation.3 | loop fusion | flops 786432 | bytes 3145776 | tf_op jit(solution)/shard_map/jit(_where)/select_n | solution.py:133
  36.9 4.1 %collective-permute-start = (bf16[512,256]{1,0:T(8,128)(2,1)S(1)}, bf16[512,256]{1,0:T(8,128)(2,1)S(1)}, u32[]{:S(2)}, u32[]{:S(2)}) collective-permute-start(bf16[512,256]{1,0:T(8,128)(2,1)S(1)} %bitcast.63), channel_id=1, source_target_pairs={{0,4},{4,8},{8,12},{12,16},{16,20},{20,24},{24,28},{1,5},{5,9},{9,... | collective-permute-start | bytes 786440 | tf_op jit(solution)/shard_map/ppermute | solution.py:17
  41.0 3.4 %collective-permute-start.1 = (bf16[512,256]{1,0:T(8,128)(2,1)S(1)}, bf16[512,256]{1,0:T(8,128)(2,1)S(1)}, u32[]{:S(2)}, u32[]{:S(2)}) collective-permute-start(bf16[512,256]{1,0:T(8,128)(2,1)S(1)} %bitcast.60), channel_id=1, source_target_pairs={{0,4},{4,8},{8,12},{12,16},{16,20},{20,24},{24,28},{1,5},{5,9},{9,... | collective-permute-start | bytes 786440 | tf_op jit(solution)/shard_map/ppermute | solution.py:17
  45.4 5.0 %collective-permute-done = bf16[512,256]{1,0:T(8,128)(2,1)S(1)} collective-permute-done((bf16[512,256]{1,0:T(8,128)(2,1)S(1)}, bf16[512,256]{1,0:T(8,128)(2,1)S(1)}, u32[]{:S(2)}, u32[]{:S(2)}) %collective-permute-start) | collective-permute-done | bytes 262176 | tf_op jit(solution)/shard_map/ppermute | solution.py:17
  50.4 0.8 pad_maximum_fusion.k_ref
  51.2 7.2 %collective-permute-done.1 = bf16[512,256]{1,0:T(8,128)(2,1)S(1)} collective-permute-done((bf16[512,256]{1,0:T(8,128)(2,1)S(1)}, bf16[512,256]{1,0:T(8,128)(2,1)S(1)}, u32[]{:S(2)}, u32[]{:S(2)}) %collective-permute-start.1) | collective-permute-done | bytes 262176 | tf_op jit(solution)/shard_map/ppermute | solution.py:17
  59.3 77.5 %all-reduce.3.cloned.1.call-done = (bf16[16,192,128]{2,1,0:T(8,128)(2,1)}, bf16[16,192,128]{2,1,0:T(8,128)(2,1)}) async-done(((bf16[16,192,128]{2,1,0:T(8,128)(2,1)}, bf16[16,192,128]{2,1,0:T(8,128)(2,1)}), (bf16[16,192,128]{2,1,0:T(8,128)(2,1)}, bf16[16,192,128]{2,1,0:T(8,128)(2,1)})) %all-reduce.3.cloned.1.call-update) | async-done | bytes 1572880 | tf_op jit(solution)/shard_map/psum | solution.py:132
  136.7 37.4 %shard_map.55 = bf16[512,2048]{1,0:T(8,128)(2,1)} custom-call(s32[97]{0:T(128)} %pad_add_fusion.meta_ref, bf16[512,2048]{1,0:T(8,128)(2,1)} %bitcast.52, bf16[1024,256]{1,0:T(8,128)(2,1)} %pad_maximum_fusion.k_ref, bf16[1024,256]{1,0:T(8,128)(2,1)} %pad_maximum_fusion.1.v_ref, bf16[16,192,128]{2,1,0:T(8,128)(2,1)} %get-tuple-element.5.vk_ref, ...), custom_call_target="tpu_custom_call" | custom-call | tf_op jit(solution)/shard_map/pallas_call | solution.py:89
  174.7 3.9 %reduce = bf16[512,2048]{1,0:T(8,128)(2,1)S(1)} reduce(bf16[512,1,2048]{2,0,1:T(8,128)(2,1)} %bitcast.53, bf16[]{:T(256)} %broadcast.122), dimensions={1}, to_apply=%copy.62.reduce_sub_computation | reduce | bytes 4194306 | tf_op jit(solution)/shard_map/reshape | solution.py:151
  178.6 2.8 %reshape.94 = bf16[4,2,131072]{2,1,0:T(2,128)(2,1)} reshape(bf16[512,2048]{1,0:T(8,128)(2,1)S(1)} %reduce) | data formatting | bytes 4194304
  181.4 29.3 %all_to_all.60 = bf16[4,2,131072]{2,1,0:T(2,128)(2,1)S(1)} all-to-all(bf16[4,2,131072]{2,1,0:T(2,128)(2,1)} %reshape.94), channel_id=1, replica_groups=mesh['seq'=8,'grp'=4] {'grp'}, dimensions={0} | all-to-all | bytes 4194304 | tf_op jit(solution)/shard_map/all_to_all | solution.py:152
  210.6 3.4 %reshape.95 = bf16[512,1,2048]{2,1,0:T(2,128)(2,1)} reshape(bf16[4,2,131072]{2,1,0:T(2,128)(2,1)S(1)} %all_to_all.60) | data formatting | bytes 4194304
  214.0 3.5 %copy.65 = bf16[512,1,2048]{2,0,1:T(8,128)(2,1)S(1)} copy(bf16[512,1,2048]{2,1,0:T(2,128)(2,1)} %reshape.95) | data formatting | bytes 4194304
  217.5 2.5 %copy.63 = bf16[128,4,1,2048]{0,3,1,2:T(8,128)(2,1)} copy(bf16[128,4,1,2048]{3,0,1,2:T(8,128)(2,1)S(1)} %bitcast.51) | data formatting | bytes 4194304 | tf_op jit(solution)/shard_map/all_to_all | solution.py:152
  220.0 4.1 %copy.64 = bf16[128,8192]{1,0:T(8,128)(2,1)} copy(bf16[128,8192]{0,1:T(8,128)(2,1)} %bitcast.54) | data formatting | bytes 4194304 | tf_op jit(solution)/shard_map/reshape | solution.py:153
  (38 shorter events, 3.7 us)
Async XLA Ops:
  6.5 37.9 %copy-start = (s32[64,3]{0,1:T(4,128)S(1)}, s32[64,3]{0,1:T(4,128)}, u32[]{:S(2)}) copy-start(s32[64,3]{0,1:T(4,128)} %param.9) | copy-start | bytes 2308
  8.2 10.2 %all-to-all-start.2 = ((bf16[128,4,256]{2,0,1:T(8,128)(2,1)}), bf16[128,4,256]{2,0,1:T(8,128)(2,1)S(1)}, u32[]{:S(2)}, u32[]{:S(2)}) async-start(bf16[128,4,256]{2,0,1:T(8,128)(2,1)} %bitcast.49), calls=%async_computation.2 | async-start | bytes 524288 | tf_op jit(solution)/shard_map/all_to_all | solution.py:110
  12.4 3.2 %copy-start.6 = (bf16[128,1024]{1,0:T(8,128)(2,1)S(1)}, bf16[128,1024]{1,0:T(8,128)(2,1)}, u32[]{:S(2)}) copy-start(bf16[128,1024]{1,0:T(8,128)(2,1)} %param.6) | copy-start | bytes 786436
  12.4 3.9 %copy-start.7 = (s32[64,3]{0,1:T(4,128)S(1)}, s32[64,3]{0,1:T(4,128)}, u32[]{:S(2)}) copy-start(s32[64,3]{0,1:T(4,128)} %param.8) | copy-start | bytes 2308
  18.5 9.4 %copy-start.2 = (bf16[128,4,256]{2,0,1:T(8,128)(2,1)}, bf16[128,4,256]{2,0,1:T(8,128)(2,1)S(1)}, u32[]{:S(2)}) copy-start(bf16[128,4,256]{2,0,1:T(8,128)(2,1)S(1)} %all-to-all-done.2) | copy-start | bytes 786436
  18.5 9.4 %all-to-all-start.1 = ((bf16[128,4,256]{2,0,1:T(8,128)(2,1)}), bf16[128,4,256]{2,0,1:T(8,128)(2,1)S(1)}, u32[]{:S(2)}, u32[]{:S(2)}) async-start(bf16[128,4,256]{2,0,1:T(8,128)(2,1)} %bitcast.50), calls=%async_computation.1 | async-start | bytes 524288 | tf_op jit(solution)/shard_map/all_to_all | solution.py:109
  27.9 3.7 %copy-start.4 = (bf16[128,4,256]{2,0,1:T(8,128)(2,1)}, bf16[128,4,256]{2,0,1:T(8,128)(2,1)S(1)}, u32[]{:S(2)}) copy-start(bf16[128,4,256]{2,0,1:T(8,128)(2,1)S(1)} %all-to-all-done.1) | copy-start | bytes 786436
  27.9 31.4 %all-to-all-start = ((bf16[128,4,2048]{2,0,1:T(8,128)(2,1)}), bf16[128,4,2048]{2,0,1:T(8,128)(2,1)S(1)}, u32[]{:S(2)}, u32[]{:S(2)}) async-start(bf16[128,4,2048]{2,0,1:T(8,128)(2,1)} %bitcast.48), calls=%async_computation | async-start | bytes 4194304 | tf_op jit(solution)/shard_map/all_to_all | solution.py:108
  31.5 105.2 %all-reduce.3.cloned.1.call-start = ((), (), s32[]{:S(2)}) async-start(), calls=%async_computation.4 | async-start | bytes 3145728 | tf_op jit(solution)/shard_map/psum | solution.py:132
  34.3 2.6 %copy-start.5 = (bf16[128,4,256]{2,0,1:T(8,128)(2,1)S(1)}, bf16[128,4,256]{2,0,1:T(8,128)(2,1)}, u32[]{:S(2)}) copy-start(bf16[128,4,256]{2,0,1:T(8,128)(2,1)} %copy-done.4) | copy-start | bytes 786436
  34.3 6.6 %copy-start.3 = (bf16[128,4,256]{2,0,1:T(8,128)(2,1)S(1)}, bf16[128,4,256]{2,0,1:T(8,128)(2,1)}, u32[]{:S(2)}) copy-start(bf16[128,4,256]{2,0,1:T(8,128)(2,1)} %copy-done.2) | copy-start | bytes 786436
  36.9 13.5 %collective-permute-start = (bf16[512,256]{1,0:T(8,128)(2,1)S(1)}, bf16[512,256]{1,0:T(8,128)(2,1)S(1)}, u32[]{:S(2)}, u32[]{:S(2)}) collective-permute-start(bf16[512,256]{1,0:T(8,128)(2,1)S(1)} %bitcast.63), channel_id=1, source_target_pairs={{0,4},{4,8},{8,12},{12,16},{16,20},{20,24},{24,28},{1,5},{5,9},{9,... | collective-permute-start | bytes 786440 | tf_op jit(solution)/shard_map/ppermute | solution.py:17
  41.0 17.4 %collective-permute-start.1 = (bf16[512,256]{1,0:T(8,128)(2,1)S(1)}, bf16[512,256]{1,0:T(8,128)(2,1)S(1)}, u32[]{:S(2)}, u32[]{:S(2)}) collective-permute-start(bf16[512,256]{1,0:T(8,128)(2,1)S(1)} %bitcast.60), channel_id=1, source_target_pairs={{0,4},{4,8},{8,12},{12,16},{16,20},{20,24},{24,28},{1,5},{5,9},{9,... | collective-permute-start | bytes 786440 | tf_op jit(solution)/shard_map/ppermute | solution.py:17
  59.3 77.5 %copy-start.1 = (bf16[128,4,2048]{2,0,1:T(8,128)(2,1)}, bf16[128,4,2048]{2,0,1:T(8,128)(2,1)S(1)}, u32[]{:S(2)}) copy-start(bf16[128,4,2048]{2,0,1:T(8,128)(2,1)S(1)} %all-to-all-done) | copy-start | bytes 6291460
Sparse Core Ops, SparseCore 0:
  37.0 99.6 all-reduce.2

commit v2 on v1

--- a/solution.py
+++ b/solution.py
@@ -31,35 +31,31 @@
         vert_values = vv_ref[0]
         col = lax.broadcasted_iota(jnp.int32, (block, key_count), 1)
         row = lax.broadcasted_iota(jnp.int32, (block, key_count), 0)
-        col_block = col // block
-        col_pos = col % block
+        reach = col % block - row
+        lane = lax.broadcasted_iota(jnp.int32, (1, key_count), 1) // block
+        never = jnp.int32(-4 * block)
         for b in range(group_blocks):
             qb = first + b
             q = q_ref[pl.ds(b * block, block), :]
             starts = [pl.multiple_of((group_blocks + b - offs[j]) * block, block) for j in range(SLASH_COUNT)]
             keys = jnp.concatenate([k_ref[pl.ds(s, block), :] for s in starts] + [vert_keys], 0)
             values = jnp.concatenate([v_ref[pl.ds(s, block), :] for s in starts] + [vert_values], 0)
-            ids = [qb - offs[j] for j in range(SLASH_COUNT)] + verts
-            goods = [qb - offs[j] >= 0 for j in range(SLASH_COUNT)]
+            limits = [jnp.where(qb - offs[j] >= 0, offs[j] * block, never) for j in range(SLASH_COUNT)]
             for v in verts:
                 ok = v <= qb
                 for o in offs:
                     ok = jnp.logical_and(ok, qb - v != o)
-                goods.append(ok)
-            block_id = jnp.full((block, key_count), ids[-1], jnp.int32)
-            goods = [g.astype(jnp.int32) for g in goods]
-            block_good = jnp.full((block, key_count), goods[-1], jnp.int32)
-            for i in range(len(ids) - 2, -1, -1):
-                here = col_block == i
-                block_id = jnp.where(here, ids[i], block_id)
-                block_good = jnp.where(here, goods[i], block_good)
-            allowed = jnp.logical_and(block_good > 0, block_id * block + col_pos <= qb * block + row)
+                limits.append(jnp.where(ok, (qb - v) * block, never))
+            limit = jnp.full((1, key_count), limits[-1], jnp.int32)
+            for i in range(len(limits) - 2, -1, -1):
+                limit = jnp.where(lane == i, limits[i], limit)
+            allowed = reach <= limit
             scores = lax.dot_general(
                 q, keys, (((1,), (1,)), ((), ())), preferred_element_type=jnp.float32
             ) * scale
             masked = jnp.where(allowed, scores, -1e30)
             top = jnp.max(masked, axis=1, keepdims=True)
-            weight = jnp.where(allowed, jnp.exp(masked - top), 0.0)
+            weight = jnp.exp(masked - top)
             total = jnp.sum(weight, axis=1, keepdims=True)
             rounded = weight.astype(jnp.bfloat16)
             acc = jnp.dot(rounded, values, preferred_element_type=jnp.float32)
@@ -148,9 +144,9 @@
         meta, queries, key_window, value_window, vert_keys, vert_values, local_heads,
         group_sharing_factor,
     )
-    merged = results.reshape(group_rows, 1, local_heads * head_size)
-    returned = lax.all_to_all(merged, "grp", split_axis=0, concat_axis=1, tiled=True)
-    return returned.reshape(tok_rows, grp_count * local_heads * head_size)
+    merged = results.reshape(grp_count, tok_rows, local_heads * head_size)
+    returned = lax.all_to_all(merged, "grp", split_axis=0, concat_axis=0, tiled=True)
+    return returned.transpose(1, 0, 2).reshape(tok_rows, grp_count * local_heads * head_size)
 
 
 def solution(mesh):

time: 232 us -> 212 us (0.914)
  local copies, waits for them, and re-layouts: 25.9 us -> 10.6 us
  other arithmetic: 8.8 us -> 4.87 us
    unnamed x19 -> x16, local copies, waits for them, and re-layouts: 9.61 us -> 0.03 us
    reshape x1 -> x0, other arithmetic: 3.9 us -> none  [per_device(): merged = results.reshape(group_rows, 1, local_heads * head_size)]
    reshape x2 -> x1, local copies, waits for them, and re-layouts: 4.58 us -> 1.45 us  [per_device(): returned.transpose(1, 0, 2)]
    all_to_all x1 -> x0, local copies, waits for them, and re-layouts: 2.53 us -> none  [per_device(): lax.all_to_all(merged, 'grp', split_axis=0, concat_axis=1, tiled=True)]
  transfers between devices with their start and end apart: 6 -> 6, of which waited for: 5 -> 5; matrix products, arithmetic and copies ran while one was open for 5% -> 6% of each run, Pallas kernels for 0% -> 0%
where the time goes in v2:
time: 212 us
  waiting for transfers between devices  97.3 us (46%)
  Pallas kernels  37.3 us (18%)
  blocking collectives  29.3 us (14%)
  starting transfers between devices  18.7 us (9%)
  between operations  13.5 us (6%)
  local copies, waits for them, and re-layouts  10.6 us (5%)
  other arithmetic  4.87 us (2%)
    psum x1, waiting for transfers between devices, per_device(): lax.psum((jnp.where(owned, picked_keys, nothing), jnp.where(owned, picked...  77.5 us
    pallas_call x1, Pallas kernels, attend(): pl.pallas_call(attention_kernel(local_heads, group_blocks, sharing), grid...  37.3 us
    all_to_all x1, blocking collectives, per_device(): lax.all_to_all(merged, 'grp', split_axis=0, concat_axis=0, tiled=True)  29.3 us
    ppermute x2, waiting for transfers between devices, passed_along(): return lax.ppermute(shard, axis, pairs)  12.2 us
    ppermute x2, starting transfers between devices, passed_along(): return lax.ppermute(shard, axis, pairs)  7.48 us
    all_to_all x1, waiting for transfers between devices, per_device(): lax.all_to_all(key_split, 'grp', split_axis=1, concat_axis=0, tiled=True)  5.58 us
  transfers between devices with their start and end apart: 6, of which 5 were waited for; matrix products, arithmetic and copies ran while one was open for 6% of the time, Pallas kernels for 0%

profile of v2, /device:TPU:0, one launch (start us, length us, event | category | flops | bytes accessed | tf_op | source)
XLA Modules:
  0.0 211.6 jit_solution(5223334700336139574)
XLA Ops:
  6.5 1.7 copy.40
  8.2 4.2 %all-to-all-start.2 = ((bf16[128,4,256]{2,0,1:T(8,128)(2,1)}), bf16[128,4,256]{2,0,1:T(8,128)(2,1)S(1)}, u32[]{:S(2)}, u32[]{:S(2)}) async-start(bf16[128,4,256]{2,0,1:T(8,128)(2,1)} %bitcast.48), calls=%async_computation.2 | async-start | bytes 524288 | tf_op jit(solution)/shard_map/all_to_all | solution.py:106
  12.4 3.2 %copy.39 = bf16[16,4,8,2048]{3,2,0,1:T(8,128)(2,1)} copy(bf16[16,4,8,2048]{3,2,1,0:T(8,128)(2,1)} %bitcast.63) | data formatting | bytes 4194304 | tf_op jit(solution)/shard_map/reshape | solution.py:100
  15.6 0.7 copy.41
  16.4 2.0 all-to-all-done.2
  18.5 3.4 %all-to-all-start.1 = ((bf16[128,4,256]{2,0,1:T(8,128)(2,1)}), bf16[128,4,256]{2,0,1:T(8,128)(2,1)S(1)}, u32[]{:S(2)}, u32[]{:S(2)}) async-start(bf16[128,4,256]{2,0,1:T(8,128)(2,1)} %bitcast.49), calls=%async_computation.1 | async-start | bytes 524288 | tf_op jit(solution)/shard_map/all_to_all | solution.py:105
  22.1 0.1 copy.27
  22.3 5.6 %all-to-all-done.1 = bf16[128,4,256]{2,0,1:T(8,128)(2,1)S(1)} async-done(((bf16[128,4,256]{2,0,1:T(8,128)(2,1)}), bf16[128,4,256]{2,0,1:T(8,128)(2,1)S(1)}, u32[]{:S(2)}, u32[]{:S(2)}) %all-to-all-start.1) | async-done | bytes 262176 | tf_op jit(solution)/shard_map/all_to_all | solution.py:105
  27.9 3.6 %all-to-all-start = ((bf16[128,4,2048]{2,0,1:T(8,128)(2,1)}), bf16[128,4,2048]{2,0,1:T(8,128)(2,1)S(1)}, u32[]{:S(2)}, u32[]{:S(2)}) async-start(bf16[128,4,2048]{2,0,1:T(8,128)(2,1)} %bitcast.47), calls=%async_computation | async-start | bytes 4194304 | tf_op jit(solution)/shard_map/all_to_all | solution.py:104
  31.7 0.9 gather_fusion.1
  32.6 1.8 gather_fusion
  34.3 2.5 %broadcast_select_fusion = (bf16[16,3,64,128]{3,2,1,0:T(8,128)(2,1)}, bf16[16,3,64,128]{3,2,1,0:T(8,128)(2,1)}) fusion(bf16[16,3,64,128]{3,2,1,0:T(8,128)(2,1)S(1)} %bitcast.55, pred[16,3]{1,0:T(8,128)(4,1)S(1)} %copy.27, bf16[16,3,64,128]{3,2,1,0:T(8,128)(2,1)} %bitcast.56), kind=kLoop, calls=%fused_computation.3 | loop fusion | flops 786432 | bytes 3145776 | tf_op jit(solution)/shard_map/jit(_where)/select_n | solution.py:129
  36.9 4.1 %collective-permute-start = (bf16[512,256]{1,0:T(8,128)(2,1)S(1)}, bf16[512,256]{1,0:T(8,128)(2,1)S(1)}, u32[]{:S(2)}, u32[]{:S(2)}) collective-permute-start(bf16[512,256]{1,0:T(8,128)(2,1)S(1)} %bitcast.61), channel_id=1, source_target_pairs={{0,4},{4,8},{8,12},{12,16},{16,20},{20,24},{24,28},{1,5},{5,9},{9,... | collective-permute-start | bytes 786440 | tf_op jit(solution)/shard_map/ppermute | solution.py:17
  41.0 3.4 %collective-permute-start.1 = (bf16[512,256]{1,0:T(8,128)(2,1)S(1)}, bf16[512,256]{1,0:T(8,128)(2,1)S(1)}, u32[]{:S(2)}, u32[]{:S(2)}) collective-permute-start(bf16[512,256]{1,0:T(8,128)(2,1)S(1)} %bitcast.58), channel_id=1, source_target_pairs={{0,4},{4,8},{8,12},{12,16},{16,20},{20,24},{24,28},{1,5},{5,9},{9,... | collective-permute-start | bytes 786440 | tf_op jit(solution)/shard_map/ppermute | solution.py:17
  44.8 0.1 reshape.64
  44.8 0.6 pad_add_fusion.meta_ref
  45.4 5.0 %collective-permute-done = bf16[512,256]{1,0:T(8,128)(2,1)S(1)} collective-permute-done((bf16[512,256]{1,0:T(8,128)(2,1)S(1)}, bf16[512,256]{1,0:T(8,128)(2,1)S(1)}, u32[]{:S(2)}, u32[]{:S(2)}) %collective-permute-start) | collective-permute-done | bytes 262176 | tf_op jit(solution)/shard_map/ppermute | solution.py:17
  50.4 0.8 pad_maximum_fusion.k_ref
  51.2 7.2 %collective-permute-done.1 = bf16[512,256]{1,0:T(8,128)(2,1)S(1)} collective-permute-done((bf16[512,256]{1,0:T(8,128)(2,1)S(1)}, bf16[512,256]{1,0:T(8,128)(2,1)S(1)}, u32[]{:S(2)}, u32[]{:S(2)}) %collective-permute-start.1) | collective-permute-done | bytes 262176 | tf_op jit(solution)/shard_map/ppermute | solution.py:17
  58.4 0.8 pad_maximum_fusion.1.v_ref
  59.3 77.5 %all-reduce.3.cloned.1.call-done = (bf16[16,192,128]{2,1,0:T(8,128)(2,1)}, bf16[16,192,128]{2,1,0:T(8,128)(2,1)}) async-done(((bf16[16,192,128]{2,1,0:T(8,128)(2,1)}, bf16[16,192,128]{2,1,0:T(8,128)(2,1)}), (bf16[16,192,128]{2,1,0:T(8,128)(2,1)}, bf16[16,192,128]{2,1,0:T(8,128)(2,1)})) %all-reduce.3.cloned.1.call-update) | async-done | bytes 1572880 | tf_op jit(solution)/shard_map/psum | solution.py:128
  136.7 37.3 %shard_map.55 = bf16[512,2048]{1,0:T(8,128)(2,1)} custom-call(s32[97]{0:T(128)} %pad_add_fusion.meta_ref, bf16[512,2048]{1,0:T(8,128)(2,1)} %bitcast.50, bf16[1024,256]{1,0:T(8,128)(2,1)} %pad_maximum_fusion.k_ref, bf16[1024,256]{1,0:T(8,128)(2,1)} %pad_maximum_fusion.1.v_ref, bf16[16,192,128]{2,1,0:T(8,128)(2,1)} %get-tuple-element.5.vk_ref, ...), custom_call_target="tpu_custom_call" | custom-call | tf_op jit(solution)/shard_map/pallas_call | solution.py:85
  174.1 29.3 %all_to_all.50 = bf16[4,128,2048]{2,1,0:T(8,128)(2,1)S(1)} all-to-all(bf16[4,128,2048]{2,1,0:T(8,128)(2,1)} %bitcast.51), channel_id=1, replica_groups=mesh['seq'=8,'grp'=4] {'grp'}, dimensions={0} | all-to-all | bytes 4194304 | tf_op jit(solution)/shard_map/all_to_all | solution.py:148
  203.3 1.5 copy.35
  (32 shorter events, 0.9 us)
Async XLA Ops:
  6.5 37.9 %copy-start = (s32[64,3]{0,1:T(4,128)S(1)}, s32[64,3]{0,1:T(4,128)}, u32[]{:S(2)}) copy-start(s32[64,3]{0,1:T(4,128)} %param.9) | copy-start | bytes 2308
  8.2 10.2 %all-to-all-start.2 = ((bf16[128,4,256]{2,0,1:T(8,128)(2,1)}), bf16[128,4,256]{2,0,1:T(8,128)(2,1)S(1)}, u32[]{:S(2)}, u32[]{:S(2)}) async-start(bf16[128,4,256]{2,0,1:T(8,128)(2,1)} %bitcast.48), calls=%async_computation.2 | async-start | bytes 524288 | tf_op jit(solution)/shard_map/all_to_all | solution.py:106
  12.4 3.2 %copy-start.6 = (bf16[128,1024]{1,0:T(8,128)(2,1)S(1)}, bf16[128,1024]{1,0:T(8,128)(2,1)}, u32[]{:S(2)}) copy-start(bf16[128,1024]{1,0:T(8,128)(2,1)} %param.6) | copy-start | bytes 786436
  12.4 3.9 %copy-start.7 = (s32[64,3]{0,1:T(4,128)S(1)}, s32[64,3]{0,1:T(4,128)}, u32[]{:S(2)}) copy-start(s32[64,3]{0,1:T(4,128)} %param.8) | copy-start | bytes 2308
  18.5 9.4 %copy-start.2 = (bf16[128,4,256]{2,0,1:T(8,128)(2,1)}, bf16[128,4,256]{2,0,1:T(8,128)(2,1)S(1)}, u32[]{:S(2)}) copy-start(bf16[128,4,256]{2,0,1:T(8,128)(2,1)S(1)} %all-to-all-done.2) | copy-start | bytes 786436
  18.5 9.4 %all-to-all-start.1 = ((bf16[128,4,256]{2,0,1:T(8,128)(2,1)}), bf16[128,4,256]{2,0,1:T(8,128)(2,1)S(1)}, u32[]{:S(2)}, u32[]{:S(2)}) async-start(bf16[128,4,256]{2,0,1:T(8,128)(2,1)} %bitcast.49), calls=%async_computation.1 | async-start | bytes 524288 | tf_op jit(solution)/shard_map/all_to_all | solution.py:105
  27.9 3.7 %copy-start.4 = (bf16[128,4,256]{2,0,1:T(8,128)(2,1)}, bf16[128,4,256]{2,0,1:T(8,128)(2,1)S(1)}, u32[]{:S(2)}) copy-start(bf16[128,4,256]{2,0,1:T(8,128)(2,1)S(1)} %all-to-all-done.1) | copy-start | bytes 786436
  27.9 31.4 %all-to-all-start = ((bf16[128,4,2048]{2,0,1:T(8,128)(2,1)}), bf16[128,4,2048]{2,0,1:T(8,128)(2,1)S(1)}, u32[]{:S(2)}, u32[]{:S(2)}) async-start(bf16[128,4,2048]{2,0,1:T(8,128)(2,1)} %bitcast.47), calls=%async_computation | async-start | bytes 4194304 | tf_op jit(solution)/shard_map/all_to_all | solution.py:104
  31.5 105.2 %all-reduce.3.cloned.1.call-start = ((), (), s32[]{:S(2)}) async-start(), calls=%async_computation.4 | async-start | bytes 3145728 | tf_op jit(solution)/shard_map/psum | solution.py:128
  34.3 2.6 %copy-start.5 = (bf16[128,4,256]{2,0,1:T(8,128)(2,1)S(1)}, bf16[128,4,256]{2,0,1:T(8,128)(2,1)}, u32[]{:S(2)}) copy-start(bf16[128,4,256]{2,0,1:T(8,128)(2,1)} %copy-done.4) | copy-start | bytes 786436
  34.3 6.6 %copy-start.3 = (bf16[128,4,256]{2,0,1:T(8,128)(2,1)S(1)}, bf16[128,4,256]{2,0,1:T(8,128)(2,1)}, u32[]{:S(2)}) copy-start(bf16[128,4,256]{2,0,1:T(8,128)(2,1)} %copy-done.2) | copy-start | bytes 786436
  36.9 13.5 %collective-permute-start = (bf16[512,256]{1,0:T(8,128)(2,1)S(1)}, bf16[512,256]{1,0:T(8,128)(2,1)S(1)}, u32[]{:S(2)}, u32[]{:S(2)}) collective-permute-start(bf16[512,256]{1,0:T(8,128)(2,1)S(1)} %bitcast.61), channel_id=1, source_target_pairs={{0,4},{4,8},{8,12},{12,16},{16,20},{20,24},{24,28},{1,5},{5,9},{9,... | collective-permute-start | bytes 786440 | tf_op jit(solution)/shard_map/ppermute | solution.py:17
  41.0 17.4 %collective-permute-start.1 = (bf16[512,256]{1,0:T(8,128)(2,1)S(1)}, bf16[512,256]{1,0:T(8,128)(2,1)S(1)}, u32[]{:S(2)}, u32[]{:S(2)}) collective-permute-start(bf16[512,256]{1,0:T(8,128)(2,1)S(1)} %bitcast.58), channel_id=1, source_target_pairs={{0,4},{4,8},{8,12},{12,16},{16,20},{20,24},{24,28},{1,5},{5,9},{9,... | collective-permute-start | bytes 786440 | tf_op jit(solution)/shard_map/ppermute | solution.py:17
  59.2 77.5 %copy-start.1 = (bf16[128,4,2048]{2,0,1:T(8,128)(2,1)}, bf16[128,4,2048]{2,0,1:T(8,128)(2,1)S(1)}, u32[]{:S(2)}) copy-start(bf16[128,4,2048]{2,0,1:T(8,128)(2,1)S(1)} %all-to-all-done) | copy-start | bytes 6291460
Sparse Core Ops, SparseCore 0:
  37.0 99.6 all-reduce.2

commit v3 on v2

--- a/solution.py
+++ b/solution.py
@@ -9,6 +9,7 @@
 MASK_BLOCK_SIZE = 64
 SLASH_COUNT = 3
 VERT_COUNT = 3
+CHUNKS = 2
 
 
 def passed_along(shard, axis, by):
@@ -17,13 +18,13 @@
     return lax.ppermute(shard, axis, pairs)
 
 
-def attention_kernel(local_heads, group_blocks, sharing):
+def attention_kernel(local_heads, group_blocks, base):
     block = MASK_BLOCK_SIZE
     key_count = (SLASH_COUNT + VERT_COUNT) * block
     scale = HEAD_DIMENSION ** (-0.5)
 
     def kernel(meta_ref, q_ref, k_ref, v_ref, vk_ref, vv_ref, o_ref):
-        h = pl.program_id(0)
+        h = pl.program_id(0) + base
         first = meta_ref[2 * local_heads * SLASH_COUNT]
         offs = [meta_ref[h * SLASH_COUNT + j] for j in range(SLASH_COUNT)]
         verts = [meta_ref[local_heads * SLASH_COUNT + h * VERT_COUNT + j] for j in range(VERT_COUNT)]
@@ -64,28 +65,28 @@
     return kernel
 
 
-def attend(meta, queries, key_window, value_window, vert_keys, vert_values, local_heads, sharing):
+def attend(meta, queries, key_window, value_window, vert_keys, vert_values, local_heads, sharing, base):
     group_rows = queries.shape[0]
     group_blocks = group_rows // MASK_BLOCK_SIZE
     head_size = HEAD_DIMENSION
     window_rows = key_window.shape[0]
-    vert_rows = vert_keys.shape[1]
+    chunk_heads, vert_rows = vert_keys.shape[:2]
     grid_spec = pltpu.PrefetchScalarGridSpec(
         num_scalar_prefetch=1,
-        grid=(local_heads,),
+        grid=(chunk_heads,),
         in_specs=[
-            pl.BlockSpec((group_rows, head_size), lambda h, m: (0, h)),
-            pl.BlockSpec((window_rows, head_size), lambda h, m: (0, h // sharing)),
-            pl.BlockSpec((window_rows, head_size), lambda h, m: (0, h // sharing)),
+            pl.BlockSpec((group_rows, head_size), lambda h, m: (0, h + base)),
+            pl.BlockSpec((window_rows, head_size), lambda h, m: (0, (h + base) // sharing)),
+            pl.BlockSpec((window_rows, head_size), lambda h, m: (0, (h + base) // sharing)),
             pl.BlockSpec((1, vert_rows, head_size), lambda h, m: (h, 0, 0)),
             pl.BlockSpec((1, vert_rows, head_size), lambda h, m: (h, 0, 0)),
         ],
         out_specs=pl.BlockSpec((group_rows, head_size), lambda h, m: (0, h)),
     )
     return pl.pallas_call(
-        attention_kernel(local_heads, group_blocks, sharing),
+        attention_kernel(local_heads, group_blocks, base),
         grid_spec=grid_spec,
-        out_shape=jax.ShapeDtypeStruct(queries.shape, queries.dtype),
+        out_shape=jax.ShapeDtypeStruct((group_rows, chunk_heads * head_size), queries.dtype),
     )(meta, queries, key_window, value_window, vert_keys, vert_values)
 
 
@@ -125,12 +126,8 @@
     picked_values = value_blocks[local_block, :, kv_index[:, None], :]
     owned = (owner_seq == seq_index)[:, :, None, None]
     nothing = jnp.zeros((), picked_keys.dtype)
-    summed_keys, summed_values = lax.psum(
-        (jnp.where(owned, picked_keys, nothing), jnp.where(owned, picked_values, nothing)),
-        "seq",
-    )
-    vert_keys = summed_keys.reshape(local_heads, -1, head_size)
-    vert_values = summed_values.reshape(local_heads, -1, head_size)
+    mine_keys = jnp.where(owned, picked_keys, nothing)
+    mine_values = jnp.where(owned, picked_values, nothing)
     first_block = (seq_index * group_blocks).astype(jnp.int32)
     meta = jnp.concatenate(
         [
@@ -140,13 +137,26 @@
         ]
     )
     queries = query_group.reshape(group_rows, local_heads * head_size)
-    results = attend(
-        meta, queries, key_window, value_window, vert_keys, vert_values, local_heads,
-        group_sharing_factor,
-    )
-    merged = results.reshape(grp_count, tok_rows, local_heads * head_size)
-    returned = lax.all_to_all(merged, "grp", split_axis=0, concat_axis=0, tiled=True)
-    return returned.transpose(1, 0, 2).reshape(tok_rows, grp_count * local_heads * head_size)
+    chunk_heads = local_heads // CHUNKS
+    pieces = []
+    summed = ()
+    for c in range(CHUNKS):
+        heads = slice(c * chunk_heads, (c + 1) * chunk_heads)
+        chunk_keys, chunk_values, _ = lax.optimization_barrier(
+            (mine_keys[heads], mine_values[heads], summed)
+        )
+        summed = lax.psum((chunk_keys, chunk_values), "seq")
+        summed_keys, summed_values = summed
+        results = attend(
+            meta, queries, key_window, value_window,
+            summed_keys.reshape(chunk_heads, -1, head_size),
+            summed_values.reshape(chunk_heads, -1, head_size),
+            local_heads, group_sharing_factor, c * chunk_heads,
+        )
+        merged = results.reshape(grp_count, tok_rows, chunk_heads * head_size)
+        pieces.append(lax.all_to_all(merged, "grp", split_axis=0, concat_axis=0, tiled=True))
+    returned = jnp.stack(pieces, 1)
+    return returned.transpose(2, 0, 1, 3).reshape(tok_rows, grp_count * local_heads * head_size)
 
 
 def solution(mesh):

time: 212 us -> 251 us (1.18)
  waiting for transfers between devices: 97.3 us -> 133 us
  blocking collectives: 29.3 us -> 17.9 us
  local copies, waits for them, and re-layouts: 10.6 us -> 19.7 us
  starting transfers between devices: 18.7 us -> 22.3 us
    psum x1 -> x2, waiting for transfers between devices: 77.5 us -> 115 us  [per_device(): summed = lax.psum((chunk_keys, chunk_values), 'seq')]
    all_to_all x1, blocking collectives: 29.3 us -> 17.9 us  [per_device(): lax.all_to_all(merged, 'grp', split_axis=0, concat_axis=0, tiled=True)]
    all_to_all x1, waiting for transfers between devices: 2.02 us -> 5.89 us  [per_device(): lax.all_to_all(value_split, 'grp', split_axis=1, concat_axis=0, tiled=True)]
    transpose x0 -> x1, local copies, waits for them, and re-layouts: none -> 3.53 us  [per_device(): returned.transpose(2, 0, 1, 3)]
    all_to_all x0 -> x1, starting transfers between devices: none -> 3.51 us  [per_device(): lax.all_to_all(merged, 'grp', split_axis=0, concat_axis=0, tiled=True)]
    all_to_all x1, waiting for transfers between devices: 5.58 us -> 2.11 us  [per_device(): lax.all_to_all(key_split, 'grp', split_axis=1, concat_axis=0, tiled=True)]
    reshape x1, local copies, waits for them, and re-layouts: 1.45 us -> 4.47 us  [per_device(): returned.transpose(2, 0, 1, 3)]
    ppermute x2, waiting for transfers between devices: 12.2 us -> 9.3 us  [passed_along(): return lax.ppermute(shard, axis, pairs)]
  transfers between devices with their start and end apart: 6 -> 8, of which waited for: 5 -> 6; matrix products, arithmetic and copies ran while one was open for 6% -> 5% of each run, Pallas kernels for 0% -> 16%
where the time goes in v3:
time: 251 us; the launch traced here: 250 us
  waiting for transfers between devices  133 us (53%)
  Pallas kernels  39.7 us (16%)
  starting transfers between devices  22.3 us (9%)
  local copies, waits for them, and re-layouts  19.7 us (8%)
  blocking collectives  17.9 us (7%)
  between operations  13.6 us (5%)
  other arithmetic  3.9 us (2%)
    psum x2, waiting for transfers between devices, per_device(): summed = lax.psum((chunk_keys, chunk_values), 'seq')  115 us
    pallas_call x2, Pallas kernels, attend(): pl.pallas_call(attention_kernel(local_heads, group_blocks, base), grid_sp...  39.7 us
    all_to_all x1, blocking collectives, per_device(): lax.all_to_all(merged, 'grp', split_axis=0, concat_axis=0, tiled=True)  17.9 us
    ppermute x2, waiting for transfers between devices, passed_along(): return lax.ppermute(shard, axis, pairs)  9.3 us
    ppermute x2, starting transfers between devices, passed_along(): return lax.ppermute(shard, axis, pairs)  7.48 us
    all_to_all x1, waiting for transfers between devices, per_device(): lax.all_to_all(value_split, 'grp', split_axis=1, concat_axis=0, tiled=True)  5.89 us
  transfers between devices with their start and end apart: 8, of which 6 were waited for; matrix products, arithmetic and copies ran while one was open for 5% of the time, Pallas kernels for 16%

profile of v3, /device:TPU:0, one launch (start us, length us, event | category | flops | bytes accessed | tf_op | source)
XLA Modules:
  0.0 249.8 jit_solution(9980096595178097305)
XLA Ops:
  6.5 1.7 copy.40
  8.2 4.2 %all-to-all-start.1 = ((bf16[128,4,256]{2,0,1:T(8,128)(2,1)}), bf16[128,4,256]{2,0,1:T(8,128)(2,1)S(1)}, u32[]{:S(2)}, u32[]{:S(2)}) async-start(bf16[128,4,256]{2,0,1:T(8,128)(2,1)} %bitcast.53), calls=%async_computation.1 | async-start | bytes 524288 | tf_op jit(solution)/shard_map/all_to_all | solution.py:106
  12.4 3.2 %copy.38 = bf16[16,4,8,2048]{3,2,0,1:T(8,128)(2,1)} copy(bf16[16,4,8,2048]{3,2,1,0:T(8,128)(2,1)} %bitcast.69) | data formatting | bytes 4194304 | tf_op jit(solution)/shard_map/reshape | solution.py:101
  16.4 2.1 all-to-all-done.1
  18.5 3.4 %all-to-all-start.2 = ((bf16[128,4,256]{2,0,1:T(8,128)(2,1)}), bf16[128,4,256]{2,0,1:T(8,128)(2,1)S(1)}, u32[]{:S(2)}, u32[]{:S(2)}) async-start(bf16[128,4,256]{2,0,1:T(8,128)(2,1)} %bitcast.52), calls=%async_computation.2 | async-start | bytes 524288 | tf_op jit(solution)/shard_map/all_to_all | solution.py:107
  22.0 5.9 %all-to-all-done.2 = bf16[128,4,256]{2,0,1:T(8,128)(2,1)S(1)} async-done(((bf16[128,4,256]{2,0,1:T(8,128)(2,1)}), bf16[128,4,256]{2,0,1:T(8,128)(2,1)S(1)}, u32[]{:S(2)}, u32[]{:S(2)}) %all-to-all-start.2) | async-done | bytes 262176 | tf_op jit(solution)/shard_map/all_to_all | solution.py:107
  27.9 3.6 %all-to-all-start = ((bf16[128,4,2048]{2,0,1:T(8,128)(2,1)}), bf16[128,4,2048]{2,0,1:T(8,128)(2,1)S(1)}, u32[]{:S(2)}, u32[]{:S(2)}) async-start(bf16[128,4,2048]{2,0,1:T(8,128)(2,1)} %bitcast.56), calls=%async_computation | async-start | bytes 4194304 | tf_op jit(solution)/shard_map/all_to_all | solution.py:105
  32.1 0.9 gather_fusion.1
  33.0 1.8 gather_fusion
  34.8 1.3 broadcast_select_fusion
  36.1 1.2 fusion.8
  37.4 4.1 %collective-permute-start = (bf16[512,256]{1,0:T(8,128)(2,1)S(1)}, bf16[512,256]{1,0:T(8,128)(2,1)S(1)}, u32[]{:S(2)}, u32[]{:S(2)}) collective-permute-start(bf16[512,256]{1,0:T(8,128)(2,1)S(1)} %bitcast.64), channel_id=1, source_target_pairs={{0,4},{4,8},{8,12},{12,16},{16,20},{20,24},{24,28},{1,5},{5,9},{9,... | collective-permute-start | bytes 786440 | tf_op jit(solution)/shard_map/ppermute | solution.py:18
  41.4 3.4 %collective-permute-start.1 = (bf16[512,256]{1,0:T(8,128)(2,1)S(1)}, bf16[512,256]{1,0:T(8,128)(2,1)S(1)}, u32[]{:S(2)}, u32[]{:S(2)}) collective-permute-start(bf16[512,256]{1,0:T(8,128)(2,1)S(1)} %bitcast.67), channel_id=1, source_target_pairs={{0,4},{4,8},{8,12},{12,16},{16,20},{20,24},{24,28},{1,5},{5,9},{9,... | collective-permute-start | bytes 786440 | tf_op jit(solution)/shard_map/ppermute | solution.py:18
  45.9 5.0 %collective-permute-done = bf16[512,256]{1,0:T(8,128)(2,1)S(1)} collective-permute-done((bf16[512,256]{1,0:T(8,128)(2,1)S(1)}, bf16[512,256]{1,0:T(8,128)(2,1)S(1)}, u32[]{:S(2)}, u32[]{:S(2)}) %collective-permute-start) | collective-permute-done | bytes 262176 | tf_op jit(solution)/shard_map/ppermute | solution.py:18
  51.7 4.3 %collective-permute-done.1 = bf16[512,256]{1,0:T(8,128)(2,1)S(1)} collective-permute-done((bf16[512,256]{1,0:T(8,128)(2,1)S(1)}, bf16[512,256]{1,0:T(8,128)(2,1)S(1)}, u32[]{:S(2)}, u32[]{:S(2)}) %collective-permute-start.1) | collective-permute-done | bytes 262176 | tf_op jit(solution)/shard_map/ppermute | solution.py:18
  56.9 62.2 %all-reduce.7.cloned.1.call-done = (bf16[8,3,64,128]{3,2,1,0:T(8,128)(2,1)}, bf16[8,3,64,128]{3,2,1,0:T(8,128)(2,1)}) async-done(((bf16[8,3,64,128]{3,2,1,0:T(8,128)(2,1)}, bf16[8,3,64,128]{3,2,1,0:T(8,128)(2,1)}), (bf16[8,3,64,128]{3,2,1,0:T(8,128)(2,1)}, bf16[8,3,64,128]{3,2,1,0:T(8,128)(2,1)})) %all-reduce.7.cloned.1.call-update) | async-done | bytes 786448 | tf_op jit(solution)/shard_map/psum | solution.py:148
  119.1 1.3 copy-done.1
  120.4 19.8 %shard_map.55 = bf16[512,1024]{1,0:T(8,128)(2,1)} custom-call(s32[97]{0:T(128)} %pad_add_fusion.meta_ref, bf16[512,2048]{1,0:T(8,128)(2,1)} %bitcast.54, bf16[1024,256]{1,0:T(8,128)(2,1)} %pad_maximum_fusion.k_ref, bf16[1024,256]{1,0:T(8,128)(2,1)} %pad_maximum_fusion.1.v_ref, bf16[8,192,128]{2,1,0:T(8,128)(2,1)} %bitcast.72, bf16[8,192,128]{2,1,0:T(8,128)(2,1)} %bitcast.73), custom_call_target="tpu_custom_call" | custom-call | tf_op jit(solution)/shard_map/pallas_call | solution.py:86
  140.3 3.5 %all-to-all-start.3 = ((bf16[4,128,1024]{2,1,0:T(8,128)(2,1)}), bf16[4,128,1024]{2,1,0:T(8,128)(2,1)S(1)}, u32[]{:S(2)}, u32[]{:S(2)}) async-start(bf16[4,128,1024]{2,1,0:T(8,128)(2,1)} %bitcast.57), calls=%async_computation.3 | async-start | bytes 2097152 | tf_op jit(solution)/shard_map/all_to_all | solution.py:157
  143.8 53.1 %all-reduce.5.cloned.1.call-done = (bf16[8,192,128]{2,1,0:T(8,128)(2,1)}, bf16[8,192,128]{2,1,0:T(8,128)(2,1)}) async-done(((bf16[8,192,128]{2,1,0:T(8,128)(2,1)}, bf16[8,192,128]{2,1,0:T(8,128)(2,1)}), (bf16[8,192,128]{2,1,0:T(8,128)(2,1)}, bf16[8,192,128]{2,1,0:T(8,128)(2,1)})) %all-reduce.5.cloned.1.call-update) | async-done | bytes 786448 | tf_op jit(solution)/shard_map/psum | solution.py:148
  196.9 19.9 %shard_map.56 = bf16[512,1024]{1,0:T(8,128)(2,1)} custom-call(s32[97]{0:T(128)} %pad_add_fusion.meta_ref, bf16[512,2048]{1,0:T(8,128)(2,1)} %bitcast.55, bf16[1024,256]{1,0:T(8,128)(2,1)} %pad_maximum_fusion.k_ref, bf16[1024,256]{1,0:T(8,128)(2,1)} %pad_maximum_fusion.1.v_ref, bf16[8,192,128]{2,1,0:T(8,128)(2,1)} %get-tuple-element.13.vk_ref, ...), custom_call_target="tpu_custom_call" | custom-call | tf_op jit(solution)/shard_map/pallas_call | solution.py:86
  216.8 17.9 %all_to_all.55 = bf16[4,128,1024]{2,1,0:T(8,128)(2,1)S(1)} all-to-all(bf16[4,128,1024]{2,1,0:T(8,128)(2,1)} %bitcast.58), channel_id=1, replica_groups=mesh['seq'=8,'grp'=4] {'grp'}, dimensions={0} | all-to-all | bytes 2097152 | tf_op jit(solution)/shard_map/all_to_all | solution.py:157
  234.9 3.5 %copy.31 = bf16[128,4,2,1024]{3,2,1,0:T(2,128)(2,1)} copy(bf16[128,4,2,1024]{3,0,1,2:T(8,128)(2,1)S(1)} %maximum_bitcast_fusion) | data formatting | bytes 4194304 | tf_op jit(solution)/shard_map/transpose | solution.py:159
  238.5 4.5 %reshape.87 = bf16[128,8192]{1,0:T(8,128)(2,1)} reshape(bf16[128,4,2,1024]{3,2,1,0:T(2,128)(2,1)} %copy.31) | data formatting | bytes 4194304 | tf_op jit(solution)/shard_map/reshape | solution.py:159
  (41 shorter events, 4.4 us)
Async XLA Ops:
  6.5 38.3 %copy-start = (s32[64,3]{0,1:T(4,128)S(1)}, s32[64,3]{0,1:T(4,128)}, u32[]{:S(2)}) copy-start(s32[64,3]{0,1:T(4,128)} %param.9) | copy-start | bytes 2308
  8.2 10.2 %all-to-all-start.1 = ((bf16[128,4,256]{2,0,1:T(8,128)(2,1)}), bf16[128,4,256]{2,0,1:T(8,128)(2,1)S(1)}, u32[]{:S(2)}, u32[]{:S(2)}) async-start(bf16[128,4,256]{2,0,1:T(8,128)(2,1)} %bitcast.53), calls=%async_computation.1 | async-start | bytes 524288 | tf_op jit(solution)/shard_map/all_to_all | solution.py:106
  12.4 3.2 %copy-start.6 = (bf16[128,1024]{1,0:T(8,128)(2,1)S(1)}, bf16[128,1024]{1,0:T(8,128)(2,1)}, u32[]{:S(2)}) copy-start(bf16[128,1024]{1,0:T(8,128)(2,1)} %param.7) | copy-start | bytes 786436
  12.4 9.5 %copy-start.7 = (s32[64,3]{0,1:T(4,128)S(1)}, s32[64,3]{0,1:T(4,128)}, u32[]{:S(2)}) copy-start(s32[64,3]{0,1:T(4,128)} %param.8) | copy-start | bytes 2308
  18.5 13.5 %copy-start.2 = (bf16[128,4,256]{2,0,1:T(8,128)(2,1)}, bf16[128,4,256]{2,0,1:T(8,128)(2,1)S(1)}, u32[]{:S(2)}) copy-start(bf16[128,4,256]{2,0,1:T(8,128)(2,1)S(1)} %all-to-all-done.1) | copy-start | bytes 786436
  18.5 9.4 %all-to-all-start.2 = ((bf16[128,4,256]{2,0,1:T(8,128)(2,1)}), bf16[128,4,256]{2,0,1:T(8,128)(2,1)S(1)}, u32[]{:S(2)}, u32[]{:S(2)}) async-start(bf16[128,4,256]{2,0,1:T(8,128)(2,1)} %bitcast.52), calls=%async_computation.2 | async-start | bytes 524288 | tf_op jit(solution)/shard_map/all_to_all | solution.py:107
  27.9 4.0 %copy-start.4 = (bf16[128,4,256]{2,0,1:T(8,128)(2,1)}, bf16[128,4,256]{2,0,1:T(8,128)(2,1)S(1)}, u32[]{:S(2)}) copy-start(bf16[128,4,256]{2,0,1:T(8,128)(2,1)S(1)} %all-to-all-done.2) | copy-start | bytes 786436
  27.9 91.2 %all-to-all-start = ((bf16[128,4,2048]{2,0,1:T(8,128)(2,1)}), bf16[128,4,2048]{2,0,1:T(8,128)(2,1)S(1)}, u32[]{:S(2)}, u32[]{:S(2)}) async-start(bf16[128,4,2048]{2,0,1:T(8,128)(2,1)} %bitcast.56), calls=%async_computation | async-start | bytes 4194304 | tf_op jit(solution)/shard_map/all_to_all | solution.py:105
  31.5 87.6 %all-reduce.7.cloned.1.call-start = ((), (), s32[]{:S(2)}) async-start(), calls=%async_computation.6 | async-start | bytes 1572864 | tf_op jit(solution)/shard_map/psum | solution.py:148
  36.1 1.3 copy-start.3
  36.1 5.3 %copy-start.5 = (bf16[128,4,256]{2,0,1:T(8,128)(2,1)S(1)}, bf16[128,4,256]{2,0,1:T(8,128)(2,1)}, u32[]{:S(2)}) copy-start(bf16[128,4,256]{2,0,1:T(8,128)(2,1)} %copy-done.4) | copy-start | bytes 786436
  37.3 159.6 %all-reduce.5.cloned.1.call-start = ((), (), s32[]{:S(2)}) async-start(), calls=%async_computation.5 | async-start | bytes 1572864 | tf_op jit(solution)/shard_map/psum | solution.py:148
  37.4 13.5 %collective-permute-start = (bf16[512,256]{1,0:T(8,128)(2,1)S(1)}, bf16[512,256]{1,0:T(8,128)(2,1)S(1)}, u32[]{:S(2)}, u32[]{:S(2)}) collective-permute-start(bf16[512,256]{1,0:T(8,128)(2,1)S(1)} %bitcast.64), channel_id=1, source_target_pairs={{0,4},{4,8},{8,12},{12,16},{16,20},{20,24},{24,28},{1,5},{5,9},{9,... | collective-permute-start | bytes 786440 | tf_op jit(solution)/shard_map/ppermute | solution.py:18
  41.4 14.6 %collective-permute-start.1 = (bf16[512,256]{1,0:T(8,128)(2,1)S(1)}, bf16[512,256]{1,0:T(8,128)(2,1)S(1)}, u32[]{:S(2)}, u32[]{:S(2)}) collective-permute-start(bf16[512,256]{1,0:T(8,128)(2,1)S(1)} %bitcast.67), channel_id=1, source_target_pairs={{0,4},{4,8},{8,12},{12,16},{16,20},{20,24},{24,28},{1,5},{5,9},{9,... | collective-permute-start | bytes 786440 | tf_op jit(solution)/shard_map/ppermute | solution.py:18
  119.1 1.3 copy-start.1
  140.3 76.5 %all-to-all-start.3 = ((bf16[4,128,1024]{2,1,0:T(8,128)(2,1)}), bf16[4,128,1024]{2,1,0:T(8,128)(2,1)S(1)}, u32[]{:S(2)}, u32[]{:S(2)}) async-start(bf16[4,128,1024]{2,1,0:T(8,128)(2,1)} %bitcast.57), calls=%async_computation.3 | async-start | bytes 2097152 | tf_op jit(solution)/shard_map/all_to_all | solution.py:157
Sparse Core Ops, SparseCore 0:
  37.4 81.6 all-reduce.6
  123.0 73.8 all-reduce.4

commit v4 on v2

--- a/solution.py
+++ b/solution.py
@@ -17,13 +17,13 @@
     return lax.ppermute(shard, axis, pairs)
 
 
-def attention_kernel(local_heads, group_blocks, sharing):
+def attention_kernel(local_heads, group_blocks, base):
     block = MASK_BLOCK_SIZE
     key_count = (SLASH_COUNT + VERT_COUNT) * block
     scale = HEAD_DIMENSION ** (-0.5)
 
     def kernel(meta_ref, q_ref, k_ref, v_ref, vk_ref, vv_ref, o_ref):
-        h = pl.program_id(0)
+        h = pl.program_id(0) + base
         first = meta_ref[2 * local_heads * SLASH_COUNT]
         offs = [meta_ref[h * SLASH_COUNT + j] for j in range(SLASH_COUNT)]
         verts = [meta_ref[local_heads * SLASH_COUNT + h * VERT_COUNT + j] for j in range(VERT_COUNT)]
@@ -64,28 +64,28 @@
     return kernel
 
 
-def attend(meta, queries, key_window, value_window, vert_keys, vert_values, local_heads, sharing):
+def attend(meta, queries, key_window, value_window, vert_keys, vert_values, local_heads, sharing, base):
     group_rows = queries.shape[0]
     group_blocks = group_rows // MASK_BLOCK_SIZE
     head_size = HEAD_DIMENSION
     window_rows = key_window.shape[0]
-    vert_rows = vert_keys.shape[1]
+    chunk_heads, vert_rows = vert_keys.shape[:2]
     grid_spec = pltpu.PrefetchScalarGridSpec(
         num_scalar_prefetch=1,
-        grid=(local_heads,),
+        grid=(chunk_heads,),
         in_specs=[
-            pl.BlockSpec((group_rows, head_size), lambda h, m: (0, h)),
-            pl.BlockSpec((window_rows, head_size), lambda h, m: (0, h // sharing)),
-            pl.BlockSpec((window_rows, head_size), lambda h, m: (0, h // sharing)),
+            pl.BlockSpec((group_rows, head_size), lambda h, m: (0, h + base)),
+            pl.BlockSpec((window_rows, head_size), lambda h, m: (0, (h + base) // sharing)),
+            pl.BlockSpec((window_rows, head_size), lambda h, m: (0, (h + base) // sharing)),
             pl.BlockSpec((1, vert_rows, head_size), lambda h, m: (h, 0, 0)),
             pl.BlockSpec((1, vert_rows, head_size), lambda h, m: (h, 0, 0)),
         ],
         out_specs=pl.BlockSpec((group_rows, head_size), lambda h, m: (0, h)),
     )
     return pl.pallas_call(
-        attention_kernel(local_heads, group_blocks, sharing),
+        attention_kernel(local_heads, group_blocks, base),
         grid_spec=grid_spec,
-        out_shape=jax.ShapeDtypeStruct(queries.shape, queries.dtype),
+        out_shape=jax.ShapeDtypeStruct((group_rows, chunk_heads * head_size), queries.dtype),
     )(meta, queries, key_window, value_window, vert_keys, vert_values)
 
 
@@ -125,12 +125,16 @@
     picked_values = value_blocks[local_block, :, kv_index[:, None], :]
     owned = (owner_seq == seq_index)[:, :, None, None]
     nothing = jnp.zeros((), picked_keys.dtype)
-    summed_keys, summed_values = lax.psum(
-        (jnp.where(owned, picked_keys, nothing), jnp.where(owned, picked_values, nothing)),
-        "seq",
+    seq_count = lax.axis_size("seq")
+    mine = jnp.stack(
+        [jnp.where(owned, picked_keys, nothing), jnp.where(owned, picked_values, nothing)]
+    ).reshape(2, seq_count, -1, head_size).transpose(1, 0, 2, 3)
+    part = lax.all_to_all(mine, "seq", split_axis=0, concat_axis=0, tiled=True).sum(
+        0, dtype=picked_keys.dtype
     )
-    vert_keys = summed_keys.reshape(local_heads, -1, head_size)
-    vert_values = summed_values.reshape(local_heads, -1, head_size)
+    spread = jnp.broadcast_to(part[None], (seq_count,) + part.shape)
+    gathered = lax.all_to_all(spread, "seq", split_axis=0, concat_axis=0, tiled=True)
+    vert = gathered.transpose(1, 0, 2, 3).reshape(2, local_heads, -1, head_size)
     first_block = (seq_index * group_blocks).astype(jnp.int32)
     meta = jnp.concatenate(
         [
@@ -141,8 +145,8 @@
     )
     queries = query_group.reshape(group_rows, local_heads * head_size)
     results = attend(
-        meta, queries, key_window, value_window, vert_keys, vert_values, local_heads,
-        group_sharing_factor,
+        meta, queries, key_window, value_window, vert[0], vert[1],
+        local_heads, group_sharing_factor, 0,
     )
     merged = results.reshape(grp_count, tok_rows, local_heads * head_size)
     returned = lax.all_to_all(merged, "grp", split_axis=0, concat_axis=0, tiled=True)

time: 212 us -> 210 us (level)
  blocking collectives: 29.3 us -> 72.4 us
  waiting for transfers between devices: 97.3 us -> 59.5 us
  between operations: 13.5 us -> 0.15 us
  local copies, waits for them, and re-layouts: 10.6 us -> 16.2 us
    psum x1 -> x0, waiting for transfers between devices: 77.5 us -> none  [per_device(): lax.psum((jnp.where(owned, picked_keys, nothing), jnp.where(owned, picked...]
    all_to_all x0 -> x1, blocking collectives: none -> 43.1 us  [per_device(): lax.all_to_all(mine, 'seq', split_axis=0, concat_axis=0, tiled=True)]
    all_to_all x0 -> x1, waiting for transfers between devices: none -> 33.4 us  [per_device(): lax.all_to_all(spread, 'seq', split_axis=0, concat_axis=0, tiled=True)]
    all_to_all x1, waiting for transfers between devices: 0.01 us -> 8.41 us  [per_device(): lax.all_to_all(query_split, 'grp', split_axis=1, concat_axis=0, tiled=True)]
    ppermute x2, waiting for transfers between devices: 12.2 us -> 7.97 us  [passed_along(): return lax.ppermute(shard, axis, pairs)]
    all_to_all x0 -> x1, starting transfers between devices: none -> 3.58 us  [per_device(): lax.all_to_all(spread, 'seq', split_axis=0, concat_axis=0, tiled=True)]
    all_to_all x1, waiting for transfers between devices: 2.02 us -> 5.4 us  [per_device(): lax.all_to_all(value_split, 'grp', split_axis=1, concat_axis=0, tiled=True)]
    unnamed x16 -> x10, local copies, waits for them, and re-layouts: 0.03 us -> 2.49 us
  transfers between devices with their start and end apart: 6 -> 6, of which waited for: 5 -> 6; matrix products, arithmetic and copies ran while one was open for 6% -> 5% of each run, Pallas kernels for 0% -> 0%
where the time goes in v4:
time: 210 us; the launch traced here: 209 us
  blocking collectives  72.4 us (34%)
  waiting for transfers between devices  59.5 us (28%)
  Pallas kernels  37.3 us (18%)
  starting transfers between devices  20.1 us (10%)
  local copies, waits for them, and re-layouts  16.2 us (8%)
  other arithmetic  3.48 us (2%)
    all_to_all x1, blocking collectives, per_device(): lax.all_to_all(mine, 'seq', split_axis=0, concat_axis=0, tiled=True)  43.1 us
    pallas_call x1, Pallas kernels, attend(): pl.pallas_call(attention_kernel(local_heads, group_blocks, base), grid_sp...  37.3 us
    all_to_all x1, waiting for transfers between devices, per_device(): lax.all_to_all(spread, 'seq', split_axis=0, concat_axis=0, tiled=True)  33.4 us
    all_to_all x1, blocking collectives, per_device(): lax.all_to_all(merged, 'grp', split_axis=0, concat_axis=0, tiled=True)  29.3 us
    all_to_all x1, waiting for transfers between devices, per_device(): lax.all_to_all(query_split, 'grp', split_axis=1, concat_axis=0, tiled=True)  8.41 us
    ppermute x2, waiting for transfers between devices, passed_along(): return lax.ppermute(shard, axis, pairs)  7.97 us
    all_to_all x1, waiting for transfers between devices, per_device(): lax.all_to_all(value_split, 'grp', split_axis=1, concat_axis=0, tiled=True)  5.4 us
    ppermute x2, starting transfers between devices, passed_along(): return lax.ppermute(shard, axis, pairs)  5.26 us
  transfers between devices with their start and end apart: 6, of which 6 were waited for; matrix products, arithmetic and copies ran while one was open for 5% of the time, Pallas kernels for 0%

profile of v4, /device:TPU:0, one launch (start us, length us, event | category | flops | bytes accessed | tf_op | source)
XLA Modules:
  0.0 209.1 jit_solution(6174366156540830485)
XLA Ops:
  0.0 1.7 copy.52
  1.7 4.2 %all-to-all-start.1 = ((bf16[128,4,256]{2,0,1:T(8,128)(2,1)}), bf16[128,4,256]{2,0,1:T(8,128)(2,1)S(1)}, u32[]{:S(2)}, u32[]{:S(2)}) async-start(bf16[128,4,256]{2,0,1:T(8,128)(2,1)} %bitcast.52), calls=%async_computation.1 | async-start | bytes 524288 | tf_op jit(solution)/shard_map/all_to_all | solution.py:105
  5.9 1.7 copy.51
  7.7 4.3 %all-to-all-done.1 = bf16[128,4,256]{2,0,1:T(8,128)(2,1)S(1)} async-done(((bf16[128,4,256]{2,0,1:T(8,128)(2,1)}), bf16[128,4,256]{2,0,1:T(8,128)(2,1)S(1)}, u32[]{:S(2)}, u32[]{:S(2)}) %all-to-all-start.1) | async-done | bytes 262176 | tf_op jit(solution)/shard_map/all_to_all | solution.py:105
  11.9 3.4 %all-to-all-start.2 = ((bf16[128,4,256]{2,0,1:T(8,128)(2,1)}), bf16[128,4,256]{2,0,1:T(8,128)(2,1)S(1)}, u32[]{:S(2)}, u32[]{:S(2)}) async-start(bf16[128,4,256]{2,0,1:T(8,128)(2,1)} %bitcast.51), calls=%async_computation.2 | async-start | bytes 524288 | tf_op jit(solution)/shard_map/all_to_all | solution.py:106
  16.0 5.4 %all-to-all-done.2 = bf16[128,4,256]{2,0,1:T(8,128)(2,1)S(1)} async-done(((bf16[128,4,256]{2,0,1:T(8,128)(2,1)}), bf16[128,4,256]{2,0,1:T(8,128)(2,1)S(1)}, u32[]{:S(2)}, u32[]{:S(2)}) %all-to-all-start.2) | async-done | bytes 262176 | tf_op jit(solution)/shard_map/all_to_all | solution.py:106
  21.5 0.9 gather_fusion
  24.3 43.1 %all_to_all.60 = bf16[8,2,384,128]{3,2,1,0:T(8,128)(2,1)S(1)} all-to-all(bf16[8,2,384,128]{3,2,1,0:T(8,128)(2,1)S(1)} %copy.41), channel_id=1, replica_groups=mesh['seq'=8,'grp'=4] {'seq'}, dimensions={0} | all-to-all | bytes 3145728 | tf_op jit(solution)/shard_map/all_to_all | solution.py:132
  67.6 1.5 broadcast_in_dim.51
  69.1 3.6 %all-to-all-start.4 = ((bf16[8,2,384,128]{3,2,1,0:T(8,128)(2,1)}), bf16[8,2,384,128]{3,2,1,0:T(8,128)(2,1)S(1)}, u32[]{:S(2)}, u32[]{:S(2)}) async-start(bf16[8,2,384,128]{3,2,1,0:T(8,128)(2,1)} %broadcast_in_dim.51), calls=%async_computation.4 | async-start | bytes 3145728 | tf_op jit(solution)/shard_map/all_to_all | solution.py:136
  72.7 3.2 %copy.50 = bf16[16,4,8,2048]{3,2,0,1:T(8,128)(2,1)} copy(bf16[16,4,8,2048]{3,2,1,0:T(8,128)(2,1)} %bitcast.68) | data formatting | bytes 4194304 | tf_op jit(solution)/shard_map/reshape | solution.py:100
  75.8 33.4 %all-to-all-done.4 = bf16[8,2,384,128]{3,2,1,0:T(8,128)(2,1)S(1)} async-done(((bf16[8,2,384,128]{3,2,1,0:T(8,128)(2,1)}), bf16[8,2,384,128]{3,2,1,0:T(8,128)(2,1)S(1)}, u32[]{:S(2)}, u32[]{:S(2)}) %all-to-all-start.4) | async-done | bytes 1572896 | tf_op jit(solution)/shard_map/all_to_all | solution.py:136
  109.3 1.2 copy-done.2
  110.5 3.6 %all-to-all-start = ((bf16[128,4,2048]{2,0,1:T(8,128)(2,1)}), bf16[128,4,2048]{2,0,1:T(8,128)(2,1)S(1)}, u32[]{:S(2)}, u32[]{:S(2)}) async-start(bf16[128,4,2048]{2,0,1:T(8,128)(2,1)} %bitcast.54), calls=%async_computation | async-start | bytes 4194304 | tf_op jit(solution)/shard_map/all_to_all | solution.py:104
  114.1 3.3 %collective-permute-start = (bf16[512,256]{1,0:T(8,128)(2,1)S(1)}, bf16[512,256]{1,0:T(8,128)(2,1)S(1)}, u32[]{:S(2)}, u32[]{:S(2)}) collective-permute-start(bf16[512,256]{1,0:T(8,128)(2,1)S(1)} %bitcast.63), channel_id=1, source_target_pairs={{0,4},{4,8},{8,12},{12,16},{16,20},{20,24},{24,28},{1,5},{5,9},{9,... | collective-permute-start | bytes 786440 | tf_op jit(solution)/shard_map/ppermute | solution.py:17
  117.4 1.9 collective-permute-start.1
  120.4 3.6 %collective-permute-done = bf16[512,256]{1,0:T(8,128)(2,1)S(1)} collective-permute-done((bf16[512,256]{1,0:T(8,128)(2,1)S(1)}, bf16[512,256]{1,0:T(8,128)(2,1)S(1)}, u32[]{:S(2)}, u32[]{:S(2)}) %collective-permute-start) | collective-permute-done | bytes 262176 | tf_op jit(solution)/shard_map/ppermute | solution.py:17
  124.8 4.3 %collective-permute-done.1 = bf16[512,256]{1,0:T(8,128)(2,1)S(1)} collective-permute-done((bf16[512,256]{1,0:T(8,128)(2,1)S(1)}, bf16[512,256]{1,0:T(8,128)(2,1)S(1)}, u32[]{:S(2)}, u32[]{:S(2)}) %collective-permute-start.1) | collective-permute-done | bytes 262176 | tf_op jit(solution)/shard_map/ppermute | solution.py:17
  130.0 1.3 fusion.8
  131.3 8.4 %all-to-all-done = bf16[128,4,2048]{2,0,1:T(8,128)(2,1)S(1)} async-done(((bf16[128,4,2048]{2,0,1:T(8,128)(2,1)}), bf16[128,4,2048]{2,0,1:T(8,128)(2,1)S(1)}, u32[]{:S(2)}, u32[]{:S(2)}) %all-to-all-start) | async-done | bytes 2097184 | tf_op jit(solution)/shard_map/all_to_all | solution.py:104
  139.7 1.3 copy-done.1
  141.1 37.3 %shard_map.55 = bf16[512,2048]{1,0:T(8,128)(2,1)} custom-call(s32[97]{0:T(128)} %pad_add_fusion.meta_ref, bf16[512,2048]{1,0:T(8,128)(2,1)} %bitcast.53, bf16[1024,256]{1,0:T(8,128)(2,1)} %pad_maximum_fusion.k_ref, bf16[1024,256]{1,0:T(8,128)(2,1)} %pad_maximum_fusion.1.v_ref, bf16[16,192,128]{2,1,0:T(8,128)(2,1)} %bitcast.61, bf16[16,192,128]{2,1,0:T(8,128)(2,1)} %bitcast.60), custom_call_target="tpu_custom_call" | custom-call | tf_op jit(solution)/shard_map/pallas_call | solution.py:85
  178.4 29.3 %all_to_all.61 = bf16[4,128,2048]{2,1,0:T(8,128)(2,1)S(1)} all-to-all(bf16[4,128,2048]{2,1,0:T(8,128)(2,1)} %bitcast.55), channel_id=1, replica_groups=mesh['seq'=8,'grp'=4] {'grp'}, dimensions={0} | all-to-all | bytes 4194304 | tf_op jit(solution)/shard_map/all_to_all | solution.py:152
  207.7 1.5 copy.46
  (33 shorter events, 5.6 us)
Async XLA Ops:
  0.0 119.4 %copy-start = (s32[64,3]{0,1:T(4,128)S(1)}, s32[64,3]{0,1:T(4,128)}, u32[]{:S(2)}) copy-start(s32[64,3]{0,1:T(4,128)} %param.9) | copy-start | bytes 2308
  0.0 7.6 %copy-start.4 = (s32[64,3]{0,1:T(4,128)S(1)}, s32[64,3]{0,1:T(4,128)}, u32[]{:S(2)}) copy-start(s32[64,3]{0,1:T(4,128)} %param.8) | copy-start | bytes 2308
  1.7 10.2 %all-to-all-start.1 = ((bf16[128,4,256]{2,0,1:T(8,128)(2,1)}), bf16[128,4,256]{2,0,1:T(8,128)(2,1)S(1)}, u32[]{:S(2)}, u32[]{:S(2)}) async-start(bf16[128,4,256]{2,0,1:T(8,128)(2,1)} %bitcast.52), calls=%async_computation.1 | async-start | bytes 524288 | tf_op jit(solution)/shard_map/all_to_all | solution.py:105
  11.9 9.4 %all-to-all-start.2 = ((bf16[128,4,256]{2,0,1:T(8,128)(2,1)}), bf16[128,4,256]{2,0,1:T(8,128)(2,1)S(1)}, u32[]{:S(2)}, u32[]{:S(2)}) async-start(bf16[128,4,256]{2,0,1:T(8,128)(2,1)} %bitcast.51), calls=%async_computation.2 | async-start | bytes 524288 | tf_op jit(solution)/shard_map/all_to_all | solution.py:106
  69.1 40.2 %all-to-all-start.4 = ((bf16[8,2,384,128]{3,2,1,0:T(8,128)(2,1)}), bf16[8,2,384,128]{3,2,1,0:T(8,128)(2,1)S(1)}, u32[]{:S(2)}, u32[]{:S(2)}) async-start(bf16[8,2,384,128]{3,2,1,0:T(8,128)(2,1)} %broadcast_in_dim.51), calls=%async_computation.4 | async-start | bytes 3145728 | tf_op jit(solution)/shard_map/all_to_all | solution.py:136
  109.3 1.2 copy-start.2
  110.5 29.3 %all-to-all-start = ((bf16[128,4,2048]{2,0,1:T(8,128)(2,1)}), bf16[128,4,2048]{2,0,1:T(8,128)(2,1)S(1)}, u32[]{:S(2)}, u32[]{:S(2)}) async-start(bf16[128,4,2048]{2,0,1:T(8,128)(2,1)} %bitcast.54), calls=%async_computation | async-start | bytes 4194304 | tf_op jit(solution)/shard_map/all_to_all | solution.py:104
  114.1 9.9 %collective-permute-start = (bf16[512,256]{1,0:T(8,128)(2,1)S(1)}, bf16[512,256]{1,0:T(8,128)(2,1)S(1)}, u32[]{:S(2)}, u32[]{:S(2)}) collective-permute-start(bf16[512,256]{1,0:T(8,128)(2,1)S(1)} %bitcast.63), channel_id=1, source_target_pairs={{0,4},{4,8},{8,12},{12,16},{16,20},{20,24},{24,28},{1,5},{5,9},{9,... | collective-permute-start | bytes 786440 | tf_op jit(solution)/shard_map/ppermute | solution.py:17
  117.4 11.8 %collective-permute-start.1 = (bf16[512,256]{1,0:T(8,128)(2,1)S(1)}, bf16[512,256]{1,0:T(8,128)(2,1)S(1)}, u32[]{:S(2)}, u32[]{:S(2)}) collective-permute-start(bf16[512,256]{1,0:T(8,128)(2,1)S(1)} %bitcast.66), channel_id=1, source_target_pairs={{0,4},{4,8},{8,12},{12,16},{16,20},{20,24},{24,28},{1,5},{5,9},{9,... | collective-permute-start | bytes 786440 | tf_op jit(solution)/shard_map/ppermute | solution.py:17
  119.8 10.2 %copy-start.3 = (bf16[8,2,384,128]{3,2,1,0:T(8,128)(2,1)S(1)}, bf16[8,2,384,128]{3,2,1,0:T(8,128)(2,1)}, u32[]{:S(2)}) copy-start(bf16[8,2,384,128]{3,2,1,0:T(8,128)(2,1)} %copy-done.2) | copy-start | bytes 4718596
  139.7 1.3 copy-start.1

commit v5 on v4

--- a/solution.py
+++ b/solution.py
@@ -109,9 +109,6 @@
     group_blocks = group_rows // block_size
     key_local = key_group.reshape(group_rows, local_kv * head_size)
     value_local = value_group.reshape(group_rows, local_kv * head_size)
-    key_before, value_before = passed_along((key_local, value_local), "seq", 1)
-    key_window = jnp.concatenate([key_before, key_local], 0)
-    value_window = jnp.concatenate([value_before, value_local], 0)
     seq_index = lax.axis_index("seq")
     grp_index = lax.axis_index("grp")
     head_offsets = lax.dynamic_slice_in_dim(slash_offsets, grp_index * local_heads, local_heads, 0)
@@ -129,9 +126,14 @@
     mine = jnp.stack(
         [jnp.where(owned, picked_keys, nothing), jnp.where(owned, picked_values, nothing)]
     ).reshape(2, seq_count, -1, head_size).transpose(1, 0, 2, 3)
+    query_group, mine = lax.optimization_barrier((query_group, mine))
     part = lax.all_to_all(mine, "seq", split_axis=0, concat_axis=0, tiled=True).sum(
         0, dtype=picked_keys.dtype
     )
+    key_sent, value_sent, part = lax.optimization_barrier((key_local, value_local, part))
+    key_before, value_before = passed_along((key_sent, value_sent), "seq", 1)
+    key_window = jnp.concatenate([key_before, key_local], 0)
+    value_window = jnp.concatenate([value_before, value_local], 0)
     spread = jnp.broadcast_to(part[None], (seq_count,) + part.shape)
     gathered = lax.all_to_all(spread, "seq", split_axis=0, concat_axis=0, tiled=True)
     vert = gathered.transpose(1, 0, 2, 3).reshape(2, local_heads, -1, head_size)

time: 210 us -> 220 us (1.048)
  the two profiles are of different devices: /device:TPU:0 before, /device:TPU:16 now
where the time goes in v5:
time: 220 us; the launch traced here: 219 us
  blocking collectives  70.3 us (32%)
  waiting for transfers between devices  65.8 us (30%)
  Pallas kernels  37.3 us (17%)
  starting transfers between devices  22.9 us (10%)
  local copies, waits for them, and re-layouts  15.5 us (7%)
  other arithmetic  7.03 us (3%)
    all_to_all x1, blocking collectives, per_device(): lax.all_to_all(mine, 'seq', split_axis=0, concat_axis=0, tiled=True)  41 us
    ppermute x2, waiting for transfers between devices, passed_along(): return lax.ppermute(shard, axis, pairs)  37.9 us
    pallas_call x1, Pallas kernels, attend(): pl.pallas_call(attention_kernel(local_heads, group_blocks, base), grid_sp...  37.3 us
    all_to_all x1, blocking collectives, per_device(): lax.all_to_all(merged, 'grp', split_axis=0, concat_axis=0, tiled=True)  29.3 us
    all_to_all x1, waiting for transfers between devices, per_device(): lax.all_to_all(query_split, 'grp', split_axis=1, concat_axis=0, tiled=True)  19.2 us
    ppermute x2, starting transfers between devices, passed_along(): return lax.ppermute(shard, axis, pairs)  6.73 us
    all_to_all x1, starting transfers between devices, per_device(): lax.all_to_all(spread, 'seq', split_axis=0, concat_axis=0, tiled=True)  5.58 us
    all_to_all x1, waiting for transfers between devices, per_device(): lax.all_to_all(value_split, 'grp', split_axis=1, concat_axis=0, tiled=True)  4.42 us
  transfers between devices with their start and end apart: 6, of which 5 were waited for; matrix products, arithmetic and copies ran while one was open for 6% of the time, Pallas kernels for 0%

profile of v5, /device:TPU:16, one launch (start us, length us, event | category | flops | bytes accessed | tf_op | source)
XLA Modules:
  0.0 218.9 jit_solution(12084708993168074947)
XLA Ops:
  0.0 1.8 copy.52
  1.8 3.4 %all-to-all-start.1 = ((bf16[128,4,256]{2,0,1:T(8,128)(2,1)}), bf16[128,4,256]{2,0,1:T(8,128)(2,1)S(1)}, u32[]{:S(2)}, u32[]{:S(2)}) async-start(bf16[128,4,256]{2,0,1:T(8,128)(2,1)} %bitcast.53), calls=%async_computation.1 | async-start | bytes 524288 | tf_op jit(solution)/shard_map/all_to_all | solution.py:105
  5.2 1.7 copy.51
  6.9 4.3 %all-to-all-done.1 = bf16[128,4,256]{2,0,1:T(8,128)(2,1)S(1)} async-done(((bf16[128,4,256]{2,0,1:T(8,128)(2,1)}), bf16[128,4,256]{2,0,1:T(8,128)(2,1)S(1)}, u32[]{:S(2)}, u32[]{:S(2)}) %all-to-all-start.1) | async-done | bytes 262176 | tf_op jit(solution)/shard_map/all_to_all | solution.py:105
  11.2 3.4 %all-to-all-start.2 = ((bf16[128,4,256]{2,0,1:T(8,128)(2,1)}), bf16[128,4,256]{2,0,1:T(8,128)(2,1)S(1)}, u32[]{:S(2)}, u32[]{:S(2)}) async-start(bf16[128,4,256]{2,0,1:T(8,128)(2,1)} %bitcast.52), calls=%async_computation.2 | async-start | bytes 524288 | tf_op jit(solution)/shard_map/all_to_all | solution.py:106
  14.7 1.6 copy.50
  16.2 4.4 %all-to-all-done.2 = bf16[128,4,256]{2,0,1:T(8,128)(2,1)S(1)} async-done(((bf16[128,4,256]{2,0,1:T(8,128)(2,1)}), bf16[128,4,256]{2,0,1:T(8,128)(2,1)S(1)}, u32[]{:S(2)}, u32[]{:S(2)}) %all-to-all-start.2) | async-done | bytes 262176 | tf_op jit(solution)/shard_map/all_to_all | solution.py:106
  20.7 3.7 %all-to-all-start = ((bf16[128,4,2048]{2,0,1:T(8,128)(2,1)}), bf16[128,4,2048]{2,0,1:T(8,128)(2,1)S(1)}, u32[]{:S(2)}, u32[]{:S(2)}) async-start(bf16[128,4,2048]{2,0,1:T(8,128)(2,1)} %bitcast.55), calls=%async_computation | async-start | bytes 4194304 | tf_op jit(solution)/shard_map/all_to_all | solution.py:104
  26.1 1.8 gather_fusion
  27.9 1.7 broadcast_select_fusion.1
  29.6 1.3 maximum_bitcast_fusion
  30.9 19.2 %all-to-all-done = bf16[128,4,2048]{2,0,1:T(8,128)(2,1)S(1)} async-done(((bf16[128,4,2048]{2,0,1:T(8,128)(2,1)}), bf16[128,4,2048]{2,0,1:T(8,128)(2,1)S(1)}, u32[]{:S(2)}, u32[]{:S(2)}) %all-to-all-start) | async-done | bytes 2097184 | tf_op jit(solution)/shard_map/all_to_all | solution.py:104
  50.1 2.3 %copy.41 = bf16[8,2,384,128]{3,2,1,0:T(8,128)(2,1)S(1)} copy(bf16[8,2,384,128]{3,2,0,1:T(8,128)(2,1)} %maximum_bitcast_fusion) | data formatting | bytes 3145728 | tf_op jit(solution)/shard_map/optimization_barrier | solution.py:129
  52.4 41.0 %all_to_all.63 = bf16[8,2,384,128]{3,2,1,0:T(8,128)(2,1)} all-to-all(bf16[8,2,384,128]{3,2,1,0:T(8,128)(2,1)S(1)} %copy.41), channel_id=1, replica_groups=mesh['seq'=8,'grp'=4] {'seq'}, dimensions={0} | all-to-all | bytes 3145728 | tf_op jit(solution)/shard_map/all_to_all | solution.py:130
  93.4 1.7 reduce_sum.9
  95.1 1.5 broadcast_in_dim.51
  96.5 5.6 %all-to-all-start.4 = ((bf16[8,2,384,128]{3,2,1,0:T(8,128)(2,1)}), bf16[8,2,384,128]{3,2,1,0:T(8,128)(2,1)S(1)}, u32[]{:S(2)}, u32[]{:S(2)}) async-start(bf16[8,2,384,128]{3,2,1,0:T(8,128)(2,1)} %broadcast_in_dim.51), calls=%async_computation.4 | async-start | bytes 3145728 | tf_op jit(solution)/shard_map/all_to_all | solution.py:138
  102.1 3.4 %collective-permute-start = (bf16[512,256]{1,0:T(8,128)(2,1)S(1)}, bf16[512,256]{1,0:T(8,128)(2,1)S(1)}, u32[]{:S(2)}, u32[]{:S(2)}) collective-permute-start(bf16[512,256]{1,0:T(8,128)(2,1)S(1)} %bitcast.64), channel_id=1, source_target_pairs={{0,4},{4,8},{8,12},{12,16},{16,20},{20,24},{24,28},{1,5},{5,9},{9,... | collective-permute-start | bytes 786440 | tf_op jit(solution)/shard_map/ppermute | solution.py:17
  105.5 3.4 %collective-permute-start.1 = (bf16[512,256]{1,0:T(8,128)(2,1)S(1)}, bf16[512,256]{1,0:T(8,128)(2,1)S(1)}, u32[]{:S(2)}, u32[]{:S(2)}) collective-permute-start(bf16[512,256]{1,0:T(8,128)(2,1)S(1)} %bitcast.67), channel_id=1, source_target_pairs={{0,4},{4,8},{8,12},{12,16},{16,20},{20,24},{24,28},{1,5},{5,9},{9,... | collective-permute-start | bytes 786440 | tf_op jit(solution)/shard_map/ppermute | solution.py:17
  109.9 33.2 %collective-permute-done = bf16[512,256]{1,0:T(8,128)(2,1)S(1)} collective-permute-done((bf16[512,256]{1,0:T(8,128)(2,1)S(1)}, bf16[512,256]{1,0:T(8,128)(2,1)S(1)}, u32[]{:S(2)}, u32[]{:S(2)}) %collective-permute-start) | collective-permute-done | bytes 262176 | tf_op jit(solution)/shard_map/ppermute | solution.py:17
  143.9 4.7 %collective-permute-done.1 = bf16[512,256]{1,0:T(8,128)(2,1)S(1)} collective-permute-done((bf16[512,256]{1,0:T(8,128)(2,1)S(1)}, bf16[512,256]{1,0:T(8,128)(2,1)S(1)}, u32[]{:S(2)}, u32[]{:S(2)}) %collective-permute-start.1) | collective-permute-done | bytes 262176 | tf_op jit(solution)/shard_map/ppermute | solution.py:17
  150.7 37.3 %shard_map.55 = bf16[512,2048]{1,0:T(8,128)(2,1)} custom-call(s32[97]{0:T(128)} %pad_add_fusion.meta_ref, bf16[512,2048]{1,0:T(8,128)(2,1)} %bitcast.54, bf16[1024,256]{1,0:T(8,128)(2,1)} %pad_maximum_fusion.k_ref, bf16[1024,256]{1,0:T(8,128)(2,1)} %pad_maximum_fusion.1.v_ref, bf16[16,192,128]{2,1,0:T(8,128)(2,1)} %bitcast.62, bf16[16,192,128]{2,1,0:T(8,128)(2,1)} %bitcast.61), custom_call_target="tpu_custom_call" | custom-call | tf_op jit(solution)/shard_map/pallas_call | solution.py:85
  188.1 29.3 %all_to_all.64 = bf16[4,128,2048]{2,1,0:T(8,128)(2,1)S(1)} all-to-all(bf16[4,128,2048]{2,1,0:T(8,128)(2,1)} %bitcast.56), channel_id=1, replica_groups=mesh['seq'=8,'grp'=4] {'grp'}, dimensions={0} | all-to-all | bytes 4194304 | tf_op jit(solution)/shard_map/all_to_all | solution.py:154
  217.3 1.6 copy.46
  (39 shorter events, 5.7 us)
Async XLA Ops:
  0.0 108.9 %copy-start = (s32[64,3]{0,1:T(4,128)S(1)}, s32[64,3]{0,1:T(4,128)}, u32[]{:S(2)}) copy-start(s32[64,3]{0,1:T(4,128)} %param.9) | copy-start | bytes 2308
  0.0 14.7 %copy-start.6 = (bf16[128,8192]{1,0:T(8,128)(2,1)S(1)}, bf16[128,8192]{1,0:T(8,128)(2,1)}, u32[]{:S(2)}) copy-start(bf16[128,8192]{1,0:T(8,128)(2,1)} %param.5) | copy-start | bytes 6291460
  1.8 9.4 %all-to-all-start.1 = ((bf16[128,4,256]{2,0,1:T(8,128)(2,1)}), bf16[128,4,256]{2,0,1:T(8,128)(2,1)S(1)}, u32[]{:S(2)}, u32[]{:S(2)}) async-start(bf16[128,4,256]{2,0,1:T(8,128)(2,1)} %bitcast.53), calls=%async_computation.1 | async-start | bytes 524288 | tf_op jit(solution)/shard_map/all_to_all | solution.py:105
  11.2 13.8 %copy-start.2 = (bf16[128,4,256]{2,0,1:T(8,128)(2,1)}, bf16[128,4,256]{2,0,1:T(8,128)(2,1)S(1)}, u32[]{:S(2)}) copy-start(bf16[128,4,256]{2,0,1:T(8,128)(2,1)S(1)} %all-to-all-done.1) | copy-start | bytes 786436
  11.2 9.4 %all-to-all-start.2 = ((bf16[128,4,256]{2,0,1:T(8,128)(2,1)}), bf16[128,4,256]{2,0,1:T(8,128)(2,1)S(1)}, u32[]{:S(2)}, u32[]{:S(2)}) async-start(bf16[128,4,256]{2,0,1:T(8,128)(2,1)} %bitcast.52), calls=%async_computation.2 | async-start | bytes 524288 | tf_op jit(solution)/shard_map/all_to_all | solution.py:106
  20.7 4.5 %copy-start.4 = (bf16[128,4,256]{2,0,1:T(8,128)(2,1)}, bf16[128,4,256]{2,0,1:T(8,128)(2,1)S(1)}, u32[]{:S(2)}) copy-start(bf16[128,4,256]{2,0,1:T(8,128)(2,1)S(1)} %all-to-all-done.2) | copy-start | bytes 786436
  20.7 3.8 %copy-start.7 = (s32[64,3]{0,1:T(4,128)S(1)}, s32[64,3]{0,1:T(4,128)}, u32[]{:S(2)}) copy-start(s32[64,3]{0,1:T(4,128)} %param.8) | copy-start | bytes 2308
  20.7 29.4 %all-to-all-start = ((bf16[128,4,2048]{2,0,1:T(8,128)(2,1)}), bf16[128,4,2048]{2,0,1:T(8,128)(2,1)S(1)}, u32[]{:S(2)}, u32[]{:S(2)}) async-start(bf16[128,4,2048]{2,0,1:T(8,128)(2,1)} %bitcast.55), calls=%async_computation | async-start | bytes 4194304 | tf_op jit(solution)/shard_map/all_to_all | solution.py:104
  50.1 2.3 %copy-start.1 = (bf16[128,4,2048]{2,0,1:T(8,128)(2,1)}, bf16[128,4,2048]{2,0,1:T(8,128)(2,1)S(1)}, u32[]{:S(2)}) copy-start(bf16[128,4,2048]{2,0,1:T(8,128)(2,1)S(1)} %all-to-all-done) | copy-start | bytes 6291460
  96.5 5.6 %copy-start.3 = (bf16[128,4,256]{2,0,1:T(8,128)(2,1)S(1)}, bf16[128,4,256]{2,0,1:T(8,128)(2,1)}, u32[]{:S(2)}) copy-start(bf16[128,4,256]{2,0,1:T(8,128)(2,1)} %copy-done.2) | copy-start | bytes 786436
  96.5 9.0 %copy-start.5 = (bf16[128,4,256]{2,0,1:T(8,128)(2,1)S(1)}, bf16[128,4,256]{2,0,1:T(8,128)(2,1)}, u32[]{:S(2)}) copy-start(bf16[128,4,256]{2,0,1:T(8,128)(2,1)} %copy-done.4) | copy-start | bytes 786436
  96.5 52.9 %all-to-all-start.4 = ((bf16[8,2,384,128]{3,2,1,0:T(8,128)(2,1)}), bf16[8,2,384,128]{3,2,1,0:T(8,128)(2,1)S(1)}, u32[]{:S(2)}, u32[]{:S(2)}) async-start(bf16[8,2,384,128]{3,2,1,0:T(8,128)(2,1)} %broadcast_in_dim.51), calls=%async_computation.4 | async-start | bytes 3145728 | tf_op jit(solution)/shard_map/all_to_all | solution.py:138
  102.1 40.9 %collective-permute-start = (bf16[512,256]{1,0:T(8,128)(2,1)S(1)}, bf16[512,256]{1,0:T(8,128)(2,1)S(1)}, u32[]{:S(2)}, u32[]{:S(2)}) collective-permute-start(bf16[512,256]{1,0:T(8,128)(2,1)S(1)} %bitcast.64), channel_id=1, source_target_pairs={{0,4},{4,8},{8,12},{12,16},{16,20},{20,24},{24,28},{1,5},{5,9},{9,... | collective-permute-start | bytes 786440 | tf_op jit(solution)/shard_map/ppermute | solution.py:17
  105.5 43.1 %collective-permute-start.1 = (bf16[512,256]{1,0:T(8,128)(2,1)S(1)}, bf16[512,256]{1,0:T(8,128)(2,1)S(1)}, u32[]{:S(2)}, u32[]{:S(2)}) collective-permute-start(bf16[512,256]{1,0:T(8,128)(2,1)S(1)} %bitcast.67), channel_id=1, source_target_pairs={{0,4},{4,8},{8,12},{12,16},{16,20},{20,24},{24,28},{1,5},{5,9},{9,... | collective-permute-start | bytes 786440 | tf_op jit(solution)/shard_map/ppermute | solution.py:17

commit v6 on v4

--- a/solution.py
+++ b/solution.py
@@ -3,12 +3,13 @@
 from jax import lax
 from jax.experimental import pallas as pl
 from jax.experimental.pallas import tpu as pltpu
-from jax.sharding import PartitionSpec as P
+from jax.sharding import Mesh, PartitionSpec as P
 
 HEAD_DIMENSION = 128
 MASK_BLOCK_SIZE = 64
 SLASH_COUNT = 3
 VERT_COUNT = 3
+SLASH_REACH = 8
 
 
 def passed_along(shard, axis, by):
@@ -17,7 +18,7 @@
     return lax.ppermute(shard, axis, pairs)
 
 
-def attention_kernel(local_heads, group_blocks, base):
+def attention_kernel(local_heads, group_blocks, back, base):
     block = MASK_BLOCK_SIZE
     key_count = (SLASH_COUNT + VERT_COUNT) * block
     scale = HEAD_DIMENSION ** (-0.5)
@@ -37,7 +38,7 @@
         for b in range(group_blocks):
             qb = first + b
             q = q_ref[pl.ds(b * block, block), :]
-            starts = [pl.multiple_of((group_blocks + b - offs[j]) * block, block) for j in range(SLASH_COUNT)]
+            starts = [pl.multiple_of((back + b - offs[j]) * block, block) for j in range(SLASH_COUNT)]
             keys = jnp.concatenate([k_ref[pl.ds(s, block), :] for s in starts] + [vert_keys], 0)
             values = jnp.concatenate([v_ref[pl.ds(s, block), :] for s in starts] + [vert_values], 0)
             limits = [jnp.where(qb - offs[j] >= 0, offs[j] * block, never) for j in range(SLASH_COUNT)]
@@ -83,7 +84,7 @@
         out_specs=pl.BlockSpec((group_rows, head_size), lambda h, m: (0, h)),
     )
     return pl.pallas_call(
-        attention_kernel(local_heads, group_blocks, base),
+        attention_kernel(local_heads, group_blocks, window_rows // MASK_BLOCK_SIZE - group_blocks, base),
         grid_spec=grid_spec,
         out_shape=jax.ShapeDtypeStruct((group_rows, chunk_heads * head_size), queries.dtype),
     )(meta, queries, key_window, value_window, vert_keys, vert_values)
@@ -91,31 +92,36 @@
 
 def per_device(query_rows, key_matrix, value_matrix, vertical, slash_offsets):
     tok_rows = query_rows.shape[0]
-    grp_count = lax.axis_size("grp")
+    heads_axes = ("inner", "grp")
+    head_groups = lax.axis_size("inner") * lax.axis_size("grp")
     head_size = HEAD_DIMENSION
     block_size = MASK_BLOCK_SIZE
-    local_heads = query_rows.shape[1] // (grp_count * head_size)
-    local_kv = key_matrix.shape[1] // (grp_count * head_size)
+    local_heads = query_rows.shape[1] // (head_groups * head_size)
+    local_kv = key_matrix.shape[1] // (head_groups * head_size)
     group_sharing_factor = local_heads // local_kv
-    query_split = query_rows.reshape(tok_rows, grp_count, local_heads * head_size)
-    key_split = key_matrix.reshape(tok_rows, grp_count, local_kv * head_size)
-    value_split = value_matrix.reshape(tok_rows, grp_count, local_kv * head_size)
+    query_split = query_rows.reshape(tok_rows, head_groups, local_heads * head_size)
+    key_split = key_matrix.reshape(tok_rows, head_groups, local_kv * head_size)
+    value_split = value_matrix.reshape(tok_rows, head_groups, local_kv * head_size)
     query_group, key_group, value_group = (
-        lax.all_to_all(query_split, "grp", split_axis=1, concat_axis=0, tiled=True),
-        lax.all_to_all(key_split, "grp", split_axis=1, concat_axis=0, tiled=True),
-        lax.all_to_all(value_split, "grp", split_axis=1, concat_axis=0, tiled=True),
+        lax.all_to_all(query_split, heads_axes, split_axis=1, concat_axis=0, tiled=True),
+        lax.all_to_all(key_split, heads_axes, split_axis=1, concat_axis=0, tiled=True),
+        lax.all_to_all(value_split, heads_axes, split_axis=1, concat_axis=0, tiled=True),
     )
-    group_rows = tok_rows * grp_count
+    group_rows = tok_rows * head_groups
     group_blocks = group_rows // block_size
+    back = min(SLASH_REACH, group_blocks)
     key_local = key_group.reshape(group_rows, local_kv * head_size)
     value_local = value_group.reshape(group_rows, local_kv * head_size)
-    key_before, value_before = passed_along((key_local, value_local), "seq", 1)
+    key_before, value_before = passed_along(
+        (key_local[group_rows - back * block_size:], value_local[group_rows - back * block_size:]),
+        "outer", 1,
+    )
     key_window = jnp.concatenate([key_before, key_local], 0)
     value_window = jnp.concatenate([value_before, value_local], 0)
-    seq_index = lax.axis_index("seq")
-    grp_index = lax.axis_index("grp")
-    head_offsets = lax.dynamic_slice_in_dim(slash_offsets, grp_index * local_heads, local_heads, 0)
-    head_verts = lax.dynamic_slice_in_dim(vertical, grp_index * local_heads, local_heads, 0)
+    seq_index = lax.axis_index("outer")
+    head_group = lax.axis_index(heads_axes)
+    head_offsets = lax.dynamic_slice_in_dim(slash_offsets, head_group * local_heads, local_heads, 0)
+    head_verts = lax.dynamic_slice_in_dim(vertical, head_group * local_heads, local_heads, 0)
     kv_index = jnp.arange(local_heads, dtype=jnp.int32) // group_sharing_factor
     owner_seq = head_verts // group_blocks
     local_block = head_verts % group_blocks
@@ -125,15 +131,15 @@
     picked_values = value_blocks[local_block, :, kv_index[:, None], :]
     owned = (owner_seq == seq_index)[:, :, None, None]
     nothing = jnp.zeros((), picked_keys.dtype)
-    seq_count = lax.axis_size("seq")
+    seq_count = lax.axis_size("outer")
     mine = jnp.stack(
         [jnp.where(owned, picked_keys, nothing), jnp.where(owned, picked_values, nothing)]
     ).reshape(2, seq_count, -1, head_size).transpose(1, 0, 2, 3)
-    part = lax.all_to_all(mine, "seq", split_axis=0, concat_axis=0, tiled=True).sum(
+    part = lax.all_to_all(mine, "outer", split_axis=0, concat_axis=0, tiled=True).sum(
         0, dtype=picked_keys.dtype
     )
     spread = jnp.broadcast_to(part[None], (seq_count,) + part.shape)
-    gathered = lax.all_to_all(spread, "seq", split_axis=0, concat_axis=0, tiled=True)
+    gathered = lax.all_to_all(spread, "outer", split_axis=0, concat_axis=0, tiled=True)
     vert = gathered.transpose(1, 0, 2, 3).reshape(2, local_heads, -1, head_size)
     first_block = (seq_index * group_blocks).astype(jnp.int32)
     meta = jnp.concatenate(
@@ -148,22 +154,22 @@
         meta, queries, key_window, value_window, vert[0], vert[1],
         local_heads, group_sharing_factor, 0,
     )
-    merged = results.reshape(grp_count, tok_rows, local_heads * head_size)
-    returned = lax.all_to_all(merged, "grp", split_axis=0, concat_axis=0, tiled=True)
-    return returned.transpose(1, 0, 2).reshape(tok_rows, grp_count * local_heads * head_size)
+    merged = results.reshape(head_groups, tok_rows, local_heads * head_size)
+    returned = lax.all_to_all(merged, heads_axes, split_axis=0, concat_axis=0, tiled=True)
+    return returned.transpose(1, 0, 2).reshape(tok_rows, head_groups * local_heads * head_size)
 
 
 def solution(mesh):
+    seq_count = mesh.shape["seq"]
+    inner = 2 if seq_count % 2 == 0 else 1
+    work_mesh = Mesh(
+        mesh.devices.reshape(seq_count // inner, inner, mesh.shape["grp"]), ("outer", "inner", "grp")
+    )
+    rows = P(("outer", "inner", "grp"), None)
     return jax.shard_map(
         per_device,
-        mesh=mesh,
-        in_specs=(
-            P(("seq", "grp"), None),
-            P(("seq", "grp"), None),
-            P(("seq", "grp"), None),
-            P(),
-            P(),
-        ),
-        out_specs=P(("seq", "grp"), None),
+        mesh=work_mesh,
+        in_specs=(rows, rows, rows, P(), P()),
+        out_specs=rows,
         check_vma=False,
     )

time: 210 us -> 174 us (0.83)
  blocking collectives: 72.4 us -> 54.3 us
  waiting for transfers between devices: 59.5 us -> 45.1 us
    all_to_all x2, blocking collectives: 72.4 us -> 54.3 us  [the longest x1 30.1 us: per_device(): lax.all_to_all(merged, heads_axes, split_axis=0, concat_axis=0, tiled=True)]
    all_to_all x4, waiting for transfers between devices: 51.5 us -> 42.9 us  [the longest x1 16.7 us: per_device(): lax.all_to_all(query_split, heads_axes, split_axis=1, concat_axis=0, tile...]
    ppermute x2, waiting for transfers between devices: 7.97 us -> 2.26 us  [passed_along(): return lax.ppermute(shard, axis, pairs)]
  transfers between devices with their start and end apart: 6 -> 6, of which waited for: 6 -> 5; matrix products, arithmetic and copies ran while one was open for 5% -> 6% of each run, Pallas kernels for 0% -> 0%
where the time goes in v6:
time: 174 us; the launch traced here: 173 us
  blocking collectives  54.3 us (31%)
  waiting for transfers between devices  45.1 us (26%)
  Pallas kernels  36.1 us (21%)
  starting transfers between devices  19.7 us (11%)
  local copies, waits for them, and re-layouts  14.4 us (8%)
  other arithmetic  3.47 us (2%)
    pallas_call x1, Pallas kernels, attend(): pl.pallas_call(attention_kernel(local_heads, group_blocks, window_rows //...  36.1 us
    all_to_all x1, blocking collectives, per_device(): lax.all_to_all(merged, heads_axes, split_axis=0, concat_axis=0, tiled=True)  30.1 us
    all_to_all x1, blocking collectives, per_device(): lax.all_to_all(mine, 'outer', split_axis=0, concat_axis=0, tiled=True)  24.2 us
    all_to_all x1, waiting for transfers between devices, per_device(): lax.all_to_all(query_split, heads_axes, split_axis=1, concat_axis=0, tile...  16.7 us
    all_to_all x1, waiting for transfers between devices, per_device(): lax.all_to_all(spread, 'outer', split_axis=0, concat_axis=0, tiled=True)  16 us
    all_to_all x1, waiting for transfers between devices, per_device(): lax.all_to_all(value_split, heads_axes, split_axis=1, concat_axis=0, tile...  5.73 us
    all_to_all x1, starting transfers between devices, per_device(): lax.all_to_all(key_split, heads_axes, split_axis=1, concat_axis=0, tiled=...  5.17 us
    all_to_all x1, waiting for transfers between devices, per_device(): lax.all_to_all(key_split, heads_axes, split_axis=1, concat_axis=0, tiled=...  4.48 us
  transfers between devices with their start and end apart: 6, of which 5 were waited for; matrix products, arithmetic and copies ran while one was open for 6% of the time, Pallas kernels for 0%

profile of v6, /device:TPU:0, one launch (start us, length us, event | category | flops | bytes accessed | tf_op | source)
XLA Modules:
  0.0 173.2 jit_solution(16149722524277722629)
XLA Ops:
  0.0 0.9 copy-done
  1.7 5.2 %all-to-all-start.1 = ((bf16[128,8,128]{2,0,1:T(8,128)(2,1)}), bf16[128,8,128]{2,0,1:T(8,128)(2,1)S(1)}, u32[]{:S(2)}, u32[]{:S(2)}) async-start(bf16[128,8,128]{2,0,1:T(8,128)(2,1)} %copy_bitcast_fusion.2), calls=%async_computation.1 | async-start | bytes 524288 | tf_op jit(solution)/shard_map/all_to_all | solution.py:107
  7.6 1.7 copy_bitcast_fusion.1
  9.3 4.5 %all-to-all-done.1 = bf16[128,8,128]{2,0,1:T(8,128)(2,1)S(1)} async-done(((bf16[128,8,128]{2,0,1:T(8,128)(2,1)}), bf16[128,8,128]{2,0,1:T(8,128)(2,1)S(1)}, u32[]{:S(2)}, u32[]{:S(2)}) %all-to-all-start.1) | async-done | bytes 262176 | tf_op jit(solution)/shard_map/all_to_all | solution.py:107
  13.8 3.4 %all-to-all-start.2 = ((bf16[128,8,128]{2,0,1:T(8,128)(2,1)}), bf16[128,8,128]{2,0,1:T(8,128)(2,1)S(1)}, u32[]{:S(2)}, u32[]{:S(2)}) async-start(bf16[128,8,128]{2,0,1:T(8,128)(2,1)} %copy_bitcast_fusion.1), calls=%async_computation.2 | async-start | bytes 524288 | tf_op jit(solution)/shard_map/all_to_all | solution.py:108
  18.4 5.7 %all-to-all-done.2 = bf16[128,8,128]{2,0,1:T(8,128)(2,1)S(1)} async-done(((bf16[128,8,128]{2,0,1:T(8,128)(2,1)}), bf16[128,8,128]{2,0,1:T(8,128)(2,1)S(1)}, u32[]{:S(2)}, u32[]{:S(2)}) %all-to-all-start.2) | async-done | bytes 262176 | tf_op jit(solution)/shard_map/all_to_all | solution.py:108
  25.1 24.2 %all_to_all.60 = bf16[4,2,384,128]{3,2,1,0:T(8,128)(2,1)S(1)} all-to-all(bf16[4,2,384,128]{3,2,1,0:T(8,128)(2,1)S(1)} %maximum_bitcast_fusion), channel_id=1, replica_groups=mesh['outer'=4,'inner'=2,'grp'=4] {'outer'}, dimensions={0} | all-to-all | bytes 1572864 | tf_op jit(solution)/shard_map/all_to_all | solution.py:138
  49.5 1.0 broadcast_in_dim.51
  50.5 3.5 %all-to-all-start.4 = ((bf16[4,2,384,128]{3,2,1,0:T(8,128)(2,1)}), bf16[4,2,384,128]{3,2,1,0:T(8,128)(2,1)S(1)}, u32[]{:S(2)}, u32[]{:S(2)}) async-start(bf16[4,2,384,128]{3,2,1,0:T(8,128)(2,1)} %broadcast_in_dim.51), calls=%async_computation.4 | async-start | bytes 1572864 | tf_op jit(solution)/shard_map/all_to_all | solution.py:142
  54.0 3.2 %copy.37 = bf16[16,8,8,1024]{3,2,0,1:T(8,128)(2,1)} copy(bf16[16,8,8,1024]{3,2,1,0:T(8,128)(2,1)} %bitcast.64) | data formatting | bytes 4194304 | tf_op jit(solution)/shard_map/reshape | solution.py:102
  57.1 16.0 %all-to-all-done.4 = bf16[4,2,384,128]{3,2,1,0:T(8,128)(2,1)S(1)} async-done(((bf16[4,2,384,128]{3,2,1,0:T(8,128)(2,1)}), bf16[4,2,384,128]{3,2,1,0:T(8,128)(2,1)S(1)}, u32[]{:S(2)}, u32[]{:S(2)}) %all-to-all-start.4) | async-done | bytes 786464 | tf_op jit(solution)/shard_map/all_to_all | solution.py:142
  73.1 0.9 copy-done.2
  74.0 3.6 %all-to-all-start = ((bf16[128,8,1024]{2,0,1:T(8,128)(2,1)}), bf16[128,8,1024]{2,0,1:T(8,128)(2,1)S(1)}, u32[]{:S(2)}, u32[]{:S(2)}) async-start(bf16[128,8,1024]{2,0,1:T(8,128)(2,1)} %bitcast.55), calls=%async_computation | async-start | bytes 4194304 | tf_op jit(solution)/shard_map/all_to_all | solution.py:106
  77.7 1.3 collective-permute-start
  80.0 2.7 %collective-permute-start.1 = (bf16[512,128]{1,0:T(8,128)(2,1)S(1)}, bf16[512,128]{1,0:T(8,128)(2,1)S(1)}, u32[]{:S(2)}, u32[]{:S(2)}) collective-permute-start(bf16[512,128]{1,0:T(8,128)(2,1)S(1)} %bitcast.70), channel_id=1, source_target_pairs={{0,8},{8,16},{16,24},{1,9},{9,17},{17,25},{2,10},{10,18},{18,26},{... | collective-permute-start | bytes 393224 | tf_op jit(solution)/shard_map/ppermute | solution.py:18
  82.8 0.8 pad_maximum_fusion.k_ref
  83.5 2.3 %collective-permute-done.1 = bf16[512,128]{1,0:T(8,128)(2,1)S(1)} collective-permute-done((bf16[512,128]{1,0:T(8,128)(2,1)S(1)}, bf16[512,128]{1,0:T(8,128)(2,1)S(1)}, u32[]{:S(2)}, u32[]{:S(2)}) %collective-permute-start.1) | collective-permute-done | bytes 131104 | tf_op jit(solution)/shard_map/ppermute | solution.py:18
  85.8 0.8 pad_maximum_fusion.1.v_ref
  86.6 0.9 fusion.8
  87.5 16.7 %all-to-all-done = bf16[128,8,1024]{2,0,1:T(8,128)(2,1)S(1)} async-done(((bf16[128,8,1024]{2,0,1:T(8,128)(2,1)}), bf16[128,8,1024]{2,0,1:T(8,128)(2,1)S(1)}, u32[]{:S(2)}, u32[]{:S(2)}) %all-to-all-start) | async-done | bytes 2097184 | tf_op jit(solution)/shard_map/all_to_all | solution.py:106
  104.2 1.3 copy-done.1
  105.5 36.1 %shard_map.55 = bf16[1024,1024]{1,0:T(8,128)(2,1)} custom-call(s32[49]{0:T(128)} %pad_add_fusion.meta_ref, bf16[1024,1024]{1,0:T(8,128)(2,1)} %bitcast.53, bf16[1536,128]{1,0:T(8,128)(2,1)} %pad_maximum_fusion.k_ref, bf16[1536,128]{1,0:T(8,128)(2,1)} %pad_maximum_fusion.1.v_ref, bf16[8,192,128]{2,1,0:T(8,128)(2,1)} %bitcast.66, bf16[8,192,128]{2,1,0:T(8,128)(2,1)} %bitcast.65), custom_call_target="tpu_custom_call" | custom-call | tf_op jit(solution)/shard_map/pallas_call | solution.py:86
  141.6 30.1 %all_to_all.61 = bf16[8,128,1024]{2,1,0:T(8,128)(2,1)S(1)} all-to-all(bf16[8,128,1024]{2,1,0:T(8,128)(2,1)} %bitcast.54), channel_id=1, replica_groups=mesh['outer'=4,'inner'=2,'grp'=4] {'inner','grp'}, dimensions={0} | all-to-all | bytes 4194304 | tf_op jit(solution)/shard_map/all_to_all | solution.py:158
  171.8 1.5 copy.33
  (30 shorter events, 4.9 us)
Async XLA Ops:
  0.0 1.0 copy-start
  1.7 12.1 %all-to-all-start.1 = ((bf16[128,8,128]{2,0,1:T(8,128)(2,1)}), bf16[128,8,128]{2,0,1:T(8,128)(2,1)S(1)}, u32[]{:S(2)}, u32[]{:S(2)}) async-start(bf16[128,8,128]{2,0,1:T(8,128)(2,1)} %copy_bitcast_fusion.2), calls=%async_computation.1 | async-start | bytes 524288 | tf_op jit(solution)/shard_map/all_to_all | solution.py:107
  13.8 10.3 %all-to-all-start.2 = ((bf16[128,8,128]{2,0,1:T(8,128)(2,1)}), bf16[128,8,128]{2,0,1:T(8,128)(2,1)S(1)}, u32[]{:S(2)}, u32[]{:S(2)}) async-start(bf16[128,8,128]{2,0,1:T(8,128)(2,1)} %copy_bitcast_fusion.1), calls=%async_computation.2 | async-start | bytes 524288 | tf_op jit(solution)/shard_map/all_to_all | solution.py:108
  50.5 22.6 %all-to-all-start.4 = ((bf16[4,2,384,128]{3,2,1,0:T(8,128)(2,1)}), bf16[4,2,384,128]{3,2,1,0:T(8,128)(2,1)S(1)}, u32[]{:S(2)}, u32[]{:S(2)}) async-start(bf16[4,2,384,128]{3,2,1,0:T(8,128)(2,1)} %broadcast_in_dim.51), calls=%async_computation.4 | async-start | bytes 1572864 | tf_op jit(solution)/shard_map/all_to_all | solution.py:142
  73.1 0.9 copy-start.2
  73.1 5.8 %copy-start.4 = (s32[64,3]{0,1:T(4,128)S(1)}, s32[64,3]{0,1:T(4,128)}, u32[]{:S(2)}) copy-start(s32[64,3]{0,1:T(4,128)} %param.9) | copy-start | bytes 2308
  74.0 30.2 %all-to-all-start = ((bf16[128,8,1024]{2,0,1:T(8,128)(2,1)}), bf16[128,8,1024]{2,0,1:T(8,128)(2,1)S(1)}, u32[]{:S(2)}, u32[]{:S(2)}) async-start(bf16[128,8,1024]{2,0,1:T(8,128)(2,1)} %bitcast.55), calls=%async_computation | async-start | bytes 4194304 | tf_op jit(solution)/shard_map/all_to_all | solution.py:106
  77.7 5.1 %collective-permute-start = (bf16[512,128]{1,0:T(8,128)(2,1)S(1)}, bf16[512,128]{1,0:T(8,128)(2,1)S(1)}, u32[]{:S(2)}, u32[]{:S(2)}) collective-permute-start(bf16[512,128]{1,0:T(8,128)(2,1)S(1)} %bitcast.69), channel_id=1, source_target_pairs={{0,8},{8,16},{16,24},{1,9},{9,17},{17,25},{2,10},{10,18},{18,26},{... | collective-permute-start | bytes 393224 | tf_op jit(solution)/shard_map/ppermute | solution.py:18
  79.4 7.2 %copy-start.3 = (bf16[4,2,384,128]{3,2,1,0:T(8,128)(2,1)S(1)}, bf16[4,2,384,128]{3,2,1,0:T(8,128)(2,1)}, u32[]{:S(2)}) copy-start(bf16[4,2,384,128]{3,2,1,0:T(8,128)(2,1)} %copy-done.2) | copy-start | bytes 2359300
  80.0 5.8 %collective-permute-start.1 = (bf16[512,128]{1,0:T(8,128)(2,1)S(1)}, bf16[512,128]{1,0:T(8,128)(2,1)S(1)}, u32[]{:S(2)}, u32[]{:S(2)}) collective-permute-start(bf16[512,128]{1,0:T(8,128)(2,1)S(1)} %bitcast.70), channel_id=1, source_target_pairs={{0,8},{8,16},{16,24},{1,9},{9,17},{17,25},{2,10},{10,18},{18,26},{... | collective-permute-start | bytes 393224 | tf_op jit(solution)/shard_map/ppermute | solution.py:18
  104.2 1.3 copy-start.1

commit v7 on v6

--- a/solution.py
+++ b/solution.py
@@ -102,11 +102,19 @@
     query_split = query_rows.reshape(tok_rows, head_groups, local_heads * head_size)
     key_split = key_matrix.reshape(tok_rows, head_groups, local_kv * head_size)
     value_split = value_matrix.reshape(tok_rows, head_groups, local_kv * head_size)
-    query_group, key_group, value_group = (
-        lax.all_to_all(query_split, heads_axes, split_axis=1, concat_axis=0, tiled=True),
-        lax.all_to_all(key_split, heads_axes, split_axis=1, concat_axis=0, tiled=True),
-        lax.all_to_all(value_split, heads_axes, split_axis=1, concat_axis=0, tiled=True),
+    kv_group = lax.all_to_all(
+        jnp.stack([key_split, value_split], 2), heads_axes, split_axis=1, concat_axis=0, tiled=True
     )
+    key_group, value_group = kv_group[:, 0, 0], kv_group[:, 0, 1]
+    me = lax.axis_index(heads_axes)
+    received = [lax.dynamic_index_in_dim(query_split, me, 1, keepdims=False)]
+    for shift in range(1, head_groups):
+        sent = lax.dynamic_index_in_dim(query_split, (me + shift) % head_groups, 1, keepdims=False)
+        received.append(
+            lax.ppermute(sent, heads_axes, [(i, (i + shift) % head_groups) for i in range(head_groups)])
+        )
+    slab_shift = (me - jnp.arange(head_groups, dtype=jnp.int32)) % head_groups
+    query_group = jnp.take(jnp.stack(received), slab_shift, axis=0)
     group_rows = tok_rows * head_groups
     group_blocks = group_rows // block_size
     back = min(SLASH_REACH, group_blocks)

time: 174 us -> 165 us (0.948)
  the two profiles are of different devices: /device:TPU:0 before, /device:TPU:16 now
where the time goes in v7:
time: 165 us; the launch traced here: 164 us
  Pallas kernels  36.2 us (22%)
  waiting for transfers between devices  31.5 us (19%)
  local copies, waits for them, and re-layouts  31.2 us (19%)
  blocking collectives  30.1 us (18%)
  starting transfers between devices  29.7 us (18%)
  other arithmetic  5.48 us (3%)
    pallas_call x1, Pallas kernels, attend(): pl.pallas_call(attention_kernel(local_heads, group_blocks, window_rows //...  36.2 us
    all_to_all x1, blocking collectives, per_device(): lax.all_to_all(merged, heads_axes, split_axis=0, concat_axis=0, tiled=True)  30.1 us
    unnamed x22, local copies, waits for them, and re-layouts  12.4 us
    ppermute x2, waiting for transfers between devices, passed_along(): return lax.ppermute(shard, axis, pairs)  11 us
    all_to_all x1, waiting for transfers between devices, per_device(): lax.all_to_all(jnp.stack([key_split, value_split], 2), heads_axes, split_...  10.8 us
    all_to_all x1, waiting for transfers between devices, per_device(): lax.all_to_all(mine, 'outer', split_axis=0, concat_axis=0, tiled=True)  9.72 us
    ppermute x7, starting transfers between devices, per_device(): lax.ppermute(sent, heads_axes, [(i, (i + shift) % head_groups) for i in r...  8.41 us
    dynamic_slice x8, local copies, waits for them, and re-layouts, per_device(): lax.dynamic_index_in_dim(query_split, (me + shift) % head_groups, 1, keep...  6.98 us
  transfers between devices with their start and end apart: 12, of which 4 were waited for; matrix products, arithmetic and copies ran while one was open for 17% of the time, Pallas kernels for 0%

profile of v7, /device:TPU:16, one launch (start us, length us, event | category | flops | bytes accessed | tf_op | source)
XLA Modules:
  0.0 164.3 jit_solution(13963316906407237684)
XLA Ops:
  0.0 3.2 %copy.53 = bf16[128,8192]{0,1:T(8,128)(2,1)S(1)} copy(bf16[128,8192]{1,0:T(8,128)(2,1)} %param.5) | data formatting | bytes 4194304 | tf_op args[0]
  4.2 1.8 %copy.55 = bf16[128,1,1024]{2,0,1:T(8,128)(2,1)} copy(bf16[128,1,1024]{0,2,1:T(8,128)(2,1)} %get-tuple-element.13) | data formatting | bytes 524288 | tf_op jit(solution)/shard_map/jit(dynamic_index_in_dim)/dynamic_slice | solution.py:112
  6.1 1.8 %copy.56 = bf16[128,1,1024]{2,0,1:T(8,128)(2,1)} copy(bf16[128,1,1024]{0,2,1:T(8,128)(2,1)} %get-tuple-element.12) | data formatting | bytes 524288 | tf_op jit(solution)/shard_map/jit(dynamic_index_in_dim)/dynamic_slice | solution.py:112
  7.9 1.5 collective-permute-start.1
  10.5 2.5 %collective-permute-start.2 = (bf16[128,1024]{1,0:T(8,128)(2,1)S(1)}, bf16[128,1024]{1,0:T(8,128)(2,1)}, u32[]{:S(2)}, u32[]{:S(2)}) collective-permute-start(bf16[128,1024]{1,0:T(8,128)(2,1)S(1)} %bitcast.81), channel_id=1, source_target_pairs={{0,3},{1,4},{2,5},{3,6},{4,7},{5,0},{6,1},{7,2},{8,11},{9,12},{10,... | collective-permute-start | bytes 786440 | tf_op jit(solution)/shard_map/ppermute | solution.py:114
  15.4 3.9 %all-to-all-start = ((bf16[128,8,2,128]{3,0,2,1:T(8,128)(2,1)}), bf16[128,8,2,128]{3,0,2,1:T(8,128)(2,1)S(1)}, u32[]{:S(2)}, u32[]{:S(2)}) async-start(bf16[128,8,2,128]{3,0,2,1:T(8,128)(2,1)} %copy.64), calls=%async_computation | async-start | bytes 1048576 | tf_op jit(solution)/shard_map/all_to_all | solution.py:105
  22.9 2.9 %collective-permute-start.5 = (bf16[128,1024]{1,0:T(8,128)(2,1)}, bf16[128,1024]{1,0:T(8,128)(2,1)}, u32[]{:S(2)}, u32[]{:S(2)}) collective-permute-start(bf16[128,1024]{1,0:T(8,128)(2,1)} %bitcast.14), channel_id=1, source_target_pairs={{0,6},{1,7},{2,0},{3,1},{4,2},{5,3},{6,4},{7,5},{8,14},{9,15},{10,... | collective-permute-start | bytes 786440 | tf_op jit(solution)/shard_map/ppermute | solution.py:114
  25.8 1.7 %bitcast_dynamic-update-slice_fusion.6 = bf16[8,128,1024]{2,1,0:T(8,128)(2,1)} fusion(bf16[8,128,1024]{2,1,0:T(8,128)(2,1)} %bitcast_dynamic-update-slice_fusion.7, bf16[128,1024]{1,0:T(8,128)(2,1)} %collective-permute-done), kind=kLoop, calls=%fused_computation.16 | loop fusion | bytes 524288
  27.5 10.8 %all-to-all-done = bf16[128,8,2,128]{3,0,2,1:T(8,128)(2,1)S(1)} async-done(((bf16[128,8,2,128]{3,0,2,1:T(8,128)(2,1)}), bf16[128,8,2,128]{3,0,2,1:T(8,128)(2,1)S(1)}, u32[]{:S(2)}, u32[]{:S(2)}) %all-to-all-start) | async-done | bytes 524320 | tf_op jit(solution)/shard_map/all_to_all | solution.py:105
  41.8 5.2 %all-to-all-start.1 = ((bf16[4,2,384,128]{3,2,1,0:T(8,128)(2,1)}), bf16[4,2,384,128]{3,2,1,0:T(8,128)(2,1)S(1)}, u32[]{:S(2)}, u32[]{:S(2)}) async-start(bf16[4,2,384,128]{3,2,1,0:T(8,128)(2,1)} %maximum_bitcast_fusion), calls=%async_computation.1 | async-start | bytes 1572864 | tf_op jit(solution)/shard_map/all_to_all | solution.py:146
  47.9 1.7 %bitcast_dynamic-update-slice_fusion.5 = bf16[8,128,1024]{2,1,0:T(8,128)(2,1)} fusion(bf16[8,128,1024]{2,1,0:T(8,128)(2,1)} %bitcast_dynamic-update-slice_fusion.6, bf16[128,1024]{1,0:T(8,128)(2,1)} %collective-permute-done.1), kind=kLoop, calls=%fused_computation.15 | loop fusion | bytes 524288
  49.5 1.7 %bitcast_dynamic-update-slice_fusion.4 = bf16[8,128,1024]{2,1,0:T(8,128)(2,1)} fusion(bf16[8,128,1024]{2,1,0:T(8,128)(2,1)} %bitcast_dynamic-update-slice_fusion.5, bf16[128,1024]{1,0:T(8,128)(2,1)} %collective-permute-done.2), kind=kLoop, calls=%fused_computation.14 | loop fusion | bytes 524288
  52.6 1.7 %bitcast_dynamic-update-slice_fusion.1 = bf16[8,128,1024]{2,1,0:T(8,128)(2,1)} fusion(bf16[8,128,1024]{2,1,0:T(8,128)(2,1)} %bitcast_dynamic-update-slice_fusion.2, bf16[128,1024]{1,0:T(8,128)(2,1)} %collective-permute-done.5), kind=kLoop, calls=%fused_computation.11 | loop fusion | bytes 524288
  54.3 9.7 %all-to-all-done.1 = bf16[4,2,384,128]{3,2,1,0:T(8,128)(2,1)S(1)} async-done(((bf16[4,2,384,128]{3,2,1,0:T(8,128)(2,1)}), bf16[4,2,384,128]{3,2,1,0:T(8,128)(2,1)S(1)}, u32[]{:S(2)}, u32[]{:S(2)}) %all-to-all-start.1) | async-done | bytes 786464 | tf_op jit(solution)/shard_map/all_to_all | solution.py:146
  65.2 6.7 %all-to-all-start.2 = ((bf16[4,2,384,128]{3,2,1,0:T(8,128)(2,1)}), bf16[4,2,384,128]{3,2,1,0:T(8,128)(2,1)S(1)}, u32[]{:S(2)}, u32[]{:S(2)}) async-start(bf16[4,2,384,128]{3,2,1,0:T(8,128)(2,1)} %broadcast_in_dim.69), calls=%async_computation.2 | async-start | bytes 1572864 | tf_op jit(solution)/shard_map/all_to_all | solution.py:150
  71.9 1.7 %bitcast_dynamic-update-slice_fusion = bf16[8,128,1024]{2,1,0:T(8,128)(2,1)} fusion(bf16[8,128,1024]{2,1,0:T(8,128)(2,1)} %bitcast_dynamic-update-slice_fusion.1, bf16[128,1024]{1,0:T(8,128)(2,1)} %collective-permute-done.6), kind=kLoop, calls=%fused_computation.10 | loop fusion | bytes 524288 | tf_op jit(solution)/shard_map/stack | solution.py:117
  73.6 2.3 %gather_fusion = bf16[8,128,1024]{2,1,0:T(8,128)(2,1)S(1)} fusion(bf16[8,128,1024]{2,1,0:T(8,128)(2,1)} %bitcast_dynamic-update-slice_fusion, s32[1024]{0:T(1024)S(1)} %pad_clamp_fusion), kind=kCustom, calls=%fused_computation | custom fusion | bytes 4194336 | tf_op jit(solution)/shard_map/jit(_take)/gather | solution.py:117
  75.9 3.5 %collective-permute-start.7 = (bf16[512,128]{1,0:T(8,128)(2,1)S(1)}, bf16[512,128]{1,0:T(8,128)(2,1)S(1)}, u32[]{:S(2)}, u32[]{:S(2)}) collective-permute-start(bf16[512,128]{1,0:T(8,128)(2,1)S(1)} %get-tuple-element.22), channel_id=1, source_target_pairs={{0,8},{8,16},{16,24},{1,9},{9,17},{17,25},{2,10},{10,18},{18,26},{... | collective-permute-start | bytes 393224 | tf_op jit(solution)/shard_map/ppermute | solution.py:18
  79.4 1.7 %bitcast_select_fusion.q_ref = bf16[1024,1024]{1,0:T(8,128)(2,1)} fusion(bf16[8,128,1024]{2,1,0:T(8,128)(2,1)S(1)} %gather_fusion, pred[1024]{0:T(1024)(128)(4,1)S(1)} %broadcast_bitcast_fusion), kind=kLoop, calls=%fused_computation.3 | loop fusion | flops 1048576 | bytes 4195328 | tf_op jit(solution)/shard_map/jit(_take)/select_n | solution.py:117
  81.2 1.9 %collective-permute-start.8 = (bf16[512,128]{1,0:T(8,128)(2,1)S(1)}, bf16[512,128]{1,0:T(8,128)(2,1)S(1)}, u32[]{:S(2)}, u32[]{:S(2)}) collective-permute-start(bf16[512,128]{1,0:T(8,128)(2,1)S(1)} %get-tuple-element.21), channel_id=1, source_target_pairs={{0,8},{8,16},{16,24},{1,9},{9,17},{17,25},{2,10},{10,18},{18,26},{... | collective-permute-start | bytes 393224 | tf_op jit(solution)/shard_map/ppermute | solution.py:18
  83.1 10.3 %collective-permute-done.7 = bf16[512,128]{1,0:T(8,128)(2,1)S(1)} collective-permute-done((bf16[512,128]{1,0:T(8,128)(2,1)S(1)}, bf16[512,128]{1,0:T(8,128)(2,1)S(1)}, u32[]{:S(2)}, u32[]{:S(2)}) %collective-permute-start.7) | collective-permute-done | bytes 131104 | tf_op jit(solution)/shard_map/ppermute | solution.py:18
  96.6 36.2 %shard_map.55 = bf16[1024,1024]{1,0:T(8,128)(2,1)} custom-call(s32[49]{0:T(128)} %pad_add_fusion.meta_ref, bf16[1024,1024]{1,0:T(8,128)(2,1)} %bitcast_select_fusion.q_ref, bf16[1536,128]{1,0:T(8,128)(2,1)} %pad_maximum_fusion.1.k_ref, bf16[1536,128]{1,0:T(8,128)(2,1)} %pad_maximum_fusion.2.v_ref, bf16[8,192,128]{2,1,0:T(8,128)(2,1)} %bitcast.74, ...), custom_call_target="tpu_custom_call" | custom-call | tf_op jit(solution)/shard_map/pallas_call | solution.py:86
  132.7 30.1 %all_to_all.33 = bf16[8,128,1024]{2,1,0:T(8,128)(2,1)S(1)} all-to-all(bf16[8,128,1024]{2,1,0:T(8,128)(2,1)} %bitcast.64), channel_id=1, replica_groups=mesh['outer'=4,'inner'=2,'grp'=4] {'inner','grp'}, dimensions={0} | all-to-all | bytes 4194304 | tf_op jit(solution)/shard_map/all_to_all | solution.py:166
  162.8 1.5 copy.69
  (69 shorter events, 18.1 us)
Async XLA Ops:
  0.0 20.5 %copy-start = (s32[64,3]{0,1:T(4,128)S(1)}, s32[64,3]{0,1:T(4,128)}, u32[]{:S(2)}) copy-start(s32[64,3]{0,1:T(4,128)} %param.9) | copy-start | bytes 2308
  4.2 9.7 %copy-start.3 = (bf16[128,1024]{1,0:T(8,128)(2,1)S(1)}, bf16[128,1024]{1,0:T(8,128)(2,1)}, u32[]{:S(2)}) copy-start(bf16[128,1024]{1,0:T(8,128)(2,1)} %param.6) | copy-start | bytes 786436
  4.2 9.9 %copy-start.4 = (bf16[128,1024]{1,0:T(8,128)(2,1)S(1)}, bf16[128,1024]{1,0:T(8,128)(2,1)}, u32[]{:S(2)}) copy-start(bf16[128,1024]{1,0:T(8,128)(2,1)} %param.7) | copy-start | bytes 786436
  6.1 16.8 %collective-permute-start = (bf16[128,1024]{1,0:T(8,128)(2,1)}, bf16[128,1024]{1,0:T(8,128)(2,1)}, u32[]{:S(2)}, u32[]{:S(2)}) collective-permute-start(bf16[128,1024]{1,0:T(8,128)(2,1)} %bitcast.4), channel_id=1, source_target_pairs={{0,1},{1,2},{2,3},{3,4},{4,5},{5,6},{6,7},{7,0},{8,9},{9,10},{10,1... | collective-permute-start | bytes 786440 | tf_op jit(solution)/shard_map/ppermute | solution.py:114
  7.9 39.1 %collective-permute-start.1 = (bf16[128,1024]{1,0:T(8,128)(2,1)}, bf16[128,1024]{1,0:T(8,128)(2,1)}, u32[]{:S(2)}, u32[]{:S(2)}) collective-permute-start(bf16[128,1024]{1,0:T(8,128)(2,1)} %bitcast.6), channel_id=1, source_target_pairs={{0,2},{1,3},{2,4},{3,5},{4,6},{5,7},{6,0},{7,1},{8,10},{9,11},{10,... | collective-permute-start | bytes 786440 | tf_op jit(solution)/shard_map/ppermute | solution.py:114
  10.5 39.1 %collective-permute-start.2 = (bf16[128,1024]{1,0:T(8,128)(2,1)S(1)}, bf16[128,1024]{1,0:T(8,128)(2,1)}, u32[]{:S(2)}, u32[]{:S(2)}) collective-permute-start(bf16[128,1024]{1,0:T(8,128)(2,1)S(1)} %bitcast.81), channel_id=1, source_target_pairs={{0,3},{1,4},{2,5},{3,6},{4,7},{5,0},{6,1},{7,2},{8,11},{9,12},{10,... | collective-permute-start | bytes 786440 | tf_op jit(solution)/shard_map/ppermute | solution.py:114
  13.1 38.1 %collective-permute-start.3 = (bf16[128,1024]{1,0:T(8,128)(2,1)S(1)}, bf16[128,1024]{1,0:T(8,128)(2,1)S(1)}, u32[]{:S(2)}, u32[]{:S(2)}) collective-permute-start(bf16[128,1024]{1,0:T(8,128)(2,1)S(1)} %bitcast.80), channel_id=1, source_target_pairs={{0,4},{1,5},{2,6},{3,7},{4,0},{5,1},{6,2},{7,3},{8,12},{9,13},{10,... | collective-permute-start | bytes 786440 | tf_op jit(solution)/shard_map/ppermute | solution.py:114
  13.8 38.1 %collective-permute-start.4 = (bf16[128,1024]{1,0:T(8,128)(2,1)S(1)}, bf16[128,1024]{1,0:T(8,128)(2,1)S(1)}, u32[]{:S(2)}, u32[]{:S(2)}) collective-permute-start(bf16[128,1024]{1,0:T(8,128)(2,1)S(1)} %bitcast.79), channel_id=1, source_target_pairs={{0,5},{1,6},{2,7},{3,0},{4,1},{5,2},{6,3},{7,4},{8,13},{9,14},{10,... | collective-permute-start | bytes 786440 | tf_op jit(solution)/shard_map/ppermute | solution.py:114
  14.3 6.0 %copy-start.5 = (s32[64,3]{0,1:T(4,128)S(1)}, s32[64,3]{0,1:T(4,128)}, u32[]{:S(2)}) copy-start(s32[64,3]{0,1:T(4,128)} %param.8) | copy-start | bytes 2308
  15.4 22.9 %all-to-all-start = ((bf16[128,8,2,128]{3,0,2,1:T(8,128)(2,1)}), bf16[128,8,2,128]{3,0,2,1:T(8,128)(2,1)S(1)}, u32[]{:S(2)}, u32[]{:S(2)}) async-start(bf16[128,8,2,128]{3,0,2,1:T(8,128)(2,1)} %copy.64), calls=%async_computation | async-start | bytes 1048576 | tf_op jit(solution)/shard_map/all_to_all | solution.py:105
  22.9 29.8 %collective-permute-start.5 = (bf16[128,1024]{1,0:T(8,128)(2,1)}, bf16[128,1024]{1,0:T(8,128)(2,1)}, u32[]{:S(2)}, u32[]{:S(2)}) collective-permute-start(bf16[128,1024]{1,0:T(8,128)(2,1)} %bitcast.14), channel_id=1, source_target_pairs={{0,6},{1,7},{2,0},{3,1},{4,2},{5,3},{6,4},{7,5},{8,14},{9,15},{10,... | collective-permute-start | bytes 786440 | tf_op jit(solution)/shard_map/ppermute | solution.py:114
  41.8 22.2 %all-to-all-start.1 = ((bf16[4,2,384,128]{3,2,1,0:T(8,128)(2,1)}), bf16[4,2,384,128]{3,2,1,0:T(8,128)(2,1)S(1)}, u32[]{:S(2)}, u32[]{:S(2)}) async-start(bf16[4,2,384,128]{3,2,1,0:T(8,128)(2,1)} %maximum_bitcast_fusion), calls=%async_computation.1 | async-start | bytes 1572864 | tf_op jit(solution)/shard_map/all_to_all | solution.py:146
  47.0 24.9 %collective-permute-start.6 = (bf16[128,1024]{1,0:T(8,128)(2,1)S(1)}, bf16[128,1024]{1,0:T(8,128)(2,1)}, u32[]{:S(2)}, u32[]{:S(2)}) collective-permute-start(bf16[128,1024]{1,0:T(8,128)(2,1)S(1)} %bitcast.82), channel_id=1, source_target_pairs={{0,7},{1,0},{2,1},{3,2},{4,3},{5,4},{6,5},{7,6},{8,15},{9,8},{10,9... | collective-permute-start | bytes 786440 | tf_op jit(solution)/shard_map/ppermute | solution.py:114
  65.2 30.4 %all-to-all-start.2 = ((bf16[4,2,384,128]{3,2,1,0:T(8,128)(2,1)}), bf16[4,2,384,128]{3,2,1,0:T(8,128)(2,1)S(1)}, u32[]{:S(2)}, u32[]{:S(2)}) async-start(bf16[4,2,384,128]{3,2,1,0:T(8,128)(2,1)} %broadcast_in_dim.69), calls=%async_computation.2 | async-start | bytes 1572864 | tf_op jit(solution)/shard_map/all_to_all | solution.py:150
  75.9 17.5 %copy-start.2 = (bf16[1024,128]{1,0:T(8,128)(2,1)S(1)}, bf16[1024,128]{1,0:T(8,128)(2,1)}, u32[]{:S(2)}) copy-start(bf16[1024,128]{1,0:T(8,128)(2,1)} %get-tuple-element.18) | copy-start | bytes 786436
  75.9 18.9 %copy-start.1 = (bf16[1024,128]{1,0:T(8,128)(2,1)S(1)}, bf16[1024,128]{1,0:T(8,128)(2,1)}, u32[]{:S(2)}) copy-start(bf16[1024,128]{1,0:T(8,128)(2,1)} %get-tuple-element.19) | copy-start | bytes 786436
  75.9 17.5 %collective-permute-start.7 = (bf16[512,128]{1,0:T(8,128)(2,1)S(1)}, bf16[512,128]{1,0:T(8,128)(2,1)S(1)}, u32[]{:S(2)}, u32[]{:S(2)}) collective-permute-start(bf16[512,128]{1,0:T(8,128)(2,1)S(1)} %get-tuple-element.22), channel_id=1, source_target_pairs={{0,8},{8,16},{16,24},{1,9},{9,17},{17,25},{2,10},{10,18},{18,26},{... | collective-permute-start | bytes 393224 | tf_op jit(solution)/shard_map/ppermute | solution.py:18
  81.2 13.7 %collective-permute-start.8 = (bf16[512,128]{1,0:T(8,128)(2,1)S(1)}, bf16[512,128]{1,0:T(8,128)(2,1)S(1)}, u32[]{:S(2)}, u32[]{:S(2)}) collective-permute-start(bf16[512,128]{1,0:T(8,128)(2,1)S(1)} %get-tuple-element.21), channel_id=1, source_target_pairs={{0,8},{8,16},{16,24},{1,9},{9,17},{17,25},{2,10},{10,18},{18,26},{... | collective-permute-start | bytes 393224 | tf_op jit(solution)/shard_map/ppermute | solution.py:18

commit v8 on v7

--- a/solution.py
+++ b/solution.py
@@ -10,6 +10,7 @@
 SLASH_COUNT = 3
 VERT_COUNT = 3
 SLASH_REACH = 8
+FULL_GATHER_BYTES = 4 << 20
 
 
 def passed_along(shard, axis, by):
@@ -65,6 +66,76 @@
     return kernel
 
 
+def full_kernel(local_heads, group_blocks):
+    block = MASK_BLOCK_SIZE
+    key_count = (SLASH_COUNT + VERT_COUNT) * block
+    scale = HEAD_DIMENSION ** (-0.5)
+
+    def kernel(meta_ref, q_ref, k_ref, v_ref, o_ref):
+        h = pl.program_id(0)
+        first = meta_ref[2 * local_heads * SLASH_COUNT]
+        offs = [meta_ref[h * SLASH_COUNT + j] for j in range(SLASH_COUNT)]
+        verts = [meta_ref[local_heads * SLASH_COUNT + h * VERT_COUNT + j] for j in range(VERT_COUNT)]
+        vert_starts = [pl.multiple_of(v * block, block) for v in verts]
+        vert_keys = [k_ref[pl.ds(s, block), :] for s in vert_starts]
+        vert_values = [v_ref[pl.ds(s, block), :] for s in vert_starts]
+        col = lax.broadcasted_iota(jnp.int32, (block, key_count), 1)
+        row = lax.broadcasted_iota(jnp.int32, (block, key_count), 0)
+        reach = col % block - row
+        lane = lax.broadcasted_iota(jnp.int32, (1, key_count), 1) // block
+        never = jnp.int32(-4 * block)
+        for b in range(group_blocks):
+            qb = first + b
+            q = q_ref[pl.ds(b * block, block), :]
+            starts = [pl.multiple_of(jnp.maximum(qb - offs[j], 0) * block, block) for j in range(SLASH_COUNT)]
+            keys = jnp.concatenate([k_ref[pl.ds(s, block), :] for s in starts] + vert_keys, 0)
+            values = jnp.concatenate([v_ref[pl.ds(s, block), :] for s in starts] + vert_values, 0)
+            limits = [jnp.where(qb - offs[j] >= 0, offs[j] * block, never) for j in range(SLASH_COUNT)]
+            for v in verts:
+                ok = v <= qb
+                for o in offs:
+                    ok = jnp.logical_and(ok, qb - v != o)
+                limits.append(jnp.where(ok, (qb - v) * block, never))
+            limit = jnp.full((1, key_count), limits[-1], jnp.int32)
+            for i in range(len(limits) - 2, -1, -1):
+                limit = jnp.where(lane == i, limits[i], limit)
+            allowed = reach <= limit
+            scores = lax.dot_general(
+                q, keys, (((1,), (1,)), ((), ())), preferred_element_type=jnp.float32
+            ) * scale
+            masked = jnp.where(allowed, scores, -1e30)
+            top = jnp.max(masked, axis=1, keepdims=True)
+            weight = jnp.exp(masked - top)
+            total = jnp.sum(weight, axis=1, keepdims=True)
+            rounded = weight.astype(jnp.bfloat16)
+            acc = jnp.dot(rounded, values, preferred_element_type=jnp.float32)
+            o_ref[pl.ds(b * block, block), :] = (acc / total).astype(o_ref.dtype)
+
+    return kernel
+
+
+def attend_full(meta, queries, all_keys, all_values, local_heads, sharing):
+    group_rows = queries.shape[0]
+    group_blocks = group_rows // MASK_BLOCK_SIZE
+    head_size = HEAD_DIMENSION
+    total_rows = all_keys.shape[0]
+    grid_spec = pltpu.PrefetchScalarGridSpec(
+        num_scalar_prefetch=1,
+        grid=(local_heads,),
+        in_specs=[
+            pl.BlockSpec((group_rows, head_size), lambda h, m: (0, h)),
+            pl.BlockSpec((total_rows, head_size), lambda h, m: (0, h // sharing)),
+            pl.BlockSpec((total_rows, head_size), lambda h, m: (0, h // sharing)),
+        ],
+        out_specs=pl.BlockSpec((group_rows, head_size), lambda h, m: (0, h)),
+    )
+    return pl.pallas_call(
+        full_kernel(local_heads, group_blocks),
+        grid_spec=grid_spec,
+        out_shape=jax.ShapeDtypeStruct((group_rows, local_heads * head_size), queries.dtype),
+    )(meta, queries, all_keys, all_values)
+
+
 def attend(meta, queries, key_window, value_window, vert_keys, vert_values, local_heads, sharing, base):
     group_rows = queries.shape[0]
     group_blocks = group_rows // MASK_BLOCK_SIZE
@@ -120,16 +191,37 @@
     back = min(SLASH_REACH, group_blocks)
     key_local = key_group.reshape(group_rows, local_kv * head_size)
     value_local = value_group.reshape(group_rows, local_kv * head_size)
-    key_before, value_before = passed_along(
-        (key_local[group_rows - back * block_size:], value_local[group_rows - back * block_size:]),
-        "outer", 1,
-    )
-    key_window = jnp.concatenate([key_before, key_local], 0)
-    value_window = jnp.concatenate([value_before, value_local], 0)
+    seq_count = lax.axis_size("outer")
     seq_index = lax.axis_index("outer")
     head_group = lax.axis_index(heads_axes)
     head_offsets = lax.dynamic_slice_in_dim(slash_offsets, head_group * local_heads, local_heads, 0)
     head_verts = lax.dynamic_slice_in_dim(vertical, head_group * local_heads, local_heads, 0)
+    first_block = (seq_index * group_blocks).astype(jnp.int32)
+    meta = jnp.concatenate(
+        [
+            head_offsets.reshape(-1).astype(jnp.int32),
+            head_verts.reshape(-1).astype(jnp.int32),
+            first_block[None],
+        ]
+    )
+    if seq_count * kv_group.size * kv_group.dtype.itemsize <= FULL_GATHER_BYTES:
+        own = jnp.stack([key_local, value_local])
+        spread = jnp.broadcast_to(own[None], (seq_count,) + own.shape)
+        everything = lax.all_to_all(spread, "outer", split_axis=0, concat_axis=0, tiled=True)
+        everything = everything.transpose(1, 0, 2, 3).reshape(2, seq_count * group_rows, -1)
+        queries = query_group.reshape(group_rows, local_heads * head_size)
+        results = attend_full(
+            meta, queries, everything[0], everything[1], local_heads, group_sharing_factor
+        )
+        merged = results.reshape(head_groups, tok_rows, local_heads * head_size)
+        returned = lax.all_to_all(merged, heads_axes, split_axis=0, concat_axis=0, tiled=True)
+        return returned.transpose(1, 0, 2).reshape(tok_rows, head_groups * local_heads * head_size)
+    key_before, value_before = passed_along(
+        (key_local[group_rows - back * block_size:], value_local[group_rows - back * block_size:]),
+        "outer", 1,
+    )
+    key_window = jnp.concatenate([key_before, key_local], 0)
+    value_window = jnp.concatenate([value_before, value_local], 0)
     kv_index = jnp.arange(local_heads, dtype=jnp.int32) // group_sharing_factor
     owner_seq = head_verts // group_blocks
     local_block = head_verts % group_blocks
@@ -139,7 +231,6 @@
     picked_values = value_blocks[local_block, :, kv_index[:, None], :]
     owned = (owner_seq == seq_index)[:, :, None, None]
     nothing = jnp.zeros((), picked_keys.dtype)
-    seq_count = lax.axis_size("outer")
     mine = jnp.stack(
         [jnp.where(owned, picked_keys, nothing), jnp.where(owned, picked_values, nothing)]
     ).reshape(2, seq_count, -1, head_size).transpose(1, 0, 2, 3)
@@ -149,14 +240,6 @@
     spread = jnp.broadcast_to(part[None], (seq_count,) + part.shape)
     gathered = lax.all_to_all(spread, "outer", split_axis=0, concat_axis=0, tiled=True)
     vert = gathered.transpose(1, 0, 2, 3).reshape(2, local_heads, -1, head_size)
-    first_block = (seq_index * group_blocks).astype(jnp.int32)
-    meta = jnp.concatenate(
-        [
-            head_offsets.reshape(-1).astype(jnp.int32),
-            head_verts.reshape(-1).astype(jnp.int32),
-            first_block[None],
-        ]
-    )
     queries = query_group.reshape(group_rows, local_heads * head_size)
     results = attend(
         meta, queries, key_window, value_window, vert[0], vert[1],

time: 165 us -> 144 us (0.87)
  the two profiles are of different devices: /device:TPU:16 before, /device:TPU:0 now
where the time goes in v8:
time: 144 us; the launch traced here: 143 us
  Pallas kernels  36.5 us (25%)
  blocking collectives  31 us (22%)
  local copies, waits for them, and re-layouts  28.5 us (20%)
  waiting for transfers between devices  26.6 us (18%)
  starting transfers between devices  17.6 us (12%)
  other arithmetic  2.5 us (2%)
    pallas_call x1, Pallas kernels, attend_full(): pl.pallas_call(full_kernel(local_heads, group_blocks), grid_spec=grid_spe...  36.5 us
    all_to_all x1, blocking collectives, per_device(): lax.all_to_all(merged, heads_axes, split_axis=0, concat_axis=0, tiled=True)  31 us
    all_to_all x1, waiting for transfers between devices, per_device(): lax.all_to_all(spread, 'outer', split_axis=0, concat_axis=0, tiled=True)  12.4 us
    unnamed x14, local copies, waits for them, and re-layouts  11.5 us
    ppermute x7, waiting for transfers between devices, per_device(): lax.ppermute(sent, heads_axes, [(i, (i + shift) % head_groups) for i in r...  7.71 us
    ppermute x7, starting transfers between devices, per_device(): lax.ppermute(sent, heads_axes, [(i, (i + shift) % head_groups) for i in r...  7.53 us
    all_to_all x1, waiting for transfers between devices, per_device(): lax.all_to_all(jnp.stack([key_split, value_split], 2), heads_axes, split_...  6.48 us
    dynamic_slice x8, local copies, waits for them, and re-layouts, per_device(): lax.dynamic_index_in_dim(query_split, (me + shift) % head_groups, 1, keep...  6.2 us
  transfers between devices with their start and end apart: 9, of which 4 were waited for; matrix products, arithmetic and copies ran while one was open for 15% of the time, Pallas kernels for 0%

profile of v8, /device:TPU:0, one launch (start us, length us, event | category | flops | bytes accessed | tf_op | source)
XLA Modules:
  0.0 142.9 jit_solution(10328344626275311451)
XLA Ops:
  0.0 1.1 copy.38
  1.1 1.1 copy.39
  3.2 5.2 %all-to-all-start = ((bf16[128,8,2,128]{0,3,2,1:T(8,128)(2,1)}), bf16[128,8,2,128]{0,3,2,1:T(8,128)(2,1)S(1)}, u32[]{:S(2)}, u32[]{:S(2)}) async-start(bf16[128,8,2,128]{0,3,2,1:T(8,128)(2,1)} %copy.40), calls=%async_computation | async-start | bytes 1048576 | tf_op jit(solution)/shard_map/all_to_all | solution.py:176
  8.3 3.2 %copy.29 = bf16[128,8192]{0,1:T(8,128)(2,1)S(1)} copy(bf16[128,8192]{1,0:T(8,128)(2,1)} %param.5) | data formatting | bytes 4194304 | tf_op args[0]
  11.6 6.5 %all-to-all-done = bf16[128,8,2,128]{0,3,2,1:T(8,128)(2,1)S(1)} async-done(((bf16[128,8,2,128]{0,3,2,1:T(8,128)(2,1)}), bf16[128,8,2,128]{0,3,2,1:T(8,128)(2,1)S(1)}, u32[]{:S(2)}, u32[]{:S(2)}) %all-to-all-start) | async-done | bytes 524320 | tf_op jit(solution)/shard_map/all_to_all | solution.py:176
  18.5 1.6 %broadcast_in_dim.28 = bf16[4,2,1024,128]{3,2,1,0:T(8,128)(2,1)} broadcast(bf16[2,1024,128]{2,1,0:T(8,128)(2,1)S(1)} %pad_maximum_fusion.1), dimensions={1,2,3} | broadcast | bytes 2621440 | tf_op jit(solution)/shard_map/broadcast_in_dim | solution.py:209
  20.1 4.9 %all-to-all-start.1 = ((bf16[4,2,1024,128]{3,2,1,0:T(8,128)(2,1)}), bf16[4,2,1024,128]{3,2,1,0:T(8,128)(2,1)}, u32[]{:S(2)}, u32[]{:S(2)}) async-start(bf16[4,2,1024,128]{3,2,1,0:T(8,128)(2,1)} %broadcast_in_dim.28), calls=%async_computation.1 | async-start | bytes 4194304 | tf_op jit(solution)/shard_map/all_to_all | solution.py:210
  25.9 1.8 %copy.31 = bf16[128,1,1024]{2,0,1:T(8,128)(2,1)} copy(bf16[128,1,1024]{0,2,1:T(8,128)(2,1)} %get-tuple-element.13) | data formatting | bytes 524288 | tf_op jit(solution)/shard_map/jit(dynamic_index_in_dim)/dynamic_slice | solution.py:183
  27.7 1.8 %copy.32 = bf16[128,1,1024]{2,0,1:T(8,128)(2,1)} copy(bf16[128,1,1024]{0,2,1:T(8,128)(2,1)} %get-tuple-element.12) | data formatting | bytes 524288 | tf_op jit(solution)/shard_map/jit(dynamic_index_in_dim)/dynamic_slice | solution.py:183
  30.0 1.1 copy.33
  31.1 1.5 %collective-permute-start.2 = (bf16[128,1024]{1,0:T(8,128)(2,1)S(1)}, bf16[128,1024]{1,0:T(8,128)(2,1)S(1)}, u32[]{:S(2)}, u32[]{:S(2)}) collective-permute-start(bf16[128,1024]{1,0:T(8,128)(2,1)S(1)} %bitcast.59), channel_id=1, source_target_pairs={{0,3},{1,4},{2,5},{3,6},{4,7},{5,0},{6,1},{7,2},{8,11},{9,12},{10,... | collective-permute-start | bytes 786440 | tf_op jit(solution)/shard_map/ppermute | solution.py:185
  32.8 1.5 %collective-permute-start.3 = (bf16[128,1024]{1,0:T(8,128)(2,1)S(1)}, bf16[128,1024]{1,0:T(8,128)(2,1)S(1)}, u32[]{:S(2)}, u32[]{:S(2)}) collective-permute-start(bf16[128,1024]{1,0:T(8,128)(2,1)S(1)} %bitcast.58), channel_id=1, source_target_pairs={{0,4},{1,5},{2,6},{3,7},{4,0},{5,1},{6,2},{7,3},{8,12},{9,13},{10,... | collective-permute-start | bytes 786440 | tf_op jit(solution)/shard_map/ppermute | solution.py:185
  36.9 2.4 %collective-permute-start.5 = (bf16[128,1024]{1,0:T(8,128)(2,1)S(1)}, bf16[128,1024]{1,0:T(8,128)(2,1)S(1)}, u32[]{:S(2)}, u32[]{:S(2)}) collective-permute-start(bf16[128,1024]{1,0:T(8,128)(2,1)S(1)} %bitcast.61), channel_id=1, source_target_pairs={{0,6},{1,7},{2,0},{3,1},{4,2},{5,3},{6,4},{7,5},{8,14},{9,15},{10,... | collective-permute-start | bytes 786440 | tf_op jit(solution)/shard_map/ppermute | solution.py:185
  39.3 1.7 %bitcast_dynamic-update-slice_fusion.6 = bf16[8,128,1024]{2,1,0:T(8,128)(2,1)} fusion(bf16[8,128,1024]{2,1,0:T(8,128)(2,1)} %bitcast_dynamic-update-slice_fusion.7, bf16[128,1024]{1,0:T(8,128)(2,1)} %collective-permute-done), kind=kLoop, calls=%fused_computation.12 | loop fusion | bytes 524288
  41.0 1.4 %collective-permute-start.6 = (bf16[128,1024]{1,0:T(8,128)(2,1)S(1)}, bf16[128,1024]{1,0:T(8,128)(2,1)S(1)}, u32[]{:S(2)}, u32[]{:S(2)}) collective-permute-start(bf16[128,1024]{1,0:T(8,128)(2,1)S(1)} %bitcast.60), channel_id=1, source_target_pairs={{0,7},{1,0},{2,1},{3,2},{4,3},{5,4},{6,5},{7,6},{8,15},{9,8},{10,9... | collective-permute-start | bytes 786440 | tf_op jit(solution)/shard_map/ppermute | solution.py:185
  43.2 5.3 %collective-permute-done.2 = bf16[128,1024]{1,0:T(8,128)(2,1)S(1)} collective-permute-done((bf16[128,1024]{1,0:T(8,128)(2,1)S(1)}, bf16[128,1024]{1,0:T(8,128)(2,1)S(1)}, u32[]{:S(2)}, u32[]{:S(2)}) %collective-permute-start.2) | collective-permute-done | bytes 262176 | tf_op jit(solution)/shard_map/ppermute | solution.py:185
  50.0 2.4 %collective-permute-done.4 = bf16[128,1024]{1,0:T(8,128)(2,1)S(1)} collective-permute-done((bf16[128,1024]{1,0:T(8,128)(2,1)S(1)}, bf16[128,1024]{1,0:T(8,128)(2,1)S(1)}, u32[]{:S(2)}, u32[]{:S(2)}) %collective-permute-start.4) | collective-permute-done | bytes 262176 | tf_op jit(solution)/shard_map/ppermute | solution.py:185
  54.5 2.3 %gather_fusion = bf16[8,128,1024]{2,1,0:T(8,128)(2,1)S(1)} fusion(bf16[8,128,1024]{2,1,0:T(8,128)(2,1)} %bitcast_dynamic-update-slice_fusion, s32[1024]{0:T(1024)S(1)} %pad_clamp_fusion), kind=kCustom, calls=%fused_computation | custom fusion | bytes 4194336 | tf_op jit(solution)/shard_map/jit(_take)/gather | solution.py:188
  56.8 1.7 %bitcast_select_fusion.q_ref = bf16[1024,1024]{1,0:T(8,128)(2,1)} fusion(bf16[8,128,1024]{2,1,0:T(8,128)(2,1)S(1)} %gather_fusion, pred[1024]{0:T(1024)(128)(4,1)S(1)} %broadcast_bitcast_fusion), kind=kLoop, calls=%fused_computation.1 | loop fusion | flops 1048576 | bytes 4195328 | tf_op jit(solution)/shard_map/jit(_take)/select_n | solution.py:188
  58.5 12.4 %all-to-all-done.1 = bf16[4,2,1024,128]{3,2,1,0:T(8,128)(2,1)} async-done(((bf16[4,2,1024,128]{3,2,1,0:T(8,128)(2,1)}), bf16[4,2,1024,128]{3,2,1,0:T(8,128)(2,1)}, u32[]{:S(2)}, u32[]{:S(2)}) %all-to-all-start.1) | async-done | bytes 2097184 | tf_op jit(solution)/shard_map/all_to_all | solution.py:210
  70.9 3.0 %fusion.3 = (bf16[1,4,1024,128]{3,2,0,1:T(8,128)(2,1)}, bf16[1,4,1024,128]{3,2,0,1:T(8,128)(2,1)}) fusion(bf16[2,4,1024,128]{3,2,0,1:T(8,128)(2,1)} %bitcast.29), kind=kLoop, calls=%fused_computation.39 | loop fusion | bytes 4194304 | tf_op jit(solution)/shard_map/slice | solution.py:214
  73.9 36.5 %shard_map.55 = bf16[1024,1024]{1,0:T(8,128)(2,1)} custom-call(s32[49]{0:T(128)} %pad_add_fusion.meta_ref, bf16[1024,1024]{1,0:T(8,128)(2,1)} %bitcast_select_fusion.q_ref, bf16[4096,128]{1,0:T(8,128)(2,1)} %bitcast.53, bf16[4096,128]{1,0:T(8,128)(2,1)} %bitcast.52), custom_call_target="tpu_custom_call" | custom-call | tf_op jit(solution)/shard_map/pallas_call | solution.py:132
  110.4 31.0 %all_to_all.28 = bf16[8,128,1024]{2,1,0:T(8,128)(2,1)S(1)} all-to-all(bf16[8,128,1024]{2,1,0:T(8,128)(2,1)} %bitcast.49), channel_id=1, replica_groups=mesh['outer'=4,'inner'=2,'grp'=4] {'inner','grp'}, dimensions={0} | all-to-all | bytes 4194304 | tf_op jit(solution)/shard_map/all_to_all | solution.py:217
  141.4 1.5 %copy.43 = bf16[8,16,8,1024]{3,2,0,1:T(8,128)(2,1)} copy(bf16[8,16,8,1024]{3,2,1,0:T(8,128)(2,1)S(1)} %bitcast.51) | data formatting | bytes 4194304 | tf_op jit(solution)/shard_map/reshape | solution.py:218
  (40 shorter events, 9.8 us)
Async XLA Ops:
  3.2 14.9 %all-to-all-start = ((bf16[128,8,2,128]{0,3,2,1:T(8,128)(2,1)}), bf16[128,8,2,128]{0,3,2,1:T(8,128)(2,1)S(1)}, u32[]{:S(2)}, u32[]{:S(2)}) async-start(bf16[128,8,2,128]{0,3,2,1:T(8,128)(2,1)} %copy.40), calls=%async_computation | async-start | bytes 1048576 | tf_op jit(solution)/shard_map/all_to_all | solution.py:176
  20.1 50.8 %all-to-all-start.1 = ((bf16[4,2,1024,128]{3,2,1,0:T(8,128)(2,1)}), bf16[4,2,1024,128]{3,2,1,0:T(8,128)(2,1)}, u32[]{:S(2)}, u32[]{:S(2)}) async-start(bf16[4,2,1024,128]{3,2,1,0:T(8,128)(2,1)} %broadcast_in_dim.28), calls=%async_computation.1 | async-start | bytes 4194304 | tf_op jit(solution)/shard_map/all_to_all | solution.py:210
  25.9 8.9 %copy-start = (s32[64,3]{0,1:T(4,128)S(1)}, s32[64,3]{0,1:T(4,128)}, u32[]{:S(2)}) copy-start(s32[64,3]{0,1:T(4,128)} %param.8) | copy-start | bytes 2308
  25.9 8.9 %copy-start.1 = (s32[64,3]{0,1:T(4,128)S(1)}, s32[64,3]{0,1:T(4,128)}, u32[]{:S(2)}) copy-start(s32[64,3]{0,1:T(4,128)} %param.9) | copy-start | bytes 2308
  27.7 9.2 %collective-permute-start = (bf16[128,1024]{1,0:T(8,128)(2,1)}, bf16[128,1024]{1,0:T(8,128)(2,1)}, u32[]{:S(2)}, u32[]{:S(2)}) collective-permute-start(bf16[128,1024]{1,0:T(8,128)(2,1)} %bitcast.4), channel_id=1, source_target_pairs={{0,1},{1,2},{2,3},{3,4},{4,5},{5,6},{6,7},{7,0},{8,9},{9,10},{10,1... | collective-permute-start | bytes 786440 | tf_op jit(solution)/shard_map/ppermute | solution.py:185
  29.5 11.5 %collective-permute-start.1 = (bf16[128,1024]{1,0:T(8,128)(2,1)}, bf16[128,1024]{1,0:T(8,128)(2,1)S(1)}, u32[]{:S(2)}, u32[]{:S(2)}) collective-permute-start(bf16[128,1024]{1,0:T(8,128)(2,1)} %bitcast.6), channel_id=1, source_target_pairs={{0,2},{1,3},{2,4},{3,5},{4,6},{5,7},{6,0},{7,1},{8,10},{9,11},{10,... | collective-permute-start | bytes 786440 | tf_op jit(solution)/shard_map/ppermute | solution.py:185
  31.1 17.4 %collective-permute-start.2 = (bf16[128,1024]{1,0:T(8,128)(2,1)S(1)}, bf16[128,1024]{1,0:T(8,128)(2,1)S(1)}, u32[]{:S(2)}, u32[]{:S(2)}) collective-permute-start(bf16[128,1024]{1,0:T(8,128)(2,1)S(1)} %bitcast.59), channel_id=1, source_target_pairs={{0,3},{1,4},{2,5},{3,6},{4,7},{5,0},{6,1},{7,2},{8,11},{9,12},{10,... | collective-permute-start | bytes 786440 | tf_op jit(solution)/shard_map/ppermute | solution.py:185
  32.8 16.5 %collective-permute-start.3 = (bf16[128,1024]{1,0:T(8,128)(2,1)S(1)}, bf16[128,1024]{1,0:T(8,128)(2,1)S(1)}, u32[]{:S(2)}, u32[]{:S(2)}) collective-permute-start(bf16[128,1024]{1,0:T(8,128)(2,1)S(1)} %bitcast.58), channel_id=1, source_target_pairs={{0,4},{1,5},{2,6},{3,7},{4,0},{5,1},{6,2},{7,3},{8,12},{9,13},{10,... | collective-permute-start | bytes 786440 | tf_op jit(solution)/shard_map/ppermute | solution.py:185
  34.5 17.8 %collective-permute-start.4 = (bf16[128,1024]{1,0:T(8,128)(2,1)S(1)}, bf16[128,1024]{1,0:T(8,128)(2,1)S(1)}, u32[]{:S(2)}, u32[]{:S(2)}) collective-permute-start(bf16[128,1024]{1,0:T(8,128)(2,1)S(1)} %bitcast.57), channel_id=1, source_target_pairs={{0,5},{1,6},{2,7},{3,0},{4,1},{5,2},{6,3},{7,4},{8,13},{9,14},{10,... | collective-permute-start | bytes 786440 | tf_op jit(solution)/shard_map/ppermute | solution.py:185
  36.9 16.1 %collective-permute-start.5 = (bf16[128,1024]{1,0:T(8,128)(2,1)S(1)}, bf16[128,1024]{1,0:T(8,128)(2,1)S(1)}, u32[]{:S(2)}, u32[]{:S(2)}) collective-permute-start(bf16[128,1024]{1,0:T(8,128)(2,1)S(1)} %bitcast.61), channel_id=1, source_target_pairs={{0,6},{1,7},{2,0},{3,1},{4,2},{5,3},{6,4},{7,5},{8,14},{9,15},{10,... | collective-permute-start | bytes 786440 | tf_op jit(solution)/shard_map/ppermute | solution.py:185
  41.0 12.8 %collective-permute-start.6 = (bf16[128,1024]{1,0:T(8,128)(2,1)S(1)}, bf16[128,1024]{1,0:T(8,128)(2,1)S(1)}, u32[]{:S(2)}, u32[]{:S(2)}) collective-permute-start(bf16[128,1024]{1,0:T(8,128)(2,1)S(1)} %bitcast.60), channel_id=1, source_target_pairs={{0,7},{1,0},{2,1},{3,2},{4,3},{5,4},{6,5},{7,6},{8,15},{9,8},{10,9... | collective-permute-start | bytes 786440 | tf_op jit(solution)/shard_map/ppermute | solution.py:185

commit v9 on v8

--- a/solution.py
+++ b/solution.py
@@ -11,6 +11,7 @@
 VERT_COUNT = 3
 SLASH_REACH = 8
 FULL_GATHER_BYTES = 4 << 20
+OUTPUT_CHUNKS = 2
 
 
 def passed_along(shard, axis, by):
@@ -66,13 +67,13 @@
     return kernel
 
 
-def full_kernel(local_heads, group_blocks):
+def full_kernel(local_heads, group_blocks, base):
     block = MASK_BLOCK_SIZE
     key_count = (SLASH_COUNT + VERT_COUNT) * block
     scale = HEAD_DIMENSION ** (-0.5)
 
     def kernel(meta_ref, q_ref, k_ref, v_ref, o_ref):
-        h = pl.program_id(0)
+        h = pl.program_id(0) + base
         first = meta_ref[2 * local_heads * SLASH_COUNT]
         offs = [meta_ref[h * SLASH_COUNT + j] for j in range(SLASH_COUNT)]
         verts = [meta_ref[local_heads * SLASH_COUNT + h * VERT_COUNT + j] for j in range(VERT_COUNT)]
@@ -114,25 +115,25 @@
     return kernel
 
 
-def attend_full(meta, queries, all_keys, all_values, local_heads, sharing):
+def attend_full(meta, queries, all_keys, all_values, local_heads, sharing, base, chunk_heads):
     group_rows = queries.shape[0]
     group_blocks = group_rows // MASK_BLOCK_SIZE
     head_size = HEAD_DIMENSION
     total_rows = all_keys.shape[0]
     grid_spec = pltpu.PrefetchScalarGridSpec(
         num_scalar_prefetch=1,
-        grid=(local_heads,),
+        grid=(chunk_heads,),
         in_specs=[
-            pl.BlockSpec((group_rows, head_size), lambda h, m: (0, h)),
-            pl.BlockSpec((total_rows, head_size), lambda h, m: (0, h // sharing)),
-            pl.BlockSpec((total_rows, head_size), lambda h, m: (0, h // sharing)),
+            pl.BlockSpec((group_rows, head_size), lambda h, m: (0, h + base)),
+            pl.BlockSpec((total_rows, head_size), lambda h, m: (0, (h + base) // sharing)),
+            pl.BlockSpec((total_rows, head_size), lambda h, m: (0, (h + base) // sharing)),
         ],
         out_specs=pl.BlockSpec((group_rows, head_size), lambda h, m: (0, h)),
     )
     return pl.pallas_call(
-        full_kernel(local_heads, group_blocks),
+        full_kernel(local_heads, group_blocks, base),
         grid_spec=grid_spec,
-        out_shape=jax.ShapeDtypeStruct((group_rows, local_heads * head_size), queries.dtype),
+        out_shape=jax.ShapeDtypeStruct((group_rows, chunk_heads * head_size), queries.dtype),
     )(meta, queries, all_keys, all_values)
 
 
@@ -210,12 +211,17 @@
         everything = lax.all_to_all(spread, "outer", split_axis=0, concat_axis=0, tiled=True)
         everything = everything.transpose(1, 0, 2, 3).reshape(2, seq_count * group_rows, -1)
         queries = query_group.reshape(group_rows, local_heads * head_size)
-        results = attend_full(
-            meta, queries, everything[0], everything[1], local_heads, group_sharing_factor
-        )
-        merged = results.reshape(head_groups, tok_rows, local_heads * head_size)
-        returned = lax.all_to_all(merged, heads_axes, split_axis=0, concat_axis=0, tiled=True)
-        return returned.transpose(1, 0, 2).reshape(tok_rows, head_groups * local_heads * head_size)
+        chunk_heads = local_heads // OUTPUT_CHUNKS
+        pieces = []
+        for c in range(OUTPUT_CHUNKS):
+            results = attend_full(
+                meta, queries, everything[0], everything[1], local_heads, group_sharing_factor,
+                c * chunk_heads, chunk_heads,
+            )
+            merged = results.reshape(head_groups, tok_rows, chunk_heads * head_size)
+            pieces.append(lax.all_to_all(merged, heads_axes, split_axis=0, concat_axis=0, tiled=True))
+        returned = jnp.stack(pieces, 1)
+        return returned.transpose(2, 0, 1, 3).reshape(tok_rows, head_groups * local_heads * head_size)
     key_before, value_before = passed_along(
         (key_local[group_rows - back * block_size:], value_local[group_rows - back * block_size:]),
         "outer", 1,

time: 144 us -> 143 us (level)
  blocking collectives: 31 us -> 19.6 us
  starting transfers between devices: 17.6 us -> 22 us
  local copies, waits for them, and re-layouts: 28.5 us -> 32 us
  Pallas kernels: 36.5 us -> 39.5 us
    all_to_all x1, blocking collectives: 31 us -> 19.6 us  [per_device(): lax.all_to_all(merged, heads_axes, split_axis=0, concat_axis=0, tiled=True)]
    all_to_all x0 -> x1, starting transfers between devices: none -> 4.42 us  [per_device(): lax.all_to_all(merged, heads_axes, split_axis=0, concat_axis=0, tiled=True)]
    pallas_call x1 -> x2, Pallas kernels: 36.5 us -> 39.5 us  [attend_full(): pl.pallas_call(full_kernel(local_heads, group_blocks, base), grid_spec=gr...]
    transpose x0 -> x1, local copies, waits for them, and re-layouts: none -> 2.17 us  [per_device(): returned.transpose(2, 0, 1, 3)]
  transfers between devices with their start and end apart: 9 -> 10, of which waited for: 4 -> 4; matrix products, arithmetic and copies ran while one was open for 15% -> 15% of each run, Pallas kernels for 0% -> 14%
where the time goes in v9:
time: 143 us
  Pallas kernels  39.5 us (28%)
  local copies, waits for them, and re-layouts  32 us (22%)
  waiting for transfers between devices  26.7 us (19%)
  starting transfers between devices  22 us (15%)
  blocking collectives  19.6 us (14%)
  other arithmetic  2.62 us (2%)
    pallas_call x2, Pallas kernels, attend_full(): pl.pallas_call(full_kernel(local_heads, group_blocks, base), grid_spec=gr...  39.5 us
    all_to_all x1, blocking collectives, per_device(): lax.all_to_all(merged, heads_axes, split_axis=0, concat_axis=0, tiled=True)  19.6 us
    all_to_all x1, waiting for transfers between devices, per_device(): lax.all_to_all(spread, 'outer', split_axis=0, concat_axis=0, tiled=True)  12.4 us
    unnamed x14, local copies, waits for them, and re-layouts  11.5 us
    ppermute x7, waiting for transfers between devices, per_device(): lax.ppermute(sent, heads_axes, [(i, (i + shift) % head_groups) for i in r...  7.79 us
    ppermute x7, starting transfers between devices, per_device(): lax.ppermute(sent, heads_axes, [(i, (i + shift) % head_groups) for i in r...  7.53 us
    all_to_all x1, waiting for transfers between devices, per_device(): lax.all_to_all(jnp.stack([key_split, value_split], 2), heads_axes, split_...  6.48 us
    dynamic_slice x8, local copies, waits for them, and re-layouts, per_device(): lax.dynamic_index_in_dim(query_split, (me + shift) % head_groups, 1, keep...  6.19 us
  transfers between devices with their start and end apart: 10, of which 4 were waited for; matrix products, arithmetic and copies ran while one was open for 15% of the time, Pallas kernels for 14%

profile of v9, /device:TPU:0, one launch (start us, length us, event | category | flops | bytes accessed | tf_op | source)
XLA Modules:
  0.0 142.5 jit_solution(17585872393748563589)
XLA Ops:
  3.1 5.2 %all-to-all-start = ((bf16[128,8,2,128]{0,3,2,1:T(8,128)(2,1)}), bf16[128,8,2,128]{0,3,2,1:T(8,128)(2,1)S(1)}, u32[]{:S(2)}, u32[]{:S(2)}) async-start(bf16[128,8,2,128]{0,3,2,1:T(8,128)(2,1)} %copy.40), calls=%async_computation | async-start | bytes 1048576 | tf_op jit(solution)/shard_map/all_to_all | solution.py:177
  8.3 3.2 %copy.29 = bf16[128,8192]{0,1:T(8,128)(2,1)S(1)} copy(bf16[128,8192]{1,0:T(8,128)(2,1)} %param.5) | data formatting | bytes 4194304 | tf_op args[0]
  11.6 6.5 %all-to-all-done = bf16[128,8,2,128]{0,3,2,1:T(8,128)(2,1)S(1)} async-done(((bf16[128,8,2,128]{0,3,2,1:T(8,128)(2,1)}), bf16[128,8,2,128]{0,3,2,1:T(8,128)(2,1)S(1)}, u32[]{:S(2)}, u32[]{:S(2)}) %all-to-all-start) | async-done | bytes 524320 | tf_op jit(solution)/shard_map/all_to_all | solution.py:177
  18.4 1.6 %broadcast_in_dim.28 = bf16[4,2,1024,128]{3,2,1,0:T(8,128)(2,1)} broadcast(bf16[2,1024,128]{2,1,0:T(8,128)(2,1)S(1)} %pad_maximum_fusion.1), dimensions={1,2,3} | broadcast | bytes 2621440 | tf_op jit(solution)/shard_map/broadcast_in_dim | solution.py:210
  20.0 4.9 %all-to-all-start.1 = ((bf16[4,2,1024,128]{3,2,1,0:T(8,128)(2,1)}), bf16[4,2,1024,128]{3,2,1,0:T(8,128)(2,1)}, u32[]{:S(2)}, u32[]{:S(2)}) async-start(bf16[4,2,1024,128]{3,2,1,0:T(8,128)(2,1)} %broadcast_in_dim.28), calls=%async_computation.1 | async-start | bytes 4194304 | tf_op jit(solution)/shard_map/all_to_all | solution.py:211
  25.8 1.8 %copy.31 = bf16[128,1,1024]{2,0,1:T(8,128)(2,1)} copy(bf16[128,1,1024]{0,2,1:T(8,128)(2,1)} %get-tuple-element.13) | data formatting | bytes 524288 | tf_op jit(solution)/shard_map/jit(dynamic_index_in_dim)/dynamic_slice | solution.py:184
  27.7 1.8 %copy.32 = bf16[128,1,1024]{2,0,1:T(8,128)(2,1)} copy(bf16[128,1,1024]{0,2,1:T(8,128)(2,1)} %get-tuple-element.12) | data formatting | bytes 524288 | tf_op jit(solution)/shard_map/jit(dynamic_index_in_dim)/dynamic_slice | solution.py:184
  31.1 1.5 %collective-permute-start.2 = (bf16[128,1024]{1,0:T(8,128)(2,1)S(1)}, bf16[128,1024]{1,0:T(8,128)(2,1)S(1)}, u32[]{:S(2)}, u32[]{:S(2)}) collective-permute-start(bf16[128,1024]{1,0:T(8,128)(2,1)S(1)} %bitcast.65), channel_id=1, source_target_pairs={{0,3},{1,4},{2,5},{3,6},{4,7},{5,0},{6,1},{7,2},{8,11},{9,12},{10,... | collective-permute-start | bytes 786440 | tf_op jit(solution)/shard_map/ppermute | solution.py:186
  32.8 1.5 %collective-permute-start.3 = (bf16[128,1024]{1,0:T(8,128)(2,1)S(1)}, bf16[128,1024]{1,0:T(8,128)(2,1)S(1)}, u32[]{:S(2)}, u32[]{:S(2)}) collective-permute-start(bf16[128,1024]{1,0:T(8,128)(2,1)S(1)} %bitcast.64), channel_id=1, source_target_pairs={{0,4},{1,5},{2,6},{3,7},{4,0},{5,1},{6,2},{7,3},{8,12},{9,13},{10,... | collective-permute-start | bytes 786440 | tf_op jit(solution)/shard_map/ppermute | solution.py:186
  36.8 2.4 %collective-permute-start.5 = (bf16[128,1024]{1,0:T(8,128)(2,1)S(1)}, bf16[128,1024]{1,0:T(8,128)(2,1)S(1)}, u32[]{:S(2)}, u32[]{:S(2)}) collective-permute-start(bf16[128,1024]{1,0:T(8,128)(2,1)S(1)} %bitcast.67), channel_id=1, source_target_pairs={{0,6},{1,7},{2,0},{3,1},{4,2},{5,3},{6,4},{7,5},{8,14},{9,15},{10,... | collective-permute-start | bytes 786440 | tf_op jit(solution)/shard_map/ppermute | solution.py:186
  39.2 1.7 %bitcast_dynamic-update-slice_fusion.6 = bf16[8,128,1024]{2,1,0:T(8,128)(2,1)} fusion(bf16[8,128,1024]{2,1,0:T(8,128)(2,1)} %bitcast_dynamic-update-slice_fusion.7, bf16[128,1024]{1,0:T(8,128)(2,1)} %collective-permute-done), kind=kLoop, calls=%fused_computation.13 | loop fusion | bytes 524288
  40.9 1.4 %collective-permute-start.6 = (bf16[128,1024]{1,0:T(8,128)(2,1)S(1)}, bf16[128,1024]{1,0:T(8,128)(2,1)S(1)}, u32[]{:S(2)}, u32[]{:S(2)}) collective-permute-start(bf16[128,1024]{1,0:T(8,128)(2,1)S(1)} %bitcast.66), channel_id=1, source_target_pairs={{0,7},{1,0},{2,1},{3,2},{4,3},{5,4},{6,5},{7,6},{8,15},{9,8},{10,9... | collective-permute-start | bytes 786440 | tf_op jit(solution)/shard_map/ppermute | solution.py:186
  43.1 5.4 %collective-permute-done.2 = bf16[128,1024]{1,0:T(8,128)(2,1)S(1)} collective-permute-done((bf16[128,1024]{1,0:T(8,128)(2,1)S(1)}, bf16[128,1024]{1,0:T(8,128)(2,1)S(1)}, u32[]{:S(2)}, u32[]{:S(2)}) %collective-permute-start.2) | collective-permute-done | bytes 262176 | tf_op jit(solution)/shard_map/ppermute | solution.py:186
  49.9 2.4 %collective-permute-done.4 = bf16[128,1024]{1,0:T(8,128)(2,1)S(1)} collective-permute-done((bf16[128,1024]{1,0:T(8,128)(2,1)S(1)}, bf16[128,1024]{1,0:T(8,128)(2,1)S(1)}, u32[]{:S(2)}, u32[]{:S(2)}) %collective-permute-start.4) | collective-permute-done | bytes 262176 | tf_op jit(solution)/shard_map/ppermute | solution.py:186
  54.5 2.3 %gather_fusion = bf16[8,128,1024]{2,1,0:T(8,128)(2,1)S(1)} fusion(bf16[8,128,1024]{2,1,0:T(8,128)(2,1)} %bitcast_dynamic-update-slice_fusion, s32[1024]{0:T(1024)S(1)} %pad_clamp_fusion), kind=kCustom, calls=%fused_computation | custom fusion | bytes 4194336 | tf_op jit(solution)/shard_map/jit(_take)/gather | solution.py:189
  56.7 1.7 %bitcast_select_fusion.q_ref = bf16[1024,1024]{1,0:T(8,128)(2,1)} fusion(bf16[8,128,1024]{2,1,0:T(8,128)(2,1)S(1)} %gather_fusion, pred[1024]{0:T(1024)(128)(4,1)S(1)} %broadcast_bitcast_fusion), kind=kLoop, calls=%fused_computation.2 | loop fusion | flops 1048576 | bytes 4195328 | tf_op jit(solution)/shard_map/jit(_take)/select_n | solution.py:189
  58.5 12.4 %all-to-all-done.1 = bf16[4,2,1024,128]{3,2,1,0:T(8,128)(2,1)} async-done(((bf16[4,2,1024,128]{3,2,1,0:T(8,128)(2,1)}), bf16[4,2,1024,128]{3,2,1,0:T(8,128)(2,1)}, u32[]{:S(2)}, u32[]{:S(2)}) %all-to-all-start.1) | async-done | bytes 2097184 | tf_op jit(solution)/shard_map/all_to_all | solution.py:211
  70.9 3.0 %fusion.3 = (bf16[1,4,1024,128]{3,2,0,1:T(8,128)(2,1)}, bf16[1,4,1024,128]{3,2,0,1:T(8,128)(2,1)}) fusion(bf16[2,4,1024,128]{3,2,0,1:T(8,128)(2,1)} %bitcast.29), kind=kLoop, calls=%fused_computation.40 | loop fusion | bytes 4194304 | tf_op jit(solution)/shard_map/slice | solution.py:218
  73.9 19.8 %shard_map.55 = bf16[1024,512]{1,0:T(8,128)(2,1)} custom-call(s32[49]{0:T(128)} %pad_add_fusion.meta_ref, bf16[1024,1024]{1,0:T(8,128)(2,1)} %bitcast_select_fusion.q_ref, bf16[4096,128]{1,0:T(8,128)(2,1)} %bitcast.53, bf16[4096,128]{1,0:T(8,128)(2,1)} %bitcast.51), custom_call_target="tpu_custom_call" | custom-call | tf_op jit(solution)/shard_map/pallas_call | solution.py:133
  93.6 4.4 %all-to-all-start.2 = ((bf16[8,128,512]{2,1,0:T(8,128)(2,1)}), bf16[8,128,512]{2,1,0:T(8,128)(2,1)S(1)}, u32[]{:S(2)}, u32[]{:S(2)}) async-start(bf16[8,128,512]{2,1,0:T(8,128)(2,1)} %bitcast.57), calls=%async_computation.2 | async-start | bytes 2097152 | tf_op jit(solution)/shard_map/all_to_all | solution.py:222
  98.1 19.7 %shard_map.56 = bf16[1024,512]{1,0:T(8,128)(2,1)} custom-call(s32[49]{0:T(128)} %pad_add_fusion.meta_ref, bf16[1024,1024]{1,0:T(8,128)(2,1)} %bitcast_select_fusion.q_ref, bf16[4096,128]{1,0:T(8,128)(2,1)} %bitcast.54, bf16[4096,128]{1,0:T(8,128)(2,1)} %bitcast.52), custom_call_target="tpu_custom_call" | custom-call | tf_op jit(solution)/shard_map/pallas_call | solution.py:133
  117.8 19.6 %all_to_all.33 = bf16[8,128,512]{2,1,0:T(8,128)(2,1)S(1)} all-to-all(bf16[8,128,512]{2,1,0:T(8,128)(2,1)} %bitcast.58), channel_id=1, replica_groups=mesh['outer'=4,'inner'=2,'grp'=4] {'inner','grp'}, dimensions={0} | all-to-all | bytes 2097152 | tf_op jit(solution)/shard_map/all_to_all | solution.py:222
  137.5 2.2 %copy.42 = bf16[128,8,2,512]{3,2,1,0:T(2,128)(2,1)S(1)} copy(bf16[128,8,2,512]{3,0,1,2:T(8,128)(2,1)S(1)} %maximum_bitcast_fusion) | data formatting | bytes 4194304 | tf_op jit(solution)/shard_map/transpose | solution.py:224
  139.7 2.8 %reshape.87 = bf16[128,8192]{1,0:T(8,128)(2,1)} reshape(bf16[128,8,2,512]{3,2,1,0:T(2,128)(2,1)S(1)} %copy.42) | data formatting | bytes 4194304 | tf_op jit(solution)/shard_map/reshape | solution.py:224
  (45 shorter events, 13.2 us)
Async XLA Ops:
  3.1 14.9 %all-to-all-start = ((bf16[128,8,2,128]{0,3,2,1:T(8,128)(2,1)}), bf16[128,8,2,128]{0,3,2,1:T(8,128)(2,1)S(1)}, u32[]{:S(2)}, u32[]{:S(2)}) async-start(bf16[128,8,2,128]{0,3,2,1:T(8,128)(2,1)} %copy.40), calls=%async_computation | async-start | bytes 1048576 | tf_op jit(solution)/shard_map/all_to_all | solution.py:177
  20.0 50.8 %all-to-all-start.1 = ((bf16[4,2,1024,128]{3,2,1,0:T(8,128)(2,1)}), bf16[4,2,1024,128]{3,2,1,0:T(8,128)(2,1)}, u32[]{:S(2)}, u32[]{:S(2)}) async-start(bf16[4,2,1024,128]{3,2,1,0:T(8,128)(2,1)} %broadcast_in_dim.28), calls=%async_computation.1 | async-start | bytes 4194304 | tf_op jit(solution)/shard_map/all_to_all | solution.py:211
  25.8 8.9 %copy-start = (s32[64,3]{0,1:T(4,128)S(1)}, s32[64,3]{0,1:T(4,128)}, u32[]{:S(2)}) copy-start(s32[64,3]{0,1:T(4,128)} %param.8) | copy-start | bytes 2308
  25.8 8.9 %copy-start.1 = (s32[64,3]{0,1:T(4,128)S(1)}, s32[64,3]{0,1:T(4,128)}, u32[]{:S(2)}) copy-start(s32[64,3]{0,1:T(4,128)} %param.9) | copy-start | bytes 2308
  27.7 9.2 %collective-permute-start = (bf16[128,1024]{1,0:T(8,128)(2,1)}, bf16[128,1024]{1,0:T(8,128)(2,1)}, u32[]{:S(2)}, u32[]{:S(2)}) collective-permute-start(bf16[128,1024]{1,0:T(8,128)(2,1)} %bitcast.4), channel_id=1, source_target_pairs={{0,1},{1,2},{2,3},{3,4},{4,5},{5,6},{6,7},{7,0},{8,9},{9,10},{10,1... | collective-permute-start | bytes 786440 | tf_op jit(solution)/shard_map/ppermute | solution.py:186
  29.4 11.5 %collective-permute-start.1 = (bf16[128,1024]{1,0:T(8,128)(2,1)}, bf16[128,1024]{1,0:T(8,128)(2,1)S(1)}, u32[]{:S(2)}, u32[]{:S(2)}) collective-permute-start(bf16[128,1024]{1,0:T(8,128)(2,1)} %bitcast.6), channel_id=1, source_target_pairs={{0,2},{1,3},{2,4},{3,5},{4,6},{5,7},{6,0},{7,1},{8,10},{9,11},{10,... | collective-permute-start | bytes 786440 | tf_op jit(solution)/shard_map/ppermute | solution.py:186
  31.1 17.4 %collective-permute-start.2 = (bf16[128,1024]{1,0:T(8,128)(2,1)S(1)}, bf16[128,1024]{1,0:T(8,128)(2,1)S(1)}, u32[]{:S(2)}, u32[]{:S(2)}) collective-permute-start(bf16[128,1024]{1,0:T(8,128)(2,1)S(1)} %bitcast.65), channel_id=1, source_target_pairs={{0,3},{1,4},{2,5},{3,6},{4,7},{5,0},{6,1},{7,2},{8,11},{9,12},{10,... | collective-permute-start | bytes 786440 | tf_op jit(solution)/shard_map/ppermute | solution.py:186
  32.8 16.5 %collective-permute-start.3 = (bf16[128,1024]{1,0:T(8,128)(2,1)S(1)}, bf16[128,1024]{1,0:T(8,128)(2,1)S(1)}, u32[]{:S(2)}, u32[]{:S(2)}) collective-permute-start(bf16[128,1024]{1,0:T(8,128)(2,1)S(1)} %bitcast.64), channel_id=1, source_target_pairs={{0,4},{1,5},{2,6},{3,7},{4,0},{5,1},{6,2},{7,3},{8,12},{9,13},{10,... | collective-permute-start | bytes 786440 | tf_op jit(solution)/shard_map/ppermute | solution.py:186
  34.4 17.9 %collective-permute-start.4 = (bf16[128,1024]{1,0:T(8,128)(2,1)S(1)}, bf16[128,1024]{1,0:T(8,128)(2,1)S(1)}, u32[]{:S(2)}, u32[]{:S(2)}) collective-permute-start(bf16[128,1024]{1,0:T(8,128)(2,1)S(1)} %bitcast.63), channel_id=1, source_target_pairs={{0,5},{1,6},{2,7},{3,0},{4,1},{5,2},{6,3},{7,4},{8,13},{9,14},{10,... | collective-permute-start | bytes 786440 | tf_op jit(solution)/shard_map/ppermute | solution.py:186
  36.8 16.2 %collective-permute-start.5 = (bf16[128,1024]{1,0:T(8,128)(2,1)S(1)}, bf16[128,1024]{1,0:T(8,128)(2,1)S(1)}, u32[]{:S(2)}, u32[]{:S(2)}) collective-permute-start(bf16[128,1024]{1,0:T(8,128)(2,1)S(1)} %bitcast.67), channel_id=1, source_target_pairs={{0,6},{1,7},{2,0},{3,1},{4,2},{5,3},{6,4},{7,5},{8,14},{9,15},{10,... | collective-permute-start | bytes 786440 | tf_op jit(solution)/shard_map/ppermute | solution.py:186
  40.9 12.8 %collective-permute-start.6 = (bf16[128,1024]{1,0:T(8,128)(2,1)S(1)}, bf16[128,1024]{1,0:T(8,128)(2,1)S(1)}, u32[]{:S(2)}, u32[]{:S(2)}) collective-permute-start(bf16[128,1024]{1,0:T(8,128)(2,1)S(1)} %bitcast.66), channel_id=1, source_target_pairs={{0,7},{1,0},{2,1},{3,2},{4,3},{5,4},{6,5},{7,6},{8,15},{9,8},{10,9... | collective-permute-start | bytes 786440 | tf_op jit(solution)/shard_map/ppermute | solution.py:186
  93.6 24.1 %all-to-all-start.2 = ((bf16[8,128,512]{2,1,0:T(8,128)(2,1)}), bf16[8,128,512]{2,1,0:T(8,128)(2,1)S(1)}, u32[]{:S(2)}, u32[]{:S(2)}) async-start(bf16[8,128,512]{2,1,0:T(8,128)(2,1)} %bitcast.57), calls=%async_computation.2 | async-start | bytes 2097152 | tf_op jit(solution)/shard_map/all_to_all | solution.py:222

commit v10 on v9

--- a/solution.py
+++ b/solution.py
@@ -207,8 +207,11 @@
     )
     if seq_count * kv_group.size * kv_group.dtype.itemsize <= FULL_GATHER_BYTES:
         own = jnp.stack([key_local, value_local])
-        spread = jnp.broadcast_to(own[None], (seq_count,) + own.shape)
-        everything = lax.all_to_all(spread, "outer", split_axis=0, concat_axis=0, tiled=True)
+        relayed = [own]
+        for _ in range(1, seq_count):
+            relayed.append(passed_along(relayed[-1], "outer", 1))
+        order = (seq_index - jnp.arange(seq_count, dtype=jnp.int32)) % seq_count
+        everything = jnp.take(jnp.stack(relayed), order, axis=0)
         everything = everything.transpose(1, 0, 2, 3).reshape(2, seq_count * group_rows, -1)
         queries = query_group.reshape(group_rows, local_heads * head_size)
         chunk_heads = local_heads // OUTPUT_CHUNKS

time: 143 us -> 159 us (1.11)
  starting transfers between devices: 22 us -> 30.3 us
  waiting for transfers between devices: 26.7 us -> 31.4 us
  other arithmetic: 2.62 us -> 5.99 us
    ppermute x0 -> x3, waiting for transfers between devices: none -> 16.2 us  [passed_along(): return lax.ppermute(shard, axis, pairs)]
    ppermute x0 -> x3, starting transfers between devices: none -> 14.7 us  [passed_along(): return lax.ppermute(shard, axis, pairs)]
    all_to_all x1 -> x0, waiting for transfers between devices: 12.4 us -> none  [per_device(): lax.all_to_all(spread, 'outer', split_axis=0, concat_axis=0, tiled=True)]
    all_to_all x1, waiting for transfers between devices: 6.48 us -> 15.2 us  [per_device(): lax.all_to_all(jnp.stack([key_split, value_split], 2), heads_axes, split_...]
    ppermute x7, waiting for transfers between devices: 7.79 us -> 0.02 us  [per_device(): lax.ppermute(sent, heads_axes, [(i, (i + shift) % head_groups) for i in r...]
    all_to_all x1 -> x0, starting transfers between devices: 4.87 us -> none  [per_device(): lax.all_to_all(spread, 'outer', split_axis=0, concat_axis=0, tiled=True)]
    gather x0 -> x1, local copies, waits for them, and re-layouts: none -> 2.14 us  [per_device(): everything = jnp.take(jnp.stack(relayed), order, axis=0)]
    select_n x0 -> x2, other arithmetic: none -> 1.86 us  [per_device(): everything = jnp.take(jnp.stack(relayed), order, axis=0)]
  transfers between devices with their start and end apart: 10 -> 12, of which waited for: 4 -> 4; matrix products, arithmetic and copies ran while one was open for 15% -> 12% of each run, Pallas kernels for 14% -> 12%
where the time goes in v10:
time: 159 us
  Pallas kernels  39.5 us (25%)
  local copies, waits for them, and re-layouts  31.7 us (20%)
  waiting for transfers between devices  31.4 us (20%)
  starting transfers between devices  30.3 us (19%)
  blocking collectives  19.5 us (12%)
  other arithmetic  5.99 us (4%)
    pallas_call x2, Pallas kernels, attend_full(): pl.pallas_call(full_kernel(local_heads, group_blocks, base), grid_spec=gr...  39.5 us
    all_to_all x1, blocking collectives, per_device(): lax.all_to_all(merged, heads_axes, split_axis=0, concat_axis=0, tiled=True)  19.5 us
    ppermute x3, waiting for transfers between devices, passed_along(): return lax.ppermute(shard, axis, pairs)  16.2 us
    all_to_all x1, waiting for transfers between devices, per_device(): lax.all_to_all(jnp.stack([key_split, value_split], 2), heads_axes, split_...  15.2 us
    ppermute x3, starting transfers between devices, passed_along(): return lax.ppermute(shard, axis, pairs)  14.7 us
    unnamed x20, local copies, waits for them, and re-layouts  12.2 us
    ppermute x7, starting transfers between devices, per_device(): lax.ppermute(sent, heads_axes, [(i, (i + shift) % head_groups) for i in r...  8.15 us
    dynamic_slice x8, local copies, waits for them, and re-layouts, per_device(): lax.dynamic_index_in_dim(query_split, (me + shift) % head_groups, 1, keep...  6.22 us
  transfers between devices with their start and end apart: 12, of which 4 were waited for; matrix products, arithmetic and copies ran while one was open for 12% of the time, Pallas kernels for 12%

profile of v10, /device:TPU:0, one launch (start us, length us, event | category | flops | bytes accessed | tf_op | source)
XLA Modules:
  0.0 158.7 jit_solution(4553922231167816903)
XLA Ops:
  0.0 3.2 %copy.30 = bf16[128,8192]{0,1:T(8,128)(2,1)S(1)} copy(bf16[128,8192]{1,0:T(8,128)(2,1)} %param.5) | data formatting | bytes 4194304 | tf_op args[0]
  5.9 1.8 %copy.33 = bf16[128,1,1024]{2,0,1:T(8,128)(2,1)} copy(bf16[128,1,1024]{0,2,1:T(8,128)(2,1)} %get-tuple-element.12) | data formatting | bytes 524288 | tf_op jit(solution)/shard_map/jit(dynamic_index_in_dim)/dynamic_slice | solution.py:184
  7.6 2.5 %collective-permute-start.1 = (bf16[128,1024]{1,0:T(8,128)(2,1)}, bf16[128,1024]{1,0:T(8,128)(2,1)}, u32[]{:S(2)}, u32[]{:S(2)}) collective-permute-start(bf16[128,1024]{1,0:T(8,128)(2,1)} %bitcast.6), channel_id=1, source_target_pairs={{0,2},{1,3},{2,4},{3,5},{4,6},{5,7},{6,0},{7,1},{8,10},{9,11},{10,... | collective-permute-start | bytes 786440 | tf_op jit(solution)/shard_map/ppermute | solution.py:186
  10.1 1.8 %copy.34 = bf16[128,1,1024]{2,0,1:T(8,128)(2,1)} copy(bf16[128,1,1024]{0,2,1:T(8,128)(2,1)} %get-tuple-element.11) | data formatting | bytes 524288 | tf_op jit(solution)/shard_map/jit(dynamic_index_in_dim)/dynamic_slice | solution.py:184
  11.9 2.4 %collective-permute-start.2 = (bf16[128,1024]{1,0:T(8,128)(2,1)}, bf16[128,1024]{1,0:T(8,128)(2,1)}, u32[]{:S(2)}, u32[]{:S(2)}) collective-permute-start(bf16[128,1024]{1,0:T(8,128)(2,1)} %bitcast.8), channel_id=1, source_target_pairs={{0,3},{1,4},{2,5},{3,6},{4,7},{5,0},{6,1},{7,2},{8,11},{9,12},{10,... | collective-permute-start | bytes 786440 | tf_op jit(solution)/shard_map/ppermute | solution.py:186
  16.6 3.9 %all-to-all-start = ((bf16[128,8,2,128]{0,3,2,1:T(8,128)(2,1)}), bf16[128,8,2,128]{0,3,2,1:T(8,128)(2,1)S(1)}, u32[]{:S(2)}, u32[]{:S(2)}) async-start(bf16[128,8,2,128]{0,3,2,1:T(8,128)(2,1)} %copy.41), calls=%async_computation | async-start | bytes 1048576 | tf_op jit(solution)/shard_map/all_to_all | solution.py:177
  22.9 15.2 %all-to-all-done = bf16[128,8,2,128]{0,3,2,1:T(8,128)(2,1)S(1)} async-done(((bf16[128,8,2,128]{0,3,2,1:T(8,128)(2,1)}), bf16[128,8,2,128]{0,3,2,1:T(8,128)(2,1)S(1)}, u32[]{:S(2)}, u32[]{:S(2)}) %all-to-all-start) | async-done | bytes 524320 | tf_op jit(solution)/shard_map/all_to_all | solution.py:177
  39.2 4.2 %collective-permute-start.7 = (bf16[2,1024,128]{2,1,0:T(8,128)(2,1)S(1)}, bf16[2,1024,128]{2,1,0:T(8,128)(2,1)S(1)}, u32[]{:S(2)}, u32[]{:S(2)}) collective-permute-start(bf16[2,1024,128]{2,1,0:T(8,128)(2,1)S(1)} %get-tuple-element.16), channel_id=1, source_target_pairs={{0,8},{8,16},{16,24},{1,9},{9,17},{17,25},{2,10},{10,18},{18,26},{... | collective-permute-start | bytes 1572872 | tf_op jit(solution)/shard_map/ppermute | solution.py:20
  46.8 2.0 %collective-permute-start.6 = (bf16[128,1024]{1,0:T(8,128)(2,1)S(1)}, bf16[128,1024]{1,0:T(8,128)(2,1)S(1)}, u32[]{:S(2)}, u32[]{:S(2)}) collective-permute-start(bf16[128,1024]{1,0:T(8,128)(2,1)S(1)} %bitcast.74), channel_id=1, source_target_pairs={{0,7},{1,0},{2,1},{3,2},{4,3},{5,4},{6,5},{7,6},{8,15},{9,8},{10,9... | collective-permute-start | bytes 786440 | tf_op jit(solution)/shard_map/ppermute | solution.py:186
  50.5 4.3 %collective-permute-done.7 = bf16[2,1024,128]{2,1,0:T(8,128)(2,1)S(1)} collective-permute-done((bf16[2,1024,128]{2,1,0:T(8,128)(2,1)S(1)}, bf16[2,1024,128]{2,1,0:T(8,128)(2,1)S(1)}, u32[]{:S(2)}, u32[]{:S(2)}) %collective-permute-start.7) | collective-permute-done | bytes 524320 | tf_op jit(solution)/shard_map/ppermute | solution.py:20
  54.8 5.2 %collective-permute-start.8 = (bf16[2,1024,128]{2,1,0:T(8,128)(2,1)S(1)}, bf16[2,1024,128]{2,1,0:T(8,128)(2,1)}, u32[]{:S(2)}, u32[]{:S(2)}) collective-permute-start(bf16[2,1024,128]{2,1,0:T(8,128)(2,1)S(1)} %collective-permute-done.7), channel_id=1, source_target_pairs={{0,8},{8,16},{16,24},{1,9},{9,17},{17,25},{2,10},{10,18},{18,26},{... | collective-permute-start | bytes 1572872 | tf_op jit(solution)/shard_map/ppermute | solution.py:20
  62.1 7.5 %collective-permute-done.8 = bf16[2,1024,128]{2,1,0:T(8,128)(2,1)} collective-permute-done((bf16[2,1024,128]{2,1,0:T(8,128)(2,1)S(1)}, bf16[2,1024,128]{2,1,0:T(8,128)(2,1)}, u32[]{:S(2)}, u32[]{:S(2)}) %collective-permute-start.8) | collective-permute-done | bytes 524320 | tf_op jit(solution)/shard_map/ppermute | solution.py:20
  69.7 5.3 %collective-permute-start.9 = (bf16[2,1024,128]{2,1,0:T(8,128)(2,1)}, bf16[2,1024,128]{2,1,0:T(8,128)(2,1)}, u32[]{:S(2)}, u32[]{:S(2)}) collective-permute-start(bf16[2,1024,128]{2,1,0:T(8,128)(2,1)} %collective-permute-done.8), channel_id=1, source_target_pairs={{0,8},{8,16},{16,24},{1,9},{9,17},{17,25},{2,10},{10,18},{18,26},{... | collective-permute-start | bytes 1572872 | tf_op jit(solution)/shard_map/ppermute | solution.py:20
  75.7 2.3 %gather_fusion = bf16[8,128,1024]{2,1,0:T(8,128)(2,1)S(1)} fusion(bf16[8,128,1024]{2,1,0:T(8,128)(2,1)} %bitcast_dynamic-update-slice_fusion, s32[1024]{0:T(1024)S(1)} %pad_clamp_fusion.1), kind=kCustom, calls=%fused_computation | custom fusion | bytes 4194336 | tf_op jit(solution)/shard_map/jit(_take)/gather | solution.py:189
  77.9 1.7 %bitcast_select_fusion.q_ref = bf16[1024,1024]{1,0:T(8,128)(2,1)} fusion(bf16[8,128,1024]{2,1,0:T(8,128)(2,1)S(1)} %gather_fusion, pred[1024]{0:T(1024)(128)(4,1)S(1)} %broadcast_bitcast_fusion), kind=kLoop, calls=%fused_computation.4 | loop fusion | flops 1048576 | bytes 4195328 | tf_op jit(solution)/shard_map/jit(_take)/select_n | solution.py:189
  79.6 4.4 %collective-permute-done.9 = bf16[2,1024,128]{2,1,0:T(8,128)(2,1)} collective-permute-done((bf16[2,1024,128]{2,1,0:T(8,128)(2,1)}, bf16[2,1024,128]{2,1,0:T(8,128)(2,1)}, u32[]{:S(2)}, u32[]{:S(2)}) %collective-permute-start.9) | collective-permute-done | bytes 524320 | tf_op jit(solution)/shard_map/ppermute | solution.py:20
  85.5 2.1 %gather_fusion.1 = bf16[4,2,1024,128]{3,2,1,0:T(8,128)(2,1)} fusion(bf16[4,2,1024,128]{3,2,1,0:T(8,128)(2,1)S(1)} %pad_maximum_fusion, s32[1024]{0:T(1024)S(1)} %pad_clamp_fusion), kind=kCustom, calls=%fused_computation.1 | custom fusion | bytes 4194320 | tf_op jit(solution)/shard_map/jit(_take)/gather | solution.py:214
  87.6 1.9 %select_bitcast_fusion = bf16[2,4,1024,128]{3,2,0,1:T(8,128)(2,1)S(1)} fusion(bf16[4,2,1024,128]{3,2,1,0:T(8,128)(2,1)} %gather_fusion.1, pred[4]{0:T(512)(128)(4,1)S(1)} %compare_and_fusion), kind=kLoop, calls=%fused_computation.5 | loop fusion | flops 1048576 | bytes 4194308 | tf_op jit(solution)/shard_map/jit(_take)/select_n | solution.py:214
  91.0 19.8 %shard_map.55 = bf16[1024,512]{1,0:T(8,128)(2,1)} custom-call(s32[49]{0:T(128)} %pad_add_fusion.meta_ref, bf16[1024,1024]{1,0:T(8,128)(2,1)} %bitcast_select_fusion.q_ref, bf16[4096,128]{1,0:T(8,128)(2,1)} %bitcast.61, bf16[4096,128]{1,0:T(8,128)(2,1)} %bitcast.59), custom_call_target="tpu_custom_call" | custom-call | tf_op jit(solution)/shard_map/pallas_call | solution.py:133
  110.7 3.6 %all-to-all-start.1 = ((bf16[8,128,512]{2,1,0:T(8,128)(2,1)}), bf16[8,128,512]{2,1,0:T(8,128)(2,1)S(1)}, u32[]{:S(2)}, u32[]{:S(2)}) async-start(bf16[8,128,512]{2,1,0:T(8,128)(2,1)} %bitcast.65), calls=%async_computation.1 | async-start | bytes 2097152 | tf_op jit(solution)/shard_map/all_to_all | solution.py:225
  114.3 19.8 %shard_map.56 = bf16[1024,512]{1,0:T(8,128)(2,1)} custom-call(s32[49]{0:T(128)} %pad_add_fusion.meta_ref, bf16[1024,1024]{1,0:T(8,128)(2,1)} %bitcast_select_fusion.q_ref, bf16[4096,128]{1,0:T(8,128)(2,1)} %bitcast.62, bf16[4096,128]{1,0:T(8,128)(2,1)} %bitcast.60), custom_call_target="tpu_custom_call" | custom-call | tf_op jit(solution)/shard_map/pallas_call | solution.py:133
  134.1 19.5 %all_to_all.28 = bf16[8,128,512]{2,1,0:T(8,128)(2,1)S(1)} all-to-all(bf16[8,128,512]{2,1,0:T(8,128)(2,1)} %bitcast.66), channel_id=1, replica_groups=mesh['outer'=4,'inner'=2,'grp'=4] {'inner','grp'}, dimensions={0} | all-to-all | bytes 2097152 | tf_op jit(solution)/shard_map/all_to_all | solution.py:225
  153.7 2.2 %copy.43 = bf16[128,8,2,512]{3,2,1,0:T(2,128)(2,1)S(1)} copy(bf16[128,8,2,512]{3,0,1,2:T(8,128)(2,1)S(1)} %maximum_bitcast_fusion) | data formatting | bytes 4194304 | tf_op jit(solution)/shard_map/transpose | solution.py:227
  155.9 2.8 %reshape.140 = bf16[128,8192]{1,0:T(8,128)(2,1)} reshape(bf16[128,8,2,512]{3,2,1,0:T(2,128)(2,1)S(1)} %copy.43) | data formatting | bytes 4194304 | tf_op jit(solution)/shard_map/reshape | solution.py:227
  (60 shorter events, 19.2 us)
Async XLA Ops:
  4.2 11.1 %copy-start = (bf16[128,1024]{1,0:T(8,128)(2,1)S(1)}, bf16[128,1024]{1,0:T(8,128)(2,1)}, u32[]{:S(2)}) copy-start(bf16[128,1024]{1,0:T(8,128)(2,1)} %param.6) | copy-start | bytes 786436
  4.2 11.3 %copy-start.1 = (bf16[128,1024]{1,0:T(8,128)(2,1)S(1)}, bf16[128,1024]{1,0:T(8,128)(2,1)}, u32[]{:S(2)}) copy-start(bf16[128,1024]{1,0:T(8,128)(2,1)} %param.7) | copy-start | bytes 786436
  5.4 33.2 %collective-permute-start = (bf16[128,1024]{1,0:T(8,128)(2,1)S(1)}, bf16[128,1024]{1,0:T(8,128)(2,1)S(1)}, u32[]{:S(2)}, u32[]{:S(2)}) collective-permute-start(bf16[128,1024]{1,0:T(8,128)(2,1)S(1)} %bitcast.75), channel_id=1, source_target_pairs={{0,1},{1,2},{2,3},{3,4},{4,5},{5,6},{6,7},{7,0},{8,9},{9,10},{10,1... | collective-permute-start | bytes 786440 | tf_op jit(solution)/shard_map/ppermute | solution.py:186
  7.6 37.5 %collective-permute-start.1 = (bf16[128,1024]{1,0:T(8,128)(2,1)}, bf16[128,1024]{1,0:T(8,128)(2,1)}, u32[]{:S(2)}, u32[]{:S(2)}) collective-permute-start(bf16[128,1024]{1,0:T(8,128)(2,1)} %bitcast.6), channel_id=1, source_target_pairs={{0,2},{1,3},{2,4},{3,5},{4,6},{5,7},{6,0},{7,1},{8,10},{9,11},{10,... | collective-permute-start | bytes 786440 | tf_op jit(solution)/shard_map/ppermute | solution.py:186
  11.9 34.9 %collective-permute-start.2 = (bf16[128,1024]{1,0:T(8,128)(2,1)}, bf16[128,1024]{1,0:T(8,128)(2,1)}, u32[]{:S(2)}, u32[]{:S(2)}) collective-permute-start(bf16[128,1024]{1,0:T(8,128)(2,1)} %bitcast.8), channel_id=1, source_target_pairs={{0,3},{1,4},{2,5},{3,6},{4,7},{5,0},{6,1},{7,2},{8,11},{9,12},{10,... | collective-permute-start | bytes 786440 | tf_op jit(solution)/shard_map/ppermute | solution.py:186
  14.5 45.5 %collective-permute-start.3 = (bf16[128,1024]{1,0:T(8,128)(2,1)S(1)}, bf16[128,1024]{1,0:T(8,128)(2,1)S(1)}, u32[]{:S(2)}, u32[]{:S(2)}) collective-permute-start(bf16[128,1024]{1,0:T(8,128)(2,1)S(1)} %bitcast.73), channel_id=1, source_target_pairs={{0,4},{1,5},{2,6},{3,7},{4,0},{5,1},{6,2},{7,3},{8,12},{9,13},{10,... | collective-permute-start | bytes 786440 | tf_op jit(solution)/shard_map/ppermute | solution.py:186
  15.2 45.5 %collective-permute-start.4 = (bf16[128,1024]{1,0:T(8,128)(2,1)S(1)}, bf16[128,1024]{1,0:T(8,128)(2,1)S(1)}, u32[]{:S(2)}, u32[]{:S(2)}) collective-permute-start(bf16[128,1024]{1,0:T(8,128)(2,1)S(1)} %bitcast.72), channel_id=1, source_target_pairs={{0,5},{1,6},{2,7},{3,0},{4,1},{5,2},{6,3},{7,4},{8,13},{9,14},{10,... | collective-permute-start | bytes 786440 | tf_op jit(solution)/shard_map/ppermute | solution.py:186
  15.7 5.3 %copy-start.3 = (s32[64,3]{0,1:T(4,128)S(1)}, s32[64,3]{0,1:T(4,128)}, u32[]{:S(2)}) copy-start(s32[64,3]{0,1:T(4,128)} %param.8) | copy-start | bytes 2308
  15.8 5.3 %copy-start.4 = (s32[64,3]{0,1:T(4,128)S(1)}, s32[64,3]{0,1:T(4,128)}, u32[]{:S(2)}) copy-start(s32[64,3]{0,1:T(4,128)} %param.9) | copy-start | bytes 2308
  16.6 21.5 %all-to-all-start = ((bf16[128,8,2,128]{0,3,2,1:T(8,128)(2,1)}), bf16[128,8,2,128]{0,3,2,1:T(8,128)(2,1)S(1)}, u32[]{:S(2)}, u32[]{:S(2)}) async-start(bf16[128,8,2,128]{0,3,2,1:T(8,128)(2,1)} %copy.41), calls=%async_computation | async-start | bytes 1048576 | tf_op jit(solution)/shard_map/all_to_all | solution.py:177
  38.5 0.7 copy-start.2
  39.2 15.5 %collective-permute-start.7 = (bf16[2,1024,128]{2,1,0:T(8,128)(2,1)S(1)}, bf16[2,1024,128]{2,1,0:T(8,128)(2,1)S(1)}, u32[]{:S(2)}, u32[]{:S(2)}) collective-permute-start(bf16[2,1024,128]{2,1,0:T(8,128)(2,1)S(1)} %get-tuple-element.16), channel_id=1, source_target_pairs={{0,8},{8,16},{16,24},{1,9},{9,17},{17,25},{2,10},{10,18},{18,26},{... | collective-permute-start | bytes 1572872 | tf_op jit(solution)/shard_map/ppermute | solution.py:20
  45.1 16.3 %collective-permute-start.5 = (bf16[128,1024]{1,0:T(8,128)(2,1)S(1)}, bf16[128,1024]{1,0:T(8,128)(2,1)S(1)}, u32[]{:S(2)}, u32[]{:S(2)}) collective-permute-start(bf16[128,1024]{1,0:T(8,128)(2,1)S(1)} %bitcast.76), channel_id=1, source_target_pairs={{0,6},{1,7},{2,0},{3,1},{4,2},{5,3},{6,4},{7,5},{8,14},{9,15},{10,... | collective-permute-start | bytes 786440 | tf_op jit(solution)/shard_map/ppermute | solution.py:186
  46.8 28.1 %collective-permute-start.6 = (bf16[128,1024]{1,0:T(8,128)(2,1)S(1)}, bf16[128,1024]{1,0:T(8,128)(2,1)S(1)}, u32[]{:S(2)}, u32[]{:S(2)}) collective-permute-start(bf16[128,1024]{1,0:T(8,128)(2,1)S(1)} %bitcast.74), channel_id=1, source_target_pairs={{0,7},{1,0},{2,1},{3,2},{4,3},{5,4},{6,5},{7,6},{8,15},{9,8},{10,9... | collective-permute-start | bytes 786440 | tf_op jit(solution)/shard_map/ppermute | solution.py:186
  54.8 14.9 %collective-permute-start.8 = (bf16[2,1024,128]{2,1,0:T(8,128)(2,1)S(1)}, bf16[2,1024,128]{2,1,0:T(8,128)(2,1)}, u32[]{:S(2)}, u32[]{:S(2)}) collective-permute-start(bf16[2,1024,128]{2,1,0:T(8,128)(2,1)S(1)} %collective-permute-done.7), channel_id=1, source_target_pairs={{0,8},{8,16},{16,24},{1,9},{9,17},{17,25},{2,10},{10,18},{18,26},{... | collective-permute-start | bytes 1572872 | tf_op jit(solution)/shard_map/ppermute | solution.py:20
  69.7 14.4 %collective-permute-start.9 = (bf16[2,1024,128]{2,1,0:T(8,128)(2,1)}, bf16[2,1024,128]{2,1,0:T(8,128)(2,1)}, u32[]{:S(2)}, u32[]{:S(2)}) collective-permute-start(bf16[2,1024,128]{2,1,0:T(8,128)(2,1)} %collective-permute-done.8), channel_id=1, source_target_pairs={{0,8},{8,16},{16,24},{1,9},{9,17},{17,25},{2,10},{10,18},{18,26},{... | collective-permute-start | bytes 1572872 | tf_op jit(solution)/shard_map/ppermute | solution.py:20
  110.7 23.3 %all-to-all-start.1 = ((bf16[8,128,512]{2,1,0:T(8,128)(2,1)}), bf16[8,128,512]{2,1,0:T(8,128)(2,1)S(1)}, u32[]{:S(2)}, u32[]{:S(2)}) async-start(bf16[8,128,512]{2,1,0:T(8,128)(2,1)} %bitcast.65), calls=%async_computation.1 | async-start | bytes 2097152 | tf_op jit(solution)/shard_map/all_to_all | solution.py:225

commit v11 on v8

--- a/solution.py
+++ b/solution.py
@@ -173,10 +173,19 @@
     query_split = query_rows.reshape(tok_rows, head_groups, local_heads * head_size)
     key_split = key_matrix.reshape(tok_rows, head_groups, local_kv * head_size)
     value_split = value_matrix.reshape(tok_rows, head_groups, local_kv * head_size)
-    kv_group = lax.all_to_all(
-        jnp.stack([key_split, value_split], 2), heads_axes, split_axis=1, concat_axis=0, tiled=True
-    )
-    key_group, value_group = kv_group[:, 0, 0], kv_group[:, 0, 1]
+    seq_count = lax.axis_size("outer")
+    kv_split = jnp.stack([key_split, value_split], 2)
+    whole = seq_count * head_groups * kv_split.size * kv_split.dtype.itemsize // head_groups
+    if whole <= FULL_GATHER_BYTES:
+        spread = jnp.broadcast_to(
+            kv_split.transpose(1, 0, 2, 3)[None], (seq_count,) + kv_split.transpose(1, 0, 2, 3).shape
+        ).reshape((seq_count * head_groups,) + kv_split.transpose(1, 0, 2, 3).shape[1:])
+        everything = lax.all_to_all(
+            spread, ("outer",) + heads_axes, split_axis=0, concat_axis=0, tiled=True
+        )
+    else:
+        kv_group = lax.all_to_all(kv_split, heads_axes, split_axis=1, concat_axis=0, tiled=True)
+        key_group, value_group = kv_group[:, 0, 0], kv_group[:, 0, 1]
     me = lax.axis_index(heads_axes)
     received = [lax.dynamic_index_in_dim(query_split, me, 1, keepdims=False)]
     for shift in range(1, head_groups):
@@ -189,9 +198,6 @@
     group_rows = tok_rows * head_groups
     group_blocks = group_rows // block_size
     back = min(SLASH_REACH, group_blocks)
-    key_local = key_group.reshape(group_rows, local_kv * head_size)
-    value_local = value_group.reshape(group_rows, local_kv * head_size)
-    seq_count = lax.axis_size("outer")
     seq_index = lax.axis_index("outer")
     head_group = lax.axis_index(heads_axes)
     head_offsets = lax.dynamic_slice_in_dim(slash_offsets, head_group * local_heads, local_heads, 0)
@@ -204,11 +210,8 @@
             first_block[None],
         ]
     )
-    if seq_count * kv_group.size * kv_group.dtype.itemsize <= FULL_GATHER_BYTES:
-        own = jnp.stack([key_local, value_local])
-        spread = jnp.broadcast_to(own[None], (seq_count,) + own.shape)
-        everything = lax.all_to_all(spread, "outer", split_axis=0, concat_axis=0, tiled=True)
-        everything = everything.transpose(1, 0, 2, 3).reshape(2, seq_count * group_rows, -1)
+    if whole <= FULL_GATHER_BYTES:
+        everything = everything.reshape(-1, 2, local_kv * head_size).transpose(1, 0, 2)
         queries = query_group.reshape(group_rows, local_heads * head_size)
         results = attend_full(
             meta, queries, everything[0], everything[1], local_heads, group_sharing_factor
@@ -216,6 +219,8 @@
         merged = results.reshape(head_groups, tok_rows, local_heads * head_size)
         returned = lax.all_to_all(merged, heads_axes, split_axis=0, concat_axis=0, tiled=True)
         return returned.transpose(1, 0, 2).reshape(tok_rows, head_groups * local_heads * head_size)
+    key_local = key_group.reshape(group_rows, local_kv * head_size)
+    value_local = value_group.reshape(group_rows, local_kv * head_size)
     key_before, value_before = passed_along(
         (key_local[group_rows - back * block_size:], value_local[group_rows - back * block_size:]),
         "outer", 1,

time: 144 us -> 137 us (0.951)
  waiting for transfers between devices: 26.6 us -> 22.3 us
  local copies, waits for them, and re-layouts: 28.5 us -> 26 us
    all_to_all x2 -> x1, waiting for transfers between devices: 18.9 us -> 0.01 us  [per_device(): lax.all_to_all(spread, ('outer',) + heads_axes, split_axis=0, concat_axis...]
    ppermute x7, waiting for transfers between devices: 7.71 us -> 22.3 us  [per_device(): lax.ppermute(sent, heads_axes, [(i, (i + shift) % head_groups) for i in r...]
    slice x1 -> x0, local copies, waits for them, and re-layouts: 3.02 us -> none  [per_device(): everything[1]]
    all_to_all x2 -> x1, starting transfers between devices: 10 us -> 7.43 us  [per_device(): lax.all_to_all(spread, ('outer',) + heads_axes, split_axis=0, concat_axis...]
    ppermute x7, starting transfers between devices: 7.53 us -> 10.1 us  [per_device(): lax.ppermute(sent, heads_axes, [(i, (i + shift) % head_groups) for i in r...]
    all_to_all x1, local copies, waits for them, and re-layouts: 0.28 us -> 1.73 us  [per_device(): lax.all_to_all(spread, ('outer',) + heads_axes, split_axis=0, concat_axis...]
    squeeze x0 -> x1, local copies, waits for them, and re-layouts: none -> 1.44 us  [per_device(): everything[1]]
  transfers between devices with their start and end apart: 9 -> 8, of which waited for: 4 -> 5; matrix products, arithmetic and copies ran while one was open for 15% -> 14% of each run, Pallas kernels for 0% -> 0%
where the time goes in v11:
time: 137 us
  Pallas kernels  36.5 us (27%)
  blocking collectives  31.5 us (23%)
  local copies, waits for them, and re-layouts  26 us (19%)
  waiting for transfers between devices  22.3 us (16%)
  starting transfers between devices  17.5 us (13%)
  other arithmetic  2.45 us (2%)
    pallas_call x1, Pallas kernels, attend_full(): pl.pallas_call(full_kernel(local_heads, group_blocks), grid_spec=grid_spe...  36.5 us
    all_to_all x1, blocking collectives, per_device(): lax.all_to_all(merged, heads_axes, split_axis=0, concat_axis=0, tiled=True)  31.5 us
    ppermute x7, waiting for transfers between devices, per_device(): lax.ppermute(sent, heads_axes, [(i, (i + shift) % head_groups) for i in r...  22.3 us
    unnamed x14, local copies, waits for them, and re-layouts  10.3 us
    ppermute x7, starting transfers between devices, per_device(): lax.ppermute(sent, heads_axes, [(i, (i + shift) % head_groups) for i in r...  10.1 us
    all_to_all x1, starting transfers between devices, per_device(): lax.all_to_all(spread, ('outer',) + heads_axes, split_axis=0, concat_axis...  7.43 us
    dynamic_slice x8, local copies, waits for them, and re-layouts, per_device(): lax.dynamic_index_in_dim(query_split, (me + shift) % head_groups, 1, keep...  5.51 us
  transfers between devices with their start and end apart: 8, of which 5 were waited for; matrix products, arithmetic and copies ran while one was open for 14% of the time, Pallas kernels for 0%

profile of v11, /device:TPU:0, one launch (start us, length us, event | category | flops | bytes accessed | tf_op | source)
XLA Modules:
  0.0 136.6 jit_solution(13081295061796413172)
XLA Ops:
  0.0 1.0 copy.42
  1.0 1.0 copy.43
  2.2 1.9 %broadcast_in_dim.28 = bf16[4,8,128,2,128]{4,2,3,1,0:T(8,128)(2,1)} broadcast(bf16[8,128,2,128]{3,1,2,0:T(8,128)(2,1)S(1)} %copy.38), dimensions={1,2,3,4} | broadcast | bytes 2621440 | tf_op jit(solution)/shard_map/broadcast_in_dim | solution.py:180
  4.0 7.4 %all-to-all-start = ((bf16[32,128,2,128]{3,1,2,0:T(8,128)(2,1)}), bf16[32,128,2,128]{3,1,2,0:T(8,128)(2,1)}, u32[]{:S(2)}, u32[]{:S(2)}) async-start(bf16[32,128,2,128]{3,1,2,0:T(8,128)(2,1)} %bitcast.21), calls=%async_computation | async-start | bytes 4194304 | tf_op jit(solution)/shard_map/all_to_all | solution.py:183
  11.6 3.2 %copy.29 = bf16[128,8192]{0,1:T(8,128)(2,1)S(1)} copy(bf16[128,8192]{1,0:T(8,128)(2,1)} %param.5) | data formatting | bytes 4194304 | tf_op args[0]
  14.8 1.0 constant_dynamic-slice_fusion
  15.8 1.8 %copy.31 = bf16[128,1,1024]{2,0,1:T(8,128)(2,1)} copy(bf16[128,1,1024]{0,2,1:T(8,128)(2,1)} %get-tuple-element.13) | data formatting | bytes 524288 | tf_op jit(solution)/shard_map/jit(dynamic_index_in_dim)/dynamic_slice | solution.py:192
  17.8 1.1 copy.32
  18.9 1.7 %collective-permute-start.1 = (bf16[128,1024]{1,0:T(8,128)(2,1)S(1)}, bf16[128,1024]{1,0:T(8,128)(2,1)S(1)}, u32[]{:S(2)}, u32[]{:S(2)}) collective-permute-start(bf16[128,1024]{1,0:T(8,128)(2,1)S(1)} %bitcast.64), channel_id=1, source_target_pairs={{0,2},{1,3},{2,4},{3,5},{4,6},{5,7},{6,0},{7,1},{8,10},{9,11},{10,... | collective-permute-start | bytes 786440 | tf_op jit(solution)/shard_map/ppermute | solution.py:194
  20.6 1.1 copy.33
  21.7 2.3 %collective-permute-start.2 = (bf16[128,1024]{1,0:T(8,128)(2,1)S(1)}, bf16[128,1024]{1,0:T(8,128)(2,1)S(1)}, u32[]{:S(2)}, u32[]{:S(2)}) collective-permute-start(bf16[128,1024]{1,0:T(8,128)(2,1)S(1)} %bitcast.63), channel_id=1, source_target_pairs={{0,3},{1,4},{2,5},{3,6},{4,7},{5,0},{6,1},{7,2},{8,11},{9,12},{10,... | collective-permute-start | bytes 786440 | tf_op jit(solution)/shard_map/ppermute | solution.py:194
  25.4 0.7 bitcast_dynamic-update-slice_fusion.7
  27.5 12.5 %collective-permute-done = bf16[128,1024]{1,0:T(8,128)(2,1)S(1)} collective-permute-done((bf16[128,1024]{1,0:T(8,128)(2,1)}, bf16[128,1024]{1,0:T(8,128)(2,1)S(1)}, u32[]{:S(2)}, u32[]{:S(2)}) %collective-permute-start) | collective-permute-done | bytes 262176 | tf_op jit(solution)/shard_map/ppermute | solution.py:194
  41.2 5.1 %collective-permute-start.6 = (bf16[128,1024]{1,0:T(8,128)(2,1)S(1)}, bf16[128,1024]{1,0:T(8,128)(2,1)S(1)}, u32[]{:S(2)}, u32[]{:S(2)}) collective-permute-start(bf16[128,1024]{1,0:T(8,128)(2,1)S(1)} %bitcast.65), channel_id=1, source_target_pairs={{0,7},{1,0},{2,1},{3,2},{4,3},{5,4},{6,5},{7,6},{8,15},{9,8},{10,9... | collective-permute-start | bytes 786440 | tf_op jit(solution)/shard_map/ppermute | solution.py:194
  47.0 5.9 %collective-permute-done.2 = bf16[128,1024]{1,0:T(8,128)(2,1)S(1)} collective-permute-done((bf16[128,1024]{1,0:T(8,128)(2,1)S(1)}, bf16[128,1024]{1,0:T(8,128)(2,1)S(1)}, u32[]{:S(2)}, u32[]{:S(2)}) %collective-permute-start.2) | collective-permute-done | bytes 262176 | tf_op jit(solution)/shard_map/ppermute | solution.py:194
  54.6 3.1 %collective-permute-done.4 = bf16[128,1024]{1,0:T(8,128)(2,1)S(1)} collective-permute-done((bf16[128,1024]{1,0:T(8,128)(2,1)S(1)}, bf16[128,1024]{1,0:T(8,128)(2,1)S(1)}, u32[]{:S(2)}, u32[]{:S(2)}) %collective-permute-start.4) | collective-permute-done | bytes 262176 | tf_op jit(solution)/shard_map/ppermute | solution.py:194
  58.4 0.7 bitcast_dynamic-update-slice_fusion.1
  59.9 2.3 %gather_fusion = bf16[8,128,1024]{2,1,0:T(8,128)(2,1)S(1)} fusion(bf16[8,128,1024]{2,1,0:T(8,128)(2,1)} %bitcast_dynamic-update-slice_fusion, s32[1024]{0:T(1024)S(1)} %pad_clamp_fusion), kind=kCustom, calls=%fused_computation | custom fusion | bytes 4194336 | tf_op jit(solution)/shard_map/jit(_take)/gather | solution.py:197
  62.2 1.7 %bitcast_select_fusion.q_ref = bf16[1024,1024]{1,0:T(8,128)(2,1)} fusion(bf16[8,128,1024]{2,1,0:T(8,128)(2,1)S(1)} %gather_fusion, pred[1024]{0:T(1024)(128)(4,1)S(1)} %broadcast_bitcast_fusion), kind=kLoop, calls=%fused_computation.1 | loop fusion | flops 1048576 | bytes 4195328 | tf_op jit(solution)/shard_map/jit(_take)/select_n | solution.py:197
  63.9 1.7 %copy.39 = bf16[32,128,2,128]{3,1,0,2:T(8,128)(2,1)S(1)} copy(bf16[32,128,2,128]{3,1,2,0:T(8,128)(2,1)} %all-to-all-done) | data formatting | bytes 4194304 | tf_op jit(solution)/shard_map/all_to_all | solution.py:183
  65.6 1.4 %slice_bitcast_fusion = (bf16[4096,128]{1,0:T(8,128)(2,1)}, bf16[4096,128]{1,0:T(8,128)(2,1)}) fusion(bf16[2,4096,128]{2,1,0:T(8,128)(2,1)S(1)} %bitcast.55), kind=kLoop, calls=%fused_computation.2 | loop fusion | bytes 4194304 | tf_op jit(solution)/shard_map/squeeze | solution.py:217
  67.1 36.5 %shard_map.55 = bf16[1024,1024]{1,0:T(8,128)(2,1)} custom-call(s32[49]{0:T(128)} %pad_add_fusion.meta_ref, bf16[1024,1024]{1,0:T(8,128)(2,1)} %bitcast_select_fusion.q_ref, bf16[4096,128]{1,0:T(8,128)(2,1)} %get-tuple-element.6.k_ref, bf16[4096,128]{1,0:T(8,128)(2,1)} %get-tuple-element.5.v_ref), custom_call_target="tpu_custom_call" | custom-call | tf_op jit(solution)/shard_map/pallas_call | solution.py:132
  103.6 31.5 %all_to_all.10 = bf16[8,128,1024]{2,1,0:T(8,128)(2,1)S(1)} all-to-all(bf16[8,128,1024]{2,1,0:T(8,128)(2,1)} %bitcast.53), channel_id=1, replica_groups=mesh['outer'=4,'inner'=2,'grp'=4] {'inner','grp'}, dimensions={0} | all-to-all | bytes 4194304 | tf_op jit(solution)/shard_map/all_to_all | solution.py:220
  135.1 1.5 %copy.41 = bf16[8,16,8,1024]{3,2,0,1:T(8,128)(2,1)} copy(bf16[8,16,8,1024]{3,2,1,0:T(8,128)(2,1)S(1)} %bitcast.56) | data formatting | bytes 4194304 | tf_op jit(solution)/shard_map/reshape | solution.py:221
  (36 shorter events, 8.1 us)
Async XLA Ops:
  4.0 59.8 %all-to-all-start = ((bf16[32,128,2,128]{3,1,2,0:T(8,128)(2,1)}), bf16[32,128,2,128]{3,1,2,0:T(8,128)(2,1)}, u32[]{:S(2)}, u32[]{:S(2)}) async-start(bf16[32,128,2,128]{3,1,2,0:T(8,128)(2,1)} %bitcast.21), calls=%async_computation | async-start | bytes 4194304 | tf_op jit(solution)/shard_map/all_to_all | solution.py:183
  15.8 9.5 %copy-start = (s32[64,3]{0,1:T(4,128)S(1)}, s32[64,3]{0,1:T(4,128)}, u32[]{:S(2)}) copy-start(s32[64,3]{0,1:T(4,128)} %param.8) | copy-start | bytes 2308
  15.8 9.5 %copy-start.1 = (s32[64,3]{0,1:T(4,128)S(1)}, s32[64,3]{0,1:T(4,128)}, u32[]{:S(2)}) copy-start(s32[64,3]{0,1:T(4,128)} %param.9) | copy-start | bytes 2308
  17.6 22.3 %collective-permute-start = (bf16[128,1024]{1,0:T(8,128)(2,1)}, bf16[128,1024]{1,0:T(8,128)(2,1)S(1)}, u32[]{:S(2)}, u32[]{:S(2)}) collective-permute-start(bf16[128,1024]{1,0:T(8,128)(2,1)} %bitcast.4), channel_id=1, source_target_pairs={{0,1},{1,2},{2,3},{3,4},{4,5},{5,6},{6,7},{7,0},{8,9},{9,10},{10,1... | collective-permute-start | bytes 786440 | tf_op jit(solution)/shard_map/ppermute | solution.py:194
  18.9 22.3 %collective-permute-start.1 = (bf16[128,1024]{1,0:T(8,128)(2,1)S(1)}, bf16[128,1024]{1,0:T(8,128)(2,1)S(1)}, u32[]{:S(2)}, u32[]{:S(2)}) collective-permute-start(bf16[128,1024]{1,0:T(8,128)(2,1)S(1)} %bitcast.64), channel_id=1, source_target_pairs={{0,2},{1,3},{2,4},{3,5},{4,6},{5,7},{6,0},{7,1},{8,10},{9,11},{10,... | collective-permute-start | bytes 786440 | tf_op jit(solution)/shard_map/ppermute | solution.py:194
  21.7 31.3 %collective-permute-start.2 = (bf16[128,1024]{1,0:T(8,128)(2,1)S(1)}, bf16[128,1024]{1,0:T(8,128)(2,1)S(1)}, u32[]{:S(2)}, u32[]{:S(2)}) collective-permute-start(bf16[128,1024]{1,0:T(8,128)(2,1)S(1)} %bitcast.63), channel_id=1, source_target_pairs={{0,3},{1,4},{2,5},{3,6},{4,7},{5,0},{6,1},{7,2},{8,11},{9,12},{10,... | collective-permute-start | bytes 786440 | tf_op jit(solution)/shard_map/ppermute | solution.py:194
  24.1 29.8 %collective-permute-start.3 = (bf16[128,1024]{1,0:T(8,128)(2,1)S(1)}, bf16[128,1024]{1,0:T(8,128)(2,1)S(1)}, u32[]{:S(2)}, u32[]{:S(2)}) collective-permute-start(bf16[128,1024]{1,0:T(8,128)(2,1)S(1)} %bitcast.62), channel_id=1, source_target_pairs={{0,4},{1,5},{2,6},{3,7},{4,0},{5,1},{6,2},{7,3},{8,12},{9,13},{10,... | collective-permute-start | bytes 786440 | tf_op jit(solution)/shard_map/ppermute | solution.py:194
  24.9 32.8 %collective-permute-start.4 = (bf16[128,1024]{1,0:T(8,128)(2,1)S(1)}, bf16[128,1024]{1,0:T(8,128)(2,1)S(1)}, u32[]{:S(2)}, u32[]{:S(2)}) collective-permute-start(bf16[128,1024]{1,0:T(8,128)(2,1)S(1)} %bitcast.61), channel_id=1, source_target_pairs={{0,5},{1,6},{2,7},{3,0},{4,1},{5,2},{6,3},{7,4},{8,13},{9,14},{10,... | collective-permute-start | bytes 786440 | tf_op jit(solution)/shard_map/ppermute | solution.py:194
  40.0 18.5 %collective-permute-start.5 = (bf16[128,1024]{1,0:T(8,128)(2,1)S(1)}, bf16[128,1024]{1,0:T(8,128)(2,1)S(1)}, u32[]{:S(2)}, u32[]{:S(2)}) collective-permute-start(bf16[128,1024]{1,0:T(8,128)(2,1)S(1)} %bitcast.66), channel_id=1, source_target_pairs={{0,6},{1,7},{2,0},{3,1},{4,2},{5,3},{6,4},{7,5},{8,14},{9,15},{10,... | collective-permute-start | bytes 786440 | tf_op jit(solution)/shard_map/ppermute | solution.py:194
  41.2 18.0 %collective-permute-start.6 = (bf16[128,1024]{1,0:T(8,128)(2,1)S(1)}, bf16[128,1024]{1,0:T(8,128)(2,1)S(1)}, u32[]{:S(2)}, u32[]{:S(2)}) collective-permute-start(bf16[128,1024]{1,0:T(8,128)(2,1)S(1)} %bitcast.65), channel_id=1, source_target_pairs={{0,7},{1,0},{2,1},{3,2},{4,3},{5,4},{6,5},{7,6},{8,15},{9,8},{10,9... | collective-permute-start | bytes 786440 | tf_op jit(solution)/shard_map/ppermute | solution.py:194

commit v12 on v11

--- a/solution.py
+++ b/solution.py
@@ -66,7 +66,7 @@
     return kernel
 
 
-def full_kernel(local_heads, group_blocks):
+def full_kernel(local_heads, group_blocks, slab_rows, slabs):
     block = MASK_BLOCK_SIZE
     key_count = (SLASH_COUNT + VERT_COUNT) * block
     scale = HEAD_DIMENSION ** (-0.5)
@@ -74,6 +74,7 @@
     def kernel(meta_ref, q_ref, k_ref, v_ref, o_ref):
         h = pl.program_id(0)
         first = meta_ref[2 * local_heads * SLASH_COUNT]
+        me = meta_ref[2 * local_heads * SLASH_COUNT + 1]
         offs = [meta_ref[h * SLASH_COUNT + j] for j in range(SLASH_COUNT)]
         verts = [meta_ref[local_heads * SLASH_COUNT + h * VERT_COUNT + j] for j in range(VERT_COUNT)]
         vert_starts = [pl.multiple_of(v * block, block) for v in verts]
@@ -86,7 +87,9 @@
         never = jnp.int32(-4 * block)
         for b in range(group_blocks):
             qb = first + b
-            q = q_ref[pl.ds(b * block, block), :]
+            slab_blocks = slab_rows // block
+            slab = (me - b // slab_blocks + slabs) % slabs
+            q = q_ref[pl.ds(pl.multiple_of(slab * slab_rows + (b % slab_blocks) * block, block), block), :]
             starts = [pl.multiple_of(jnp.maximum(qb - offs[j], 0) * block, block) for j in range(SLASH_COUNT)]
             keys = jnp.concatenate([k_ref[pl.ds(s, block), :] for s in starts] + vert_keys, 0)
             values = jnp.concatenate([v_ref[pl.ds(s, block), :] for s in starts] + vert_values, 0)
@@ -114,26 +117,27 @@
     return kernel
 
 
-def attend_full(meta, queries, all_keys, all_values, local_heads, sharing):
+def attend_full(meta, queries, all_kv, local_heads, sharing, slab_rows):
     group_rows = queries.shape[0]
     group_blocks = group_rows // MASK_BLOCK_SIZE
     head_size = HEAD_DIMENSION
-    total_rows = all_keys.shape[0]
+    total_rows = all_kv.shape[0]
+    value_base = all_kv.shape[1] // (2 * head_size)
     grid_spec = pltpu.PrefetchScalarGridSpec(
         num_scalar_prefetch=1,
         grid=(local_heads,),
         in_specs=[
             pl.BlockSpec((group_rows, head_size), lambda h, m: (0, h)),
             pl.BlockSpec((total_rows, head_size), lambda h, m: (0, h // sharing)),
-            pl.BlockSpec((total_rows, head_size), lambda h, m: (0, h // sharing)),
+            pl.BlockSpec((total_rows, head_size), lambda h, m: (0, value_base + h // sharing)),
         ],
         out_specs=pl.BlockSpec((group_rows, head_size), lambda h, m: (0, h)),
     )
     return pl.pallas_call(
-        full_kernel(local_heads, group_blocks),
+        full_kernel(local_heads, group_blocks, slab_rows, group_rows // slab_rows),
         grid_spec=grid_spec,
         out_shape=jax.ShapeDtypeStruct((group_rows, local_heads * head_size), queries.dtype),
-    )(meta, queries, all_keys, all_values)
+    )(meta, queries, all_kv, all_kv)
 
 
 def attend(meta, queries, key_window, value_window, vert_keys, vert_values, local_heads, sharing, base):
@@ -193,8 +197,7 @@
         received.append(
             lax.ppermute(sent, heads_axes, [(i, (i + shift) % head_groups) for i in range(head_groups)])
         )
-    slab_shift = (me - jnp.arange(head_groups, dtype=jnp.int32)) % head_groups
-    query_group = jnp.take(jnp.stack(received), slab_shift, axis=0)
+    received = jnp.stack(received)
     group_rows = tok_rows * head_groups
     group_blocks = group_rows // block_size
     back = min(SLASH_REACH, group_blocks)
@@ -211,14 +214,17 @@
         ]
     )
     if whole <= FULL_GATHER_BYTES:
-        everything = everything.reshape(-1, 2, local_kv * head_size).transpose(1, 0, 2)
-        queries = query_group.reshape(group_rows, local_heads * head_size)
+        everything = everything.reshape(-1, 2 * local_kv * head_size)
+        queries = received.reshape(group_rows, local_heads * head_size)
         results = attend_full(
-            meta, queries, everything[0], everything[1], local_heads, group_sharing_factor
+            jnp.concatenate([meta, me.astype(jnp.int32)[None]]), queries, everything,
+            local_heads, group_sharing_factor, tok_rows,
         )
         merged = results.reshape(head_groups, tok_rows, local_heads * head_size)
         returned = lax.all_to_all(merged, heads_axes, split_axis=0, concat_axis=0, tiled=True)
         return returned.transpose(1, 0, 2).reshape(tok_rows, head_groups * local_heads * head_size)
+    slab_shift = (me - jnp.arange(head_groups, dtype=jnp.int32)) % head_groups
+    query_group = jnp.take(received, slab_shift, axis=0)
     key_local = key_group.reshape(group_rows, local_kv * head_size)
     value_local = value_group.reshape(group_rows, local_kv * head_size)
     key_before, value_before = passed_along(

time: 137 us -> 135 us (0.985)
  other arithmetic: 2.45 us -> 0.71 us
    gather x1 -> x0, local copies, waits for them, and re-layouts: 2.27 us -> none  [per_device(): query_group = jnp.take(jnp.stack(received), slab_shift, axis=0)]
    dynamic_slice x8, local copies, waits for them, and re-layouts: 5.51 us -> 7.63 us  [per_device(): lax.dynamic_index_in_dim(query_split, (me + shift) % head_groups, 1, keep...]
    unnamed x14 -> x17, local copies, waits for them, and re-layouts: 10.3 us -> 12.3 us
    all_to_all x1, waiting for transfers between devices: 0.01 us -> 1.82 us  [per_device(): lax.all_to_all(spread, ('outer',) + heads_axes, split_axis=0, concat_axis...]
    all_to_all x1 -> x0, local copies, waits for them, and re-layouts: 1.73 us -> none  [per_device(): lax.all_to_all(spread, ('outer',) + heads_axes, split_axis=0, concat_axis...]
    select_n x2 -> x0, other arithmetic: 1.72 us -> none  [per_device(): query_group = jnp.take(jnp.stack(received), slab_shift, axis=0)]
    squeeze x1 -> x0, local copies, waits for them, and re-layouts: 1.44 us -> none  [per_device(): everything[1]]
    broadcast_in_dim x1, local copies, waits for them, and re-layouts: 1.88 us -> 3.27 us  [per_device(): jnp.broadcast_to(kv_split.transpose(1, 0, 2, 3)[None], (seq_count,) + kv_...]
  transfers between devices with their start and end apart: 8 -> 8, of which waited for: 5 -> 6; matrix products, arithmetic and copies ran while one was open for 14% -> 12% of each run, Pallas kernels for 0% -> 0%
where the time goes in v12:
time: 135 us; the launch traced here: 134 us
  Pallas kernels  36.6 us (27%)
  blocking collectives  30.6 us (23%)
  local copies, waits for them, and re-layouts  25.8 us (19%)
  waiting for transfers between devices  22.8 us (17%)
  starting transfers between devices  17.3 us (13%)
    pallas_call x1, Pallas kernels, attend_full(): pl.pallas_call(full_kernel(local_heads, group_blocks, slab_rows, group_ro...  36.6 us
    all_to_all x1, blocking collectives, per_device(): lax.all_to_all(merged, heads_axes, split_axis=0, concat_axis=0, tiled=True)  30.6 us
    ppermute x7, waiting for transfers between devices, per_device(): lax.ppermute(sent, heads_axes, [(i, (i + shift) % head_groups) for i in r...  21 us
    unnamed x17, local copies, waits for them, and re-layouts  12.3 us
    ppermute x7, starting transfers between devices, per_device(): lax.ppermute(sent, heads_axes, [(i, (i + shift) % head_groups) for i in r...  9.9 us
    dynamic_slice x8, local copies, waits for them, and re-layouts, per_device(): lax.dynamic_index_in_dim(query_split, (me + shift) % head_groups, 1, keep...  7.63 us
    all_to_all x1, starting transfers between devices, per_device(): lax.all_to_all(spread, ('outer',) + heads_axes, split_axis=0, concat_axis...  7.43 us
    broadcast_in_dim x1, local copies, waits for them, and re-layouts, per_device(): jnp.broadcast_to(kv_split.transpose(1, 0, 2, 3)[None], (seq_count,) + kv_...  3.27 us
  transfers between devices with their start and end apart: 8, of which 6 were waited for; matrix products, arithmetic and copies ran while one was open for 12% of the time, Pallas kernels for 0%

profile of v12, /device:TPU:0, one launch (start us, length us, event | category | flops | bytes accessed | tf_op | source)
XLA Modules:
  0.0 134.1 jit_solution(12210083677507295378)
XLA Ops:
  0.0 1.0 copy.28
  1.0 1.0 copy.29
  2.6 3.3 %broadcast_in_dim.14 = bf16[4,8,128,2,128]{4,3,2,1,0:T(2,128)(2,1)} broadcast(bf16[8,128,2,128]{3,2,1,0:T(2,128)(2,1)S(1)} %copy.25), dimensions={1,2,3,4} | broadcast | bytes 2621440 | tf_op jit(solution)/shard_map/broadcast_in_dim | solution.py:184
  5.9 7.4 %all-to-all-start = ((bf16[32,128,2,128]{3,2,1,0:T(2,128)(2,1)}), bf16[32,128,2,128]{3,2,1,0:T(2,128)(2,1)}, u32[]{:S(2)}, u32[]{:S(2)}) async-start(bf16[32,128,2,128]{3,2,1,0:T(2,128)(2,1)} %bitcast.20), calls=%async_computation | async-start | bytes 4194304 | tf_op jit(solution)/shard_map/all_to_all | solution.py:187
  13.4 3.2 %copy.16 = bf16[128,8192]{0,1:T(8,128)(2,1)S(1)} copy(bf16[128,8192]{1,0:T(8,128)(2,1)} %param.5) | data formatting | bytes 4194304 | tf_op args[0]
  16.7 0.9 constant_dynamic-slice_fusion
  17.6 1.8 %copy.18 = bf16[128,1,1024]{2,0,1:T(8,128)(2,1)} copy(bf16[128,1,1024]{0,2,1:T(8,128)(2,1)} %get-tuple-element.11) | data formatting | bytes 524288 | tf_op jit(solution)/shard_map/jit(dynamic_index_in_dim)/dynamic_slice | solution.py:196
  19.6 1.8 %copy.19 = bf16[128,1,1024]{2,0,1:T(8,128)(2,1)} copy(bf16[128,1,1024]{0,2,1:T(8,128)(2,1)} %get-tuple-element.10) | data formatting | bytes 524288 | tf_op jit(solution)/shard_map/jit(dynamic_index_in_dim)/dynamic_slice | solution.py:196
  21.4 1.7 %collective-permute-start.1 = (bf16[128,1024]{1,0:T(8,128)(2,1)}, bf16[128,1024]{1,0:T(8,128)(2,1)}, u32[]{:S(2)}, u32[]{:S(2)}) collective-permute-start(bf16[128,1024]{1,0:T(8,128)(2,1)} %bitcast.6), channel_id=1, source_target_pairs={{0,2},{1,3},{2,4},{3,5},{4,6},{5,7},{6,0},{7,1},{8,10},{9,11},{10,... | collective-permute-start | bytes 786440 | tf_op jit(solution)/shard_map/ppermute | solution.py:198
  23.1 1.8 %copy.20 = bf16[128,1,1024]{2,0,1:T(8,128)(2,1)} copy(bf16[128,1,1024]{0,2,1:T(8,128)(2,1)} %get-tuple-element.9) | data formatting | bytes 524288 | tf_op jit(solution)/shard_map/jit(dynamic_index_in_dim)/dynamic_slice | solution.py:196
  24.9 2.2 %collective-permute-start.2 = (bf16[128,1024]{1,0:T(8,128)(2,1)}, bf16[128,1024]{1,0:T(8,128)(2,1)}, u32[]{:S(2)}, u32[]{:S(2)}) collective-permute-start(bf16[128,1024]{1,0:T(8,128)(2,1)} %bitcast.8), channel_id=1, source_target_pairs={{0,3},{1,4},{2,5},{3,6},{4,7},{5,0},{6,1},{7,2},{8,11},{9,12},{10,... | collective-permute-start | bytes 786440 | tf_op jit(solution)/shard_map/ppermute | solution.py:198
  30.4 11.5 %collective-permute-done = bf16[128,1024]{1,0:T(8,128)(2,1)} collective-permute-done((bf16[128,1024]{1,0:T(8,128)(2,1)}, bf16[128,1024]{1,0:T(8,128)(2,1)}, u32[]{:S(2)}, u32[]{:S(2)}) %collective-permute-start) | collective-permute-done | bytes 262176 | tf_op jit(solution)/shard_map/ppermute | solution.py:198
  41.9 1.0 bitcast_dynamic-update-slice_fusion.6
  43.2 5.1 %collective-permute-start.6 = (bf16[128,1024]{1,0:T(8,128)(2,1)S(1)}, bf16[128,1024]{1,0:T(8,128)(2,1)S(1)}, u32[]{:S(2)}, u32[]{:S(2)}) collective-permute-start(bf16[128,1024]{1,0:T(8,128)(2,1)S(1)} %bitcast.58), channel_id=1, source_target_pairs={{0,7},{1,0},{2,1},{3,2},{4,3},{5,4},{6,5},{7,6},{8,15},{9,8},{10,9... | collective-permute-start | bytes 786440 | tf_op jit(solution)/shard_map/ppermute | solution.py:198
  48.3 1.0 bitcast_dynamic-update-slice_fusion.5
  49.3 6.2 %collective-permute-done.2 = bf16[128,1024]{1,0:T(8,128)(2,1)} collective-permute-done((bf16[128,1024]{1,0:T(8,128)(2,1)}, bf16[128,1024]{1,0:T(8,128)(2,1)}, u32[]{:S(2)}, u32[]{:S(2)}) %collective-permute-start.2) | collective-permute-done | bytes 262176 | tf_op jit(solution)/shard_map/ppermute | solution.py:198
  55.5 1.0 bitcast_dynamic-update-slice_fusion.4
  56.5 1.0 bitcast_dynamic-update-slice_fusion.3
  57.5 2.7 %collective-permute-done.4 = bf16[128,1024]{1,0:T(8,128)(2,1)S(1)} collective-permute-done((bf16[128,1024]{1,0:T(8,128)(2,1)S(1)}, bf16[128,1024]{1,0:T(8,128)(2,1)S(1)}, u32[]{:S(2)}, u32[]{:S(2)}) %collective-permute-start.4) | collective-permute-done | bytes 262176 | tf_op jit(solution)/shard_map/ppermute | solution.py:198
  60.5 1.8 %all-to-all-done = bf16[32,128,2,128]{3,2,1,0:T(2,128)(2,1)} async-done(((bf16[32,128,2,128]{3,2,1,0:T(2,128)(2,1)}), bf16[32,128,2,128]{3,2,1,0:T(2,128)(2,1)}, u32[]{:S(2)}, u32[]{:S(2)}) %all-to-all-start) | async-done | bytes 2097184 | tf_op jit(solution)/shard_map/all_to_all | solution.py:187
  62.3 3.2 %copy.32 = bf16[512,8,2,128]{3,1,2,0:T(8,128)(2,1)} copy(bf16[512,8,2,128]{3,2,1,0:T(2,128)(2,1)} %bitcast.34) | data formatting | bytes 4194304
  65.5 36.6 %shard_map.55 = bf16[1024,1024]{1,0:T(8,128)(2,1)} custom-call(s32[50]{0:T(128)} %pad_add_fusion.meta_ref, bf16[1024,1024]{1,0:T(8,128)(2,1)} %bitcast.52, bf16[4096,256]{1,0:T(8,128)(2,1)} %bitcast.47, bf16[4096,256]{1,0:T(8,128)(2,1)} %bitcast.48), custom_call_target="tpu_custom_call" | custom-call | tf_op jit(solution)/shard_map/pallas_call | solution.py:136
  102.0 30.6 %all_to_all.10 = bf16[8,128,1024]{2,1,0:T(8,128)(2,1)S(1)} all-to-all(bf16[8,128,1024]{2,1,0:T(8,128)(2,1)} %bitcast.51), channel_id=1, replica_groups=mesh['outer'=4,'inner'=2,'grp'=4] {'inner','grp'}, dimensions={0} | all-to-all | bytes 4194304 | tf_op jit(solution)/shard_map/all_to_all | solution.py:224
  132.6 1.5 %copy.27 = bf16[8,16,8,1024]{3,2,0,1:T(8,128)(2,1)} copy(bf16[8,16,8,1024]{3,2,1,0:T(8,128)(2,1)S(1)} %bitcast.50) | data formatting | bytes 4194304 | tf_op jit(solution)/shard_map/reshape | solution.py:225
  (31 shorter events, 4.6 us)
Async XLA Ops:
  5.9 56.4 %all-to-all-start = ((bf16[32,128,2,128]{3,2,1,0:T(2,128)(2,1)}), bf16[32,128,2,128]{3,2,1,0:T(2,128)(2,1)}, u32[]{:S(2)}, u32[]{:S(2)}) async-start(bf16[32,128,2,128]{3,2,1,0:T(2,128)(2,1)} %bitcast.20), calls=%async_computation | async-start | bytes 4194304 | tf_op jit(solution)/shard_map/all_to_all | solution.py:187
  17.6 11.4 %copy-start.1 = (s32[64,3]{0,1:T(4,128)S(1)}, s32[64,3]{0,1:T(4,128)}, u32[]{:S(2)}) copy-start(s32[64,3]{0,1:T(4,128)} %param.8) | copy-start | bytes 2308
  17.6 11.4 %copy-start.2 = (s32[64,3]{0,1:T(4,128)S(1)}, s32[64,3]{0,1:T(4,128)}, u32[]{:S(2)}) copy-start(s32[64,3]{0,1:T(4,128)} %param.9) | copy-start | bytes 2308
  19.4 22.5 %collective-permute-start = (bf16[128,1024]{1,0:T(8,128)(2,1)}, bf16[128,1024]{1,0:T(8,128)(2,1)}, u32[]{:S(2)}, u32[]{:S(2)}) collective-permute-start(bf16[128,1024]{1,0:T(8,128)(2,1)} %bitcast.4), channel_id=1, source_target_pairs={{0,1},{1,2},{2,3},{3,4},{4,5},{5,6},{6,7},{7,0},{8,9},{9,10},{10,1... | collective-permute-start | bytes 786440 | tf_op jit(solution)/shard_map/ppermute | solution.py:198
  21.4 21.8 %collective-permute-start.1 = (bf16[128,1024]{1,0:T(8,128)(2,1)}, bf16[128,1024]{1,0:T(8,128)(2,1)}, u32[]{:S(2)}, u32[]{:S(2)}) collective-permute-start(bf16[128,1024]{1,0:T(8,128)(2,1)} %bitcast.6), channel_id=1, source_target_pairs={{0,2},{1,3},{2,4},{3,5},{4,6},{5,7},{6,0},{7,1},{8,10},{9,11},{10,... | collective-permute-start | bytes 786440 | tf_op jit(solution)/shard_map/ppermute | solution.py:198
  24.9 30.6 %collective-permute-start.2 = (bf16[128,1024]{1,0:T(8,128)(2,1)}, bf16[128,1024]{1,0:T(8,128)(2,1)}, u32[]{:S(2)}, u32[]{:S(2)}) collective-permute-start(bf16[128,1024]{1,0:T(8,128)(2,1)} %bitcast.8), channel_id=1, source_target_pairs={{0,3},{1,4},{2,5},{3,6},{4,7},{5,0},{6,1},{7,2},{8,11},{9,12},{10,... | collective-permute-start | bytes 786440 | tf_op jit(solution)/shard_map/ppermute | solution.py:198
  27.9 28.5 %collective-permute-start.3 = (bf16[128,1024]{1,0:T(8,128)(2,1)}, bf16[128,1024]{1,0:T(8,128)(2,1)}, u32[]{:S(2)}, u32[]{:S(2)}) collective-permute-start(bf16[128,1024]{1,0:T(8,128)(2,1)} %bitcast.10), channel_id=1, source_target_pairs={{0,4},{1,5},{2,6},{3,7},{4,0},{5,1},{6,2},{7,3},{8,12},{9,13},{10,... | collective-permute-start | bytes 786440 | tf_op jit(solution)/shard_map/ppermute | solution.py:198
  28.7 31.5 %collective-permute-start.4 = (bf16[128,1024]{1,0:T(8,128)(2,1)S(1)}, bf16[128,1024]{1,0:T(8,128)(2,1)S(1)}, u32[]{:S(2)}, u32[]{:S(2)}) collective-permute-start(bf16[128,1024]{1,0:T(8,128)(2,1)S(1)} %bitcast.57), channel_id=1, source_target_pairs={{0,5},{1,6},{2,7},{3,0},{4,1},{5,2},{6,3},{7,4},{8,13},{9,14},{10,... | collective-permute-start | bytes 786440 | tf_op jit(solution)/shard_map/ppermute | solution.py:198
  41.9 18.3 %collective-permute-start.5 = (bf16[128,1024]{1,0:T(8,128)(2,1)S(1)}, bf16[128,1024]{1,0:T(8,128)(2,1)S(1)}, u32[]{:S(2)}, u32[]{:S(2)}) collective-permute-start(bf16[128,1024]{1,0:T(8,128)(2,1)S(1)} %bitcast.59), channel_id=1, source_target_pairs={{0,6},{1,7},{2,0},{3,1},{4,2},{5,3},{6,4},{7,5},{8,14},{9,15},{10,... | collective-permute-start | bytes 786440 | tf_op jit(solution)/shard_map/ppermute | solution.py:198
  43.2 17.2 %collective-permute-start.6 = (bf16[128,1024]{1,0:T(8,128)(2,1)S(1)}, bf16[128,1024]{1,0:T(8,128)(2,1)S(1)}, u32[]{:S(2)}, u32[]{:S(2)}) collective-permute-start(bf16[128,1024]{1,0:T(8,128)(2,1)S(1)} %bitcast.58), channel_id=1, source_target_pairs={{0,7},{1,0},{2,1},{3,2},{4,3},{5,4},{6,5},{7,6},{8,15},{9,8},{10,9... | collective-permute-start | bytes 786440 | tf_op jit(solution)/shard_map/ppermute | solution.py:198
  60.5 5.0 %copy-start = (bf16[8,128,1024]{2,1,0:T(8,128)(2,1)}, bf16[8,128,1024]{2,1,0:T(8,128)(2,1)S(1)}, u32[]{:S(2)}) copy-start(bf16[8,128,1024]{2,1,0:T(8,128)(2,1)S(1)} %bitcast_dynamic-update-slice_fusion) | copy-start | bytes 6291460

commit v13 on v12

--- a/solution.py
+++ b/solution.py
@@ -178,16 +178,17 @@
     key_split = key_matrix.reshape(tok_rows, head_groups, local_kv * head_size)
     value_split = value_matrix.reshape(tok_rows, head_groups, local_kv * head_size)
     seq_count = lax.axis_size("outer")
-    kv_split = jnp.stack([key_split, value_split], 2)
-    whole = seq_count * head_groups * kv_split.size * kv_split.dtype.itemsize // head_groups
+    whole = seq_count * (key_split.size + value_split.size) * key_split.dtype.itemsize
     if whole <= FULL_GATHER_BYTES:
-        spread = jnp.broadcast_to(
-            kv_split.transpose(1, 0, 2, 3)[None], (seq_count,) + kv_split.transpose(1, 0, 2, 3).shape
-        ).reshape((seq_count * head_groups,) + kv_split.transpose(1, 0, 2, 3).shape[1:])
+        kv_rows = jnp.concatenate([key_split, value_split], 2).transpose(1, 0, 2)
+        spread = jnp.broadcast_to(kv_rows[None], (seq_count,) + kv_rows.shape).reshape(
+            (seq_count * head_groups,) + kv_rows.shape[1:]
+        )
         everything = lax.all_to_all(
             spread, ("outer",) + heads_axes, split_axis=0, concat_axis=0, tiled=True
         )
     else:
+        kv_split = jnp.stack([key_split, value_split], 2)
         kv_group = lax.all_to_all(kv_split, heads_axes, split_axis=1, concat_axis=0, tiled=True)
         key_group, value_group = kv_group[:, 0, 0], kv_group[:, 0, 1]
     me = lax.axis_index(heads_axes)

time: 135 us -> 134 us (level)
  waiting for transfers between devices: 22.8 us -> 15.9 us
  local copies, waits for them, and re-layouts: 25.8 us -> 30.8 us
    ppermute x7, waiting for transfers between devices: 21 us -> 15.9 us  [per_device(): lax.ppermute(sent, heads_axes, [(i, (i + shift) % head_groups) for i in r...]
    unnamed x17 -> x16, local copies, waits for them, and re-layouts: 12.3 us -> 17.2 us
    all_to_all x1, waiting for transfers between devices: 1.82 us -> 0.01 us  [per_device(): lax.all_to_all(spread, ('outer',) + heads_axes, split_axis=0, concat_axis...]
    broadcast_in_dim x1, local copies, waits for them, and re-layouts: 3.27 us -> 1.58 us  [per_device(): jnp.broadcast_to(kv_rows[None], (seq_count,) + kv_rows.shape)]
    dynamic_slice x8, local copies, waits for them, and re-layouts: 7.63 us -> 9.14 us  [per_device(): lax.dynamic_index_in_dim(query_split, (me + shift) % head_groups, 1, keep...]
  transfers between devices with their start and end apart: 8 -> 8, of which waited for: 6 -> 3; matrix products, arithmetic and copies ran while one was open for 12% -> 19% of each run, Pallas kernels for 0% -> 0%
where the time goes in v13:
time: 134 us; the launch traced here: 133 us
  Pallas kernels  36.6 us (27%)
  blocking collectives  31.8 us (24%)
  local copies, waits for them, and re-layouts  30.8 us (23%)
  starting transfers between devices  16.9 us (13%)
  waiting for transfers between devices  15.9 us (12%)
    pallas_call x1, Pallas kernels, attend_full(): pl.pallas_call(full_kernel(local_heads, group_blocks, slab_rows, group_ro...  36.6 us
    all_to_all x1, blocking collectives, per_device(): lax.all_to_all(merged, heads_axes, split_axis=0, concat_axis=0, tiled=True)  31.8 us
    unnamed x16, local copies, waits for them, and re-layouts  17.2 us
    ppermute x7, waiting for transfers between devices, per_device(): lax.ppermute(sent, heads_axes, [(i, (i + shift) % head_groups) for i in r...  15.9 us
    ppermute x7, starting transfers between devices, per_device(): lax.ppermute(sent, heads_axes, [(i, (i + shift) % head_groups) for i in r...  9.58 us
    dynamic_slice x8, local copies, waits for them, and re-layouts, per_device(): lax.dynamic_index_in_dim(query_split, (me + shift) % head_groups, 1, keep...  9.14 us
    all_to_all x1, starting transfers between devices, per_device(): lax.all_to_all(spread, ('outer',) + heads_axes, split_axis=0, concat_axis...  7.3 us
  transfers between devices with their start and end apart: 8, of which 3 were waited for; matrix products, arithmetic and copies ran while one was open for 19% of the time, Pallas kernels for 0%

profile of v13, /device:TPU:0, one launch (start us, length us, event | category | flops | bytes accessed | tf_op | source)
XLA Modules:
  0.0 132.9 jit_solution(17560225837064099106)
XLA Ops:
  0.0 1.0 copy.28
  1.0 1.0 copy.29
  2.2 1.6 %broadcast_in_dim.14 = bf16[4,8,128,256]{3,2,1,0:T(8,128)(2,1)} broadcast(bf16[8,128,256]{2,1,0:T(8,128)(2,1)S(1)} %copy.25), dimensions={1,2,3} | broadcast | bytes 2621440 | tf_op jit(solution)/shard_map/broadcast_in_dim | solution.py:184
  3.8 7.3 %all-to-all-start = ((bf16[32,128,256]{2,1,0:T(8,128)(2,1)}), bf16[32,128,256]{2,1,0:T(8,128)(2,1)S(1)}, u32[]{:S(2)}, u32[]{:S(2)}) async-start(bf16[32,128,256]{2,1,0:T(8,128)(2,1)} %bitcast.41), calls=%async_computation | async-start | bytes 4194304 | tf_op jit(solution)/shard_map/all_to_all | solution.py:187
  11.2 4.1 %copy.16 = bf16[128,8192]{0,1:T(8,128)(2,1)} copy(bf16[128,8192]{1,0:T(8,128)(2,1)} %param.5) | data formatting | bytes 4194304 | tf_op args[0]
  15.2 2.5 %constant_dynamic-slice_fusion = (bf16[128,1,1024]{0,2,1:T(8,128)(2,1)S(1)}, bf16[128,1,1024]{0,2,1:T(8,128)(2,1)S(1)}, bf16[128,1,1024]{0,2,1:T(8,128)(2,1)S(1)...) fusion(bf16[128,8,1024]{0,2,1:T(8,128)(2,1)} %bitcast.42, ...), kind=kLoop, calls=%fused_computation.9 | loop fusion | bytes 4194336 | tf_op jit(solution)/shard_map/jit(dynamic_index_in_dim)/dynamic_slice | solution.py:197
  17.7 1.8 %copy.18 = bf16[128,1,1024]{2,0,1:T(8,128)(2,1)} copy(bf16[128,1,1024]{0,2,1:T(8,128)(2,1)} %get-tuple-element.11) | data formatting | bytes 524288 | tf_op jit(solution)/shard_map/jit(dynamic_index_in_dim)/dynamic_slice | solution.py:197
  19.8 1.8 %copy.19 = bf16[128,1,1024]{2,0,1:T(8,128)(2,1)} copy(bf16[128,1,1024]{0,2,1:T(8,128)(2,1)} %get-tuple-element.10) | data formatting | bytes 524288 | tf_op jit(solution)/shard_map/jit(dynamic_index_in_dim)/dynamic_slice | solution.py:197
  21.6 1.7 %collective-permute-start.1 = (bf16[128,1024]{1,0:T(8,128)(2,1)}, bf16[128,1024]{1,0:T(8,128)(2,1)}, u32[]{:S(2)}, u32[]{:S(2)}) collective-permute-start(bf16[128,1024]{1,0:T(8,128)(2,1)} %bitcast.53), channel_id=1, source_target_pairs={{0,2},{1,3},{2,4},{3,5},{4,6},{5,7},{6,0},{7,1},{8,10},{9,11},{10,... | collective-permute-start | bytes 786440 | tf_op jit(solution)/shard_map/ppermute | solution.py:199
  23.2 1.8 %copy.20 = bf16[128,1,1024]{2,0,1:T(8,128)(2,1)} copy(bf16[128,1,1024]{0,2,1:T(8,128)(2,1)} %get-tuple-element.9) | data formatting | bytes 524288 | tf_op jit(solution)/shard_map/jit(dynamic_index_in_dim)/dynamic_slice | solution.py:197
  25.0 2.2 %collective-permute-start.2 = (bf16[128,1024]{1,0:T(8,128)(2,1)}, bf16[128,1024]{1,0:T(8,128)(2,1)}, u32[]{:S(2)}, u32[]{:S(2)}) collective-permute-start(bf16[128,1024]{1,0:T(8,128)(2,1)} %bitcast.52), channel_id=1, source_target_pairs={{0,3},{1,4},{2,5},{3,6},{4,7},{5,0},{6,1},{7,2},{8,11},{9,12},{10,... | collective-permute-start | bytes 786440 | tf_op jit(solution)/shard_map/ppermute | solution.py:199
  31.2 8.4 %collective-permute-done = bf16[128,1024]{1,0:T(8,128)(2,1)} collective-permute-done((bf16[128,1024]{1,0:T(8,128)(2,1)}, bf16[128,1024]{1,0:T(8,128)(2,1)}, u32[]{:S(2)}, u32[]{:S(2)}) %collective-permute-start) | collective-permute-done | bytes 262176 | tf_op jit(solution)/shard_map/ppermute | solution.py:199
  39.6 1.7 %bitcast_dynamic-update-slice_fusion.6 = bf16[8,128,1024]{2,1,0:T(8,128)(2,1)} fusion(bf16[8,128,1024]{2,1,0:T(8,128)(2,1)} %bitcast_dynamic-update-slice_fusion.7, bf16[128,1024]{1,0:T(8,128)(2,1)} %collective-permute-done), kind=kLoop, calls=%fused_computation.7 | loop fusion | bytes 524288
  41.3 4.7 %collective-permute-start.6 = (bf16[128,1024]{1,0:T(8,128)(2,1)S(1)}, bf16[128,1024]{1,0:T(8,128)(2,1)S(1)}, u32[]{:S(2)}, u32[]{:S(2)}) collective-permute-start(bf16[128,1024]{1,0:T(8,128)(2,1)S(1)} %bitcast.55), channel_id=1, source_target_pairs={{0,7},{1,0},{2,1},{3,2},{4,3},{5,4},{6,5},{7,6},{8,15},{9,8},{10,9... | collective-permute-start | bytes 786440 | tf_op jit(solution)/shard_map/ppermute | solution.py:199
  46.0 1.7 %bitcast_dynamic-update-slice_fusion.5 = bf16[8,128,1024]{2,1,0:T(8,128)(2,1)} fusion(bf16[8,128,1024]{2,1,0:T(8,128)(2,1)} %bitcast_dynamic-update-slice_fusion.6, bf16[128,1024]{1,0:T(8,128)(2,1)} %collective-permute-done.1), kind=kLoop, calls=%fused_computation.6 | loop fusion | bytes 524288
  47.7 5.7 %collective-permute-done.2 = bf16[128,1024]{1,0:T(8,128)(2,1)} collective-permute-done((bf16[128,1024]{1,0:T(8,128)(2,1)}, bf16[128,1024]{1,0:T(8,128)(2,1)}, u32[]{:S(2)}, u32[]{:S(2)}) %collective-permute-start.2) | collective-permute-done | bytes 262176 | tf_op jit(solution)/shard_map/ppermute | solution.py:199
  53.4 1.7 %bitcast_dynamic-update-slice_fusion.4 = bf16[8,128,1024]{2,1,0:T(8,128)(2,1)} fusion(bf16[8,128,1024]{2,1,0:T(8,128)(2,1)} %bitcast_dynamic-update-slice_fusion.5, bf16[128,1024]{1,0:T(8,128)(2,1)} %collective-permute-done.2), kind=kLoop, calls=%fused_computation.5 | loop fusion | bytes 524288
  55.1 1.7 %bitcast_dynamic-update-slice_fusion.3 = bf16[8,128,1024]{2,1,0:T(8,128)(2,1)} fusion(bf16[8,128,1024]{2,1,0:T(8,128)(2,1)} %bitcast_dynamic-update-slice_fusion.4, bf16[128,1024]{1,0:T(8,128)(2,1)} %collective-permute-done.3), kind=kLoop, calls=%fused_computation.4 | loop fusion | bytes 524288
  56.7 1.7 %collective-permute-done.4 = bf16[128,1024]{1,0:T(8,128)(2,1)} collective-permute-done((bf16[128,1024]{1,0:T(8,128)(2,1)S(1)}, bf16[128,1024]{1,0:T(8,128)(2,1)}, u32[]{:S(2)}, u32[]{:S(2)}) %collective-permute-start.4) | collective-permute-done | bytes 262176 | tf_op jit(solution)/shard_map/ppermute | solution.py:199
  58.5 1.7 %bitcast_dynamic-update-slice_fusion.2 = bf16[8,128,1024]{2,1,0:T(8,128)(2,1)} fusion(bf16[8,128,1024]{2,1,0:T(8,128)(2,1)} %bitcast_dynamic-update-slice_fusion.3, bf16[128,1024]{1,0:T(8,128)(2,1)} %collective-permute-done.4), kind=kLoop, calls=%fused_computation.3 | loop fusion | bytes 524288
  61.6 1.3 copy-done
  62.9 36.6 %shard_map.55 = bf16[1024,1024]{1,0:T(8,128)(2,1)} custom-call(s32[50]{0:T(128)} %pad_add_fusion.meta_ref, bf16[1024,1024]{1,0:T(8,128)(2,1)} %bitcast.45, bf16[4096,256]{1,0:T(8,128)(2,1)} %bitcast.39, bf16[4096,256]{1,0:T(8,128)(2,1)} %bitcast.40), custom_call_target="tpu_custom_call" | custom-call | tf_op jit(solution)/shard_map/pallas_call | solution.py:136
  99.5 31.8 %all_to_all.10 = bf16[8,128,1024]{2,1,0:T(8,128)(2,1)S(1)} all-to-all(bf16[8,128,1024]{2,1,0:T(8,128)(2,1)} %bitcast.44), channel_id=1, replica_groups=mesh['outer'=4,'inner'=2,'grp'=4] {'inner','grp'}, dimensions={0} | all-to-all | bytes 4194304 | tf_op jit(solution)/shard_map/all_to_all | solution.py:225
  131.3 1.6 %copy.27 = bf16[8,16,8,1024]{3,2,0,1:T(8,128)(2,1)} copy(bf16[8,16,8,1024]{3,2,1,0:T(8,128)(2,1)S(1)} %bitcast.43) | data formatting | bytes 4194304 | tf_op jit(solution)/shard_map/reshape | solution.py:226
  (30 shorter events, 5.8 us)
Async XLA Ops:
  3.8 57.9 %all-to-all-start = ((bf16[32,128,256]{2,1,0:T(8,128)(2,1)}), bf16[32,128,256]{2,1,0:T(8,128)(2,1)S(1)}, u32[]{:S(2)}, u32[]{:S(2)}) async-start(bf16[32,128,256]{2,1,0:T(8,128)(2,1)} %bitcast.41), calls=%async_computation | async-start | bytes 4194304 | tf_op jit(solution)/shard_map/all_to_all | solution.py:187
  17.7 11.5 %copy-start.1 = (s32[64,3]{0,1:T(4,128)S(1)}, s32[64,3]{0,1:T(4,128)}, u32[]{:S(2)}) copy-start(s32[64,3]{0,1:T(4,128)} %param.8) | copy-start | bytes 2308
  17.7 11.5 %copy-start.2 = (s32[64,3]{0,1:T(4,128)S(1)}, s32[64,3]{0,1:T(4,128)}, u32[]{:S(2)}) copy-start(s32[64,3]{0,1:T(4,128)} %param.9) | copy-start | bytes 2308
  19.5 20.1 %collective-permute-start = (bf16[128,1024]{1,0:T(8,128)(2,1)}, bf16[128,1024]{1,0:T(8,128)(2,1)}, u32[]{:S(2)}, u32[]{:S(2)}) collective-permute-start(bf16[128,1024]{1,0:T(8,128)(2,1)} %bitcast.54), channel_id=1, source_target_pairs={{0,1},{1,2},{2,3},{3,4},{4,5},{5,6},{6,7},{7,0},{8,9},{9,10},{10,1... | collective-permute-start | bytes 786440 | tf_op jit(solution)/shard_map/ppermute | solution.py:199
  21.6 19.8 %collective-permute-start.1 = (bf16[128,1024]{1,0:T(8,128)(2,1)}, bf16[128,1024]{1,0:T(8,128)(2,1)}, u32[]{:S(2)}, u32[]{:S(2)}) collective-permute-start(bf16[128,1024]{1,0:T(8,128)(2,1)} %bitcast.53), channel_id=1, source_target_pairs={{0,2},{1,3},{2,4},{3,5},{4,6},{5,7},{6,0},{7,1},{8,10},{9,11},{10,... | collective-permute-start | bytes 786440 | tf_op jit(solution)/shard_map/ppermute | solution.py:199
  25.0 28.4 %collective-permute-start.2 = (bf16[128,1024]{1,0:T(8,128)(2,1)}, bf16[128,1024]{1,0:T(8,128)(2,1)}, u32[]{:S(2)}, u32[]{:S(2)}) collective-permute-start(bf16[128,1024]{1,0:T(8,128)(2,1)} %bitcast.52), channel_id=1, source_target_pairs={{0,3},{1,4},{2,5},{3,6},{4,7},{5,0},{6,1},{7,2},{8,11},{9,12},{10,... | collective-permute-start | bytes 786440 | tf_op jit(solution)/shard_map/ppermute | solution.py:199
  28.1 27.0 %collective-permute-start.3 = (bf16[128,1024]{1,0:T(8,128)(2,1)}, bf16[128,1024]{1,0:T(8,128)(2,1)}, u32[]{:S(2)}, u32[]{:S(2)}) collective-permute-start(bf16[128,1024]{1,0:T(8,128)(2,1)} %bitcast.51), channel_id=1, source_target_pairs={{0,4},{1,5},{2,6},{3,7},{4,0},{5,1},{6,2},{7,3},{8,12},{9,13},{10,... | collective-permute-start | bytes 786440 | tf_op jit(solution)/shard_map/ppermute | solution.py:199
  28.8 29.7 %collective-permute-start.4 = (bf16[128,1024]{1,0:T(8,128)(2,1)S(1)}, bf16[128,1024]{1,0:T(8,128)(2,1)}, u32[]{:S(2)}, u32[]{:S(2)}) collective-permute-start(bf16[128,1024]{1,0:T(8,128)(2,1)S(1)} %bitcast.50), channel_id=1, source_target_pairs={{0,5},{1,6},{2,7},{3,0},{4,1},{5,2},{6,3},{7,4},{8,13},{9,14},{10,... | collective-permute-start | bytes 786440 | tf_op jit(solution)/shard_map/ppermute | solution.py:199
  39.6 20.5 %collective-permute-start.5 = (bf16[128,1024]{1,0:T(8,128)(2,1)S(1)}, bf16[128,1024]{1,0:T(8,128)(2,1)S(1)}, u32[]{:S(2)}, u32[]{:S(2)}) collective-permute-start(bf16[128,1024]{1,0:T(8,128)(2,1)S(1)} %bitcast.56), channel_id=1, source_target_pairs={{0,6},{1,7},{2,0},{3,1},{4,2},{5,3},{6,4},{7,5},{8,14},{9,15},{10,... | collective-permute-start | bytes 786440 | tf_op jit(solution)/shard_map/ppermute | solution.py:199
  41.3 19.6 %collective-permute-start.6 = (bf16[128,1024]{1,0:T(8,128)(2,1)S(1)}, bf16[128,1024]{1,0:T(8,128)(2,1)S(1)}, u32[]{:S(2)}, u32[]{:S(2)}) collective-permute-start(bf16[128,1024]{1,0:T(8,128)(2,1)S(1)} %bitcast.55), channel_id=1, source_target_pairs={{0,7},{1,0},{2,1},{3,2},{4,3},{5,4},{6,5},{7,6},{8,15},{9,8},{10,9... | collective-permute-start | bytes 786440 | tf_op jit(solution)/shard_map/ppermute | solution.py:199
  61.6 1.3 copy-start

commit v14 on v13

--- a/solution.py
+++ b/solution.py
@@ -199,6 +199,7 @@
             lax.ppermute(sent, heads_axes, [(i, (i + shift) % head_groups) for i in range(head_groups)])
         )
     received = jnp.stack(received)
+    slab_shift = (me - jnp.arange(head_groups, dtype=jnp.int32)) % head_groups
     group_rows = tok_rows * head_groups
     group_blocks = group_rows // block_size
     back = min(SLASH_REACH, group_blocks)
@@ -221,10 +222,18 @@
             jnp.concatenate([meta, me.astype(jnp.int32)[None]]), queries, everything,
             local_heads, group_sharing_factor, tok_rows,
         )
+        half = local_heads // 2 * head_size
         merged = results.reshape(head_groups, tok_rows, local_heads * head_size)
-        returned = lax.all_to_all(merged, heads_axes, split_axis=0, concat_axis=0, tiled=True)
+        first_half = lax.all_to_all(merged[:, :, :half], heads_axes, split_axis=0, concat_axis=0, tiled=True)
+        back_by_shift = [lax.dynamic_index_in_dim(merged[:, :, half:], me, 0, keepdims=False)]
+        for shift in range(1, head_groups):
+            sent = lax.dynamic_index_in_dim(merged[:, :, half:], (me + shift) % head_groups, 0, keepdims=False)
+            back_by_shift.append(
+                lax.ppermute(sent, heads_axes, [(i, (i + shift) % head_groups) for i in range(head_groups)])
+            )
+        second_half = jnp.take(jnp.stack(back_by_shift), slab_shift, axis=0)
+        returned = jnp.concatenate([first_half, second_half], 2)
         return returned.transpose(1, 0, 2).reshape(tok_rows, head_groups * local_heads * head_size)
-    slab_shift = (me - jnp.arange(head_groups, dtype=jnp.int32)) % head_groups
     query_group = jnp.take(received, slab_shift, axis=0)
     key_local = key_group.reshape(group_rows, local_kv * head_size)
     value_local = value_group.reshape(group_rows, local_kv * head_size)

time: 134 us -> 136 us (1.015)
  blocking collectives: 31.8 us -> 0 us
  starting transfers between devices: 16.9 us -> 31.1 us
  waiting for transfers between devices: 15.9 us -> 30 us
  local copies, waits for them, and re-layouts: 30.8 us -> 34.3 us
  other arithmetic: 0.64 us -> 2.3 us
    all_to_all x1 -> x0, blocking collectives: 31.8 us -> none  [per_device(): lax.all_to_all(merged, heads_axes, split_axis=0, concat_axis=0, tiled=True)]
    ppermute x7 -> x14, waiting for transfers between devices: 15.9 us -> 30 us  [per_device(): lax.ppermute(sent, heads_axes, [(i, (i + shift) % head_groups) for i in r...]
    ppermute x7 -> x14, starting transfers between devices: 9.58 us -> 19.5 us  [per_device(): lax.ppermute(sent, heads_axes, [(i, (i + shift) % head_groups) for i in r...]
    all_to_all x0 -> x1, starting transfers between devices: none -> 4.24 us  [per_device(): lax.all_to_all(merged[:, :, :half], heads_axes, split_axis=0, concat_axis...]
    slice x0 -> x1, local copies, waits for them, and re-layouts: none -> 2.7 us  [per_device(): merged[:, :, :half]]
    unnamed x0 -> x1, other arithmetic: none -> 1.48 us
    unnamed x16 -> x22, local copies, waits for them, and re-layouts: 17.2 us -> 17.2 us
  transfers between devices with their start and end apart: 8 -> 16, of which waited for: 3 -> 6; matrix products, arithmetic and copies ran while one was open for 19% -> 19% of each run, Pallas kernels for 0% -> 0%
where the time goes in v14:
time: 136 us; the launch traced here: 135 us
  Pallas kernels  36.5 us (27%)
  local copies, waits for them, and re-layouts  34.3 us (25%)
  starting transfers between devices  31.1 us (23%)
  waiting for transfers between devices  30 us (22%)
  other arithmetic  2.3 us (2%)
    pallas_call x1, Pallas kernels, attend_full(): pl.pallas_call(full_kernel(local_heads, group_blocks, slab_rows, group_ro...  36.5 us
    ppermute x14, waiting for transfers between devices, per_device(): lax.ppermute(sent, heads_axes, [(i, (i + shift) % head_groups) for i in r...  30 us
    ppermute x14, starting transfers between devices, per_device(): lax.ppermute(sent, heads_axes, [(i, (i + shift) % head_groups) for i in r...  19.5 us
    unnamed x22, local copies, waits for them, and re-layouts  17.2 us
    dynamic_slice x8, local copies, waits for them, and re-layouts, per_device(): lax.dynamic_index_in_dim(query_split, (me + shift) % head_groups, 1, keep...  9.15 us
    all_to_all x1, starting transfers between devices, per_device(): lax.all_to_all(spread, ('outer',) + heads_axes, split_axis=0, concat_axis...  7.3 us
    all_to_all x1, starting transfers between devices, per_device(): lax.all_to_all(merged[:, :, :half], heads_axes, split_axis=0, concat_axis...  4.24 us
  transfers between devices with their start and end apart: 16, of which 6 were waited for; matrix products, arithmetic and copies ran while one was open for 19% of the time, Pallas kernels for 0%

profile of v14, /device:TPU:0, one launch (start us, length us, event | category | flops | bytes accessed | tf_op | source)
XLA Modules:
  0.0 134.5 jit_solution(1299979332382981774)
XLA Ops:
  3.8 7.3 %all-to-all-start = ((bf16[32,128,256]{2,1,0:T(8,128)(2,1)}), bf16[32,128,256]{2,1,0:T(8,128)(2,1)S(1)}, u32[]{:S(2)}, u32[]{:S(2)}) async-start(bf16[32,128,256]{2,1,0:T(8,128)(2,1)} %bitcast.72), calls=%async_computation | async-start | bytes 4194304 | tf_op jit(solution)/shard_map/all_to_all | solution.py:187
  11.2 4.1 %copy.16 = bf16[128,8192]{0,1:T(8,128)(2,1)} copy(bf16[128,8192]{1,0:T(8,128)(2,1)} %param.5) | data formatting | bytes 4194304 | tf_op args[0]
  15.2 2.5 %constant_dynamic-slice_fusion = (bf16[128,1,1024]{0,2,1:T(8,128)(2,1)S(1)}, bf16[128,1,1024]{0,2,1:T(8,128)(2,1)S(1)}, bf16[128,1,1024]{0,2,1:T(8,128)(2,1)S(1)...) fusion(bf16[128,8,1024]{0,2,1:T(8,128)(2,1)} %bitcast.73, ...), kind=kLoop, calls=%fused_computation.27 | loop fusion | bytes 4194336 | tf_op jit(solution)/shard_map/jit(dynamic_index_in_dim)/dynamic_slice | solution.py:197
  17.7 1.8 %copy.18 = bf16[128,1,1024]{2,0,1:T(8,128)(2,1)} copy(bf16[128,1,1024]{0,2,1:T(8,128)(2,1)} %get-tuple-element.13) | data formatting | bytes 524288 | tf_op jit(solution)/shard_map/jit(dynamic_index_in_dim)/dynamic_slice | solution.py:197
  19.8 1.8 %copy.19 = bf16[128,1,1024]{2,0,1:T(8,128)(2,1)} copy(bf16[128,1,1024]{0,2,1:T(8,128)(2,1)} %get-tuple-element.12) | data formatting | bytes 524288 | tf_op jit(solution)/shard_map/jit(dynamic_index_in_dim)/dynamic_slice | solution.py:197
  21.6 1.7 %collective-permute-start.1 = (bf16[128,1024]{1,0:T(8,128)(2,1)}, bf16[128,1024]{1,0:T(8,128)(2,1)}, u32[]{:S(2)}, u32[]{:S(2)}) collective-permute-start(bf16[128,1024]{1,0:T(8,128)(2,1)} %bitcast.83), channel_id=1, source_target_pairs={{0,2},{1,3},{2,4},{3,5},{4,6},{5,7},{6,0},{7,1},{8,10},{9,11},{10,... | collective-permute-start | bytes 786440 | tf_op jit(solution)/shard_map/ppermute | solution.py:199
  23.2 1.8 %copy.20 = bf16[128,1,1024]{2,0,1:T(8,128)(2,1)} copy(bf16[128,1,1024]{0,2,1:T(8,128)(2,1)} %get-tuple-element.11) | data formatting | bytes 524288 | tf_op jit(solution)/shard_map/jit(dynamic_index_in_dim)/dynamic_slice | solution.py:197
  25.0 2.2 %collective-permute-start.2 = (bf16[128,1024]{1,0:T(8,128)(2,1)}, bf16[128,1024]{1,0:T(8,128)(2,1)}, u32[]{:S(2)}, u32[]{:S(2)}) collective-permute-start(bf16[128,1024]{1,0:T(8,128)(2,1)} %bitcast.82), channel_id=1, source_target_pairs={{0,3},{1,4},{2,5},{3,6},{4,7},{5,0},{6,1},{7,2},{8,11},{9,12},{10,... | collective-permute-start | bytes 786440 | tf_op jit(solution)/shard_map/ppermute | solution.py:199
  31.2 8.5 %collective-permute-done = bf16[128,1024]{1,0:T(8,128)(2,1)} collective-permute-done((bf16[128,1024]{1,0:T(8,128)(2,1)}, bf16[128,1024]{1,0:T(8,128)(2,1)}, u32[]{:S(2)}, u32[]{:S(2)}) %collective-permute-start) | collective-permute-done | bytes 262176 | tf_op jit(solution)/shard_map/ppermute | solution.py:199
  39.7 1.7 %bitcast_dynamic-update-slice_fusion.6 = bf16[8,128,1024]{2,1,0:T(8,128)(2,1)} fusion(bf16[8,128,1024]{2,1,0:T(8,128)(2,1)} %bitcast_dynamic-update-slice_fusion.7, bf16[128,1024]{1,0:T(8,128)(2,1)} %collective-permute-done), kind=kLoop, calls=%fused_computation.10 | loop fusion | bytes 524288
  41.3 4.7 %collective-permute-start.6 = (bf16[128,1024]{1,0:T(8,128)(2,1)S(1)}, bf16[128,1024]{1,0:T(8,128)(2,1)S(1)}, u32[]{:S(2)}, u32[]{:S(2)}) collective-permute-start(bf16[128,1024]{1,0:T(8,128)(2,1)S(1)} %bitcast.85), channel_id=1, source_target_pairs={{0,7},{1,0},{2,1},{3,2},{4,3},{5,4},{6,5},{7,6},{8,15},{9,8},{10,9... | collective-permute-start | bytes 786440 | tf_op jit(solution)/shard_map/ppermute | solution.py:199
  46.0 1.7 %bitcast_dynamic-update-slice_fusion.5 = bf16[8,128,1024]{2,1,0:T(8,128)(2,1)} fusion(bf16[8,128,1024]{2,1,0:T(8,128)(2,1)} %bitcast_dynamic-update-slice_fusion.6, bf16[128,1024]{1,0:T(8,128)(2,1)} %collective-permute-done.1), kind=kLoop, calls=%fused_computation.9 | loop fusion | bytes 524288
  47.7 5.7 %collective-permute-done.2 = bf16[128,1024]{1,0:T(8,128)(2,1)} collective-permute-done((bf16[128,1024]{1,0:T(8,128)(2,1)}, bf16[128,1024]{1,0:T(8,128)(2,1)}, u32[]{:S(2)}, u32[]{:S(2)}) %collective-permute-start.2) | collective-permute-done | bytes 262176 | tf_op jit(solution)/shard_map/ppermute | solution.py:199
  53.4 1.7 %bitcast_dynamic-update-slice_fusion.4 = bf16[8,128,1024]{2,1,0:T(8,128)(2,1)} fusion(bf16[8,128,1024]{2,1,0:T(8,128)(2,1)} %bitcast_dynamic-update-slice_fusion.5, bf16[128,1024]{1,0:T(8,128)(2,1)} %collective-permute-done.2), kind=kLoop, calls=%fused_computation.8 | loop fusion | bytes 524288
  55.1 1.7 %bitcast_dynamic-update-slice_fusion.3 = bf16[8,128,1024]{2,1,0:T(8,128)(2,1)} fusion(bf16[8,128,1024]{2,1,0:T(8,128)(2,1)} %bitcast_dynamic-update-slice_fusion.4, bf16[128,1024]{1,0:T(8,128)(2,1)} %collective-permute-done.3), kind=kLoop, calls=%fused_computation.7 | loop fusion | bytes 524288
  56.8 1.7 %collective-permute-done.4 = bf16[128,1024]{1,0:T(8,128)(2,1)} collective-permute-done((bf16[128,1024]{1,0:T(8,128)(2,1)S(1)}, bf16[128,1024]{1,0:T(8,128)(2,1)}, u32[]{:S(2)}, u32[]{:S(2)}) %collective-permute-start.4) | collective-permute-done | bytes 262176 | tf_op jit(solution)/shard_map/ppermute | solution.py:199
  58.5 1.7 %bitcast_dynamic-update-slice_fusion.2 = bf16[8,128,1024]{2,1,0:T(8,128)(2,1)} fusion(bf16[8,128,1024]{2,1,0:T(8,128)(2,1)} %bitcast_dynamic-update-slice_fusion.3, bf16[128,1024]{1,0:T(8,128)(2,1)} %collective-permute-done.4), kind=kLoop, calls=%fused_computation.6 | loop fusion | bytes 524288
  63.0 36.5 %shard_map.55 = bf16[1024,1024]{1,0:T(8,128)(2,1)} custom-call(s32[50]{0:T(128)} %pad_add_fusion.meta_ref, bf16[1024,1024]{1,0:T(8,128)(2,1)} %bitcast.75, bf16[4096,256]{1,0:T(8,128)(2,1)} %bitcast.70, bf16[4096,256]{1,0:T(8,128)(2,1)} %bitcast.71), custom_call_target="tpu_custom_call" | custom-call | tf_op jit(solution)/shard_map/pallas_call | solution.py:136
  99.5 2.7 %fusion.3 = (bf16[8,128,512]{2,1,0:T(8,128)(2,1)}, bf16[8,128,512]{2,1,0:T(8,128)(2,1)S(1)}) fusion(bf16[8,128,1024]{2,1,0:T(8,128)(2,1)} %bitcast.74), kind=kLoop, calls=%fused_computation.51 | loop fusion | bytes 4194304 | tf_op jit(solution)/shard_map/slice | solution.py:227
  102.3 4.0 %collective-permute-start.7 = (bf16[128,512]{1,0:T(8,128)(2,1)S(1)}, bf16[128,512]{1,0:T(8,128)(2,1)S(1)}, u32[]{:S(2)}, u32[]{:S(2)}) collective-permute-start(bf16[128,512]{1,0:T(8,128)(2,1)S(1)} %get-tuple-element.21), channel_id=1, source_target_pairs={{0,1},{1,2},{2,3},{3,4},{4,5},{5,6},{6,7},{7,0},{8,9},{9,10},{10,1... | collective-permute-start | bytes 393224 | tf_op jit(solution)/shard_map/ppermute | solution.py:232
  107.4 1.8 %collective-permute-start.10 = (bf16[128,512]{1,0:T(8,128)(2,1)S(1)}, bf16[128,512]{1,0:T(8,128)(2,1)S(1)}, u32[]{:S(2)}, u32[]{:S(2)}) collective-permute-start(bf16[128,512]{1,0:T(8,128)(2,1)S(1)} %get-tuple-element.18), channel_id=1, source_target_pairs={{0,4},{1,5},{2,6},{3,7},{4,0},{5,1},{6,2},{7,3},{8,12},{9,13},{10,... | collective-permute-start | bytes 393224 | tf_op jit(solution)/shard_map/ppermute | solution.py:232
  109.2 4.2 %all-to-all-start.1 = ((bf16[8,128,512]{2,1,0:T(8,128)(2,1)}), bf16[8,128,512]{2,1,0:T(8,128)(2,1)}, u32[]{:S(2)}, u32[]{:S(2)}) async-start(bf16[8,128,512]{2,1,0:T(8,128)(2,1)} %get-tuple-element.5), calls=%async_computation.1 | async-start | bytes 2097152 | tf_op jit(solution)/shard_map/all_to_all | solution.py:227
  113.4 2.8 %collective-permute-start.12 = (bf16[128,512]{1,0:T(8,128)(2,1)S(1)}, bf16[128,512]{1,0:T(8,128)(2,1)S(1)}, u32[]{:S(2)}, u32[]{:S(2)}) collective-permute-start(bf16[128,512]{1,0:T(8,128)(2,1)S(1)} %get-tuple-element.16), channel_id=1, source_target_pairs={{0,6},{1,7},{2,0},{3,1},{4,2},{5,3},{6,4},{7,5},{8,14},{9,15},{10,... | collective-permute-start | bytes 393224 | tf_op jit(solution)/shard_map/ppermute | solution.py:232
  117.5 13.1 %collective-permute-done.12 = bf16[128,512]{1,0:T(8,128)(2,1)S(1)} collective-permute-done((bf16[128,512]{1,0:T(8,128)(2,1)S(1)}, bf16[128,512]{1,0:T(8,128)(2,1)S(1)}, u32[]{:S(2)}, u32[]{:S(2)}) %collective-permute-start.12) | collective-permute-done | bytes 131104 | tf_op jit(solution)/shard_map/ppermute | solution.py:232
  (60 shorter events, 16.9 us)
Async XLA Ops:
  3.8 57.9 %all-to-all-start = ((bf16[32,128,256]{2,1,0:T(8,128)(2,1)}), bf16[32,128,256]{2,1,0:T(8,128)(2,1)S(1)}, u32[]{:S(2)}, u32[]{:S(2)}) async-start(bf16[32,128,256]{2,1,0:T(8,128)(2,1)} %bitcast.72), calls=%async_computation | async-start | bytes 4194304 | tf_op jit(solution)/shard_map/all_to_all | solution.py:187
  17.7 12.2 %copy-start.1 = (s32[64,3]{0,1:T(4,128)S(1)}, s32[64,3]{0,1:T(4,128)}, u32[]{:S(2)}) copy-start(s32[64,3]{0,1:T(4,128)} %param.8) | copy-start | bytes 2308
  17.7 12.2 %copy-start.2 = (s32[64,3]{0,1:T(4,128)S(1)}, s32[64,3]{0,1:T(4,128)}, u32[]{:S(2)}) copy-start(s32[64,3]{0,1:T(4,128)} %param.9) | copy-start | bytes 2308
  19.5 20.1 %collective-permute-start = (bf16[128,1024]{1,0:T(8,128)(2,1)}, bf16[128,1024]{1,0:T(8,128)(2,1)}, u32[]{:S(2)}, u32[]{:S(2)}) collective-permute-start(bf16[128,1024]{1,0:T(8,128)(2,1)} %bitcast.84), channel_id=1, source_target_pairs={{0,1},{1,2},{2,3},{3,4},{4,5},{5,6},{6,7},{7,0},{8,9},{9,10},{10,1... | collective-permute-start | bytes 786440 | tf_op jit(solution)/shard_map/ppermute | solution.py:199
  21.6 19.7 %collective-permute-start.1 = (bf16[128,1024]{1,0:T(8,128)(2,1)}, bf16[128,1024]{1,0:T(8,128)(2,1)}, u32[]{:S(2)}, u32[]{:S(2)}) collective-permute-start(bf16[128,1024]{1,0:T(8,128)(2,1)} %bitcast.83), channel_id=1, source_target_pairs={{0,2},{1,3},{2,4},{3,5},{4,6},{5,7},{6,0},{7,1},{8,10},{9,11},{10,... | collective-permute-start | bytes 786440 | tf_op jit(solution)/shard_map/ppermute | solution.py:199
  25.0 28.4 %collective-permute-start.2 = (bf16[128,1024]{1,0:T(8,128)(2,1)}, bf16[128,1024]{1,0:T(8,128)(2,1)}, u32[]{:S(2)}, u32[]{:S(2)}) collective-permute-start(bf16[128,1024]{1,0:T(8,128)(2,1)} %bitcast.82), channel_id=1, source_target_pairs={{0,3},{1,4},{2,5},{3,6},{4,7},{5,0},{6,1},{7,2},{8,11},{9,12},{10,... | collective-permute-start | bytes 786440 | tf_op jit(solution)/shard_map/ppermute | solution.py:199
  28.1 27.0 %collective-permute-start.3 = (bf16[128,1024]{1,0:T(8,128)(2,1)}, bf16[128,1024]{1,0:T(8,128)(2,1)}, u32[]{:S(2)}, u32[]{:S(2)}) collective-permute-start(bf16[128,1024]{1,0:T(8,128)(2,1)} %bitcast.81), channel_id=1, source_target_pairs={{0,4},{1,5},{2,6},{3,7},{4,0},{5,1},{6,2},{7,3},{8,12},{9,13},{10,... | collective-permute-start | bytes 786440 | tf_op jit(solution)/shard_map/ppermute | solution.py:199
  28.8 29.7 %collective-permute-start.4 = (bf16[128,1024]{1,0:T(8,128)(2,1)S(1)}, bf16[128,1024]{1,0:T(8,128)(2,1)}, u32[]{:S(2)}, u32[]{:S(2)}) collective-permute-start(bf16[128,1024]{1,0:T(8,128)(2,1)S(1)} %bitcast.80), channel_id=1, source_target_pairs={{0,5},{1,6},{2,7},{3,0},{4,1},{5,2},{6,3},{7,4},{8,13},{9,14},{10,... | collective-permute-start | bytes 786440 | tf_op jit(solution)/shard_map/ppermute | solution.py:199
  39.7 20.5 %collective-permute-start.5 = (bf16[128,1024]{1,0:T(8,128)(2,1)S(1)}, bf16[128,1024]{1,0:T(8,128)(2,1)S(1)}, u32[]{:S(2)}, u32[]{:S(2)}) collective-permute-start(bf16[128,1024]{1,0:T(8,128)(2,1)S(1)} %bitcast.86), channel_id=1, source_target_pairs={{0,6},{1,7},{2,0},{3,1},{4,2},{5,3},{6,4},{7,5},{8,14},{9,15},{10,... | collective-permute-start | bytes 786440 | tf_op jit(solution)/shard_map/ppermute | solution.py:199
  41.3 19.6 %collective-permute-start.6 = (bf16[128,1024]{1,0:T(8,128)(2,1)S(1)}, bf16[128,1024]{1,0:T(8,128)(2,1)S(1)}, u32[]{:S(2)}, u32[]{:S(2)}) collective-permute-start(bf16[128,1024]{1,0:T(8,128)(2,1)S(1)} %bitcast.85), channel_id=1, source_target_pairs={{0,7},{1,0},{2,1},{3,2},{4,3},{5,4},{6,5},{7,6},{8,15},{9,8},{10,9... | collective-permute-start | bytes 786440 | tf_op jit(solution)/shard_map/ppermute | solution.py:199
  61.6 1.3 copy-start
  102.3 11.1 %collective-permute-start.7 = (bf16[128,512]{1,0:T(8,128)(2,1)S(1)}, bf16[128,512]{1,0:T(8,128)(2,1)S(1)}, u32[]{:S(2)}, u32[]{:S(2)}) collective-permute-start(bf16[128,512]{1,0:T(8,128)(2,1)S(1)} %get-tuple-element.21), channel_id=1, source_target_pairs={{0,1},{1,2},{2,3},{3,4},{4,5},{5,6},{6,7},{7,0},{8,9},{9,10},{10,1... | collective-permute-start | bytes 393224 | tf_op jit(solution)/shard_map/ppermute | solution.py:232
  106.3 10.0 %collective-permute-start.8 = (bf16[128,512]{1,0:T(8,128)(2,1)S(1)}, bf16[128,512]{1,0:T(8,128)(2,1)S(1)}, u32[]{:S(2)}, u32[]{:S(2)}) collective-permute-start(bf16[128,512]{1,0:T(8,128)(2,1)S(1)} %get-tuple-element.20), channel_id=1, source_target_pairs={{0,2},{1,3},{2,4},{3,5},{4,6},{5,7},{6,0},{7,1},{8,10},{9,11},{10,... | collective-permute-start | bytes 393224 | tf_op jit(solution)/shard_map/ppermute | solution.py:232
  106.3 10.2 %collective-permute-start.9 = (bf16[128,512]{1,0:T(8,128)(2,1)S(1)}, bf16[128,512]{1,0:T(8,128)(2,1)S(1)}, u32[]{:S(2)}, u32[]{:S(2)}) collective-permute-start(bf16[128,512]{1,0:T(8,128)(2,1)S(1)} %get-tuple-element.19), channel_id=1, source_target_pairs={{0,3},{1,4},{2,5},{3,6},{4,7},{5,0},{6,1},{7,2},{8,11},{9,12},{10,... | collective-permute-start | bytes 393224 | tf_op jit(solution)/shard_map/ppermute | solution.py:232
  107.4 9.7 %collective-permute-start.10 = (bf16[128,512]{1,0:T(8,128)(2,1)S(1)}, bf16[128,512]{1,0:T(8,128)(2,1)S(1)}, u32[]{:S(2)}, u32[]{:S(2)}) collective-permute-start(bf16[128,512]{1,0:T(8,128)(2,1)S(1)} %get-tuple-element.18), channel_id=1, source_target_pairs={{0,4},{1,5},{2,6},{3,7},{4,0},{5,1},{6,2},{7,3},{8,12},{9,13},{10,... | collective-permute-start | bytes 393224 | tf_op jit(solution)/shard_map/ppermute | solution.py:232
  109.2 8.3 %collective-permute-start.11 = (bf16[128,512]{1,0:T(8,128)(2,1)S(1)}, bf16[128,512]{1,0:T(8,128)(2,1)S(1)}, u32[]{:S(2)}, u32[]{:S(2)}) collective-permute-start(bf16[128,512]{1,0:T(8,128)(2,1)S(1)} %get-tuple-element.17), channel_id=1, source_target_pairs={{0,5},{1,6},{2,7},{3,0},{4,1},{5,2},{6,3},{7,4},{8,13},{9,14},{10,... | collective-permute-start | bytes 393224 | tf_op jit(solution)/shard_map/ppermute | solution.py:232
  109.2 22.3 %all-to-all-start.1 = ((bf16[8,128,512]{2,1,0:T(8,128)(2,1)}), bf16[8,128,512]{2,1,0:T(8,128)(2,1)}, u32[]{:S(2)}, u32[]{:S(2)}) async-start(bf16[8,128,512]{2,1,0:T(8,128)(2,1)} %get-tuple-element.5), calls=%async_computation.1 | async-start | bytes 2097152 | tf_op jit(solution)/shard_map/all_to_all | solution.py:227
  113.4 17.2 %collective-permute-start.12 = (bf16[128,512]{1,0:T(8,128)(2,1)S(1)}, bf16[128,512]{1,0:T(8,128)(2,1)S(1)}, u32[]{:S(2)}, u32[]{:S(2)}) collective-permute-start(bf16[128,512]{1,0:T(8,128)(2,1)S(1)} %get-tuple-element.16), channel_id=1, source_target_pairs={{0,6},{1,7},{2,0},{3,1},{4,2},{5,3},{6,4},{7,5},{8,14},{9,15},{10,... | collective-permute-start | bytes 393224 | tf_op jit(solution)/shard_map/ppermute | solution.py:232
  116.3 14.4 %collective-permute-start.13 = (bf16[128,512]{1,0:T(8,128)(2,1)S(1)}, bf16[128,512]{1,0:T(8,128)(2,1)S(1)}, u32[]{:S(2)}, u32[]{:S(2)}) collective-permute-start(bf16[128,512]{1,0:T(8,128)(2,1)S(1)} %get-tuple-element.15), channel_id=1, source_target_pairs={{0,7},{1,0},{2,1},{3,2},{4,3},{5,4},{6,5},{7,6},{8,15},{9,8},{10,9... | collective-permute-start | bytes 393224 | tf_op jit(solution)/shard_map/ppermute | solution.py:232

commit v15 on v13

--- a/solution.py
+++ b/solution.py
@@ -11,6 +11,7 @@
 VERT_COUNT = 3
 SLASH_REACH = 8
 FULL_GATHER_BYTES = 4 << 20
+OUTPUT_CHUNKS = 2
 
 
 def passed_along(shard, axis, by):
@@ -66,13 +67,13 @@
     return kernel
 
 
-def full_kernel(local_heads, group_blocks, slab_rows, slabs):
+def full_kernel(local_heads, group_blocks, slab_rows, slabs, base):
     block = MASK_BLOCK_SIZE
     key_count = (SLASH_COUNT + VERT_COUNT) * block
     scale = HEAD_DIMENSION ** (-0.5)
 
     def kernel(meta_ref, q_ref, k_ref, v_ref, o_ref):
-        h = pl.program_id(0)
+        h = pl.program_id(0) + base
         first = meta_ref[2 * local_heads * SLASH_COUNT]
         me = meta_ref[2 * local_heads * SLASH_COUNT + 1]
         offs = [meta_ref[h * SLASH_COUNT + j] for j in range(SLASH_COUNT)]
@@ -117,7 +118,7 @@
     return kernel
 
 
-def attend_full(meta, queries, all_kv, local_heads, sharing, slab_rows):
+def attend_full(meta, queries, all_kv, local_heads, sharing, slab_rows, base, chunk_heads):
     group_rows = queries.shape[0]
     group_blocks = group_rows // MASK_BLOCK_SIZE
     head_size = HEAD_DIMENSION
@@ -125,18 +126,18 @@
     value_base = all_kv.shape[1] // (2 * head_size)
     grid_spec = pltpu.PrefetchScalarGridSpec(
         num_scalar_prefetch=1,
-        grid=(local_heads,),
+        grid=(chunk_heads,),
         in_specs=[
-            pl.BlockSpec((group_rows, head_size), lambda h, m: (0, h)),
-            pl.BlockSpec((total_rows, head_size), lambda h, m: (0, h // sharing)),
-            pl.BlockSpec((total_rows, head_size), lambda h, m: (0, value_base + h // sharing)),
+            pl.BlockSpec((group_rows, head_size), lambda h, m: (0, h + base)),
+            pl.BlockSpec((total_rows, head_size), lambda h, m: (0, (h + base) // sharing)),
+            pl.BlockSpec((total_rows, head_size), lambda h, m: (0, value_base + (h + base) // sharing)),
         ],
         out_specs=pl.BlockSpec((group_rows, head_size), lambda h, m: (0, h)),
     )
     return pl.pallas_call(
-        full_kernel(local_heads, group_blocks, slab_rows, group_rows // slab_rows),
+        full_kernel(local_heads, group_blocks, slab_rows, group_rows // slab_rows, base),
         grid_spec=grid_spec,
-        out_shape=jax.ShapeDtypeStruct((group_rows, local_heads * head_size), queries.dtype),
+        out_shape=jax.ShapeDtypeStruct((group_rows, chunk_heads * head_size), queries.dtype),
     )(meta, queries, all_kv, all_kv)
 
 
@@ -217,12 +218,16 @@
     if whole <= FULL_GATHER_BYTES:
         everything = everything.reshape(-1, 2 * local_kv * head_size)
         queries = received.reshape(group_rows, local_heads * head_size)
-        results = attend_full(
-            jnp.concatenate([meta, me.astype(jnp.int32)[None]]), queries, everything,
-            local_heads, group_sharing_factor, tok_rows,
-        )
-        merged = results.reshape(head_groups, tok_rows, local_heads * head_size)
-        returned = lax.all_to_all(merged, heads_axes, split_axis=0, concat_axis=0, tiled=True)
+        chunk_heads = local_heads // OUTPUT_CHUNKS
+        pieces = []
+        for c in range(OUTPUT_CHUNKS):
+            results = attend_full(
+                jnp.concatenate([meta, me.astype(jnp.int32)[None]]), queries, everything,
+                local_heads, group_sharing_factor, tok_rows, c * chunk_heads, chunk_heads,
+            )
+            merged = results.reshape(head_groups, tok_rows, chunk_heads * head_size)
+            pieces.append(lax.all_to_all(merged, heads_axes, split_axis=0, concat_axis=0, tiled=True))
+        returned = jnp.concatenate(pieces, 2)
         return returned.transpose(1, 0, 2).reshape(tok_rows, head_groups * local_heads * head_size)
     slab_shift = (me - jnp.arange(head_groups, dtype=jnp.int32)) % head_groups
     query_group = jnp.take(received, slab_shift, axis=0)

time: 134 us -> 130 us (0.970)
  blocking collectives: 31.8 us -> 19.6 us
  starting transfers between devices: 16.9 us -> 22.1 us
  Pallas kernels: 36.6 us -> 39.6 us
    all_to_all x1, blocking collectives: 31.8 us -> 19.6 us  [per_device(): lax.all_to_all(merged, heads_axes, split_axis=0, concat_axis=0, tiled=True)]
    all_to_all x0 -> x1, starting transfers between devices: none -> 5.19 us  [per_device(): lax.all_to_all(merged, heads_axes, split_axis=0, concat_axis=0, tiled=True)]
    pallas_call x1 -> x2, Pallas kernels: 36.6 us -> 39.6 us  [attend_full(): pl.pallas_call(full_kernel(local_heads, group_blocks, slab_rows, group_ro...]
  transfers between devices with their start and end apart: 8 -> 9, of which waited for: 3 -> 3; matrix products, arithmetic and copies ran while one was open for 19% -> 19% of each run, Pallas kernels for 0% -> 15%
where the time goes in v15:
time: 130 us; the launch traced here: 129 us
  Pallas kernels  39.6 us (30%)
  local copies, waits for them, and re-layouts  30.8 us (24%)
  starting transfers between devices  22.1 us (17%)
  blocking collectives  19.6 us (15%)
  waiting for transfers between devices  15.9 us (12%)
    pallas_call x2, Pallas kernels, attend_full(): pl.pallas_call(full_kernel(local_heads, group_blocks, slab_rows, group_ro...  39.6 us
    all_to_all x1, blocking collectives, per_device(): lax.all_to_all(merged, heads_axes, split_axis=0, concat_axis=0, tiled=True)  19.6 us
    unnamed x16, local copies, waits for them, and re-layouts  17.2 us
    ppermute x7, waiting for transfers between devices, per_device(): lax.ppermute(sent, heads_axes, [(i, (i + shift) % head_groups) for i in r...  15.8 us
    ppermute x7, starting transfers between devices, per_device(): lax.ppermute(sent, heads_axes, [(i, (i + shift) % head_groups) for i in r...  9.58 us
    dynamic_slice x8, local copies, waits for them, and re-layouts, per_device(): lax.dynamic_index_in_dim(query_split, (me + shift) % head_groups, 1, keep...  9.16 us
    all_to_all x1, starting transfers between devices, per_device(): lax.all_to_all(spread, ('outer',) + heads_axes, split_axis=0, concat_axis...  7.3 us
    all_to_all x1, starting transfers between devices, per_device(): lax.all_to_all(merged, heads_axes, split_axis=0, concat_axis=0, tiled=True)  5.19 us
  transfers between devices with their start and end apart: 9, of which 3 were waited for; matrix products, arithmetic and copies ran while one was open for 19% of the time, Pallas kernels for 15%

profile of v15, /device:TPU:0, one launch (start us, length us, event | category | flops | bytes accessed | tf_op | source)
XLA Modules:
  0.0 129.1 jit_solution(15872569839591378389)
XLA Ops:
  2.2 1.6 %broadcast_in_dim.15 = bf16[4,8,128,256]{3,2,1,0:T(8,128)(2,1)} broadcast(bf16[8,128,256]{2,1,0:T(8,128)(2,1)S(1)} %copy.25), dimensions={1,2,3} | broadcast | bytes 2621440 | tf_op jit(solution)/shard_map/broadcast_in_dim | solution.py:185
  3.8 7.3 %all-to-all-start = ((bf16[32,128,256]{2,1,0:T(8,128)(2,1)}), bf16[32,128,256]{2,1,0:T(8,128)(2,1)S(1)}, u32[]{:S(2)}, u32[]{:S(2)}) async-start(bf16[32,128,256]{2,1,0:T(8,128)(2,1)} %bitcast.47), calls=%async_computation | async-start | bytes 4194304 | tf_op jit(solution)/shard_map/all_to_all | solution.py:188
  11.2 4.1 %copy.16 = bf16[128,8192]{0,1:T(8,128)(2,1)} copy(bf16[128,8192]{1,0:T(8,128)(2,1)} %param.5) | data formatting | bytes 4194304 | tf_op args[0]
  15.2 2.4 %constant_dynamic-slice_fusion = (bf16[128,1,1024]{0,2,1:T(8,128)(2,1)S(1)}, bf16[128,1,1024]{0,2,1:T(8,128)(2,1)S(1)}, bf16[128,1,1024]{0,2,1:T(8,128)(2,1)S(1)...) fusion(bf16[128,8,1024]{0,2,1:T(8,128)(2,1)} %bitcast.48, ...), kind=kLoop, calls=%fused_computation.10 | loop fusion | bytes 4194336 | tf_op jit(solution)/shard_map/jit(dynamic_index_in_dim)/dynamic_slice | solution.py:198
  17.7 1.8 %copy.18 = bf16[128,1,1024]{2,0,1:T(8,128)(2,1)} copy(bf16[128,1,1024]{0,2,1:T(8,128)(2,1)} %get-tuple-element.11) | data formatting | bytes 524288 | tf_op jit(solution)/shard_map/jit(dynamic_index_in_dim)/dynamic_slice | solution.py:198
  19.8 1.8 %copy.19 = bf16[128,1,1024]{2,0,1:T(8,128)(2,1)} copy(bf16[128,1,1024]{0,2,1:T(8,128)(2,1)} %get-tuple-element.10) | data formatting | bytes 524288 | tf_op jit(solution)/shard_map/jit(dynamic_index_in_dim)/dynamic_slice | solution.py:198
  21.6 1.7 %collective-permute-start.1 = (bf16[128,1024]{1,0:T(8,128)(2,1)}, bf16[128,1024]{1,0:T(8,128)(2,1)}, u32[]{:S(2)}, u32[]{:S(2)}) collective-permute-start(bf16[128,1024]{1,0:T(8,128)(2,1)} %bitcast.58), channel_id=1, source_target_pairs={{0,2},{1,3},{2,4},{3,5},{4,6},{5,7},{6,0},{7,1},{8,10},{9,11},{10,... | collective-permute-start | bytes 786440 | tf_op jit(solution)/shard_map/ppermute | solution.py:200
  23.2 1.8 %copy.20 = bf16[128,1,1024]{2,0,1:T(8,128)(2,1)} copy(bf16[128,1,1024]{0,2,1:T(8,128)(2,1)} %get-tuple-element.9) | data formatting | bytes 524288 | tf_op jit(solution)/shard_map/jit(dynamic_index_in_dim)/dynamic_slice | solution.py:198
  25.0 2.2 %collective-permute-start.2 = (bf16[128,1024]{1,0:T(8,128)(2,1)}, bf16[128,1024]{1,0:T(8,128)(2,1)}, u32[]{:S(2)}, u32[]{:S(2)}) collective-permute-start(bf16[128,1024]{1,0:T(8,128)(2,1)} %bitcast.57), channel_id=1, source_target_pairs={{0,3},{1,4},{2,5},{3,6},{4,7},{5,0},{6,1},{7,2},{8,11},{9,12},{10,... | collective-permute-start | bytes 786440 | tf_op jit(solution)/shard_map/ppermute | solution.py:200
  31.3 8.4 %collective-permute-done = bf16[128,1024]{1,0:T(8,128)(2,1)} collective-permute-done((bf16[128,1024]{1,0:T(8,128)(2,1)}, bf16[128,1024]{1,0:T(8,128)(2,1)}, u32[]{:S(2)}, u32[]{:S(2)}) %collective-permute-start) | collective-permute-done | bytes 262176 | tf_op jit(solution)/shard_map/ppermute | solution.py:200
  39.7 1.7 %bitcast_dynamic-update-slice_fusion.6 = bf16[8,128,1024]{2,1,0:T(8,128)(2,1)} fusion(bf16[8,128,1024]{2,1,0:T(8,128)(2,1)} %bitcast_dynamic-update-slice_fusion.7, bf16[128,1024]{1,0:T(8,128)(2,1)} %collective-permute-done), kind=kLoop, calls=%fused_computation.8 | loop fusion | bytes 524288
  41.3 4.7 %collective-permute-start.6 = (bf16[128,1024]{1,0:T(8,128)(2,1)S(1)}, bf16[128,1024]{1,0:T(8,128)(2,1)S(1)}, u32[]{:S(2)}, u32[]{:S(2)}) collective-permute-start(bf16[128,1024]{1,0:T(8,128)(2,1)S(1)} %bitcast.60), channel_id=1, source_target_pairs={{0,7},{1,0},{2,1},{3,2},{4,3},{5,4},{6,5},{7,6},{8,15},{9,8},{10,9... | collective-permute-start | bytes 786440 | tf_op jit(solution)/shard_map/ppermute | solution.py:200
  46.0 1.7 %bitcast_dynamic-update-slice_fusion.5 = bf16[8,128,1024]{2,1,0:T(8,128)(2,1)} fusion(bf16[8,128,1024]{2,1,0:T(8,128)(2,1)} %bitcast_dynamic-update-slice_fusion.6, bf16[128,1024]{1,0:T(8,128)(2,1)} %collective-permute-done.1), kind=kLoop, calls=%fused_computation.7 | loop fusion | bytes 524288
  47.7 5.7 %collective-permute-done.2 = bf16[128,1024]{1,0:T(8,128)(2,1)} collective-permute-done((bf16[128,1024]{1,0:T(8,128)(2,1)}, bf16[128,1024]{1,0:T(8,128)(2,1)}, u32[]{:S(2)}, u32[]{:S(2)}) %collective-permute-start.2) | collective-permute-done | bytes 262176 | tf_op jit(solution)/shard_map/ppermute | solution.py:200
  53.4 1.7 %bitcast_dynamic-update-slice_fusion.4 = bf16[8,128,1024]{2,1,0:T(8,128)(2,1)} fusion(bf16[8,128,1024]{2,1,0:T(8,128)(2,1)} %bitcast_dynamic-update-slice_fusion.5, bf16[128,1024]{1,0:T(8,128)(2,1)} %collective-permute-done.2), kind=kLoop, calls=%fused_computation.6 | loop fusion | bytes 524288
  55.1 1.7 %bitcast_dynamic-update-slice_fusion.3 = bf16[8,128,1024]{2,1,0:T(8,128)(2,1)} fusion(bf16[8,128,1024]{2,1,0:T(8,128)(2,1)} %bitcast_dynamic-update-slice_fusion.4, bf16[128,1024]{1,0:T(8,128)(2,1)} %collective-permute-done.3), kind=kLoop, calls=%fused_computation.5 | loop fusion | bytes 524288
  56.8 1.7 %collective-permute-done.4 = bf16[128,1024]{1,0:T(8,128)(2,1)} collective-permute-done((bf16[128,1024]{1,0:T(8,128)(2,1)S(1)}, bf16[128,1024]{1,0:T(8,128)(2,1)}, u32[]{:S(2)}, u32[]{:S(2)}) %collective-permute-start.4) | collective-permute-done | bytes 262176 | tf_op jit(solution)/shard_map/ppermute | solution.py:200
  58.5 1.7 %bitcast_dynamic-update-slice_fusion.2 = bf16[8,128,1024]{2,1,0:T(8,128)(2,1)} fusion(bf16[8,128,1024]{2,1,0:T(8,128)(2,1)} %bitcast_dynamic-update-slice_fusion.3, bf16[128,1024]{1,0:T(8,128)(2,1)} %collective-permute-done.4), kind=kLoop, calls=%fused_computation.4 | loop fusion | bytes 524288
  61.6 1.3 %copy-done = bf16[32,128,256]{2,1,0:T(8,128)(2,1)} copy-done((bf16[32,128,256]{2,1,0:T(8,128)(2,1)}, bf16[32,128,256]{2,1,0:T(8,128)(2,1)S(1)}, u32[]{:S(2)}) %copy-start) | copy-done | bytes 2097176
  63.0 19.8 %shard_map.55 = bf16[1024,512]{1,0:T(8,128)(2,1)} custom-call(s32[50]{0:T(128)} %pad_add_fusion.meta_ref, bf16[1024,1024]{1,0:T(8,128)(2,1)} %bitcast.45, bf16[4096,256]{1,0:T(8,128)(2,1)} %bitcast.41, bf16[4096,256]{1,0:T(8,128)(2,1)} %bitcast.42), custom_call_target="tpu_custom_call" | custom-call | tf_op jit(solution)/shard_map/pallas_call | solution.py:137
  82.7 5.2 %all-to-all-start.1 = ((bf16[8,128,512]{2,1,0:T(8,128)(2,1)}), bf16[8,128,512]{2,1,0:T(8,128)(2,1)S(1)}, u32[]{:S(2)}, u32[]{:S(2)}) async-start(bf16[8,128,512]{2,1,0:T(8,128)(2,1)} %bitcast.49), calls=%async_computation.1 | async-start | bytes 2097152 | tf_op jit(solution)/shard_map/all_to_all | solution.py:229
  87.9 19.8 %shard_map.56 = bf16[1024,512]{1,0:T(8,128)(2,1)} custom-call(s32[50]{0:T(128)} %pad_add_fusion.meta_ref, bf16[1024,1024]{1,0:T(8,128)(2,1)} %bitcast.46, bf16[4096,256]{1,0:T(8,128)(2,1)} %bitcast.43, bf16[4096,256]{1,0:T(8,128)(2,1)} %bitcast.44), custom_call_target="tpu_custom_call" | custom-call | tf_op jit(solution)/shard_map/pallas_call | solution.py:137
  107.7 19.6 %all_to_all.15 = bf16[8,128,512]{2,1,0:T(8,128)(2,1)S(1)} all-to-all(bf16[8,128,512]{2,1,0:T(8,128)(2,1)} %bitcast.50), channel_id=1, replica_groups=mesh['outer'=4,'inner'=2,'grp'=4] {'inner','grp'}, dimensions={0} | all-to-all | bytes 2097152 | tf_op jit(solution)/shard_map/all_to_all | solution.py:229
  127.6 1.5 %copy.27 = bf16[8,16,8,1024]{3,2,0,1:T(8,128)(2,1)} copy(bf16[8,16,8,1024]{3,2,1,0:T(8,128)(2,1)S(1)} %maximum_bitcast_fusion) | data formatting | bytes 4194304 | tf_op jit(solution)/shard_map/reshape | solution.py:231
  (34 shorter events, 8.1 us)
Async XLA Ops:
  3.8 57.9 %all-to-all-start = ((bf16[32,128,256]{2,1,0:T(8,128)(2,1)}), bf16[32,128,256]{2,1,0:T(8,128)(2,1)S(1)}, u32[]{:S(2)}, u32[]{:S(2)}) async-start(bf16[32,128,256]{2,1,0:T(8,128)(2,1)} %bitcast.47), calls=%async_computation | async-start | bytes 4194304 | tf_op jit(solution)/shard_map/all_to_all | solution.py:188
  17.7 11.5 %copy-start.1 = (s32[64,3]{0,1:T(4,128)S(1)}, s32[64,3]{0,1:T(4,128)}, u32[]{:S(2)}) copy-start(s32[64,3]{0,1:T(4,128)} %param.8) | copy-start | bytes 2308
  17.7 11.5 %copy-start.2 = (s32[64,3]{0,1:T(4,128)S(1)}, s32[64,3]{0,1:T(4,128)}, u32[]{:S(2)}) copy-start(s32[64,3]{0,1:T(4,128)} %param.9) | copy-start | bytes 2308
  19.5 20.1 %collective-permute-start = (bf16[128,1024]{1,0:T(8,128)(2,1)}, bf16[128,1024]{1,0:T(8,128)(2,1)}, u32[]{:S(2)}, u32[]{:S(2)}) collective-permute-start(bf16[128,1024]{1,0:T(8,128)(2,1)} %bitcast.59), channel_id=1, source_target_pairs={{0,1},{1,2},{2,3},{3,4},{4,5},{5,6},{6,7},{7,0},{8,9},{9,10},{10,1... | collective-permute-start | bytes 786440 | tf_op jit(solution)/shard_map/ppermute | solution.py:200
  21.6 19.8 %collective-permute-start.1 = (bf16[128,1024]{1,0:T(8,128)(2,1)}, bf16[128,1024]{1,0:T(8,128)(2,1)}, u32[]{:S(2)}, u32[]{:S(2)}) collective-permute-start(bf16[128,1024]{1,0:T(8,128)(2,1)} %bitcast.58), channel_id=1, source_target_pairs={{0,2},{1,3},{2,4},{3,5},{4,6},{5,7},{6,0},{7,1},{8,10},{9,11},{10,... | collective-permute-start | bytes 786440 | tf_op jit(solution)/shard_map/ppermute | solution.py:200
  25.0 28.4 %collective-permute-start.2 = (bf16[128,1024]{1,0:T(8,128)(2,1)}, bf16[128,1024]{1,0:T(8,128)(2,1)}, u32[]{:S(2)}, u32[]{:S(2)}) collective-permute-start(bf16[128,1024]{1,0:T(8,128)(2,1)} %bitcast.57), channel_id=1, source_target_pairs={{0,3},{1,4},{2,5},{3,6},{4,7},{5,0},{6,1},{7,2},{8,11},{9,12},{10,... | collective-permute-start | bytes 786440 | tf_op jit(solution)/shard_map/ppermute | solution.py:200
  28.1 27.0 %collective-permute-start.3 = (bf16[128,1024]{1,0:T(8,128)(2,1)}, bf16[128,1024]{1,0:T(8,128)(2,1)}, u32[]{:S(2)}, u32[]{:S(2)}) collective-permute-start(bf16[128,1024]{1,0:T(8,128)(2,1)} %bitcast.56), channel_id=1, source_target_pairs={{0,4},{1,5},{2,6},{3,7},{4,0},{5,1},{6,2},{7,3},{8,12},{9,13},{10,... | collective-permute-start | bytes 786440 | tf_op jit(solution)/shard_map/ppermute | solution.py:200
  28.8 29.7 %collective-permute-start.4 = (bf16[128,1024]{1,0:T(8,128)(2,1)S(1)}, bf16[128,1024]{1,0:T(8,128)(2,1)}, u32[]{:S(2)}, u32[]{:S(2)}) collective-permute-start(bf16[128,1024]{1,0:T(8,128)(2,1)S(1)} %bitcast.55), channel_id=1, source_target_pairs={{0,5},{1,6},{2,7},{3,0},{4,1},{5,2},{6,3},{7,4},{8,13},{9,14},{10,... | collective-permute-start | bytes 786440 | tf_op jit(solution)/shard_map/ppermute | solution.py:200
  39.6 20.5 %collective-permute-start.5 = (bf16[128,1024]{1,0:T(8,128)(2,1)S(1)}, bf16[128,1024]{1,0:T(8,128)(2,1)S(1)}, u32[]{:S(2)}, u32[]{:S(2)}) collective-permute-start(bf16[128,1024]{1,0:T(8,128)(2,1)S(1)} %bitcast.61), channel_id=1, source_target_pairs={{0,6},{1,7},{2,0},{3,1},{4,2},{5,3},{6,4},{7,5},{8,14},{9,15},{10,... | collective-permute-start | bytes 786440 | tf_op jit(solution)/shard_map/ppermute | solution.py:200
  41.3 19.6 %collective-permute-start.6 = (bf16[128,1024]{1,0:T(8,128)(2,1)S(1)}, bf16[128,1024]{1,0:T(8,128)(2,1)S(1)}, u32[]{:S(2)}, u32[]{:S(2)}) collective-permute-start(bf16[128,1024]{1,0:T(8,128)(2,1)S(1)} %bitcast.60), channel_id=1, source_target_pairs={{0,7},{1,0},{2,1},{3,2},{4,3},{5,4},{6,5},{7,6},{8,15},{9,8},{10,9... | collective-permute-start | bytes 786440 | tf_op jit(solution)/shard_map/ppermute | solution.py:200
  61.6 1.3 %copy-start = (bf16[32,128,256]{2,1,0:T(8,128)(2,1)}, bf16[32,128,256]{2,1,0:T(8,128)(2,1)S(1)}, u32[]{:S(2)}) copy-start(bf16[32,128,256]{2,1,0:T(8,128)(2,1)S(1)} %all-to-all-done) | copy-start | bytes 6291460
  82.7 25.0 %all-to-all-start.1 = ((bf16[8,128,512]{2,1,0:T(8,128)(2,1)}), bf16[8,128,512]{2,1,0:T(8,128)(2,1)S(1)}, u32[]{:S(2)}, u32[]{:S(2)}) async-start(bf16[8,128,512]{2,1,0:T(8,128)(2,1)} %bitcast.49), calls=%async_computation.1 | async-start | bytes 2097152 | tf_op jit(solution)/shard_map/all_to_all | solution.py:229

commit v16 on v15

--- a/solution.py
+++ b/solution.py
@@ -67,15 +67,24 @@
     return kernel
 
 
-def full_kernel(local_heads, group_blocks, slab_rows, slabs, base):
+def full_kernel(local_heads, group_blocks, slab_rows, slabs, base, kv_heads, sharing):
     block = MASK_BLOCK_SIZE
     key_count = (SLASH_COUNT + VERT_COUNT) * block
     scale = HEAD_DIMENSION ** (-0.5)
 
-    def kernel(meta_ref, q_ref, k_ref, v_ref, o_ref):
+    def kernel(meta_ref, q_ref, kv_ref, o_ref):
         h = pl.program_id(0) + base
         first = meta_ref[2 * local_heads * SLASH_COUNT]
         me = meta_ref[2 * local_heads * SLASH_COUNT + 1]
+        if kv_heads == 1:
+            k_ref = kv_ref.at[:, pl.ds(0, HEAD_DIMENSION)]
+            v_ref = kv_ref.at[:, pl.ds(HEAD_DIMENSION, HEAD_DIMENSION)]
+        else:
+            kv = h // sharing
+            k_ref = kv_ref.at[:, pl.ds(pl.multiple_of(kv * HEAD_DIMENSION, HEAD_DIMENSION), HEAD_DIMENSION)]
+            v_ref = kv_ref.at[
+                :, pl.ds(pl.multiple_of((kv_heads + kv) * HEAD_DIMENSION, HEAD_DIMENSION), HEAD_DIMENSION)
+            ]
         offs = [meta_ref[h * SLASH_COUNT + j] for j in range(SLASH_COUNT)]
         verts = [meta_ref[local_heads * SLASH_COUNT + h * VERT_COUNT + j] for j in range(VERT_COUNT)]
         vert_starts = [pl.multiple_of(v * block, block) for v in verts]
@@ -122,23 +131,21 @@
     group_rows = queries.shape[0]
     group_blocks = group_rows // MASK_BLOCK_SIZE
     head_size = HEAD_DIMENSION
-    total_rows = all_kv.shape[0]
     value_base = all_kv.shape[1] // (2 * head_size)
     grid_spec = pltpu.PrefetchScalarGridSpec(
         num_scalar_prefetch=1,
         grid=(chunk_heads,),
         in_specs=[
             pl.BlockSpec((group_rows, head_size), lambda h, m: (0, h + base)),
-            pl.BlockSpec((total_rows, head_size), lambda h, m: (0, (h + base) // sharing)),
-            pl.BlockSpec((total_rows, head_size), lambda h, m: (0, value_base + (h + base) // sharing)),
+            pl.BlockSpec(memory_space=pltpu.VMEM),
         ],
         out_specs=pl.BlockSpec((group_rows, head_size), lambda h, m: (0, h)),
     )
     return pl.pallas_call(
-        full_kernel(local_heads, group_blocks, slab_rows, group_rows // slab_rows, base),
+        full_kernel(local_heads, group_blocks, slab_rows, group_rows // slab_rows, base, value_base, sharing),
         grid_spec=grid_spec,
         out_shape=jax.ShapeDtypeStruct((group_rows, chunk_heads * head_size), queries.dtype),
-    )(meta, queries, all_kv, all_kv)
+    )(meta, queries, all_kv)
 
 
 def attend(meta, queries, key_window, value_window, vert_keys, vert_values, local_heads, sharing, base):

time: 130 us -> 130 us (level)
  no operation moved by 1% of the time
where the time goes in v16:
time: 130 us; the launch traced here: 129 us
  Pallas kernels  39.5 us (30%)
  local copies, waits for them, and re-layouts  30.8 us (24%)
  starting transfers between devices  22.1 us (17%)
  blocking collectives  19.6 us (15%)
  waiting for transfers between devices  15.9 us (12%)
    pallas_call x2, Pallas kernels, attend_full(): pl.pallas_call(full_kernel(local_heads, group_blocks, slab_rows, group_ro...  39.5 us
    all_to_all x1, blocking collectives, per_device(): lax.all_to_all(merged, heads_axes, split_axis=0, concat_axis=0, tiled=True)  19.6 us
    unnamed x16, local copies, waits for them, and re-layouts  17.2 us
    ppermute x7, waiting for transfers between devices, per_device(): lax.ppermute(sent, heads_axes, [(i, (i + shift) % head_groups) for i in r...  15.8 us
    ppermute x7, starting transfers between devices, per_device(): lax.ppermute(sent, heads_axes, [(i, (i + shift) % head_groups) for i in r...  9.58 us
    dynamic_slice x8, local copies, waits for them, and re-layouts, per_device(): lax.dynamic_index_in_dim(query_split, (me + shift) % head_groups, 1, keep...  9.16 us
    all_to_all x1, starting transfers between devices, per_device(): lax.all_to_all(spread, ('outer',) + heads_axes, split_axis=0, concat_axis...  7.3 us
    all_to_all x1, starting transfers between devices, per_device(): lax.all_to_all(merged, heads_axes, split_axis=0, concat_axis=0, tiled=True)  5.19 us
  transfers between devices with their start and end apart: 9, of which 3 were waited for; matrix products, arithmetic and copies ran while one was open for 19% of the time, Pallas kernels for 15%

profile of v16, /device:TPU:0, one launch (start us, length us, event | category | flops | bytes accessed | tf_op | source)
XLA Modules:
  0.0 129.0 jit_solution(13991717235429687046)
XLA Ops:
  2.2 1.6 %broadcast_in_dim.15 = bf16[4,8,128,256]{3,2,1,0:T(8,128)(2,1)} broadcast(bf16[8,128,256]{2,1,0:T(8,128)(2,1)S(1)} %copy.25), dimensions={1,2,3} | broadcast | bytes 2621440 | tf_op jit(solution)/shard_map/broadcast_in_dim | solution.py:192
  3.8 7.3 %all-to-all-start = ((bf16[32,128,256]{2,1,0:T(8,128)(2,1)}), bf16[32,128,256]{2,1,0:T(8,128)(2,1)S(1)}, u32[]{:S(2)}, u32[]{:S(2)}) async-start(bf16[32,128,256]{2,1,0:T(8,128)(2,1)} %bitcast.45), calls=%async_computation | async-start | bytes 4194304 | tf_op jit(solution)/shard_map/all_to_all | solution.py:195
  11.2 4.1 %copy.16 = bf16[128,8192]{0,1:T(8,128)(2,1)} copy(bf16[128,8192]{1,0:T(8,128)(2,1)} %param.5) | data formatting | bytes 4194304 | tf_op args[0]
  15.2 2.4 %constant_dynamic-slice_fusion = (bf16[128,1,1024]{0,2,1:T(8,128)(2,1)S(1)}, bf16[128,1,1024]{0,2,1:T(8,128)(2,1)S(1)}, bf16[128,1,1024]{0,2,1:T(8,128)(2,1)S(1)...) fusion(bf16[128,8,1024]{0,2,1:T(8,128)(2,1)} %bitcast.46, ...), kind=kLoop, calls=%fused_computation.10 | loop fusion | bytes 4194336 | tf_op jit(solution)/shard_map/jit(dynamic_index_in_dim)/dynamic_slice | solution.py:205
  17.7 1.8 %copy.18 = bf16[128,1,1024]{2,0,1:T(8,128)(2,1)} copy(bf16[128,1,1024]{0,2,1:T(8,128)(2,1)} %get-tuple-element.11) | data formatting | bytes 524288 | tf_op jit(solution)/shard_map/jit(dynamic_index_in_dim)/dynamic_slice | solution.py:205
  19.8 1.8 %copy.19 = bf16[128,1,1024]{2,0,1:T(8,128)(2,1)} copy(bf16[128,1,1024]{0,2,1:T(8,128)(2,1)} %get-tuple-element.10) | data formatting | bytes 524288 | tf_op jit(solution)/shard_map/jit(dynamic_index_in_dim)/dynamic_slice | solution.py:205
  21.6 1.7 %collective-permute-start.1 = (bf16[128,1024]{1,0:T(8,128)(2,1)}, bf16[128,1024]{1,0:T(8,128)(2,1)}, u32[]{:S(2)}, u32[]{:S(2)}) collective-permute-start(bf16[128,1024]{1,0:T(8,128)(2,1)} %bitcast.56), channel_id=1, source_target_pairs={{0,2},{1,3},{2,4},{3,5},{4,6},{5,7},{6,0},{7,1},{8,10},{9,11},{10,... | collective-permute-start | bytes 786440 | tf_op jit(solution)/shard_map/ppermute | solution.py:207
  23.2 1.8 %copy.20 = bf16[128,1,1024]{2,0,1:T(8,128)(2,1)} copy(bf16[128,1,1024]{0,2,1:T(8,128)(2,1)} %get-tuple-element.9) | data formatting | bytes 524288 | tf_op jit(solution)/shard_map/jit(dynamic_index_in_dim)/dynamic_slice | solution.py:205
  25.0 2.2 %collective-permute-start.2 = (bf16[128,1024]{1,0:T(8,128)(2,1)}, bf16[128,1024]{1,0:T(8,128)(2,1)}, u32[]{:S(2)}, u32[]{:S(2)}) collective-permute-start(bf16[128,1024]{1,0:T(8,128)(2,1)} %bitcast.55), channel_id=1, source_target_pairs={{0,3},{1,4},{2,5},{3,6},{4,7},{5,0},{6,1},{7,2},{8,11},{9,12},{10,... | collective-permute-start | bytes 786440 | tf_op jit(solution)/shard_map/ppermute | solution.py:207
  31.3 8.4 %collective-permute-done = bf16[128,1024]{1,0:T(8,128)(2,1)} collective-permute-done((bf16[128,1024]{1,0:T(8,128)(2,1)}, bf16[128,1024]{1,0:T(8,128)(2,1)}, u32[]{:S(2)}, u32[]{:S(2)}) %collective-permute-start) | collective-permute-done | bytes 262176 | tf_op jit(solution)/shard_map/ppermute | solution.py:207
  39.7 1.7 %bitcast_dynamic-update-slice_fusion.6 = bf16[8,128,1024]{2,1,0:T(8,128)(2,1)} fusion(bf16[8,128,1024]{2,1,0:T(8,128)(2,1)} %bitcast_dynamic-update-slice_fusion.7, bf16[128,1024]{1,0:T(8,128)(2,1)} %collective-permute-done), kind=kLoop, calls=%fused_computation.8 | loop fusion | bytes 524288
  41.3 4.7 %collective-permute-start.6 = (bf16[128,1024]{1,0:T(8,128)(2,1)S(1)}, bf16[128,1024]{1,0:T(8,128)(2,1)S(1)}, u32[]{:S(2)}, u32[]{:S(2)}) collective-permute-start(bf16[128,1024]{1,0:T(8,128)(2,1)S(1)} %bitcast.58), channel_id=1, source_target_pairs={{0,7},{1,0},{2,1},{3,2},{4,3},{5,4},{6,5},{7,6},{8,15},{9,8},{10,9... | collective-permute-start | bytes 786440 | tf_op jit(solution)/shard_map/ppermute | solution.py:207
  46.0 1.7 %bitcast_dynamic-update-slice_fusion.5 = bf16[8,128,1024]{2,1,0:T(8,128)(2,1)} fusion(bf16[8,128,1024]{2,1,0:T(8,128)(2,1)} %bitcast_dynamic-update-slice_fusion.6, bf16[128,1024]{1,0:T(8,128)(2,1)} %collective-permute-done.1), kind=kLoop, calls=%fused_computation.7 | loop fusion | bytes 524288
  47.7 5.7 %collective-permute-done.2 = bf16[128,1024]{1,0:T(8,128)(2,1)} collective-permute-done((bf16[128,1024]{1,0:T(8,128)(2,1)}, bf16[128,1024]{1,0:T(8,128)(2,1)}, u32[]{:S(2)}, u32[]{:S(2)}) %collective-permute-start.2) | collective-permute-done | bytes 262176 | tf_op jit(solution)/shard_map/ppermute | solution.py:207
  53.4 1.7 %bitcast_dynamic-update-slice_fusion.4 = bf16[8,128,1024]{2,1,0:T(8,128)(2,1)} fusion(bf16[8,128,1024]{2,1,0:T(8,128)(2,1)} %bitcast_dynamic-update-slice_fusion.5, bf16[128,1024]{1,0:T(8,128)(2,1)} %collective-permute-done.2), kind=kLoop, calls=%fused_computation.6 | loop fusion | bytes 524288
  55.1 1.7 %bitcast_dynamic-update-slice_fusion.3 = bf16[8,128,1024]{2,1,0:T(8,128)(2,1)} fusion(bf16[8,128,1024]{2,1,0:T(8,128)(2,1)} %bitcast_dynamic-update-slice_fusion.4, bf16[128,1024]{1,0:T(8,128)(2,1)} %collective-permute-done.3), kind=kLoop, calls=%fused_computation.5 | loop fusion | bytes 524288
  56.8 1.7 %collective-permute-done.4 = bf16[128,1024]{1,0:T(8,128)(2,1)} collective-permute-done((bf16[128,1024]{1,0:T(8,128)(2,1)S(1)}, bf16[128,1024]{1,0:T(8,128)(2,1)}, u32[]{:S(2)}, u32[]{:S(2)}) %collective-permute-start.4) | collective-permute-done | bytes 262176 | tf_op jit(solution)/shard_map/ppermute | solution.py:207
  58.5 1.7 %bitcast_dynamic-update-slice_fusion.2 = bf16[8,128,1024]{2,1,0:T(8,128)(2,1)} fusion(bf16[8,128,1024]{2,1,0:T(8,128)(2,1)} %bitcast_dynamic-update-slice_fusion.3, bf16[128,1024]{1,0:T(8,128)(2,1)} %collective-permute-done.4), kind=kLoop, calls=%fused_computation.4 | loop fusion | bytes 524288
  61.6 1.3 %copy-done = bf16[32,128,256]{2,1,0:T(8,128)(2,1)} copy-done((bf16[32,128,256]{2,1,0:T(8,128)(2,1)}, bf16[32,128,256]{2,1,0:T(8,128)(2,1)S(1)}, u32[]{:S(2)}) %copy-start) | copy-done | bytes 2097176
  63.0 19.7 %shard_map.55 = bf16[1024,512]{1,0:T(8,128)(2,1)} custom-call(s32[50]{0:T(128)} %pad_add_fusion.meta_ref, bf16[1024,1024]{1,0:T(8,128)(2,1)} %bitcast.43, bf16[4096,256]{1,0:T(8,128)(2,1)} %bitcast.41), custom_call_target="tpu_custom_call" | custom-call | tf_op jit(solution)/shard_map/pallas_call | solution.py:144
  82.7 5.2 %all-to-all-start.1 = ((bf16[8,128,512]{2,1,0:T(8,128)(2,1)}), bf16[8,128,512]{2,1,0:T(8,128)(2,1)S(1)}, u32[]{:S(2)}, u32[]{:S(2)}) async-start(bf16[8,128,512]{2,1,0:T(8,128)(2,1)} %bitcast.47), calls=%async_computation.1 | async-start | bytes 2097152 | tf_op jit(solution)/shard_map/all_to_all | solution.py:236
  87.9 19.8 %shard_map.56 = bf16[1024,512]{1,0:T(8,128)(2,1)} custom-call(s32[50]{0:T(128)} %pad_add_fusion.meta_ref, bf16[1024,1024]{1,0:T(8,128)(2,1)} %bitcast.44, bf16[4096,256]{1,0:T(8,128)(2,1)} %bitcast.42), custom_call_target="tpu_custom_call" | custom-call | tf_op jit(solution)/shard_map/pallas_call | solution.py:144
  107.7 19.6 %all_to_all.15 = bf16[8,128,512]{2,1,0:T(8,128)(2,1)S(1)} all-to-all(bf16[8,128,512]{2,1,0:T(8,128)(2,1)} %bitcast.48), channel_id=1, replica_groups=mesh['outer'=4,'inner'=2,'grp'=4] {'inner','grp'}, dimensions={0} | all-to-all | bytes 2097152 | tf_op jit(solution)/shard_map/all_to_all | solution.py:236
  127.5 1.5 %copy.27 = bf16[8,16,8,1024]{3,2,0,1:T(8,128)(2,1)} copy(bf16[8,16,8,1024]{3,2,1,0:T(8,128)(2,1)S(1)} %maximum_bitcast_fusion) | data formatting | bytes 4194304 | tf_op jit(solution)/shard_map/reshape | solution.py:238
  (34 shorter events, 8.1 us)
Async XLA Ops:
  3.8 57.9 %all-to-all-start = ((bf16[32,128,256]{2,1,0:T(8,128)(2,1)}), bf16[32,128,256]{2,1,0:T(8,128)(2,1)S(1)}, u32[]{:S(2)}, u32[]{:S(2)}) async-start(bf16[32,128,256]{2,1,0:T(8,128)(2,1)} %bitcast.45), calls=%async_computation | async-start | bytes 4194304 | tf_op jit(solution)/shard_map/all_to_all | solution.py:195
  17.7 11.5 %copy-start.1 = (s32[64,3]{0,1:T(4,128)S(1)}, s32[64,3]{0,1:T(4,128)}, u32[]{:S(2)}) copy-start(s32[64,3]{0,1:T(4,128)} %param.8) | copy-start | bytes 2308
  17.7 11.5 %copy-start.2 = (s32[64,3]{0,1:T(4,128)S(1)}, s32[64,3]{0,1:T(4,128)}, u32[]{:S(2)}) copy-start(s32[64,3]{0,1:T(4,128)} %param.9) | copy-start | bytes 2308
  19.5 20.1 %collective-permute-start = (bf16[128,1024]{1,0:T(8,128)(2,1)}, bf16[128,1024]{1,0:T(8,128)(2,1)}, u32[]{:S(2)}, u32[]{:S(2)}) collective-permute-start(bf16[128,1024]{1,0:T(8,128)(2,1)} %bitcast.57), channel_id=1, source_target_pairs={{0,1},{1,2},{2,3},{3,4},{4,5},{5,6},{6,7},{7,0},{8,9},{9,10},{10,1... | collective-permute-start | bytes 786440 | tf_op jit(solution)/shard_map/ppermute | solution.py:207
  21.6 19.8 %collective-permute-start.1 = (bf16[128,1024]{1,0:T(8,128)(2,1)}, bf16[128,1024]{1,0:T(8,128)(2,1)}, u32[]{:S(2)}, u32[]{:S(2)}) collective-permute-start(bf16[128,1024]{1,0:T(8,128)(2,1)} %bitcast.56), channel_id=1, source_target_pairs={{0,2},{1,3},{2,4},{3,5},{4,6},{5,7},{6,0},{7,1},{8,10},{9,11},{10,... | collective-permute-start | bytes 786440 | tf_op jit(solution)/shard_map/ppermute | solution.py:207
  25.0 28.4 %collective-permute-start.2 = (bf16[128,1024]{1,0:T(8,128)(2,1)}, bf16[128,1024]{1,0:T(8,128)(2,1)}, u32[]{:S(2)}, u32[]{:S(2)}) collective-permute-start(bf16[128,1024]{1,0:T(8,128)(2,1)} %bitcast.55), channel_id=1, source_target_pairs={{0,3},{1,4},{2,5},{3,6},{4,7},{5,0},{6,1},{7,2},{8,11},{9,12},{10,... | collective-permute-start | bytes 786440 | tf_op jit(solution)/shard_map/ppermute | solution.py:207
  28.1 27.0 %collective-permute-start.3 = (bf16[128,1024]{1,0:T(8,128)(2,1)}, bf16[128,1024]{1,0:T(8,128)(2,1)}, u32[]{:S(2)}, u32[]{:S(2)}) collective-permute-start(bf16[128,1024]{1,0:T(8,128)(2,1)} %bitcast.54), channel_id=1, source_target_pairs={{0,4},{1,5},{2,6},{3,7},{4,0},{5,1},{6,2},{7,3},{8,12},{9,13},{10,... | collective-permute-start | bytes 786440 | tf_op jit(solution)/shard_map/ppermute | solution.py:207
  28.8 29.7 %collective-permute-start.4 = (bf16[128,1024]{1,0:T(8,128)(2,1)S(1)}, bf16[128,1024]{1,0:T(8,128)(2,1)}, u32[]{:S(2)}, u32[]{:S(2)}) collective-permute-start(bf16[128,1024]{1,0:T(8,128)(2,1)S(1)} %bitcast.53), channel_id=1, source_target_pairs={{0,5},{1,6},{2,7},{3,0},{4,1},{5,2},{6,3},{7,4},{8,13},{9,14},{10,... | collective-permute-start | bytes 786440 | tf_op jit(solution)/shard_map/ppermute | solution.py:207
  39.6 20.5 %collective-permute-start.5 = (bf16[128,1024]{1,0:T(8,128)(2,1)S(1)}, bf16[128,1024]{1,0:T(8,128)(2,1)S(1)}, u32[]{:S(2)}, u32[]{:S(2)}) collective-permute-start(bf16[128,1024]{1,0:T(8,128)(2,1)S(1)} %bitcast.59), channel_id=1, source_target_pairs={{0,6},{1,7},{2,0},{3,1},{4,2},{5,3},{6,4},{7,5},{8,14},{9,15},{10,... | collective-permute-start | bytes 786440 | tf_op jit(solution)/shard_map/ppermute | solution.py:207
  41.3 19.6 %collective-permute-start.6 = (bf16[128,1024]{1,0:T(8,128)(2,1)S(1)}, bf16[128,1024]{1,0:T(8,128)(2,1)S(1)}, u32[]{:S(2)}, u32[]{:S(2)}) collective-permute-start(bf16[128,1024]{1,0:T(8,128)(2,1)S(1)} %bitcast.58), channel_id=1, source_target_pairs={{0,7},{1,0},{2,1},{3,2},{4,3},{5,4},{6,5},{7,6},{8,15},{9,8},{10,9... | collective-permute-start | bytes 786440 | tf_op jit(solution)/shard_map/ppermute | solution.py:207
  61.6 1.3 %copy-start = (bf16[32,128,256]{2,1,0:T(8,128)(2,1)}, bf16[32,128,256]{2,1,0:T(8,128)(2,1)S(1)}, u32[]{:S(2)}) copy-start(bf16[32,128,256]{2,1,0:T(8,128)(2,1)S(1)} %all-to-all-done) | copy-start | bytes 6291460
  82.7 25.0 %all-to-all-start.1 = ((bf16[8,128,512]{2,1,0:T(8,128)(2,1)}), bf16[8,128,512]{2,1,0:T(8,128)(2,1)S(1)}, u32[]{:S(2)}, u32[]{:S(2)}) async-start(bf16[8,128,512]{2,1,0:T(8,128)(2,1)} %bitcast.47), calls=%async_computation.1 | async-start | bytes 2097152 | tf_op jit(solution)/shard_map/all_to_all | solution.py:236

commit v17 on v16

--- a/solution.py
+++ b/solution.py
@@ -76,20 +76,16 @@
         h = pl.program_id(0) + base
         first = meta_ref[2 * local_heads * SLASH_COUNT]
         me = meta_ref[2 * local_heads * SLASH_COUNT + 1]
-        if kv_heads == 1:
-            k_ref = kv_ref.at[:, pl.ds(0, HEAD_DIMENSION)]
-            v_ref = kv_ref.at[:, pl.ds(HEAD_DIMENSION, HEAD_DIMENSION)]
-        else:
-            kv = h // sharing
-            k_ref = kv_ref.at[:, pl.ds(pl.multiple_of(kv * HEAD_DIMENSION, HEAD_DIMENSION), HEAD_DIMENSION)]
-            v_ref = kv_ref.at[
-                :, pl.ds(pl.multiple_of((kv_heads + kv) * HEAD_DIMENSION, HEAD_DIMENSION), HEAD_DIMENSION)
-            ]
+        kv_cols = pl.ds(pl.multiple_of((h // sharing) * HEAD_DIMENSION, HEAD_DIMENSION), HEAD_DIMENSION)
+
+        def rows(which, start):
+            return kv_ref[start // slab_rows, which, pl.ds(pl.multiple_of(start % slab_rows, block), block), kv_cols]
+
         offs = [meta_ref[h * SLASH_COUNT + j] for j in range(SLASH_COUNT)]
         verts = [meta_ref[local_heads * SLASH_COUNT + h * VERT_COUNT + j] for j in range(VERT_COUNT)]
         vert_starts = [pl.multiple_of(v * block, block) for v in verts]
-        vert_keys = [k_ref[pl.ds(s, block), :] for s in vert_starts]
-        vert_values = [v_ref[pl.ds(s, block), :] for s in vert_starts]
+        vert_keys = [rows(0, s) for s in vert_starts]
+        vert_values = [rows(1, s) for s in vert_starts]
         col = lax.broadcasted_iota(jnp.int32, (block, key_count), 1)
         row = lax.broadcasted_iota(jnp.int32, (block, key_count), 0)
         reach = col % block - row
@@ -101,8 +97,8 @@
             slab = (me - b // slab_blocks + slabs) % slabs
             q = q_ref[pl.ds(pl.multiple_of(slab * slab_rows + (b % slab_blocks) * block, block), block), :]
             starts = [pl.multiple_of(jnp.maximum(qb - offs[j], 0) * block, block) for j in range(SLASH_COUNT)]
-            keys = jnp.concatenate([k_ref[pl.ds(s, block), :] for s in starts] + vert_keys, 0)
-            values = jnp.concatenate([v_ref[pl.ds(s, block), :] for s in starts] + vert_values, 0)
+            keys = jnp.concatenate([rows(0, s) for s in starts] + vert_keys, 0)
+            values = jnp.concatenate([rows(1, s) for s in starts] + vert_values, 0)
             limits = [jnp.where(qb - offs[j] >= 0, offs[j] * block, never) for j in range(SLASH_COUNT)]
             for v in verts:
                 ok = v <= qb
@@ -131,7 +127,7 @@
     group_rows = queries.shape[0]
     group_blocks = group_rows // MASK_BLOCK_SIZE
     head_size = HEAD_DIMENSION
-    value_base = all_kv.shape[1] // (2 * head_size)
+    value_base = all_kv.shape[-1] // head_size
     grid_spec = pltpu.PrefetchScalarGridSpec(
         num_scalar_prefetch=1,
         grid=(chunk_heads,),
@@ -188,7 +184,7 @@
     seq_count = lax.axis_size("outer")
     whole = seq_count * (key_split.size + value_split.size) * key_split.dtype.itemsize
     if whole <= FULL_GATHER_BYTES:
-        kv_rows = jnp.concatenate([key_split, value_split], 2).transpose(1, 0, 2)
+        kv_rows = jnp.stack([key_split, value_split], 0).transpose(2, 0, 1, 3)
         spread = jnp.broadcast_to(kv_rows[None], (seq_count,) + kv_rows.shape).reshape(
             (seq_count * head_groups,) + kv_rows.shape[1:]
         )
@@ -223,7 +219,6 @@
         ]
     )
     if whole <= FULL_GATHER_BYTES:
-        everything = everything.reshape(-1, 2 * local_kv * head_size)
         queries = received.reshape(group_rows, local_heads * head_size)
         chunk_heads = local_heads // OUTPUT_CHUNKS
         pieces = []

time: 130 us -> 130 us (level)
  no operation moved by 1% of the time
where the time goes in v17:
time: 130 us; the launch traced here: 129 us
  Pallas kernels  39.7 us (31%)
  local copies, waits for them, and re-layouts  31.1 us (24%)
  starting transfers between devices  22.1 us (17%)
  blocking collectives  19.6 us (15%)
  waiting for transfers between devices  15.9 us (12%)
    pallas_call x2, Pallas kernels, attend_full(): pl.pallas_call(full_kernel(local_heads, group_blocks, slab_rows, group_ro...  39.7 us
    all_to_all x1, blocking collectives, per_device(): lax.all_to_all(merged, heads_axes, split_axis=0, concat_axis=0, tiled=True)  19.6 us
    unnamed x16, local copies, waits for them, and re-layouts  17.2 us
    ppermute x7, waiting for transfers between devices, per_device(): lax.ppermute(sent, heads_axes, [(i, (i + shift) % head_groups) for i in r...  15.8 us
    ppermute x7, starting transfers between devices, per_device(): lax.ppermute(sent, heads_axes, [(i, (i + shift) % head_groups) for i in r...  9.58 us
    dynamic_slice x8, local copies, waits for them, and re-layouts, per_device(): lax.dynamic_index_in_dim(query_split, (me + shift) % head_groups, 1, keep...  9.16 us
    all_to_all x1, starting transfers between devices, per_device(): lax.all_to_all(spread, ('outer',) + heads_axes, split_axis=0, concat_axis...  7.3 us
    all_to_all x1, starting transfers between devices, per_device(): lax.all_to_all(merged, heads_axes, split_axis=0, concat_axis=0, tiled=True)  5.19 us
  transfers between devices with their start and end apart: 9, of which 3 were waited for; matrix products, arithmetic and copies ran while one was open for 19% of the time, Pallas kernels for 15%

profile of v17, /device:TPU:0, one launch (start us, length us, event | category | flops | bytes accessed | tf_op | source)
XLA Modules:
  0.0 129.5 jit_solution(6704735711941308697)
XLA Ops:
  2.2 1.8 %broadcast_in_dim.15 = bf16[4,8,2,128,128]{4,3,2,1,0:T(8,128)(2,1)} broadcast(bf16[8,2,128,128]{3,2,1,0:T(8,128)(2,1)S(1)} %copy.25), dimensions={1,2,3,4} | broadcast | bytes 2621440 | tf_op jit(solution)/shard_map/broadcast_in_dim | solution.py:188
  4.0 7.3 %all-to-all-start = ((bf16[32,2,128,128]{3,2,1,0:T(8,128)(2,1)}), bf16[32,2,128,128]{3,2,1,0:T(8,128)(2,1)S(1)}, u32[]{:S(2)}, u32[]{:S(2)}) async-start(bf16[32,2,128,128]{3,2,1,0:T(8,128)(2,1)} %bitcast.44), calls=%async_computation | async-start | bytes 4194304 | tf_op jit(solution)/shard_map/all_to_all | solution.py:191
  11.4 4.1 %copy.16 = bf16[128,8192]{0,1:T(8,128)(2,1)} copy(bf16[128,8192]{1,0:T(8,128)(2,1)} %param.5) | data formatting | bytes 4194304 | tf_op args[0]
  15.5 2.4 %constant_dynamic-slice_fusion = (bf16[128,1,1024]{0,2,1:T(8,128)(2,1)S(1)}, bf16[128,1,1024]{0,2,1:T(8,128)(2,1)S(1)}, bf16[128,1,1024]{0,2,1:T(8,128)(2,1)S(1)...) fusion(bf16[128,8,1024]{0,2,1:T(8,128)(2,1)} %bitcast.45, ...), kind=kLoop, calls=%fused_computation.10 | loop fusion | bytes 4194336 | tf_op jit(solution)/shard_map/jit(dynamic_index_in_dim)/dynamic_slice | solution.py:201
  17.9 1.8 %copy.18 = bf16[128,1,1024]{2,0,1:T(8,128)(2,1)} copy(bf16[128,1,1024]{0,2,1:T(8,128)(2,1)} %get-tuple-element.11) | data formatting | bytes 524288 | tf_op jit(solution)/shard_map/jit(dynamic_index_in_dim)/dynamic_slice | solution.py:201
  20.0 1.8 %copy.19 = bf16[128,1,1024]{2,0,1:T(8,128)(2,1)} copy(bf16[128,1,1024]{0,2,1:T(8,128)(2,1)} %get-tuple-element.10) | data formatting | bytes 524288 | tf_op jit(solution)/shard_map/jit(dynamic_index_in_dim)/dynamic_slice | solution.py:201
  21.8 1.7 %collective-permute-start.1 = (bf16[128,1024]{1,0:T(8,128)(2,1)}, bf16[128,1024]{1,0:T(8,128)(2,1)}, u32[]{:S(2)}, u32[]{:S(2)}) collective-permute-start(bf16[128,1024]{1,0:T(8,128)(2,1)} %bitcast.55), channel_id=1, source_target_pairs={{0,2},{1,3},{2,4},{3,5},{4,6},{5,7},{6,0},{7,1},{8,10},{9,11},{10,... | collective-permute-start | bytes 786440 | tf_op jit(solution)/shard_map/ppermute | solution.py:203
  23.5 1.8 %copy.20 = bf16[128,1,1024]{2,0,1:T(8,128)(2,1)} copy(bf16[128,1,1024]{0,2,1:T(8,128)(2,1)} %get-tuple-element.9) | data formatting | bytes 524288 | tf_op jit(solution)/shard_map/jit(dynamic_index_in_dim)/dynamic_slice | solution.py:201
  25.3 2.2 %collective-permute-start.2 = (bf16[128,1024]{1,0:T(8,128)(2,1)}, bf16[128,1024]{1,0:T(8,128)(2,1)}, u32[]{:S(2)}, u32[]{:S(2)}) collective-permute-start(bf16[128,1024]{1,0:T(8,128)(2,1)} %bitcast.54), channel_id=1, source_target_pairs={{0,3},{1,4},{2,5},{3,6},{4,7},{5,0},{6,1},{7,2},{8,11},{9,12},{10,... | collective-permute-start | bytes 786440 | tf_op jit(solution)/shard_map/ppermute | solution.py:203
  31.5 8.4 %collective-permute-done = bf16[128,1024]{1,0:T(8,128)(2,1)} collective-permute-done((bf16[128,1024]{1,0:T(8,128)(2,1)}, bf16[128,1024]{1,0:T(8,128)(2,1)}, u32[]{:S(2)}, u32[]{:S(2)}) %collective-permute-start) | collective-permute-done | bytes 262176 | tf_op jit(solution)/shard_map/ppermute | solution.py:203
  39.9 1.7 %bitcast_dynamic-update-slice_fusion.6 = bf16[8,128,1024]{2,1,0:T(8,128)(2,1)} fusion(bf16[8,128,1024]{2,1,0:T(8,128)(2,1)} %bitcast_dynamic-update-slice_fusion.7, bf16[128,1024]{1,0:T(8,128)(2,1)} %collective-permute-done), kind=kLoop, calls=%fused_computation.8 | loop fusion | bytes 524288
  41.6 4.7 %collective-permute-start.6 = (bf16[128,1024]{1,0:T(8,128)(2,1)S(1)}, bf16[128,1024]{1,0:T(8,128)(2,1)S(1)}, u32[]{:S(2)}, u32[]{:S(2)}) collective-permute-start(bf16[128,1024]{1,0:T(8,128)(2,1)S(1)} %bitcast.57), channel_id=1, source_target_pairs={{0,7},{1,0},{2,1},{3,2},{4,3},{5,4},{6,5},{7,6},{8,15},{9,8},{10,9... | collective-permute-start | bytes 786440 | tf_op jit(solution)/shard_map/ppermute | solution.py:203
  46.2 1.7 %bitcast_dynamic-update-slice_fusion.5 = bf16[8,128,1024]{2,1,0:T(8,128)(2,1)} fusion(bf16[8,128,1024]{2,1,0:T(8,128)(2,1)} %bitcast_dynamic-update-slice_fusion.6, bf16[128,1024]{1,0:T(8,128)(2,1)} %collective-permute-done.1), kind=kLoop, calls=%fused_computation.7 | loop fusion | bytes 524288
  47.9 5.7 %collective-permute-done.2 = bf16[128,1024]{1,0:T(8,128)(2,1)} collective-permute-done((bf16[128,1024]{1,0:T(8,128)(2,1)}, bf16[128,1024]{1,0:T(8,128)(2,1)}, u32[]{:S(2)}, u32[]{:S(2)}) %collective-permute-start.2) | collective-permute-done | bytes 262176 | tf_op jit(solution)/shard_map/ppermute | solution.py:203
  53.6 1.7 %bitcast_dynamic-update-slice_fusion.4 = bf16[8,128,1024]{2,1,0:T(8,128)(2,1)} fusion(bf16[8,128,1024]{2,1,0:T(8,128)(2,1)} %bitcast_dynamic-update-slice_fusion.5, bf16[128,1024]{1,0:T(8,128)(2,1)} %collective-permute-done.2), kind=kLoop, calls=%fused_computation.6 | loop fusion | bytes 524288
  55.3 1.7 %bitcast_dynamic-update-slice_fusion.3 = bf16[8,128,1024]{2,1,0:T(8,128)(2,1)} fusion(bf16[8,128,1024]{2,1,0:T(8,128)(2,1)} %bitcast_dynamic-update-slice_fusion.4, bf16[128,1024]{1,0:T(8,128)(2,1)} %collective-permute-done.3), kind=kLoop, calls=%fused_computation.5 | loop fusion | bytes 524288
  57.0 1.7 %collective-permute-done.4 = bf16[128,1024]{1,0:T(8,128)(2,1)} collective-permute-done((bf16[128,1024]{1,0:T(8,128)(2,1)S(1)}, bf16[128,1024]{1,0:T(8,128)(2,1)}, u32[]{:S(2)}, u32[]{:S(2)}) %collective-permute-start.4) | collective-permute-done | bytes 262176 | tf_op jit(solution)/shard_map/ppermute | solution.py:203
  58.7 1.7 %bitcast_dynamic-update-slice_fusion.2 = bf16[8,128,1024]{2,1,0:T(8,128)(2,1)} fusion(bf16[8,128,1024]{2,1,0:T(8,128)(2,1)} %bitcast_dynamic-update-slice_fusion.3, bf16[128,1024]{1,0:T(8,128)(2,1)} %collective-permute-done.4), kind=kLoop, calls=%fused_computation.4 | loop fusion | bytes 524288
  61.9 1.3 %copy-done = bf16[32,2,128,128]{3,2,1,0:T(8,128)(2,1)} copy-done((bf16[32,2,128,128]{3,2,1,0:T(8,128)(2,1)}, bf16[32,2,128,128]{3,2,1,0:T(8,128)(2,1)S(1)}, u32[]{:S(2)}) %copy-start) | copy-done | bytes 2097176
  63.2 19.8 %shard_map.55 = bf16[1024,512]{1,0:T(8,128)(2,1)} custom-call(s32[50]{0:T(128)} %pad_add_fusion.meta_ref, bf16[1024,1024]{1,0:T(8,128)(2,1)} %bitcast.42, bf16[32,2,128,128]{3,2,1,0:T(8,128)(2,1)} %copy-done), custom_call_target="tpu_custom_call" | custom-call | tf_op jit(solution)/shard_map/pallas_call | solution.py:140
  83.0 5.2 %all-to-all-start.1 = ((bf16[8,128,512]{2,1,0:T(8,128)(2,1)}), bf16[8,128,512]{2,1,0:T(8,128)(2,1)S(1)}, u32[]{:S(2)}, u32[]{:S(2)}) async-start(bf16[8,128,512]{2,1,0:T(8,128)(2,1)} %bitcast.46), calls=%async_computation.1 | async-start | bytes 2097152 | tf_op jit(solution)/shard_map/all_to_all | solution.py:231
  88.2 19.9 %shard_map.56 = bf16[1024,512]{1,0:T(8,128)(2,1)} custom-call(s32[50]{0:T(128)} %pad_add_fusion.meta_ref, bf16[1024,1024]{1,0:T(8,128)(2,1)} %bitcast.43, bf16[32,2,128,128]{3,2,1,0:T(8,128)(2,1)} %copy-done), custom_call_target="tpu_custom_call" | custom-call | tf_op jit(solution)/shard_map/pallas_call | solution.py:140
  108.1 19.6 %all_to_all.15 = bf16[8,128,512]{2,1,0:T(8,128)(2,1)S(1)} all-to-all(bf16[8,128,512]{2,1,0:T(8,128)(2,1)} %bitcast.47), channel_id=1, replica_groups=mesh['outer'=4,'inner'=2,'grp'=4] {'inner','grp'}, dimensions={0} | all-to-all | bytes 2097152 | tf_op jit(solution)/shard_map/all_to_all | solution.py:231
  127.9 1.5 %copy.27 = bf16[8,16,8,1024]{3,2,0,1:T(8,128)(2,1)} copy(bf16[8,16,8,1024]{3,2,1,0:T(8,128)(2,1)S(1)} %maximum_bitcast_fusion) | data formatting | bytes 4194304 | tf_op jit(solution)/shard_map/reshape | solution.py:233
  (34 shorter events, 8.1 us)
Async XLA Ops:
  4.0 57.9 %all-to-all-start = ((bf16[32,2,128,128]{3,2,1,0:T(8,128)(2,1)}), bf16[32,2,128,128]{3,2,1,0:T(8,128)(2,1)S(1)}, u32[]{:S(2)}, u32[]{:S(2)}) async-start(bf16[32,2,128,128]{3,2,1,0:T(8,128)(2,1)} %bitcast.44), calls=%async_computation | async-start | bytes 4194304 | tf_op jit(solution)/shard_map/all_to_all | solution.py:191
  17.9 11.5 %copy-start.1 = (s32[64,3]{0,1:T(4,128)S(1)}, s32[64,3]{0,1:T(4,128)}, u32[]{:S(2)}) copy-start(s32[64,3]{0,1:T(4,128)} %param.8) | copy-start | bytes 2308
  17.9 11.5 %copy-start.2 = (s32[64,3]{0,1:T(4,128)S(1)}, s32[64,3]{0,1:T(4,128)}, u32[]{:S(2)}) copy-start(s32[64,3]{0,1:T(4,128)} %param.9) | copy-start | bytes 2308
  19.8 20.1 %collective-permute-start = (bf16[128,1024]{1,0:T(8,128)(2,1)}, bf16[128,1024]{1,0:T(8,128)(2,1)}, u32[]{:S(2)}, u32[]{:S(2)}) collective-permute-start(bf16[128,1024]{1,0:T(8,128)(2,1)} %bitcast.56), channel_id=1, source_target_pairs={{0,1},{1,2},{2,3},{3,4},{4,5},{5,6},{6,7},{7,0},{8,9},{9,10},{10,1... | collective-permute-start | bytes 786440 | tf_op jit(solution)/shard_map/ppermute | solution.py:203
  21.8 19.8 %collective-permute-start.1 = (bf16[128,1024]{1,0:T(8,128)(2,1)}, bf16[128,1024]{1,0:T(8,128)(2,1)}, u32[]{:S(2)}, u32[]{:S(2)}) collective-permute-start(bf16[128,1024]{1,0:T(8,128)(2,1)} %bitcast.55), channel_id=1, source_target_pairs={{0,2},{1,3},{2,4},{3,5},{4,6},{5,7},{6,0},{7,1},{8,10},{9,11},{10,... | collective-permute-start | bytes 786440 | tf_op jit(solution)/shard_map/ppermute | solution.py:203
  25.3 28.4 %collective-permute-start.2 = (bf16[128,1024]{1,0:T(8,128)(2,1)}, bf16[128,1024]{1,0:T(8,128)(2,1)}, u32[]{:S(2)}, u32[]{:S(2)}) collective-permute-start(bf16[128,1024]{1,0:T(8,128)(2,1)} %bitcast.54), channel_id=1, source_target_pairs={{0,3},{1,4},{2,5},{3,6},{4,7},{5,0},{6,1},{7,2},{8,11},{9,12},{10,... | collective-permute-start | bytes 786440 | tf_op jit(solution)/shard_map/ppermute | solution.py:203
  28.4 27.0 %collective-permute-start.3 = (bf16[128,1024]{1,0:T(8,128)(2,1)}, bf16[128,1024]{1,0:T(8,128)(2,1)}, u32[]{:S(2)}, u32[]{:S(2)}) collective-permute-start(bf16[128,1024]{1,0:T(8,128)(2,1)} %bitcast.53), channel_id=1, source_target_pairs={{0,4},{1,5},{2,6},{3,7},{4,0},{5,1},{6,2},{7,3},{8,12},{9,13},{10,... | collective-permute-start | bytes 786440 | tf_op jit(solution)/shard_map/ppermute | solution.py:203
  29.1 29.7 %collective-permute-start.4 = (bf16[128,1024]{1,0:T(8,128)(2,1)S(1)}, bf16[128,1024]{1,0:T(8,128)(2,1)}, u32[]{:S(2)}, u32[]{:S(2)}) collective-permute-start(bf16[128,1024]{1,0:T(8,128)(2,1)S(1)} %bitcast.52), channel_id=1, source_target_pairs={{0,5},{1,6},{2,7},{3,0},{4,1},{5,2},{6,3},{7,4},{8,13},{9,14},{10,... | collective-permute-start | bytes 786440 | tf_op jit(solution)/shard_map/ppermute | solution.py:203
  39.9 20.5 %collective-permute-start.5 = (bf16[128,1024]{1,0:T(8,128)(2,1)S(1)}, bf16[128,1024]{1,0:T(8,128)(2,1)S(1)}, u32[]{:S(2)}, u32[]{:S(2)}) collective-permute-start(bf16[128,1024]{1,0:T(8,128)(2,1)S(1)} %bitcast.58), channel_id=1, source_target_pairs={{0,6},{1,7},{2,0},{3,1},{4,2},{5,3},{6,4},{7,5},{8,14},{9,15},{10,... | collective-permute-start | bytes 786440 | tf_op jit(solution)/shard_map/ppermute | solution.py:203
  41.6 19.6 %collective-permute-start.6 = (bf16[128,1024]{1,0:T(8,128)(2,1)S(1)}, bf16[128,1024]{1,0:T(8,128)(2,1)S(1)}, u32[]{:S(2)}, u32[]{:S(2)}) collective-permute-start(bf16[128,1024]{1,0:T(8,128)(2,1)S(1)} %bitcast.57), channel_id=1, source_target_pairs={{0,7},{1,0},{2,1},{3,2},{4,3},{5,4},{6,5},{7,6},{8,15},{9,8},{10,9... | collective-permute-start | bytes 786440 | tf_op jit(solution)/shard_map/ppermute | solution.py:203
  61.9 1.3 %copy-start = (bf16[32,2,128,128]{3,2,1,0:T(8,128)(2,1)}, bf16[32,2,128,128]{3,2,1,0:T(8,128)(2,1)S(1)}, u32[]{:S(2)}) copy-start(bf16[32,2,128,128]{3,2,1,0:T(8,128)(2,1)S(1)} %all-to-all-done.kv_ref) | copy-start | bytes 6291460
  83.0 25.1 %all-to-all-start.1 = ((bf16[8,128,512]{2,1,0:T(8,128)(2,1)}), bf16[8,128,512]{2,1,0:T(8,128)(2,1)S(1)}, u32[]{:S(2)}, u32[]{:S(2)}) async-start(bf16[8,128,512]{2,1,0:T(8,128)(2,1)} %bitcast.46), calls=%async_computation.1 | async-start | bytes 2097152 | tf_op jit(solution)/shard_map/all_to_all | solution.py:231
